TPU v7x, 256 devices: a whole 4x4x8 slice. The times are simulated.
256 devices in a mesh: gz: 32 (over x, z_hi, core), gy: 8 (over y, z_lo).
Axes of the slice: x: 4, y: 4, z: 8 (z_hi: 4, z_lo: 2; z = z_hi * 2 + z_lo), core: 2. Of those that a mesh axis runs over, the one named last changes fastest.
Arguments:
- saved_order_parameter: float32 [256, 128, 512], P('gz', 'gy'), may hold values from 0 to 1
- saved_heat_level: float32 [256, 128, 512], P('gz', 'gy'), may hold values from 0 to 1.5
- kinetic_rate_field: float32 [256, 128, 512], P('gz', 'gy'), may hold values from 0.5 to 2
- order_parameter_adjoint_seed: float32 [256, 128, 512], P('gz', 'gy'), may hold values from -6 to 6
- heat_level_adjoint_seed: float32 [256, 128, 512], P('gz', 'gy'), may hold values from -6 to 6
Outputs:
- start_phase: float32 [256, 128, 512], P('gz', 'gy')
- start_temp: float32 [256, 128, 512], P('gz', 'gy')
- grad_mobility: float32 [256, 128, 512], P('gz', 'gy')
All inputs are finite; a program needn't handle non-finite values.
Results may differ from a plain program's by a relative error of at most 0.00002.
Values sent between devices are 32-bit elements; how exact they have to be, the bound alone decides.
No kernel may reach another device: no remote copies, remote signals or barrier semaphores. Data moves between devices by JAX's collectives and lax.ppermute only.
A program may use at most 64 MiB of HBM per device.

v0:
```python
import jax
import jax.numpy as jnp
from jax import lax
from jax.sharding import PartitionSpec as P

TIME_STEP = 0.15
ENERGY_SCALE = 0.5
ANISOTROPY = 0.05
GRAD_FLOOR = 0.01
LATENT_HEAT = 1.8
DRIVE_SCALE = 0.9
DRIVE_SHARP = 10.0
MELT_POINT = 1.0


def from_behind(block, axis, distance):
    devices = range(lax.axis_size(axis))
    route = [(i - distance, i) for i in devices if i - distance in devices]
    return lax.ppermute(block, axis, route)


def extended(cells, sides, width):
    for axis, dim in sides:
        count = lax.axis_size(axis)
        ends = count - 1
        head = lax.slice_in_dim(cells, 0, width, axis=dim)
        tail = lax.slice_in_dim(cells, cells.shape[dim] - width, cells.shape[dim], axis=dim)
        cells = jnp.concatenate(
            [
                lax.ppermute(tail, axis, [(i, (i + 1) % count) for i in range(ends)]),
                cells,
                lax.ppermute(head, axis, [((i + 1) % count, i) for i in range(ends)]),
            ],
            axis=dim,
        )
    return cells


def advance_solver_step(phase_wide, temp_wide, kinetic_rate_field):
    padded = jnp.pad(phase_wide, ((0, 0), (0, 0), (2, 2)))
    grad_z = 0.5 * (padded[2:, 1:-1, 1:-1] - padded[:-2, 1:-1, 1:-1])
    grad_y = 0.5 * (padded[1:-1, 2:, 1:-1] - padded[1:-1, :-2, 1:-1])
    grad_x = 0.5 * (padded[1:-1, 1:-1, 2:] - padded[1:-1, 1:-1, :-2])
    sq_z = grad_z * grad_z
    sq_y = grad_y * grad_y
    sq_x = grad_x * grad_x
    squared = sq_z + sq_y + sq_x + GRAD_FLOOR
    quartic = (sq_z * sq_z + sq_y * sq_y + sq_x * sq_x) / (squared * squared)
    anisotropy = 1.0 + ANISOTROPY * (4.0 * quartic - 3.0)
    aniso_sq = anisotropy * anisotropy
    factor_a = 16.0 * ANISOTROPY * anisotropy / squared
    flux_z = ENERGY_SCALE * (aniso_sq * grad_z + factor_a * grad_z * (sq_z - quartic * squared))
    flux_y = ENERGY_SCALE * (aniso_sq * grad_y + factor_a * grad_y * (sq_y - quartic * squared))
    flux_x = ENERGY_SCALE * (aniso_sq * grad_x + factor_a * grad_x * (sq_x - quartic * squared))
    divergence = 0.5 * (flux_z[2:, 1:-1, 1:-1] - flux_z[:-2, 1:-1, 1:-1])
    divergence = divergence + 0.5 * (flux_y[1:-1, 2:, 1:-1] - flux_y[1:-1, :-2, 1:-1])
    divergence = divergence + 0.5 * (flux_x[1:-1, 1:-1, 2:] - flux_x[1:-1, 1:-1, :-2])
    phase_now = phase_wide[2:-2, 2:-2]
    temp_now = temp_wide[2:-2, 2:-2]
    driving = DRIVE_SCALE / jnp.pi * jnp.arctan(DRIVE_SHARP * (MELT_POINT - temp_now))
    growth = kinetic_rate_field * (
        divergence + phase_now * (1.0 - phase_now) * (phase_now - 0.5 + driving)
    )
    new_phase = phase_now + TIME_STEP * growth
    temp_x = jnp.pad(temp_now, ((0, 0), (0, 0), (1, 1)))
    laplacian = (
        temp_wide[3:-1, 2:-2]
        + temp_wide[1:-3, 2:-2]
        + temp_wide[2:-2, 3:-1]
        + temp_wide[2:-2, 1:-3]
    )
    laplacian = laplacian + temp_x[:, :, 2:] + temp_x[:, :, :-2] - 6.0 * temp_now
    new_temp = temp_now + TIME_STEP * laplacian + LATENT_HEAT * (new_phase - phase_now)
    return (new_phase, new_temp)


def fold_rims(sensitivity_order_parameter, sensitivity_heat_level):
    stacked = jnp.stack((sensitivity_order_parameter, sensitivity_heat_level))
    lower_rim = stacked[:, :2]
    upper_rim = stacked[:, -2:]
    middle = stacked[:, 2:-2]
    from_above = from_behind(lower_rim, "gz", -1)
    from_below = from_behind(upper_rim, "gz", 1)
    middle = jnp.concatenate(
        (middle[:, :2] + from_below, middle[:, 2:-2], middle[:, -2:] + from_above), axis=1
    )
    lower_rim = middle[:, :, :2]
    upper_rim = middle[:, :, -2:]
    middle = middle[:, :, 2:-2]
    from_above = from_behind(lower_rim, "gy", -1)
    from_below = from_behind(upper_rim, "gy", 1)
    middle = jnp.concatenate(
        (middle[:, :, :2] + from_below, middle[:, :, 2:-2], middle[:, :, -2:] + from_above), axis=2
    )
    return (middle[0], middle[1])


def body(
    saved_order_parameter,
    saved_heat_level,
    kinetic_rate_field,
    order_parameter_adjoint_seed,
    heat_level_adjoint_seed,
):
    initial_extended = extended(
        jnp.stack((saved_order_parameter, saved_heat_level)), (("gz", 1), ("gy", 2)), 2
    )
    succeeding_order_parameter, succeeding_heat_level = advance_solver_step(
        initial_extended[0], initial_extended[1], kinetic_rate_field
    )
    state_wide = extended(
        jnp.stack((succeeding_order_parameter, succeeding_heat_level)), (("gz", 1), ("gy", 2)), 2
    )
    discarded_result, sensitivity_latest = jax.vjp(
        advance_solver_step, state_wide[0], state_wide[1], kinetic_rate_field
    )
    sensitivity_order_parameter, sensitivity_heat_level, latest_kinetic_rate = sensitivity_latest(
        (order_parameter_adjoint_seed, heat_level_adjoint_seed)
    )
    halfway_order_parameter, halfway_heat_level = fold_rims(
        sensitivity_order_parameter, sensitivity_heat_level
    )
    discarded_result, prior_backward_sweep = jax.vjp(
        advance_solver_step, initial_extended[0], initial_extended[1], kinetic_rate_field
    )
    sensitivity_order_parameter, sensitivity_heat_level, early_mob = prior_backward_sweep(
        (halfway_order_parameter, halfway_heat_level)
    )
    start_phase, start_temp = fold_rims(sensitivity_order_parameter, sensitivity_heat_level)
    return (start_phase, start_temp, latest_kinetic_rate + early_mob)


def solution(mesh):
    return jax.shard_map(
        body,
        mesh=mesh,
        in_specs=(
            P("gz", "gy", None),
            P("gz", "gy", None),
            P("gz", "gy", None),
            P("gz", "gy", None),
            P("gz", "gy", None),
        ),
        out_specs=(P("gz", "gy", None), P("gz", "gy", None), P("gz", "gy", None)),
        check_vma=False,
    )
```

profile of v0, /device:TPU:14, one launch (start us, length us, event | category | flops | bytes accessed | tf_op | source)
XLA Modules:
  0.0 130.1 jit_solution(12175630193604381503)
XLA Ops:
  0.7 1.0 pad_maximum_fusion.13
  1.7 1.9 %collective-permute-start = (f32[2,2,16,512]{3,2,1,0:T(8,128)S(1)}, f32[2,2,16,512]{3,2,1,0:T(8,128)S(1)}, u32[]{:S(2)}, u32[]{:S(2)}) collective-permute-start(f32[2,2,16,512]{3,2,1,0:T(8,128)S(1)} %get-tuple-element.80), channel_id=1, source_target_pairs={{0,8},{8,16},{16,24},{24,32},{32,40},{40,48},{48,56},{56,64},{64,7... | collective-permute-start | bytes 393224 | tf_op jit(solution)/shard_map/ppermute | solution.py:30
  3.6 7.9 %collective-permute-start.1 = (f32[2,2,16,512]{3,2,1,0:T(8,128)S(1)}, f32[2,2,16,512]{3,2,1,0:T(8,128)S(1)}, u32[]{:S(2)}, u32[]{:S(2)}) collective-permute-start(f32[2,2,16,512]{3,2,1,0:T(8,128)S(1)} %get-tuple-element.81), channel_id=1, source_target_pairs={{8,0},{16,8},{24,16},{32,24},{40,32},{48,40},{56,48},{64,56},{72,6... | collective-permute-start | bytes 393224 | tf_op jit(solution)/shard_map/ppermute | solution.py:32
  11.5 0.8 collective-permute-done
  12.3 3.1 %collective-permute-done.1 = f32[2,2,16,512]{3,2,1,0:T(8,128)S(1)} collective-permute-done((f32[2,2,16,512]{3,2,1,0:T(8,128)S(1)}, f32[2,2,16,512]{3,2,1,0:T(8,128)S(1)}, u32[]{:S(2)}, u32[]{:S(2)}) %collective-permute-start.1) | collective-permute-done | bytes 131104 | tf_op jit(solution)/shard_map/ppermute | solution.py:32
  15.4 1.2 pad_maximum_fusion.21
  16.6 1.9 %collective-permute-start.2 = (f32[2,12,2,512]{3,2,1,0:T(2,128)S(1)}, f32[2,12,2,512]{3,2,1,0:T(2,128)S(1)}, u32[]{:S(2)}, u32[]{:S(2)}) collective-permute-start(f32[2,12,2,512]{3,2,1,0:T(2,128)S(1)} %get-tuple-element.70), channel_id=1, source_target_pairs={{0,1},{1,2},{2,3},{3,4},{4,5},{5,6},{6,7},{8,9},{9,10},{10,11},{11... | collective-permute-start | bytes 294920 | tf_op jit(solution)/shard_map/ppermute | solution.py:30
  18.5 4.8 %collective-permute-start.3 = (f32[2,12,2,512]{3,2,1,0:T(2,128)S(1)}, f32[2,12,2,512]{3,2,1,0:T(2,128)S(1)}, u32[]{:S(2)}, u32[]{:S(2)}) collective-permute-start(f32[2,12,2,512]{3,2,1,0:T(2,128)S(1)} %get-tuple-element.71), channel_id=1, source_target_pairs={{1,0},{2,1},{3,2},{4,3},{5,4},{6,5},{7,6},{9,8},{10,9},{11,10},{12... | collective-permute-start | bytes 294920 | tf_op jit(solution)/shard_map/ppermute | solution.py:32
  23.4 1.3 %collective-permute-done.2 = f32[2,12,2,512]{3,2,1,0:T(2,128)S(1)} collective-permute-done((f32[2,12,2,512]{3,2,1,0:T(2,128)S(1)}, f32[2,12,2,512]{3,2,1,0:T(2,128)S(1)}, u32[]{:S(2)}, u32[]{:S(2)}) %collective-permute-start.2) | collective-permute-done | bytes 98336 | tf_op jit(solution)/shard_map/ppermute | solution.py:30
  24.7 1.5 %collective-permute-done.3 = f32[2,12,2,512]{3,2,1,0:T(2,128)S(1)} collective-permute-done((f32[2,12,2,512]{3,2,1,0:T(2,128)S(1)}, f32[2,12,2,512]{3,2,1,0:T(2,128)S(1)}, u32[]{:S(2)}, u32[]{:S(2)}) %collective-permute-start.3) | collective-permute-done | bytes 98336 | tf_op jit(solution)/shard_map/ppermute | solution.py:32
  26.6 1.0 add_multiply_fusion.11
  27.6 0.6 add_multiply_fusion.10
  28.6 0.7 fusion.79
  29.6 2.1 %collective-permute-start.4 = (f32[2,2,16,512]{3,2,1,0:T(8,128)S(1)}, f32[2,2,16,512]{3,2,1,0:T(8,128)S(1)}, u32[]{:S(2)}, u32[]{:S(2)}) collective-permute-start(f32[2,2,16,512]{3,2,1,0:T(8,128)S(1)} %get-tuple-element.78), channel_id=1, source_target_pairs={{0,8},{8,16},{16,24},{24,32},{32,40},{40,48},{48,56},{56,64},{64,7... | collective-permute-start | bytes 393224 | tf_op jit(solution)/shard_map/ppermute | solution.py:30
  31.7 6.7 %collective-permute-start.5 = (f32[2,2,16,512]{3,2,1,0:T(8,128)S(1)}, f32[2,2,16,512]{3,2,1,0:T(8,128)S(1)}, u32[]{:S(2)}, u32[]{:S(2)}) collective-permute-start(f32[2,2,16,512]{3,2,1,0:T(8,128)S(1)} %get-tuple-element.79), channel_id=1, source_target_pairs={{8,0},{16,8},{24,16},{32,24},{40,32},{48,40},{56,48},{64,56},{72,6... | collective-permute-start | bytes 393224 | tf_op jit(solution)/shard_map/ppermute | solution.py:32
  38.3 1.2 collective-permute-done.4
  39.5 1.3 %collective-permute-done.5 = f32[2,2,16,512]{3,2,1,0:T(8,128)S(1)} collective-permute-done((f32[2,2,16,512]{3,2,1,0:T(8,128)S(1)}, f32[2,2,16,512]{3,2,1,0:T(8,128)S(1)}, u32[]{:S(2)}, u32[]{:S(2)}) %collective-permute-start.5) | collective-permute-done | bytes 131104 | tf_op jit(solution)/shard_map/ppermute | solution.py:32
  40.9 4.6 %collective-permute-start.6 = (f32[2,12,2,512]{3,2,1,0:T(2,128)S(1)}, f32[2,12,2,512]{3,2,1,0:T(2,128)S(1)}, u32[]{:S(2)}, u32[]{:S(2)}) collective-permute-start(f32[2,12,2,512]{3,2,1,0:T(2,128)S(1)} %get-tuple-element.68), channel_id=1, source_target_pairs={{0,1},{1,2},{2,3},{3,4},{4,5},{5,6},{6,7},{8,9},{9,10},{10,11},{11... | collective-permute-start | bytes 294920 | tf_op jit(solution)/shard_map/ppermute | solution.py:30
  45.6 2.1 %collective-permute-start.7 = (f32[2,12,2,512]{3,2,1,0:T(2,128)S(1)}, f32[2,12,2,512]{3,2,1,0:T(2,128)S(1)}, u32[]{:S(2)}, u32[]{:S(2)}) collective-permute-start(f32[2,12,2,512]{3,2,1,0:T(2,128)S(1)} %get-tuple-element.69), channel_id=1, source_target_pairs={{1,0},{2,1},{3,2},{4,3},{5,4},{6,5},{7,6},{9,8},{10,9},{11,10},{12... | collective-permute-start | bytes 294920 | tf_op jit(solution)/shard_map/ppermute | solution.py:32
  47.7 0.7 collective-permute-done.6
  48.4 3.7 %collective-permute-done.7 = f32[2,12,2,512]{3,2,1,0:T(2,128)S(1)} collective-permute-done((f32[2,12,2,512]{3,2,1,0:T(2,128)S(1)}, f32[2,12,2,512]{3,2,1,0:T(2,128)S(1)}, u32[]{:S(2)}, u32[]{:S(2)}) %collective-permute-start.7) | collective-permute-done | bytes 98336 | tf_op jit(solution)/shard_map/ppermute | solution.py:32
  52.4 1.0 add_multiply_fusion.2
  53.5 0.7 fusion.55
  54.2 2.6 %fusion.91 = (f32[10,18,514]{2,1,0:T(8,128)S(1)}, f32[10,18,514]{2,1,0:T(8,128)S(1)}, f32[10,18,514]{2,1,0:T(8,128)S(1)}, f32[10,18,514]{2,1,0:T(8,128)S(1)}, f32[10,18,514]{2,1,0:T(8,128)S(1)}) fusion(f32[10,18,514]{2,1,0:T(8,128)S(1)} %get-tuple-element.6, f32[8,16,512]{2,1,0:T(8,128)S(1)} %get-tuple-element.67, f32[8,16,512]{2,1,0:T(8,128)S(1)} %get-tuple-element.66, ...), kind=kLoop, calls=%fused_computation.235 | loop fusion | flops 8604360 | bytes 3484928 | tf_op jit(solution)/shard_map/transpose(jvp())/neg | solution.py:43
  56.8 1.5 %fusion.93 = (f32[10,18,514]{2,1,0:T(8,128)S(1)}, f32[10,18,514]{2,1,0:T(8,128)S(1)}, f32[10,18,514]{2,1,0:T(8,128)S(1)}, f32[10,18,514]{2,1,0:T(8,128)S(1)}, f32[10,18,514]{2,1,0:T(8,128)S(1)}) fusion(f32[10,18,514]{2,1,0:T(8,128)S(1)} %get-tuple-element.7, f32[10,18,514]{2,1,0:T(8,128)S(1)} %get-tuple-element.22, ...), kind=kLoop, calls=%fused_computation.236 | loop fusion | flops 5643720 | bytes 4225088 | tf_op jit(solution)/shard_map/transpose(jvp())/neg | solution.py:42
  58.3 1.0 fusion.37
  59.3 1.9 %collective-permute-start.8 = (f32[2,2,20,512]{3,2,1,0:T(8,128)S(1)}, f32[2,2,20,512]{3,2,1,0:T(8,128)S(1)}, u32[]{:S(2)}, u32[]{:S(2)}) collective-permute-start(f32[2,2,20,512]{3,2,1,0:T(8,128)S(1)} %pad_maximum_fusion.9), channel_id=1, source_target_pairs={{0,8},{8,16},{16,24},{24,32},{32,40},{40,48},{48,56},{56,64},{64,7... | collective-permute-start | bytes 491528 | tf_op jit(solution)/shard_map/ppermute | solution.py:19
  61.3 10.2 %collective-permute-done.8 = f32[2,2,20,512]{3,2,1,0:T(8,128)S(1)} collective-permute-done((f32[2,2,20,512]{3,2,1,0:T(8,128)S(1)}, f32[2,2,20,512]{3,2,1,0:T(8,128)S(1)}, u32[]{:S(2)}, u32[]{:S(2)}) %collective-permute-start.8) | collective-permute-done | bytes 163872 | tf_op jit(solution)/shard_map/ppermute | solution.py:19
  71.5 1.9 %collective-permute-start.9 = (f32[2,2,20,512]{3,2,1,0:T(8,128)S(1)}, f32[2,2,20,512]{3,2,1,0:T(8,128)S(1)}, u32[]{:S(2)}, u32[]{:S(2)}) collective-permute-start(f32[2,2,20,512]{3,2,1,0:T(8,128)S(1)} %get-tuple-element.57), channel_id=1, source_target_pairs={{8,0},{16,8},{24,16},{32,24},{40,32},{48,40},{56,48},{64,56},{72,6... | collective-permute-start | bytes 491528 | tf_op jit(solution)/shard_map/ppermute | solution.py:19
  73.5 4.7 %collective-permute-done.9 = f32[2,2,20,512]{3,2,1,0:T(8,128)S(1)} collective-permute-done((f32[2,2,20,512]{3,2,1,0:T(8,128)S(1)}, f32[2,2,20,512]{3,2,1,0:T(8,128)S(1)}, u32[]{:S(2)}, u32[]{:S(2)}) %collective-permute-start.9) | collective-permute-done | bytes 163872 | tf_op jit(solution)/shard_map/ppermute | solution.py:19
  78.3 1.9 %collective-permute-start.10 = (f32[2,8,2,512]{3,2,1,0:T(2,128)S(1)}, f32[2,8,2,512]{3,2,1,0:T(2,128)S(1)}, u32[]{:S(2)}, u32[]{:S(2)}) collective-permute-start(f32[2,8,2,512]{3,2,1,0:T(2,128)S(1)} %pad_maximum_fusion.25), channel_id=1, source_target_pairs={{0,1},{1,2},{2,3},{3,4},{4,5},{5,6},{6,7},{8,9},{9,10},{10,11},{11... | collective-permute-start | bytes 196616 | tf_op jit(solution)/shard_map/ppermute | solution.py:19
  80.2 5.1 %collective-permute-done.10 = f32[2,8,2,512]{3,2,1,0:T(2,128)S(1)} collective-permute-done((f32[2,8,2,512]{3,2,1,0:T(2,128)S(1)}, f32[2,8,2,512]{3,2,1,0:T(2,128)S(1)}, u32[]{:S(2)}, u32[]{:S(2)}) %collective-permute-start.10) | collective-permute-done | bytes 65568 | tf_op jit(solution)/shard_map/ppermute | solution.py:19
  85.4 2.1 %collective-permute-start.11 = (f32[2,8,2,512]{3,2,1,0:T(2,128)S(1)}, f32[2,8,2,512]{3,2,1,0:T(2,128)S(1)}, u32[]{:S(2)}, u32[]{:S(2)}) collective-permute-start(f32[2,8,2,512]{3,2,1,0:T(2,128)S(1)} %get-tuple-element.65), channel_id=1, source_target_pairs={{1,0},{2,1},{3,2},{4,3},{5,4},{6,5},{7,6},{9,8},{10,9},{11,10},{12... | collective-permute-start | bytes 196616 | tf_op jit(solution)/shard_map/ppermute | solution.py:19
  87.6 3.9 %collective-permute-done.11 = f32[2,8,2,512]{3,2,1,0:T(2,128)S(1)} collective-permute-done((f32[2,8,2,512]{3,2,1,0:T(2,128)S(1)}, f32[2,8,2,512]{3,2,1,0:T(2,128)S(1)}, u32[]{:S(2)}, u32[]{:S(2)}) %collective-permute-start.11) | collective-permute-done | bytes 65568 | tf_op jit(solution)/shard_map/ppermute | solution.py:19
  91.7 1.5 %fusion.60 = (f32[8,16,512]{2,1,0:T(8,128)}, f32[8,16,512]{2,1,0:T(8,128)S(1)}, f32[8,16,512]{2,1,0:T(8,128)S(1)}) fusion(f32[10,18,514]{2,1,0:T(8,128)S(1)} %get-tuple-element.53, f32[10,18,514]{2,1,0:T(8,128)S(1)} %get-tuple-element.52, f32[10,18,514]{2,1,0:T(8,128)S(1)} %get-tuple-element.5, f32[8,16,512]{2,1,0:T(8,128)S(1)} %get-tuple-element.30, ...), kind=kLoop, calls=%fused_computation.160 | loop fusion | flops 1638400 | bytes 4194304 | tf_op jit(solution)/shard_map/add | solution.py:130
  93.2 0.7 fusion.53
  94.0 2.0 %fusion.84 = (f32[10,18,514]{2,1,0:T(8,128)S(1)}, f32[10,18,514]{2,1,0:T(8,128)S(1)}, f32[10,18,514]{2,1,0:T(8,128)S(1)}, f32[10,18,514]{2,1,0:T(8,128)S(1)}) fusion(f32[10,18,514]{2,1,0:T(8,128)S(1)} %get-tuple-element.37, f32[10,18,514]{2,1,0:T(8,128)S(1)} %get-tuple-element.47, f32[10,18,514]{2,1,0:T(8,128)S(1)} %get-tuple-element.33, ...), kind=kLoop, calls=%fused_computation.231 | loop fusion | flops 7771680 | bytes 4965248 | tf_op jit(solution)/shard_map/transpose(jvp())/neg | solution.py:43
  96.1 1.3 fusion.86
  97.4 0.9 fusion.35
  98.3 1.9 %collective-permute-start.12 = (f32[2,2,20,512]{3,2,1,0:T(8,128)S(1)}, f32[2,2,20,512]{3,2,1,0:T(8,128)S(1)}, u32[]{:S(2)}, u32[]{:S(2)}) collective-permute-start(f32[2,2,20,512]{3,2,1,0:T(8,128)S(1)} %pad_maximum_fusion.7), channel_id=1, source_target_pairs={{0,8},{8,16},{16,24},{24,32},{32,40},{40,48},{48,56},{56,64},{64,7... | collective-permute-start | bytes 491528 | tf_op jit(solution)/shard_map/ppermute | solution.py:19
  100.2 8.2 %collective-permute-done.12 = f32[2,2,20,512]{3,2,1,0:T(8,128)S(1)} collective-permute-done((f32[2,2,20,512]{3,2,1,0:T(8,128)S(1)}, f32[2,2,20,512]{3,2,1,0:T(8,128)S(1)}, u32[]{:S(2)}, u32[]{:S(2)}) %collective-permute-start.12) | collective-permute-done | bytes 163872 | tf_op jit(solution)/shard_map/ppermute | solution.py:19
  108.5 1.9 %collective-permute-start.13 = (f32[2,2,20,512]{3,2,1,0:T(8,128)S(1)}, f32[2,2,20,512]{3,2,1,0:T(8,128)S(1)}, u32[]{:S(2)}, u32[]{:S(2)}) collective-permute-start(f32[2,2,20,512]{3,2,1,0:T(8,128)S(1)} %get-tuple-element.55), channel_id=1, source_target_pairs={{8,0},{16,8},{24,16},{32,24},{40,32},{48,40},{56,48},{64,56},{72,6... | collective-permute-start | bytes 491528 | tf_op jit(solution)/shard_map/ppermute | solution.py:19
  110.4 5.3 %collective-permute-done.13 = f32[2,2,20,512]{3,2,1,0:T(8,128)S(1)} collective-permute-done((f32[2,2,20,512]{3,2,1,0:T(8,128)S(1)}, f32[2,2,20,512]{3,2,1,0:T(8,128)S(1)}, u32[]{:S(2)}, u32[]{:S(2)}) %collective-permute-start.13) | collective-permute-done | bytes 163872 | tf_op jit(solution)/shard_map/ppermute | solution.py:19
  115.8 2.0 %collective-permute-start.14 = (f32[2,8,2,512]{3,2,1,0:T(2,128)S(1)}, f32[2,8,2,512]{3,2,1,0:T(2,128)S(1)}, u32[]{:S(2)}, u32[]{:S(2)}) collective-permute-start(f32[2,8,2,512]{3,2,1,0:T(2,128)S(1)} %pad_maximum_fusion.23), channel_id=1, source_target_pairs={{0,1},{1,2},{2,3},{3,4},{4,5},{5,6},{6,7},{8,9},{9,10},{10,11},{11... | collective-permute-start | bytes 196616 | tf_op jit(solution)/shard_map/ppermute | solution.py:19
  117.8 5.1 %collective-permute-done.14 = f32[2,8,2,512]{3,2,1,0:T(2,128)S(1)} collective-permute-done((f32[2,8,2,512]{3,2,1,0:T(2,128)S(1)}, f32[2,8,2,512]{3,2,1,0:T(2,128)S(1)}, u32[]{:S(2)}, u32[]{:S(2)}) %collective-permute-start.14) | collective-permute-done | bytes 65568 | tf_op jit(solution)/shard_map/ppermute | solution.py:19
  123.0 1.9 %collective-permute-start.15 = (f32[2,8,2,512]{3,2,1,0:T(2,128)S(1)}, f32[2,8,2,512]{3,2,1,0:T(2,128)S(1)}, u32[]{:S(2)}, u32[]{:S(2)}) collective-permute-start(f32[2,8,2,512]{3,2,1,0:T(2,128)S(1)} %get-tuple-element.63), channel_id=1, source_target_pairs={{1,0},{2,1},{3,2},{4,3},{5,4},{6,5},{7,6},{9,8},{10,9},{11,10},{12... | collective-permute-start | bytes 196616 | tf_op jit(solution)/shard_map/ppermute | solution.py:19
  125.0 4.1 %collective-permute-done.15 = f32[2,8,2,512]{3,2,1,0:T(2,128)S(1)} collective-permute-done((f32[2,8,2,512]{3,2,1,0:T(2,128)S(1)}, f32[2,8,2,512]{3,2,1,0:T(2,128)S(1)}, u32[]{:S(2)}, u32[]{:S(2)}) %collective-permute-start.15) | collective-permute-done | bytes 65568 | tf_op jit(solution)/shard_map/ppermute | solution.py:19
  129.3 0.8 slice_bitcast_fusion.4
  (39 shorter events, 2.6 us)
Async XLA Ops:
  0.6 25.6 %copy-start.2 = (f32[8,16,512]{2,1,0:T(8,128)S(1)}, f32[8,16,512]{2,1,0:T(8,128)}, u32[]{:S(2)}) copy-start(f32[8,16,512]{2,1,0:T(8,128)} %param.6) | copy-start | bytes 786436
  0.6 25.6 %copy-start.3 = (f32[8,16,512]{2,1,0:T(8,128)S(1)}, f32[8,16,512]{2,1,0:T(8,128)}, u32[]{:S(2)}) copy-start(f32[8,16,512]{2,1,0:T(8,128)} %param.5) | copy-start | bytes 786436
  1.7 10.7 %collective-permute-start = (f32[2,2,16,512]{3,2,1,0:T(8,128)S(1)}, f32[2,2,16,512]{3,2,1,0:T(8,128)S(1)}, u32[]{:S(2)}, u32[]{:S(2)}) collective-permute-start(f32[2,2,16,512]{3,2,1,0:T(8,128)S(1)} %get-tuple-element.80), channel_id=1, source_target_pairs={{0,8},{8,16},{16,24},{24,32},{32,40},{40,48},{48,56},{56,64},{64,7... | collective-permute-start | bytes 393224 | tf_op jit(solution)/shard_map/ppermute | solution.py:30
  3.6 11.8 %collective-permute-start.1 = (f32[2,2,16,512]{3,2,1,0:T(8,128)S(1)}, f32[2,2,16,512]{3,2,1,0:T(8,128)S(1)}, u32[]{:S(2)}, u32[]{:S(2)}) collective-permute-start(f32[2,2,16,512]{3,2,1,0:T(8,128)S(1)} %get-tuple-element.81), channel_id=1, source_target_pairs={{8,0},{16,8},{24,16},{32,24},{40,32},{48,40},{56,48},{64,56},{72,6... | collective-permute-start | bytes 393224 | tf_op jit(solution)/shard_map/ppermute | solution.py:32
  16.6 8.1 %collective-permute-start.2 = (f32[2,12,2,512]{3,2,1,0:T(2,128)S(1)}, f32[2,12,2,512]{3,2,1,0:T(2,128)S(1)}, u32[]{:S(2)}, u32[]{:S(2)}) collective-permute-start(f32[2,12,2,512]{3,2,1,0:T(2,128)S(1)} %get-tuple-element.70), channel_id=1, source_target_pairs={{0,1},{1,2},{2,3},{3,4},{4,5},{5,6},{6,7},{8,9},{9,10},{10,11},{11... | collective-permute-start | bytes 294920 | tf_op jit(solution)/shard_map/ppermute | solution.py:30
  18.5 7.7 %collective-permute-start.3 = (f32[2,12,2,512]{3,2,1,0:T(2,128)S(1)}, f32[2,12,2,512]{3,2,1,0:T(2,128)S(1)}, u32[]{:S(2)}, u32[]{:S(2)}) collective-permute-start(f32[2,12,2,512]{3,2,1,0:T(2,128)S(1)} %get-tuple-element.71), channel_id=1, source_target_pairs={{1,0},{2,1},{3,2},{4,3},{5,4},{6,5},{7,6},{9,8},{10,9},{11,10},{12... | collective-permute-start | bytes 294920 | tf_op jit(solution)/shard_map/ppermute | solution.py:32
  27.6 1.0 copy-start
  29.6 18.1 %copy-start.1 = (f32[8,16,512]{2,1,0:T(8,128)S(1)}, f32[8,16,512]{2,1,0:T(8,128)}, u32[]{:S(2)}) copy-start(f32[8,16,512]{2,1,0:T(8,128)} %param.9) | copy-start | bytes 786436
  29.6 9.9 %collective-permute-start.4 = (f32[2,2,16,512]{3,2,1,0:T(8,128)S(1)}, f32[2,2,16,512]{3,2,1,0:T(8,128)S(1)}, u32[]{:S(2)}, u32[]{:S(2)}) collective-permute-start(f32[2,2,16,512]{3,2,1,0:T(8,128)S(1)} %get-tuple-element.78), channel_id=1, source_target_pairs={{0,8},{8,16},{16,24},{24,32},{32,40},{40,48},{48,56},{56,64},{64,7... | collective-permute-start | bytes 393224 | tf_op jit(solution)/shard_map/ppermute | solution.py:30
  31.7 9.2 %collective-permute-start.5 = (f32[2,2,16,512]{3,2,1,0:T(8,128)S(1)}, f32[2,2,16,512]{3,2,1,0:T(8,128)S(1)}, u32[]{:S(2)}, u32[]{:S(2)}) collective-permute-start(f32[2,2,16,512]{3,2,1,0:T(8,128)S(1)} %get-tuple-element.79), channel_id=1, source_target_pairs={{8,0},{16,8},{24,16},{32,24},{40,32},{48,40},{56,48},{64,56},{72,6... | collective-permute-start | bytes 393224 | tf_op jit(solution)/shard_map/ppermute | solution.py:32
  40.9 7.5 %collective-permute-start.6 = (f32[2,12,2,512]{3,2,1,0:T(2,128)S(1)}, f32[2,12,2,512]{3,2,1,0:T(2,128)S(1)}, u32[]{:S(2)}, u32[]{:S(2)}) collective-permute-start(f32[2,12,2,512]{3,2,1,0:T(2,128)S(1)} %get-tuple-element.68), channel_id=1, source_target_pairs={{0,1},{1,2},{2,3},{3,4},{4,5},{5,6},{6,7},{8,9},{9,10},{10,11},{11... | collective-permute-start | bytes 294920 | tf_op jit(solution)/shard_map/ppermute | solution.py:30
  45.6 6.5 %collective-permute-start.7 = (f32[2,12,2,512]{3,2,1,0:T(2,128)S(1)}, f32[2,12,2,512]{3,2,1,0:T(2,128)S(1)}, u32[]{:S(2)}, u32[]{:S(2)}) collective-permute-start(f32[2,12,2,512]{3,2,1,0:T(2,128)S(1)} %get-tuple-element.69), channel_id=1, source_target_pairs={{1,0},{2,1},{3,2},{4,3},{5,4},{6,5},{7,6},{9,8},{10,9},{11,10},{12... | collective-permute-start | bytes 294920 | tf_op jit(solution)/shard_map/ppermute | solution.py:32
  52.4 1.1 copy-start.4
  59.3 12.1 %collective-permute-start.8 = (f32[2,2,20,512]{3,2,1,0:T(8,128)S(1)}, f32[2,2,20,512]{3,2,1,0:T(8,128)S(1)}, u32[]{:S(2)}, u32[]{:S(2)}) collective-permute-start(f32[2,2,20,512]{3,2,1,0:T(8,128)S(1)} %pad_maximum_fusion.9), channel_id=1, source_target_pairs={{0,8},{8,16},{16,24},{24,32},{32,40},{40,48},{48,56},{56,64},{64,7... | collective-permute-start | bytes 491528 | tf_op jit(solution)/shard_map/ppermute | solution.py:19
  71.5 6.7 %collective-permute-start.9 = (f32[2,2,20,512]{3,2,1,0:T(8,128)S(1)}, f32[2,2,20,512]{3,2,1,0:T(8,128)S(1)}, u32[]{:S(2)}, u32[]{:S(2)}) collective-permute-start(f32[2,2,20,512]{3,2,1,0:T(8,128)S(1)} %get-tuple-element.57), channel_id=1, source_target_pairs={{8,0},{16,8},{24,16},{32,24},{40,32},{48,40},{56,48},{64,56},{72,6... | collective-permute-start | bytes 491528 | tf_op jit(solution)/shard_map/ppermute | solution.py:19
  78.3 7.1 %collective-permute-start.10 = (f32[2,8,2,512]{3,2,1,0:T(2,128)S(1)}, f32[2,8,2,512]{3,2,1,0:T(2,128)S(1)}, u32[]{:S(2)}, u32[]{:S(2)}) collective-permute-start(f32[2,8,2,512]{3,2,1,0:T(2,128)S(1)} %pad_maximum_fusion.25), channel_id=1, source_target_pairs={{0,1},{1,2},{2,3},{3,4},{4,5},{5,6},{6,7},{8,9},{9,10},{10,11},{11... | collective-permute-start | bytes 196616 | tf_op jit(solution)/shard_map/ppermute | solution.py:19
  85.4 6.2 %collective-permute-start.11 = (f32[2,8,2,512]{3,2,1,0:T(2,128)S(1)}, f32[2,8,2,512]{3,2,1,0:T(2,128)S(1)}, u32[]{:S(2)}, u32[]{:S(2)}) collective-permute-start(f32[2,8,2,512]{3,2,1,0:T(2,128)S(1)} %get-tuple-element.65), channel_id=1, source_target_pairs={{1,0},{2,1},{3,2},{4,3},{5,4},{6,5},{7,6},{9,8},{10,9},{11,10},{12... | collective-permute-start | bytes 196616 | tf_op jit(solution)/shard_map/ppermute | solution.py:19
  98.3 10.1 %collective-permute-start.12 = (f32[2,2,20,512]{3,2,1,0:T(8,128)S(1)}, f32[2,2,20,512]{3,2,1,0:T(8,128)S(1)}, u32[]{:S(2)}, u32[]{:S(2)}) collective-permute-start(f32[2,2,20,512]{3,2,1,0:T(8,128)S(1)} %pad_maximum_fusion.7), channel_id=1, source_target_pairs={{0,8},{8,16},{16,24},{24,32},{32,40},{40,48},{48,56},{56,64},{64,7... | collective-permute-start | bytes 491528 | tf_op jit(solution)/shard_map/ppermute | solution.py:19
  108.5 7.2 %collective-permute-start.13 = (f32[2,2,20,512]{3,2,1,0:T(8,128)S(1)}, f32[2,2,20,512]{3,2,1,0:T(8,128)S(1)}, u32[]{:S(2)}, u32[]{:S(2)}) collective-permute-start(f32[2,2,20,512]{3,2,1,0:T(8,128)S(1)} %get-tuple-element.55), channel_id=1, source_target_pairs={{8,0},{16,8},{24,16},{32,24},{40,32},{48,40},{56,48},{64,56},{72,6... | collective-permute-start | bytes 491528 | tf_op jit(solution)/shard_map/ppermute | solution.py:19
  115.8 7.1 %collective-permute-start.14 = (f32[2,8,2,512]{3,2,1,0:T(2,128)S(1)}, f32[2,8,2,512]{3,2,1,0:T(2,128)S(1)}, u32[]{:S(2)}, u32[]{:S(2)}) collective-permute-start(f32[2,8,2,512]{3,2,1,0:T(2,128)S(1)} %pad_maximum_fusion.23), channel_id=1, source_target_pairs={{0,1},{1,2},{2,3},{3,4},{4,5},{5,6},{6,7},{8,9},{9,10},{10,11},{11... | collective-permute-start | bytes 196616 | tf_op jit(solution)/shard_map/ppermute | solution.py:19
  123.0 6.2 %collective-permute-start.15 = (f32[2,8,2,512]{3,2,1,0:T(2,128)S(1)}, f32[2,8,2,512]{3,2,1,0:T(2,128)S(1)}, u32[]{:S(2)}, u32[]{:S(2)}) collective-permute-start(f32[2,8,2,512]{3,2,1,0:T(2,128)S(1)} %get-tuple-element.63), channel_id=1, source_target_pairs={{1,0},{2,1},{3,2},{4,3},{5,4},{6,5},{7,6},{9,8},{10,9},{11,10},{12... | collective-permute-start | bytes 196616 | tf_op jit(solution)/shard_map/ppermute | solution.py:19
where the time goes:
time: 131 us; the launch traced here: 130 us
  waiting for transfers between devices  60.2 us (46%)
  starting transfers between devices  47.7 us (36%)
  other arithmetic  19.7 us (15%)
  local copies, waits for them, and re-layouts  1.55 us (1%)
    ppermute x8, waiting for transfers between devices, from_behind(): return lax.ppermute(block, axis, route)  46.6 us
    ppermute x4, starting transfers between devices, extended(): lax.ppermute(head, axis, [((i + 1) % count, i) for i in range(ends)])  21.5 us
    ppermute x8, starting transfers between devices, from_behind(): return lax.ppermute(block, axis, route)  15.6 us
    ppermute x4, starting transfers between devices, extended(): lax.ppermute(tail, axis, [(i, (i + 1) % count) for i in range(ends)])  10.5 us
    ppermute x4, waiting for transfers between devices, extended(): lax.ppermute(head, axis, [((i + 1) % count, i) for i in range(ends)])  9.6 us
    neg x2, other arithmetic, advance_solver_step(): grad_x = 0.5 * (padded[1:-1, 1:-1, 2:] - padded[1:-1, 1:-1, :-2])  4.6 us
    ppermute x4, waiting for transfers between devices, extended(): lax.ppermute(tail, axis, [(i, (i + 1) % count) for i in range(ends)])  4.03 us
    neg x2, other arithmetic, advance_solver_step(): grad_y = 0.5 * (padded[1:-1, 2:, 1:-1] - padded[1:-1, :-2, 1:-1])  2.85 us
  transfers between devices with their start and end apart: 16, of which 16 were waited for; matrix products, arithmetic and copies ran while one was open for 0% of the time, Pallas kernels for 0%

commit v1 on v0

--- a/solution.py
+++ b/solution.py
@@ -95,6 +95,15 @@
     return (middle[0], middle[1])
 
 
+def inside_grid(cells, margin):
+    nz, ny = cells.shape[0] - 2 * margin, cells.shape[1] - 2 * margin
+    z = lax.axis_index("gz") * nz - margin + lax.broadcasted_iota(jnp.int32, cells.shape, 0)
+    y = lax.axis_index("gy") * ny - margin + lax.broadcasted_iota(jnp.int32, cells.shape, 1)
+    total_z = nz * lax.axis_size("gz")
+    total_y = ny * lax.axis_size("gy")
+    return (z >= 0) & (z < total_z) & (y >= 0) & (y < total_y)
+
+
 def body(
     saved_order_parameter,
     saved_heat_level,
@@ -102,26 +111,40 @@
     order_parameter_adjoint_seed,
     heat_level_adjoint_seed,
 ):
-    initial_extended = extended(
-        jnp.stack((saved_order_parameter, saved_heat_level)), (("gz", 1), ("gy", 2)), 2
+    state = extended(
+        jnp.stack((saved_order_parameter, saved_heat_level, kinetic_rate_field)),
+        (("gz", 1), ("gy", 2)),
+        6,
     )
+    seeds = extended(
+        jnp.stack((order_parameter_adjoint_seed, heat_level_adjoint_seed)),
+        (("gz", 1), ("gy", 2)),
+        2,
+    )
+    phase_wide, temp_wide, rate_wide = state[0], state[1], state[2]
     succeeding_order_parameter, succeeding_heat_level = advance_solver_step(
-        initial_extended[0], initial_extended[1], kinetic_rate_field
+        phase_wide, temp_wide, rate_wide[2:-2, 2:-2]
     )
-    state_wide = extended(
-        jnp.stack((succeeding_order_parameter, succeeding_heat_level)), (("gz", 1), ("gy", 2)), 2
-    )
+    valid = inside_grid(succeeding_order_parameter, 4)
+    succeeding_order_parameter = jnp.where(valid, succeeding_order_parameter, 0.0)
+    succeeding_heat_level = jnp.where(valid, succeeding_heat_level, 0.0)
     discarded_result, sensitivity_latest = jax.vjp(
-        advance_solver_step, state_wide[0], state_wide[1], kinetic_rate_field
+        advance_solver_step,
+        succeeding_order_parameter,
+        succeeding_heat_level,
+        rate_wide[4:-4, 4:-4],
     )
     sensitivity_order_parameter, sensitivity_heat_level, latest_kinetic_rate = sensitivity_latest(
-        (order_parameter_adjoint_seed, heat_level_adjoint_seed)
+        (seeds[0], seeds[1])
     )
-    halfway_order_parameter, halfway_heat_level = fold_rims(
-        sensitivity_order_parameter, sensitivity_heat_level
-    )
+    halfway_order_parameter = sensitivity_order_parameter[4:-4, 4:-4]
+    halfway_heat_level = sensitivity_heat_level[4:-4, 4:-4]
+    latest_kinetic_rate = latest_kinetic_rate[2:-2, 2:-2]
     discarded_result, prior_backward_sweep = jax.vjp(
-        advance_solver_step, initial_extended[0], initial_extended[1], kinetic_rate_field
+        advance_solver_step,
+        phase_wide[4:-4, 4:-4],
+        temp_wide[4:-4, 4:-4],
+        rate_wide[6:-6, 6:-6],
     )
     sensitivity_order_parameter, sensitivity_heat_level, early_mob = prior_backward_sweep(
         (halfway_order_parameter, halfway_heat_level)

time: 131 us -> 154 us (1.18); the launches traced: 130 us -> 151 us
  other arithmetic: 19.7 us -> 35.8 us
  local copies, waits for them, and re-layouts: 1.55 us -> 8.2 us
  starting transfers between devices: 47.7 us -> 45.2 us
    ppermute x4, waiting for transfers between devices: 4.03 us -> 37.5 us  [extended(): lax.ppermute(tail, axis, [(i, (i + 1) % count) for i in range(ends)])]
    ppermute x8 -> x4, waiting for transfers between devices: 46.6 us -> 15.6 us  [from_behind(): return lax.ppermute(block, axis, route)]
    mul x2 -> x3, other arithmetic: 2.09 us -> 9.06 us  [advance_solver_step(): ENERGY_SCALE * (aniso_sq * grad_z + factor_a * grad_z * (sq_z - quartic *...]
    slice x0 -> x10, local copies, waits for them, and re-layouts: none -> 3.64 us  [the longest x1 1.36 us: extended(): head = lax.slice_in_dim(cells, 0, width, axis=dim)]
    ppermute x0 -> x2, local copies, waits for them, and re-layouts: none -> 3.2 us  [the longest x1 1.6 us: extended(): lax.ppermute(tail, axis, [(i, (i + 1) % count) for i in range(ends)])]
    ppermute x4, starting transfers between devices: 10.5 us -> 7.8 us  [extended(): lax.ppermute(tail, axis, [(i, (i + 1) % count) for i in range(ends)])]
    ppermute x4, starting transfers between devices: 21.5 us -> 24.2 us  [extended(): lax.ppermute(head, axis, [((i + 1) % count, i) for i in range(ends)])]
    ppermute x8 -> x4, starting transfers between devices: 15.6 us -> 13.2 us  [from_behind(): return lax.ppermute(block, axis, route)]
  transfers between devices with their start and end apart: 16 -> 12, of which waited for: 16 -> 8; matrix products, arithmetic and copies ran while one was open for 0% -> 4% of each run, Pallas kernels for 0% -> 0%
where the time goes in v1:
time: 154 us; the launch traced here: 151 us
  waiting for transfers between devices  61.1 us (40%)
  starting transfers between devices  45.2 us (29%)
  other arithmetic  35.8 us (23%)
  local copies, waits for them, and re-layouts  8.2 us (5%)
    ppermute x4, waiting for transfers between devices, extended(): lax.ppermute(tail, axis, [(i, (i + 1) % count) for i in range(ends)])  37.5 us
    ppermute x4, starting transfers between devices, extended(): lax.ppermute(head, axis, [((i + 1) % count, i) for i in range(ends)])  24.2 us
    ppermute x4, waiting for transfers between devices, from_behind(): return lax.ppermute(block, axis, route)  15.6 us
    ppermute x4, starting transfers between devices, from_behind(): return lax.ppermute(block, axis, route)  13.2 us
    mul x3, other arithmetic, advance_solver_step(): ENERGY_SCALE * (aniso_sq * grad_z + factor_a * grad_z * (sq_z - quartic *...  9.06 us
    ppermute x4, waiting for transfers between devices, extended(): lax.ppermute(head, axis, [((i + 1) % count, i) for i in range(ends)])  8.07 us
    ppermute x4, starting transfers between devices, extended(): lax.ppermute(tail, axis, [(i, (i + 1) % count) for i in range(ends)])  7.8 us
    neg x2, other arithmetic, advance_solver_step(): grad_x = 0.5 * (padded[1:-1, 1:-1, 2:] - padded[1:-1, 1:-1, :-2])  6.18 us
  transfers between devices with their start and end apart: 12, of which 8 were waited for; matrix products, arithmetic and copies ran while one was open for 4% of the time, Pallas kernels for 0%

profile of v1, /device:TPU:14, one launch (start us, length us, event | category | flops | bytes accessed | tf_op | source)
XLA Modules:
  0.0 151.4 jit_solution(42014742983007539)
XLA Ops:
  0.6 1.2 pad_maximum_fusion.3
  2.0 2.1 %collective-permute-start.4 = (f32[3,6,16,512]{3,2,1,0:T(8,128)S(1)}, f32[3,6,16,512]{3,2,1,0:T(8,128)S(1)}, u32[]{:S(2)}, u32[]{:S(2)}) collective-permute-start(f32[3,6,16,512]{3,2,1,0:T(8,128)S(1)} %get-tuple-element.79), channel_id=1, source_target_pairs={{0,8},{8,16},{16,24},{24,32},{32,40},{40,48},{48,56},{56,64},{64,7... | collective-permute-start | bytes 1769480 | tf_op jit(solution)/shard_map/ppermute | solution.py:30
  4.1 7.9 %collective-permute-start.5 = (f32[3,6,16,512]{3,2,1,0:T(8,128)S(1)}, f32[3,6,16,512]{3,2,1,0:T(8,128)S(1)}, u32[]{:S(2)}, u32[]{:S(2)}) collective-permute-start(f32[3,6,16,512]{3,2,1,0:T(8,128)S(1)} %get-tuple-element.80), channel_id=1, source_target_pairs={{8,0},{16,8},{24,16},{32,24},{40,32},{48,40},{56,48},{64,56},{72,6... | collective-permute-start | bytes 1769480 | tf_op jit(solution)/shard_map/ppermute | solution.py:32
  12.0 7.5 %collective-permute-done.4 = f32[3,6,16,512]{3,2,1,0:T(8,128)S(1)} collective-permute-done((f32[3,6,16,512]{3,2,1,0:T(8,128)S(1)}, f32[3,6,16,512]{3,2,1,0:T(8,128)S(1)}, u32[]{:S(2)}, u32[]{:S(2)}) %collective-permute-start.4) | collective-permute-done | bytes 589856 | tf_op jit(solution)/shard_map/ppermute | solution.py:30
  19.5 6.2 %collective-permute-done.5 = f32[3,6,16,512]{3,2,1,0:T(8,128)S(1)} collective-permute-done((f32[3,6,16,512]{3,2,1,0:T(8,128)S(1)}, f32[3,6,16,512]{3,2,1,0:T(8,128)S(1)}, u32[]{:S(2)}, u32[]{:S(2)}) %collective-permute-start.5) | collective-permute-done | bytes 589856 | tf_op jit(solution)/shard_map/ppermute | solution.py:32
  26.1 0.4 copy.16
  26.5 1.9 %collective-permute-start.6 = (f32[3,20,6,512]{3,1,2,0:T(8,128)S(1)}, f32[3,20,6,512]{3,1,2,0:T(8,128)}, u32[]{:S(2)}, u32[]{:S(2)}) collective-permute-start(f32[3,20,6,512]{3,1,2,0:T(8,128)S(1)} %copy.16), channel_id=1, source_target_pairs={{0,1},{1,2},{2,3},{3,4},{4,5},{5,6},{6,7},{8,9},{9,10},{10,11},{11... | collective-permute-start | bytes 2211848 | tf_op jit(solution)/shard_map/ppermute | solution.py:30
  28.5 1.4 copy.17
  29.8 4.8 %collective-permute-start.7 = (f32[3,20,6,512]{3,1,2,0:T(8,128)}, f32[3,20,6,512]{3,1,2,0:T(8,128)}, u32[]{:S(2)}, u32[]{:S(2)}) collective-permute-start(f32[3,20,6,512]{3,1,2,0:T(8,128)} %copy.17), channel_id=1, source_target_pairs={{1,0},{2,1},{3,2},{4,3},{5,4},{6,5},{7,6},{9,8},{10,9},{11,10},{12... | collective-permute-start | bytes 2211848 | tf_op jit(solution)/shard_map/ppermute | solution.py:32
  34.7 0.7 pad_maximum_fusion.9
  35.4 1.9 %collective-permute-start = (f32[2,2,16,512]{3,2,1,0:T(8,128)}, f32[2,2,16,512]{3,2,1,0:T(8,128)S(1)}, u32[]{:S(2)}, u32[]{:S(2)}) collective-permute-start(f32[2,2,16,512]{3,2,1,0:T(8,128)} %get-tuple-element.84), channel_id=1, source_target_pairs={{0,8},{8,16},{16,24},{24,32},{32,40},{40,48},{48,56},{56,64},{64,7... | collective-permute-start | bytes 393224 | tf_op jit(solution)/shard_map/ppermute | solution.py:30
  37.3 6.7 %collective-permute-start.1 = (f32[2,2,16,512]{3,2,1,0:T(8,128)}, f32[2,2,16,512]{3,2,1,0:T(8,128)}, u32[]{:S(2)}, u32[]{:S(2)}) collective-permute-start(f32[2,2,16,512]{3,2,1,0:T(8,128)} %get-tuple-element.85), channel_id=1, source_target_pairs={{8,0},{16,8},{24,16},{32,24},{40,32},{48,40},{56,48},{64,56},{72,6... | collective-permute-start | bytes 393224 | tf_op jit(solution)/shard_map/ppermute | solution.py:32
  44.0 30.0 %collective-permute-done = f32[2,2,16,512]{3,2,1,0:T(8,128)S(1)} collective-permute-done((f32[2,2,16,512]{3,2,1,0:T(8,128)}, f32[2,2,16,512]{3,2,1,0:T(8,128)S(1)}, u32[]{:S(2)}, u32[]{:S(2)}) %collective-permute-start) | collective-permute-done | bytes 131104 | tf_op jit(solution)/shard_map/ppermute | solution.py:30
  74.0 1.0 pad_maximum_fusion.13
  74.9 1.9 %collective-permute-start.2 = (f32[2,12,2,512]{3,2,1,0:T(2,128)S(1)}, f32[2,12,2,512]{3,2,1,0:T(2,128)S(1)}, u32[]{:S(2)}, u32[]{:S(2)}) collective-permute-start(f32[2,12,2,512]{3,2,1,0:T(2,128)S(1)} %get-tuple-element.77), channel_id=1, source_target_pairs={{0,1},{1,2},{2,3},{3,4},{4,5},{5,6},{6,7},{8,9},{9,10},{10,11},{11... | collective-permute-start | bytes 294920 | tf_op jit(solution)/shard_map/ppermute | solution.py:30
  76.9 4.8 %collective-permute-start.3 = (f32[2,12,2,512]{3,2,1,0:T(2,128)S(1)}, f32[2,12,2,512]{3,2,1,0:T(2,128)S(1)}, u32[]{:S(2)}, u32[]{:S(2)}) collective-permute-start(f32[2,12,2,512]{3,2,1,0:T(2,128)S(1)} %get-tuple-element.78), channel_id=1, source_target_pairs={{1,0},{2,1},{3,2},{4,3},{5,4},{6,5},{7,6},{9,8},{10,9},{11,10},{12... | collective-permute-start | bytes 294920 | tf_op jit(solution)/shard_map/ppermute | solution.py:32
  81.7 0.8 and_and_fusion
  82.5 1.9 %collective-permute-done.3 = f32[2,12,2,512]{3,2,1,0:T(2,128)S(1)} collective-permute-done((f32[2,12,2,512]{3,2,1,0:T(2,128)S(1)}, f32[2,12,2,512]{3,2,1,0:T(2,128)S(1)}, u32[]{:S(2)}, u32[]{:S(2)}) %collective-permute-start.3) | collective-permute-done | bytes 98336 | tf_op jit(solution)/shard_map/ppermute | solution.py:32
  84.4 1.1 pad_maximum_fusion.2
  85.5 1.6 %copy.18 = f32[3,20,6,512]{3,2,1,0:T(8,128)S(1)} copy(f32[3,20,6,512]{3,1,2,0:T(8,128)} %collective-permute-done.6) | data formatting | bytes 1474560 | tf_op jit(solution)/shard_map/ppermute | solution.py:30
  87.1 1.6 %copy.19 = f32[3,20,6,512]{3,2,1,0:T(8,128)S(1)} copy(f32[3,20,6,512]{3,1,2,0:T(8,128)} %collective-permute-done.7) | data formatting | bytes 1474560 | tf_op jit(solution)/shard_map/ppermute | solution.py:32
  88.7 1.0 pad_maximum_fusion
  89.8 0.4 slice_bitcast_fusion
  90.2 6.6 %add_multiply_fusion.2 = (f32[18,26,514]{2,1,0:T(8,128)S(1)}, f32[18,26,514]{2,1,0:T(8,128)S(1)}, f32[18,26,514]{2,1,0:T(8,128)S(1)}) fusion(f32[20,28,512]{2,1,0:T(8,128)S(1)} %get-tuple-element.49), kind=kLoop, calls=%fused_computation.16 | loop fusion | flops 23814648 | bytes 4033504 | tf_op jit(solution)/shard_map/mul | solution.py:52
  97.6 2.3 %broadcast_select_fusion = (f32[16,24,512]{2,1,0:T(8,128)S(1)}, f32[16,24,512]{2,1,0:T(8,128)S(1)}, f32[16,24,512]{2,1,0:T(8,128)S(1)}, f32[16,24,512]{2,1,0:T(8,128)S(1)}) fusion(pred[24]{0:T(512)(128)(4,1)S(1)} %get-tuple-element.86, pred[24]{0:T(512)(128)(4,1)S(1)} %get-tuple-element.87, pred[16]{0:T(512)(128)(4,1)S(1)} %compare_and_fusion, ...), kind=kLoop, calls=%fused_computation.181 | loop fusion | flops 4915200 | bytes 14155840 | tf_op jit(solution)/shard_map/jit(_where)/select_n | solution.py:129
  99.9 1.4 add_multiply_fusion.5
  101.4 1.6 %fusion.51 = (f32[12,20,512]{2,1,0:T(8,128)S(1)}, f32[12,20,512]{2,1,0:T(8,128)S(1)}, f32[12,20,512]{2,1,0:T(8,128)S(1)}, f32[12,20,512]{2,1,0:T(8,128)S(1)}, f3...) fusion(f32[12,20,512]{2,1,0:T(8,128)S(1)} %get-tuple-element.36, f32[16,24,512]{2,1,0:T(8,128)S(1)} %get-tuple-element.41, ...), kind=kLoop, calls=%fused_computation.147 | loop fusion | flops 3686400 | bytes 7495680 | tf_op jit(solution)/shard_map/transpose(jvp())/add_any | solution.py:62
  102.9 3.7 %fusion.105 = (f32[14,22,514]{2,1,0:T(8,128)S(1)}, f32[14,22,514]{2,1,0:T(8,128)S(1)}, f32[14,22,514]{2,1,0:T(8,128)S(1)}, f32[14,22,514]{2,1,0:T(8,128)S(1)}) fusion(f32[14,22,514]{2,1,0:T(8,128)S(1)} %get-tuple-element.10, f32[12,20,512]{2,1,0:T(8,128)S(1)} %get-tuple-element.81, f32[12,20,512]{2,1,0:T(8,128)S(1)} %get-tuple-element.35, ...), kind=kLoop, calls=%fused_computation.255 | loop fusion | flops 14089768 | bytes 5415776 | tf_op jit(solution)/shard_map/transpose(jvp())/neg | solution.py:43
  106.6 3.0 %fusion.107 = (f32[14,22,514]{2,1,0:T(8,128)S(1)}, f32[14,22,514]{2,1,0:T(8,128)S(1)}, f32[14,22,514]{2,1,0:T(8,128)S(1)}, f32[14,22,514]{2,1,0:T(8,128)S(1)}, f...) fusion(f32[14,22,514]{2,1,0:T(8,128)S(1)} %get-tuple-element.11, f32[14,22,514]{2,1,0:T(8,128)S(1)} %get-tuple-element.30, ...), kind=kLoop, calls=%fused_computation.256 | loop fusion | flops 10606904 | bytes 7948768 | tf_op jit(solution)/shard_map/transpose(jvp())/neg | solution.py:42
  109.6 0.4 fusion.115
  110.2 0.4 fusion.114
  110.6 1.0 add_multiply_fusion.11
  111.7 0.5 fusion.64
  112.2 0.7 add_multiply_fusion.10
  112.9 2.4 %fusion.75 = (f32[8,16,512]{2,1,0:T(8,128)}, f32[8,16,512]{2,1,0:T(8,128)S(1)}, f32[8,16,512]{2,1,0:T(8,128)S(1)}) fusion(f32[10,18,514]{2,1,0:T(8,128)S(1)} %get-tuple-element.57, f32[10,18,514]{2,1,0:T(8,128)S(1)} %get-tuple-element.56, f32[10,18,514]{2,1,0:T(8,128)S(1)} %get-tuple-element.13, f32[12,20,512]{2,1,0:T(8,128)S(1)} %get-tuple-element.37, ...), kind=kLoop, calls=%fused_computation.195 | loop fusion | flops 2555904 | bytes 10516928 | tf_op jit(solution)/shard_map/add | solution.py:153
  115.4 0.7 fusion.70
  116.3 2.5 %fusion.98 = (f32[10,18,514]{2,1,0:T(8,128)S(1)}, f32[10,18,514]{2,1,0:T(8,128)S(1)}, f32[10,18,514]{2,1,0:T(8,128)S(1)}, f32[10,18,514]{2,1,0:T(8,128)S(1)}) fusion(f32[10,18,514]{2,1,0:T(8,128)S(1)} %get-tuple-element.14, f32[8,16,512]{2,1,0:T(8,128)S(1)} %get-tuple-element.59, f32[8,16,512]{2,1,0:T(8,128)S(1)} %get-tuple-element.58, ...), kind=kLoop, calls=%fused_computation.251 | loop fusion | flops 8234280 | bytes 3114848 | tf_op jit(solution)/shard_map/transpose(jvp())/neg | solution.py:43
  118.8 1.5 fusion.100
  120.3 0.9 fusion.53
  121.2 1.9 %collective-permute-start.8 = (f32[2,2,20,512]{3,2,1,0:T(8,128)S(1)}, f32[2,2,20,512]{3,2,1,0:T(8,128)S(1)}, u32[]{:S(2)}, u32[]{:S(2)}) collective-permute-start(f32[2,2,20,512]{3,2,1,0:T(8,128)S(1)} %pad_maximum_fusion.7), channel_id=1, source_target_pairs={{0,8},{8,16},{16,24},{24,32},{32,40},{40,48},{48,56},{56,64},{64,7... | collective-permute-start | bytes 491528 | tf_op jit(solution)/shard_map/ppermute | solution.py:19
  123.1 8.2 %collective-permute-done.8 = f32[2,2,20,512]{3,2,1,0:T(8,128)S(1)} collective-permute-done((f32[2,2,20,512]{3,2,1,0:T(8,128)S(1)}, f32[2,2,20,512]{3,2,1,0:T(8,128)S(1)}, u32[]{:S(2)}, u32[]{:S(2)}) %collective-permute-start.8) | collective-permute-done | bytes 163872 | tf_op jit(solution)/shard_map/ppermute | solution.py:19
  131.3 1.9 %collective-permute-start.9 = (f32[2,2,20,512]{3,2,1,0:T(8,128)S(1)}, f32[2,2,20,512]{3,2,1,0:T(8,128)S(1)}, u32[]{:S(2)}, u32[]{:S(2)}) collective-permute-start(f32[2,2,20,512]{3,2,1,0:T(8,128)S(1)} %get-tuple-element.66), channel_id=1, source_target_pairs={{8,0},{16,8},{24,16},{32,24},{40,32},{48,40},{56,48},{64,56},{72,6... | collective-permute-start | bytes 491528 | tf_op jit(solution)/shard_map/ppermute | solution.py:19
  133.3 3.1 %collective-permute-done.9 = f32[2,2,20,512]{3,2,1,0:T(8,128)S(1)} collective-permute-done((f32[2,2,20,512]{3,2,1,0:T(8,128)S(1)}, f32[2,2,20,512]{3,2,1,0:T(8,128)S(1)}, u32[]{:S(2)}, u32[]{:S(2)}) %collective-permute-start.9) | collective-permute-done | bytes 163872 | tf_op jit(solution)/shard_map/ppermute | solution.py:19
  136.5 5.4 %collective-permute-start.10 = (f32[2,8,2,512]{3,2,1,0:T(2,128)S(1)}, f32[2,8,2,512]{3,2,1,0:T(2,128)S(1)}, u32[]{:S(2)}, u32[]{:S(2)}) collective-permute-start(f32[2,8,2,512]{3,2,1,0:T(2,128)S(1)} %pad_maximum_fusion.15), channel_id=1, source_target_pairs={{0,1},{1,2},{2,3},{3,4},{4,5},{5,6},{6,7},{8,9},{9,10},{10,11},{11... | collective-permute-start | bytes 196616 | tf_op jit(solution)/shard_map/ppermute | solution.py:19
  141.9 2.1 %collective-permute-done.10 = f32[2,8,2,512]{3,2,1,0:T(2,128)S(1)} collective-permute-done((f32[2,8,2,512]{3,2,1,0:T(2,128)S(1)}, f32[2,8,2,512]{3,2,1,0:T(2,128)S(1)}, u32[]{:S(2)}, u32[]{:S(2)}) %collective-permute-start.10) | collective-permute-done | bytes 65568 | tf_op jit(solution)/shard_map/ppermute | solution.py:19
  144.1 3.9 %collective-permute-start.11 = (f32[2,8,2,512]{3,2,1,0:T(2,128)S(1)}, f32[2,8,2,512]{3,2,1,0:T(2,128)S(1)}, u32[]{:S(2)}, u32[]{:S(2)}) collective-permute-start(f32[2,8,2,512]{3,2,1,0:T(2,128)S(1)} %get-tuple-element.76), channel_id=1, source_target_pairs={{1,0},{2,1},{3,2},{4,3},{5,4},{6,5},{7,6},{9,8},{10,9},{11,10},{12... | collective-permute-start | bytes 196616 | tf_op jit(solution)/shard_map/ppermute | solution.py:19
  148.2 2.2 %collective-permute-done.11 = f32[2,8,2,512]{3,2,1,0:T(2,128)S(1)} collective-permute-done((f32[2,8,2,512]{3,2,1,0:T(2,128)S(1)}, f32[2,8,2,512]{3,2,1,0:T(2,128)S(1)}, u32[]{:S(2)}, u32[]{:S(2)}) %collective-permute-start.11) | collective-permute-done | bytes 65568 | tf_op jit(solution)/shard_map/ppermute | solution.py:19
  150.5 0.8 slice_bitcast_fusion.5
  (38 shorter events, 2.3 us)
Async XLA Ops:
  1.8 23.9 %copy-start.2 = (f32[8,16,512]{2,1,0:T(8,128)S(1)}, f32[8,16,512]{2,1,0:T(8,128)}, u32[]{:S(2)}) copy-start(f32[8,16,512]{2,1,0:T(8,128)} %param.7) | copy-start | bytes 786436
  1.8 23.9 %copy-start.3 = (f32[8,16,512]{2,1,0:T(8,128)S(1)}, f32[8,16,512]{2,1,0:T(8,128)}, u32[]{:S(2)}) copy-start(f32[8,16,512]{2,1,0:T(8,128)} %param.6) | copy-start | bytes 786436
  1.8 23.8 %copy-start.4 = (f32[8,16,512]{2,1,0:T(8,128)S(1)}, f32[8,16,512]{2,1,0:T(8,128)}, u32[]{:S(2)}) copy-start(f32[8,16,512]{2,1,0:T(8,128)} %param.5) | copy-start | bytes 786436
  2.0 17.5 %collective-permute-start.4 = (f32[3,6,16,512]{3,2,1,0:T(8,128)S(1)}, f32[3,6,16,512]{3,2,1,0:T(8,128)S(1)}, u32[]{:S(2)}, u32[]{:S(2)}) collective-permute-start(f32[3,6,16,512]{3,2,1,0:T(8,128)S(1)} %get-tuple-element.79), channel_id=1, source_target_pairs={{0,8},{8,16},{16,24},{24,32},{32,40},{40,48},{48,56},{56,64},{64,7... | collective-permute-start | bytes 1769480 | tf_op jit(solution)/shard_map/ppermute | solution.py:30
  4.1 21.6 %collective-permute-start.5 = (f32[3,6,16,512]{3,2,1,0:T(8,128)S(1)}, f32[3,6,16,512]{3,2,1,0:T(8,128)S(1)}, u32[]{:S(2)}, u32[]{:S(2)}) collective-permute-start(f32[3,6,16,512]{3,2,1,0:T(8,128)S(1)} %get-tuple-element.80), channel_id=1, source_target_pairs={{8,0},{16,8},{24,16},{32,24},{40,32},{48,40},{56,48},{64,56},{72,6... | collective-permute-start | bytes 1769480 | tf_op jit(solution)/shard_map/ppermute | solution.py:32
  26.1 8.6 %copy-start = (f32[8,16,512]{2,1,0:T(8,128)S(1)}, f32[8,16,512]{2,1,0:T(8,128)}, u32[]{:S(2)}) copy-start(f32[8,16,512]{2,1,0:T(8,128)} %param.9) | copy-start | bytes 786436
  26.1 8.6 %copy-start.1 = (f32[8,16,512]{2,1,0:T(8,128)S(1)}, f32[8,16,512]{2,1,0:T(8,128)}, u32[]{:S(2)}) copy-start(f32[8,16,512]{2,1,0:T(8,128)} %param.8) | copy-start | bytes 786436
  26.5 58.9 %collective-permute-start.6 = (f32[3,20,6,512]{3,1,2,0:T(8,128)S(1)}, f32[3,20,6,512]{3,1,2,0:T(8,128)}, u32[]{:S(2)}, u32[]{:S(2)}) collective-permute-start(f32[3,20,6,512]{3,1,2,0:T(8,128)S(1)} %copy.16), channel_id=1, source_target_pairs={{0,1},{1,2},{2,3},{3,4},{4,5},{5,6},{6,7},{8,9},{9,10},{10,11},{11... | collective-permute-start | bytes 2211848 | tf_op jit(solution)/shard_map/ppermute | solution.py:30
  29.8 57.3 %collective-permute-start.7 = (f32[3,20,6,512]{3,1,2,0:T(8,128)}, f32[3,20,6,512]{3,1,2,0:T(8,128)}, u32[]{:S(2)}, u32[]{:S(2)}) collective-permute-start(f32[3,20,6,512]{3,1,2,0:T(8,128)} %copy.17), channel_id=1, source_target_pairs={{1,0},{2,1},{3,2},{4,3},{5,4},{6,5},{7,6},{9,8},{10,9},{11,10},{12... | collective-permute-start | bytes 2211848 | tf_op jit(solution)/shard_map/ppermute | solution.py:32
  35.4 38.6 %collective-permute-start = (f32[2,2,16,512]{3,2,1,0:T(8,128)}, f32[2,2,16,512]{3,2,1,0:T(8,128)S(1)}, u32[]{:S(2)}, u32[]{:S(2)}) collective-permute-start(f32[2,2,16,512]{3,2,1,0:T(8,128)} %get-tuple-element.84), channel_id=1, source_target_pairs={{0,8},{8,16},{16,24},{24,32},{32,40},{40,48},{48,56},{56,64},{64,7... | collective-permute-start | bytes 393224 | tf_op jit(solution)/shard_map/ppermute | solution.py:30
  37.3 36.7 %collective-permute-start.1 = (f32[2,2,16,512]{3,2,1,0:T(8,128)}, f32[2,2,16,512]{3,2,1,0:T(8,128)}, u32[]{:S(2)}, u32[]{:S(2)}) collective-permute-start(f32[2,2,16,512]{3,2,1,0:T(8,128)} %get-tuple-element.85), channel_id=1, source_target_pairs={{8,0},{16,8},{24,16},{32,24},{40,32},{48,40},{56,48},{64,56},{72,6... | collective-permute-start | bytes 393224 | tf_op jit(solution)/shard_map/ppermute | solution.py:32
  74.9 7.6 %collective-permute-start.2 = (f32[2,12,2,512]{3,2,1,0:T(2,128)S(1)}, f32[2,12,2,512]{3,2,1,0:T(2,128)S(1)}, u32[]{:S(2)}, u32[]{:S(2)}) collective-permute-start(f32[2,12,2,512]{3,2,1,0:T(2,128)S(1)} %get-tuple-element.77), channel_id=1, source_target_pairs={{0,1},{1,2},{2,3},{3,4},{4,5},{5,6},{6,7},{8,9},{9,10},{10,11},{11... | collective-permute-start | bytes 294920 | tf_op jit(solution)/shard_map/ppermute | solution.py:30
  76.9 7.5 %collective-permute-start.3 = (f32[2,12,2,512]{3,2,1,0:T(2,128)S(1)}, f32[2,12,2,512]{3,2,1,0:T(2,128)S(1)}, u32[]{:S(2)}, u32[]{:S(2)}) collective-permute-start(f32[2,12,2,512]{3,2,1,0:T(2,128)S(1)} %get-tuple-element.78), channel_id=1, source_target_pairs={{1,0},{2,1},{3,2},{4,3},{5,4},{6,5},{7,6},{9,8},{10,9},{11,10},{12... | collective-permute-start | bytes 294920 | tf_op jit(solution)/shard_map/ppermute | solution.py:32
  99.9 1.4 copy-start.5
  121.2 10.1 %collective-permute-start.8 = (f32[2,2,20,512]{3,2,1,0:T(8,128)S(1)}, f32[2,2,20,512]{3,2,1,0:T(8,128)S(1)}, u32[]{:S(2)}, u32[]{:S(2)}) collective-permute-start(f32[2,2,20,512]{3,2,1,0:T(8,128)S(1)} %pad_maximum_fusion.7), channel_id=1, source_target_pairs={{0,8},{8,16},{16,24},{24,32},{32,40},{40,48},{48,56},{56,64},{64,7... | collective-permute-start | bytes 491528 | tf_op jit(solution)/shard_map/ppermute | solution.py:19
  131.3 5.1 %collective-permute-start.9 = (f32[2,2,20,512]{3,2,1,0:T(8,128)S(1)}, f32[2,2,20,512]{3,2,1,0:T(8,128)S(1)}, u32[]{:S(2)}, u32[]{:S(2)}) collective-permute-start(f32[2,2,20,512]{3,2,1,0:T(8,128)S(1)} %get-tuple-element.66), channel_id=1, source_target_pairs={{8,0},{16,8},{24,16},{32,24},{40,32},{48,40},{56,48},{64,56},{72,6... | collective-permute-start | bytes 491528 | tf_op jit(solution)/shard_map/ppermute | solution.py:19
  136.5 7.5 %collective-permute-start.10 = (f32[2,8,2,512]{3,2,1,0:T(2,128)S(1)}, f32[2,8,2,512]{3,2,1,0:T(2,128)S(1)}, u32[]{:S(2)}, u32[]{:S(2)}) collective-permute-start(f32[2,8,2,512]{3,2,1,0:T(2,128)S(1)} %pad_maximum_fusion.15), channel_id=1, source_target_pairs={{0,1},{1,2},{2,3},{3,4},{4,5},{5,6},{6,7},{8,9},{9,10},{10,11},{11... | collective-permute-start | bytes 196616 | tf_op jit(solution)/shard_map/ppermute | solution.py:19
  144.1 6.3 %collective-permute-start.11 = (f32[2,8,2,512]{3,2,1,0:T(2,128)S(1)}, f32[2,8,2,512]{3,2,1,0:T(2,128)S(1)}, u32[]{:S(2)}, u32[]{:S(2)}) collective-permute-start(f32[2,8,2,512]{3,2,1,0:T(2,128)S(1)} %get-tuple-element.76), channel_id=1, source_target_pairs={{1,0},{2,1},{3,2},{4,3},{5,4},{6,5},{7,6},{9,8},{10,9},{11,10},{12... | collective-permute-start | bytes 196616 | tf_op jit(solution)/shard_map/ppermute | solution.py:19

commit v2 on v1

--- a/solution.py
+++ b/solution.py
@@ -74,25 +74,25 @@
     return (new_phase, new_temp)
 
 
-def fold_rims(sensitivity_order_parameter, sensitivity_heat_level):
-    stacked = jnp.stack((sensitivity_order_parameter, sensitivity_heat_level))
-    lower_rim = stacked[:, :2]
-    upper_rim = stacked[:, -2:]
-    middle = stacked[:, 2:-2]
-    from_above = from_behind(lower_rim, "gz", -1)
-    from_below = from_behind(upper_rim, "gz", 1)
-    middle = jnp.concatenate(
-        (middle[:, :2] + from_below, middle[:, 2:-2], middle[:, -2:] + from_above), axis=1
-    )
-    lower_rim = middle[:, :, :2]
-    upper_rim = middle[:, :, -2:]
-    middle = middle[:, :, 2:-2]
-    from_above = from_behind(lower_rim, "gy", -1)
-    from_below = from_behind(upper_rim, "gy", 1)
-    middle = jnp.concatenate(
-        (middle[:, :, :2] + from_below, middle[:, :, 2:-2], middle[:, :, -2:] + from_above), axis=2
-    )
-    return (middle[0], middle[1])
+def fold_rims(contributions, width, sides):
+    for axis, dim in sides:
+        size = contributions.shape[dim]
+        lower_rim = lax.slice_in_dim(contributions, 0, width, axis=dim)
+        upper_rim = lax.slice_in_dim(contributions, size - width, size, axis=dim)
+        middle = lax.slice_in_dim(contributions, width, size - width, axis=dim)
+        inner = size - 2 * width
+        lower_rim, upper_rim = lax.optimization_barrier((lower_rim, upper_rim))
+        from_above = from_behind(lower_rim, axis, -1)
+        from_below = from_behind(upper_rim, axis, 1)
+        contributions = jnp.concatenate(
+            (
+                lax.slice_in_dim(middle, 0, width, axis=dim) + from_below,
+                lax.slice_in_dim(middle, width, inner - width, axis=dim),
+                lax.slice_in_dim(middle, inner - width, inner, axis=dim) + from_above,
+            ),
+            axis=dim,
+        )
+    return contributions
 
 
 def inside_grid(cells, margin):
@@ -114,18 +114,13 @@
     state = extended(
         jnp.stack((saved_order_parameter, saved_heat_level, kinetic_rate_field)),
         (("gz", 1), ("gy", 2)),
-        6,
-    )
-    seeds = extended(
-        jnp.stack((order_parameter_adjoint_seed, heat_level_adjoint_seed)),
-        (("gz", 1), ("gy", 2)),
-        2,
+        4,
     )
     phase_wide, temp_wide, rate_wide = state[0], state[1], state[2]
     succeeding_order_parameter, succeeding_heat_level = advance_solver_step(
         phase_wide, temp_wide, rate_wide[2:-2, 2:-2]
     )
-    valid = inside_grid(succeeding_order_parameter, 4)
+    valid = inside_grid(succeeding_order_parameter, 2)
     succeeding_order_parameter = jnp.where(valid, succeeding_order_parameter, 0.0)
     succeeding_heat_level = jnp.where(valid, succeeding_heat_level, 0.0)
     discarded_result, sensitivity_latest = jax.vjp(
@@ -134,23 +129,24 @@
         succeeding_heat_level,
         rate_wide[4:-4, 4:-4],
     )
-    sensitivity_order_parameter, sensitivity_heat_level, latest_kinetic_rate = sensitivity_latest(
-        (seeds[0], seeds[1])
+    halfway_order_parameter, halfway_heat_level, latest_kinetic_rate = sensitivity_latest(
+        (order_parameter_adjoint_seed, heat_level_adjoint_seed)
     )
-    halfway_order_parameter = sensitivity_order_parameter[4:-4, 4:-4]
-    halfway_heat_level = sensitivity_heat_level[4:-4, 4:-4]
-    latest_kinetic_rate = latest_kinetic_rate[2:-2, 2:-2]
+    halfway_order_parameter = jnp.where(valid, halfway_order_parameter, 0.0)
+    halfway_heat_level = jnp.where(valid, halfway_heat_level, 0.0)
     discarded_result, prior_backward_sweep = jax.vjp(
-        advance_solver_step,
-        phase_wide[4:-4, 4:-4],
-        temp_wide[4:-4, 4:-4],
-        rate_wide[6:-6, 6:-6],
+        advance_solver_step, phase_wide, temp_wide, rate_wide[2:-2, 2:-2]
     )
     sensitivity_order_parameter, sensitivity_heat_level, early_mob = prior_backward_sweep(
         (halfway_order_parameter, halfway_heat_level)
     )
-    start_phase, start_temp = fold_rims(sensitivity_order_parameter, sensitivity_heat_level)
-    return (start_phase, start_temp, latest_kinetic_rate + early_mob)
+    early_mob = jnp.pad(early_mob, ((2, 2), (2, 2), (0, 0)))
+    folded = fold_rims(
+        jnp.stack((sensitivity_order_parameter, sensitivity_heat_level, early_mob)),
+        4,
+        (("gy", 2), ("gz", 1)),
+    )
+    return (folded[0], folded[1], latest_kinetic_rate + folded[2])
 
 
 def solution(mesh):

time: 154 us -> 110 us (0.71)
  the two profiles are of different devices: /device:TPU:14 before, /device:TPU:34 now
where the time goes in v2:
time: 110 us
  waiting for transfers between devices  43.6 us (40%)
  starting transfers between devices  38.6 us (35%)
  other arithmetic  25.9 us (24%)
    ppermute x4, waiting for transfers between devices, from_behind(): return lax.ppermute(block, axis, route)  24 us
    ppermute x4, starting transfers between devices, from_behind(): return lax.ppermute(block, axis, route)  23.1 us
    ppermute x2, waiting for transfers between devices, extended(): lax.ppermute(head, axis, [((i + 1) % count, i) for i in range(ends)])  10.6 us
    ppermute x2, waiting for transfers between devices, extended(): lax.ppermute(tail, axis, [(i, (i + 1) % count) for i in range(ends)])  9.02 us
    ppermute x2, starting transfers between devices, extended(): lax.ppermute(head, axis, [((i + 1) % count, i) for i in range(ends)])  8.99 us
    ppermute x2, starting transfers between devices, extended(): lax.ppermute(tail, axis, [(i, (i + 1) % count) for i in range(ends)])  6.53 us
    neg x2, other arithmetic, advance_solver_step(): grad_x = 0.5 * (padded[1:-1, 1:-1, 2:] - padded[1:-1, 1:-1, :-2])  6.28 us
    neg x2, other arithmetic, advance_solver_step(): grad_y = 0.5 * (padded[1:-1, 2:, 1:-1] - padded[1:-1, :-2, 1:-1])  3.46 us
  transfers between devices with their start and end apart: 8, of which 8 were waited for; matrix products, arithmetic and copies ran while one was open for 0% of the time, Pallas kernels for 0%

profile of v2, /device:TPU:34, one launch (start us, length us, event | category | flops | bytes accessed | tf_op | source)
XLA Modules:
  0.0 109.9 jit_solution(18176257050877181006)
XLA Ops:
  0.7 1.2 %pad_maximum_fusion.1 = f32[3,8,16,512]{3,2,1,0:T(8,128)S(1)} fusion(f32[1,8,16,512]{3,2,1,0:T(8,128)} %bitcast.23, f32[1,8,16,512]{3,2,1,0:T(8,128)} %bitcast.26, f32[1,8,16,512]{3,2,1,0:T(8,128)} %bitcast.29), kind=kLoop, calls=%fused_computation.84 | loop fusion | flops 393216 | bytes 1572864 | tf_op jit(solution)/shard_map/stack | solution.py:115
  1.9 0.1 fusion.108
  2.0 0.0 copy-start
  2.0 6.9 %collective-permute-start.1 = (f32[3,4,16,512]{3,2,1,0:T(8,128)S(1)}, f32[3,4,16,512]{3,2,1,0:T(8,128)S(1)}, u32[]{:S(2)}, u32[]{:S(2)}) collective-permute-start(f32[3,4,16,512]{3,2,1,0:T(8,128)S(1)} %get-tuple-element.79), channel_id=1, source_target_pairs={{8,0},{16,8},{24,16},{32,24},{40,32},{48,40},{56,48},{64,56},{72,6... | collective-permute-start | bytes 1179656 | tf_op jit(solution)/shard_map/ppermute | solution.py:32
  8.8 1.9 %collective-permute-start = (f32[3,4,16,512]{3,2,1,0:T(8,128)S(1)}, f32[3,4,16,512]{3,2,1,0:T(8,128)S(1)}, u32[]{:S(2)}, u32[]{:S(2)}) collective-permute-start(f32[3,4,16,512]{3,2,1,0:T(8,128)S(1)} %get-tuple-element.78), channel_id=1, source_target_pairs={{0,8},{8,16},{16,24},{24,32},{32,40},{40,48},{48,56},{56,64},{64,7... | collective-permute-start | bytes 1179656 | tf_op jit(solution)/shard_map/ppermute | solution.py:30
  10.8 6.1 %collective-permute-done.1 = f32[3,4,16,512]{3,2,1,0:T(8,128)S(1)} collective-permute-done((f32[3,4,16,512]{3,2,1,0:T(8,128)S(1)}, f32[3,4,16,512]{3,2,1,0:T(8,128)S(1)}, u32[]{:S(2)}, u32[]{:S(2)}) %collective-permute-start.1) | collective-permute-done | bytes 393248 | tf_op jit(solution)/shard_map/ppermute | solution.py:32
  16.9 8.4 %collective-permute-done = f32[3,4,16,512]{3,2,1,0:T(8,128)S(1)} collective-permute-done((f32[3,4,16,512]{3,2,1,0:T(8,128)S(1)}, f32[3,4,16,512]{3,2,1,0:T(8,128)S(1)}, u32[]{:S(2)}, u32[]{:S(2)}) %collective-permute-start) | collective-permute-done | bytes 393248 | tf_op jit(solution)/shard_map/ppermute | solution.py:30
  25.3 0.2 pad_maximum_fusion.10
  25.5 2.1 %collective-permute-start.3 = (f32[3,16,4,512]{3,2,1,0:T(4,128)S(1)}, f32[3,16,4,512]{3,2,1,0:T(4,128)S(1)}, u32[]{:S(2)}, u32[]{:S(2)}) collective-permute-start(f32[3,16,4,512]{3,2,1,0:T(4,128)S(1)} %get-tuple-element.72), channel_id=1, source_target_pairs={{1,0},{2,1},{3,2},{4,3},{5,4},{6,5},{7,6},{9,8},{10,9},{11,10},{12... | collective-permute-start | bytes 1179656 | tf_op jit(solution)/shard_map/ppermute | solution.py:32
  27.6 4.6 %collective-permute-start.2 = (f32[3,16,4,512]{3,2,1,0:T(4,128)S(1)}, f32[3,16,4,512]{3,2,1,0:T(4,128)S(1)}, u32[]{:S(2)}, u32[]{:S(2)}) collective-permute-start(f32[3,16,4,512]{3,2,1,0:T(4,128)S(1)} %get-tuple-element.71), channel_id=1, source_target_pairs={{0,1},{1,2},{2,3},{3,4},{4,5},{5,6},{6,7},{8,9},{9,10},{10,11},{11... | collective-permute-start | bytes 1179656 | tf_op jit(solution)/shard_map/ppermute | solution.py:30
  32.3 0.1 and_and_fusion
  32.4 4.5 %collective-permute-done.3 = f32[3,16,4,512]{3,2,1,0:T(4,128)S(1)} collective-permute-done((f32[3,16,4,512]{3,2,1,0:T(4,128)S(1)}, f32[3,16,4,512]{3,2,1,0:T(4,128)S(1)}, u32[]{:S(2)}, u32[]{:S(2)}) %collective-permute-start.3) | collective-permute-done | bytes 393248 | tf_op jit(solution)/shard_map/ppermute | solution.py:32
  36.9 0.6 collective-permute-done.2
  37.5 0.4 pad_maximum_fusion
  37.9 0.2 slice_bitcast_fusion
  38.2 1.4 %add_multiply_fusion.5 = (f32[14,22,514]{2,1,0:T(8,128)S(1)}, f32[14,22,514]{2,1,0:T(8,128)S(1)}, f32[14,22,514]{2,1,0:T(8,128)S(1)}, f32[14,22,514]{2,1,0:T(8,1...) fusion(f32[16,24,512]{2,1,0:T(8,128)S(1)} %get-tuple-element.64), kind=kLoop, calls=%fused_computation.67 | loop fusion | flops 5224296 | bytes 5219168 | tf_op jit(solution)/shard_map/mul | solution.py:52
  39.6 0.1 slice.259
  39.7 0.2 pad_slice_fusion.16
  39.9 0.8 add_multiply_fusion.4
  40.7 1.8 %broadcast_select_fusion = (f32[12,20,512]{2,1,0:T(8,128)S(1)}, f32[12,20,512]{2,1,0:T(8,128)S(1)}, f32[12,20,512]{2,1,0:T(8,128)S(1)}, f32[12,20,512]{2,1,0:T(8,128)S(1)}, f32[12,20,512]{2,1,0:T(8,128)S(1)}) fusion(pred[20]{0:T(512)(128)(4,1)S(1)} %get-tuple-element.84, pred[20]{0:T(512)(128)(4,1)S(1)} %get-tuple-element.85, ...), kind=kLoop, calls=%fused_computation.177 | loop fusion | flops 3072000 | bytes 9338932 | tf_op jit(solution)/shard_map/jit(_where)/select_n | solution.py:124
  42.5 1.0 add_multiply_fusion.8
  43.6 0.6 fusion.79
  44.2 0.2 broadcast_multiply_fusion
  44.4 0.5 fusion.58
  44.9 2.8 %fusion.96 = (f32[10,18,514]{2,1,0:T(8,128)S(1)}, f32[10,18,514]{2,1,0:T(8,128)S(1)}, f32[10,18,514]{2,1,0:T(8,128)S(1)}, f32[10,18,514]{2,1,0:T(8,128)S(1)}, f32[10,18,514]{2,1,0:T(8,128)S(1)}) fusion(f32[10,18,514]{2,1,0:T(8,128)S(1)} %get-tuple-element.12, f32[8,16,512]{2,1,0:T(8,128)S(1)} %get-tuple-element.82, f32[8,16,512]{2,1,0:T(8,128)S(1)} %get-tuple-element.83, ...), kind=kLoop, calls=%fused_computation.225 | loop fusion | flops 8604360 | bytes 3484928 | tf_op jit(solution)/shard_map/transpose(jvp())/neg | solution.py:43
  47.7 1.6 %fusion.98 = (f32[10,18,514]{2,1,0:T(8,128)S(1)}, f32[10,18,514]{2,1,0:T(8,128)S(1)}, f32[10,18,514]{2,1,0:T(8,128)S(1)}, f32[10,18,514]{2,1,0:T(8,128)S(1)}, f32[10,18,514]{2,1,0:T(8,128)S(1)}) fusion(f32[10,18,514]{2,1,0:T(8,128)S(1)} %get-tuple-element.13, f32[10,18,514]{2,1,0:T(8,128)S(1)} %get-tuple-element.33, ...), kind=kLoop, calls=%fused_computation.226 | loop fusion | flops 5643720 | bytes 4225088 | tf_op jit(solution)/shard_map/transpose(jvp())/neg | solution.py:42
  49.2 2.2 %fusion.43 = (f32[12,20,512]{2,1,0:T(8,128)S(1)}, f32[12,20,512]{2,1,0:T(8,128)S(1)}) fusion(f32[16,24,512]{2,1,0:T(8,128)S(1)} %get-tuple-element.63, f32[16,24,512]{2,1,0:T(8,128)S(1)} %get-tuple-element.62, f32[16,24,512]{2,1,0:T(8,128)S(1)} %get-tuple-element.64, f32[8,16,512]{2,1,0:T(8,128)S(1)} %get-tuple-element.27, ...), kind=kLoop, calls=%fused_computation.127 | loop fusion | flops 4300800 | bytes 5464564 | tf_op jit(solution)/shard_map/transpose(jvp())/add_any | solution.py:62
  51.4 1.0 fusion.94
  52.4 0.1 pad_bitcast_fusion
  52.5 0.2 add_bitcast_fusion
  52.7 3.5 %fusion.88 = (f32[14,22,514]{2,1,0:T(8,128)S(1)}, f32[14,22,514]{2,1,0:T(8,128)S(1)}, f32[14,22,514]{2,1,0:T(8,128)S(1)}, f32[14,22,514]{2,1,0:T(8,128)S(1)}) fusion(f32[14,22,514]{2,1,0:T(8,128)S(1)} %get-tuple-element.47, f32[14,22,514]{2,1,0:T(8,128)S(1)} %get-tuple-element.55, f32[14,22,514]{2,1,0:T(8,128)S(1)} %get-tuple-element.43, ...), kind=kLoop, calls=%fused_computation.221 | loop fusion | flops 13298208 | bytes 8582016 | tf_op jit(solution)/shard_map/transpose(jvp())/neg | solution.py:43
  56.2 1.9 %fusion.90 = (f32[14,22,514]{2,1,0:T(8,128)S(1)}, f32[14,22,514]{2,1,0:T(8,128)S(1)}, f32[14,22,514]{2,1,0:T(8,128)S(1)}, f32[14,22,514]{2,1,0:T(8,128)S(1)}) fusion(f32[14,22,514]{2,1,0:T(8,128)S(1)} %get-tuple-element.46, f32[14,22,514]{2,1,0:T(8,128)S(1)} %get-tuple-element.20, f32[14,22,514]{2,1,0:T(8,128)S(1)} %get-tuple-element.19, ...), kind=kLoop, calls=%fused_computation.222 | loop fusion | flops 7598976 | bytes 9215264 | tf_op jit(solution)/shard_map/transpose(jvp())/neg | solution.py:42
  58.2 1.2 %fusion.21 = f32[1,16,24,512]{3,2,1,0:T(8,128)S(1)} fusion(f32[14,22,514]{2,1,0:T(8,128)S(1)} %get-tuple-element.53, f32[14,22,514]{2,1,0:T(8,128)S(1)} %get-tuple-element.52, f32[14,22,514]{2,1,0:T(8,128)S(1)} %get-tuple-element.22, f32[14,22,514]{2,1,0:T(8,128)S(1)} %get-tuple-element.21, f32[14,22,514]{2,1,0:T(8,128)S(1)} %get-tuple-element.18, ...), kind=kLoop, calls=%fused_computation.76 | loop fusion | flops 1179648 | bytes 5077440 | tf_op jit(solution)/shard_map/stack | solution.py:145
  59.4 0.2 pad_maximum_fusion.4
  59.6 5.3 %collective-permute-start.4 = (f32[3,16,4,512]{3,2,1,0:T(4,128)S(1)}, f32[3,16,4,512]{3,2,1,0:T(4,128)S(1)}, u32[]{:S(2)}, u32[]{:S(2)}) collective-permute-start(f32[3,16,4,512]{3,2,1,0:T(4,128)S(1)} %get-tuple-element.7), channel_id=1, source_target_pairs={{0,1},{1,2},{2,3},{3,4},{4,5},{5,6},{6,7},{8,9},{9,10},{10,11},{11... | collective-permute-start | bytes 1179656 | tf_op jit(solution)/shard_map/ppermute | solution.py:19
  64.9 1.9 %collective-permute-start.5 = (f32[3,16,4,512]{3,2,1,0:T(4,128)S(1)}, f32[3,16,4,512]{3,2,1,0:T(4,128)S(1)}, u32[]{:S(2)}, u32[]{:S(2)}) collective-permute-start(f32[3,16,4,512]{3,2,1,0:T(4,128)S(1)} %get-tuple-element.8), channel_id=1, source_target_pairs={{1,0},{2,1},{3,2},{4,3},{5,4},{6,5},{7,6},{9,8},{10,9},{11,10},{12... | collective-permute-start | bytes 1179656 | tf_op jit(solution)/shard_map/ppermute | solution.py:19
  66.8 3.3 %collective-permute-done.4 = f32[3,16,4,512]{3,2,1,0:T(4,128)S(1)} collective-permute-done((f32[3,16,4,512]{3,2,1,0:T(4,128)S(1)}, f32[3,16,4,512]{3,2,1,0:T(4,128)S(1)}, u32[]{:S(2)}, u32[]{:S(2)}) %collective-permute-start.4) | collective-permute-done | bytes 393248 | tf_op jit(solution)/shard_map/ppermute | solution.py:19
  70.2 6.9 %collective-permute-done.5 = f32[3,16,4,512]{3,2,1,0:T(4,128)S(1)} collective-permute-done((f32[3,16,4,512]{3,2,1,0:T(4,128)S(1)}, f32[3,16,4,512]{3,2,1,0:T(4,128)S(1)}, u32[]{:S(2)}, u32[]{:S(2)}) %collective-permute-start.5) | collective-permute-done | bytes 393248 | tf_op jit(solution)/shard_map/ppermute | solution.py:19
  77.1 0.3 maximum_add_fusion
  77.3 0.4 fusion.1
  77.7 0.1 fusion.107
  77.8 14.0 %collective-permute-start.7 = (f32[3,4,16,512]{3,2,1,0:T(8,128)S(1)}, f32[3,4,16,512]{3,2,1,0:T(8,128)S(1)}, u32[]{:S(2)}, u32[]{:S(2)}) collective-permute-start(f32[3,4,16,512]{3,2,1,0:T(8,128)S(1)} %get-tuple-element.10), channel_id=1, source_target_pairs={{8,0},{16,8},{24,16},{32,24},{40,32},{48,40},{56,48},{64,56},{72,6... | collective-permute-start | bytes 1179656 | tf_op jit(solution)/shard_map/ppermute | solution.py:19
  91.8 1.9 %collective-permute-start.6 = (f32[3,4,16,512]{3,2,1,0:T(8,128)S(1)}, f32[3,4,16,512]{3,2,1,0:T(8,128)S(1)}, u32[]{:S(2)}, u32[]{:S(2)}) collective-permute-start(f32[3,4,16,512]{3,2,1,0:T(8,128)S(1)} %get-tuple-element.9), channel_id=1, source_target_pairs={{0,8},{8,16},{16,24},{24,32},{32,40},{40,48},{48,56},{56,64},{64,7... | collective-permute-start | bytes 1179656 | tf_op jit(solution)/shard_map/ppermute | solution.py:19
  93.7 7.5 %collective-permute-done.7 = f32[3,4,16,512]{3,2,1,0:T(8,128)S(1)} collective-permute-done((f32[3,4,16,512]{3,2,1,0:T(8,128)S(1)}, f32[3,4,16,512]{3,2,1,0:T(8,128)S(1)}, u32[]{:S(2)}, u32[]{:S(2)}) %collective-permute-start.7) | collective-permute-done | bytes 393248 | tf_op jit(solution)/shard_map/ppermute | solution.py:19
  101.2 6.4 %collective-permute-done.6 = f32[3,4,16,512]{3,2,1,0:T(8,128)S(1)} collective-permute-done((f32[3,4,16,512]{3,2,1,0:T(8,128)S(1)}, f32[3,4,16,512]{3,2,1,0:T(8,128)S(1)}, u32[]{:S(2)}, u32[]{:S(2)}) %collective-permute-start.6) | collective-permute-done | bytes 393248 | tf_op jit(solution)/shard_map/ppermute | solution.py:19
  107.5 0.1 slice_add_fusion.3
  107.7 0.8 fusion.60
  108.5 1.4 %fusion.64 = f32[8,16,512]{2,1,0:T(8,128)} fusion(f32[3,4,16,512]{3,2,1,0:T(8,128)S(1)} %get-tuple-element.67, f32[3,4,16,512]{3,2,1,0:T(8,128)S(1)} %get-tuple-element.68, f32[10,18,514]{2,1,0:T(8,128)S(1)} %get-tuple-element.66, f32[10,18,514]{2,1,0:T(8,128)S(1)} %get-tuple-element.65, f32[10,18,514]{2,1,0:T(8,128)S(1)} %get-tuple-element.11, ...), kind=kLoop, calls=%fused_computation.188 | loop fusion | flops 1245184 | bytes 3670016 | tf_op jit(solution)/shard_map/add | solution.py:149
  (12 shorter events, 0.1 us)
Async XLA Ops:
  0.6 24.7 %copy-start.1 = (f32[8,16,512]{2,1,0:T(8,128)S(1)}, f32[8,16,512]{2,1,0:T(8,128)}, u32[]{:S(2)}) copy-start(f32[8,16,512]{2,1,0:T(8,128)} %param.7) | copy-start | bytes 786436
  0.6 24.7 %copy-start.2 = (f32[8,16,512]{2,1,0:T(8,128)S(1)}, f32[8,16,512]{2,1,0:T(8,128)}, u32[]{:S(2)}) copy-start(f32[8,16,512]{2,1,0:T(8,128)} %param.6) | copy-start | bytes 786436
  0.7 24.7 %copy-start.3 = (f32[8,16,512]{2,1,0:T(8,128)S(1)}, f32[8,16,512]{2,1,0:T(8,128)}, u32[]{:S(2)}) copy-start(f32[8,16,512]{2,1,0:T(8,128)} %param.5) | copy-start | bytes 786436
  2.0 30.4 %copy-start = (f32[8,16,512]{2,1,0:T(8,128)S(1)}, f32[8,16,512]{2,1,0:T(8,128)}, u32[]{:S(2)}) copy-start(f32[8,16,512]{2,1,0:T(8,128)} %param.9) | copy-start | bytes 786436
  2.0 14.9 %collective-permute-start.1 = (f32[3,4,16,512]{3,2,1,0:T(8,128)S(1)}, f32[3,4,16,512]{3,2,1,0:T(8,128)S(1)}, u32[]{:S(2)}, u32[]{:S(2)}) collective-permute-start(f32[3,4,16,512]{3,2,1,0:T(8,128)S(1)} %get-tuple-element.79), channel_id=1, source_target_pairs={{8,0},{16,8},{24,16},{32,24},{40,32},{48,40},{56,48},{64,56},{72,6... | collective-permute-start | bytes 1179656 | tf_op jit(solution)/shard_map/ppermute | solution.py:32
  8.8 16.5 %collective-permute-start = (f32[3,4,16,512]{3,2,1,0:T(8,128)S(1)}, f32[3,4,16,512]{3,2,1,0:T(8,128)S(1)}, u32[]{:S(2)}, u32[]{:S(2)}) collective-permute-start(f32[3,4,16,512]{3,2,1,0:T(8,128)S(1)} %get-tuple-element.78), channel_id=1, source_target_pairs={{0,8},{8,16},{16,24},{24,32},{32,40},{40,48},{48,56},{56,64},{64,7... | collective-permute-start | bytes 1179656 | tf_op jit(solution)/shard_map/ppermute | solution.py:30
  25.5 11.4 %collective-permute-start.3 = (f32[3,16,4,512]{3,2,1,0:T(4,128)S(1)}, f32[3,16,4,512]{3,2,1,0:T(4,128)S(1)}, u32[]{:S(2)}, u32[]{:S(2)}) collective-permute-start(f32[3,16,4,512]{3,2,1,0:T(4,128)S(1)} %get-tuple-element.72), channel_id=1, source_target_pairs={{1,0},{2,1},{3,2},{4,3},{5,4},{6,5},{7,6},{9,8},{10,9},{11,10},{12... | collective-permute-start | bytes 1179656 | tf_op jit(solution)/shard_map/ppermute | solution.py:32
  27.6 9.9 %collective-permute-start.2 = (f32[3,16,4,512]{3,2,1,0:T(4,128)S(1)}, f32[3,16,4,512]{3,2,1,0:T(4,128)S(1)}, u32[]{:S(2)}, u32[]{:S(2)}) collective-permute-start(f32[3,16,4,512]{3,2,1,0:T(4,128)S(1)} %get-tuple-element.71), channel_id=1, source_target_pairs={{0,1},{1,2},{2,3},{3,4},{4,5},{5,6},{6,7},{8,9},{9,10},{10,11},{11... | collective-permute-start | bytes 1179656 | tf_op jit(solution)/shard_map/ppermute | solution.py:30
  42.5 1.1 copy-start.4
  59.6 10.6 %collective-permute-start.4 = (f32[3,16,4,512]{3,2,1,0:T(4,128)S(1)}, f32[3,16,4,512]{3,2,1,0:T(4,128)S(1)}, u32[]{:S(2)}, u32[]{:S(2)}) collective-permute-start(f32[3,16,4,512]{3,2,1,0:T(4,128)S(1)} %get-tuple-element.7), channel_id=1, source_target_pairs={{0,1},{1,2},{2,3},{3,4},{4,5},{5,6},{6,7},{8,9},{9,10},{10,11},{11... | collective-permute-start | bytes 1179656 | tf_op jit(solution)/shard_map/ppermute | solution.py:19
  64.9 12.2 %collective-permute-start.5 = (f32[3,16,4,512]{3,2,1,0:T(4,128)S(1)}, f32[3,16,4,512]{3,2,1,0:T(4,128)S(1)}, u32[]{:S(2)}, u32[]{:S(2)}) collective-permute-start(f32[3,16,4,512]{3,2,1,0:T(4,128)S(1)} %get-tuple-element.8), channel_id=1, source_target_pairs={{1,0},{2,1},{3,2},{4,3},{5,4},{6,5},{7,6},{9,8},{10,9},{11,10},{12... | collective-permute-start | bytes 1179656 | tf_op jit(solution)/shard_map/ppermute | solution.py:19
  77.8 23.4 %collective-permute-start.7 = (f32[3,4,16,512]{3,2,1,0:T(8,128)S(1)}, f32[3,4,16,512]{3,2,1,0:T(8,128)S(1)}, u32[]{:S(2)}, u32[]{:S(2)}) collective-permute-start(f32[3,4,16,512]{3,2,1,0:T(8,128)S(1)} %get-tuple-element.10), channel_id=1, source_target_pairs={{8,0},{16,8},{24,16},{32,24},{40,32},{48,40},{56,48},{64,56},{72,6... | collective-permute-start | bytes 1179656 | tf_op jit(solution)/shard_map/ppermute | solution.py:19
  91.8 15.7 %collective-permute-start.6 = (f32[3,4,16,512]{3,2,1,0:T(8,128)S(1)}, f32[3,4,16,512]{3,2,1,0:T(8,128)S(1)}, u32[]{:S(2)}, u32[]{:S(2)}) collective-permute-start(f32[3,4,16,512]{3,2,1,0:T(8,128)S(1)} %get-tuple-element.9), channel_id=1, source_target_pairs={{0,8},{8,16},{16,24},{24,32},{32,40},{40,48},{48,56},{56,64},{64,7... | collective-permute-start | bytes 1179656 | tf_op jit(solution)/shard_map/ppermute | solution.py:19

commit v3 on v2

v3 whole, which is shorter than its diff:
```python
import jax
import jax.numpy as jnp
from jax import lax
from jax.sharding import PartitionSpec as P

TIME_STEP = 0.15
ENERGY_SCALE = 0.5
ANISOTROPY = 0.05
GRAD_FLOOR = 0.01
LATENT_HEAT = 1.8
DRIVE_SCALE = 0.9
DRIVE_SHARP = 10.0
MELT_POINT = 1.0


def from_behind(block, axis, distance):
    devices = range(lax.axis_size(axis))
    route = [(i - distance, i) for i in devices if i - distance in devices]
    return lax.ppermute(block, axis, route)


def swap_rims(fields, widths, axis, dim):
    lower = [lax.slice_in_dim(f, 0, w, axis=dim) for f, w in zip(fields, widths)]
    upper = [
        lax.slice_in_dim(f, f.shape[dim] - w, f.shape[dim], axis=dim)
        for f, w in zip(fields, widths)
    ]
    lower, upper = jnp.concatenate(lower, 0), jnp.concatenate(upper, 0)
    lower, upper = lax.optimization_barrier((lower, upper))
    from_above = from_behind(lower, axis, -1)
    from_below = from_behind(upper, axis, 1)
    sizes = [r.shape[0] for r in (lax.slice_in_dim(f, 0, w, axis=dim) for f, w in zip(fields, widths))]
    cuts = [sum(sizes[:i]) for i in range(len(sizes) + 1)]
    below = [from_below[cuts[i]:cuts[i + 1]] for i in range(len(sizes))]
    above = [from_above[cuts[i]:cuts[i + 1]] for i in range(len(sizes))]
    return below, above


def extended(fields, widths, axis, dim):
    below, above = swap_rims(fields, widths, axis, dim)
    return [jnp.concatenate((b, f, a), axis=dim) for f, b, a in zip(fields, below, above)]


def folded(fields, widths, axis, dim):
    below, above = swap_rims(fields, widths, axis, dim)
    result = []
    for f, w, b, a in zip(fields, widths, below, above):
        size = f.shape[dim]
        result.append(
            jnp.concatenate(
                (
                    lax.slice_in_dim(f, w, 2 * w, axis=dim) + b,
                    lax.slice_in_dim(f, 2 * w, size - 2 * w, axis=dim),
                    lax.slice_in_dim(f, size - 2 * w, size - w, axis=dim) + a,
                ),
                axis=dim,
            )
        )
    return result


def advance_solver_step(phase_wide, temp_ring, kinetic_rate_field):
    padded = jnp.pad(phase_wide, ((0, 0), (0, 0), (2, 2)))
    grad_z = 0.5 * (padded[2:, 1:-1, 1:-1] - padded[:-2, 1:-1, 1:-1])
    grad_y = 0.5 * (padded[1:-1, 2:, 1:-1] - padded[1:-1, :-2, 1:-1])
    grad_x = 0.5 * (padded[1:-1, 1:-1, 2:] - padded[1:-1, 1:-1, :-2])
    sq_z = grad_z * grad_z
    sq_y = grad_y * grad_y
    sq_x = grad_x * grad_x
    squared = sq_z + sq_y + sq_x + GRAD_FLOOR
    quartic = (sq_z * sq_z + sq_y * sq_y + sq_x * sq_x) / (squared * squared)
    anisotropy = 1.0 + ANISOTROPY * (4.0 * quartic - 3.0)
    aniso_sq = anisotropy * anisotropy
    factor_a = 16.0 * ANISOTROPY * anisotropy / squared
    flux_z = ENERGY_SCALE * (aniso_sq * grad_z + factor_a * grad_z * (sq_z - quartic * squared))
    flux_y = ENERGY_SCALE * (aniso_sq * grad_y + factor_a * grad_y * (sq_y - quartic * squared))
    flux_x = ENERGY_SCALE * (aniso_sq * grad_x + factor_a * grad_x * (sq_x - quartic * squared))
    divergence = 0.5 * (flux_z[2:, 1:-1, 1:-1] - flux_z[:-2, 1:-1, 1:-1])
    divergence = divergence + 0.5 * (flux_y[1:-1, 2:, 1:-1] - flux_y[1:-1, :-2, 1:-1])
    divergence = divergence + 0.5 * (flux_x[1:-1, 1:-1, 2:] - flux_x[1:-1, 1:-1, :-2])
    phase_now = phase_wide[2:-2, 2:-2]
    temp_now = temp_ring[1:-1, 1:-1]
    driving = DRIVE_SCALE / jnp.pi * jnp.arctan(DRIVE_SHARP * (MELT_POINT - temp_now))
    growth = kinetic_rate_field * (
        divergence + phase_now * (1.0 - phase_now) * (phase_now - 0.5 + driving)
    )
    new_phase = phase_now + TIME_STEP * growth
    temp_x = jnp.pad(temp_now, ((0, 0), (0, 0), (1, 1)))
    laplacian = (
        temp_ring[2:, 1:-1]
        + temp_ring[:-2, 1:-1]
        + temp_ring[1:-1, 2:]
        + temp_ring[1:-1, :-2]
    )
    laplacian = laplacian + temp_x[:, :, 2:] + temp_x[:, :, :-2] - 6.0 * temp_now
    new_temp = temp_now + TIME_STEP * laplacian + LATENT_HEAT * (new_phase - phase_now)
    return (new_phase, new_temp)


def inside_grid(cells, margin):
    nz, ny = cells.shape[0] - 2 * margin, cells.shape[1] - 2 * margin
    z = lax.axis_index("gz") * nz - margin + lax.broadcasted_iota(jnp.int32, cells.shape, 0)
    y = lax.axis_index("gy") * ny - margin + lax.broadcasted_iota(jnp.int32, cells.shape, 1)
    total_z = nz * lax.axis_size("gz")
    total_y = ny * lax.axis_size("gy")
    return (z >= 0) & (z < total_z) & (y >= 0) & (y < total_y)


def ring(cells, width):
    return jnp.pad(cells, ((width, width), (width, width), (0, 0)))


def body(
    saved_order_parameter,
    saved_heat_level,
    kinetic_rate_field,
    order_parameter_adjoint_seed,
    heat_level_adjoint_seed,
):
    fields = extended(
        [saved_order_parameter, saved_heat_level, kinetic_rate_field], [4, 3, 2], "gz", 0
    )
    phase_wide, temp_wide, rate_wide = extended(fields, [4, 4, 4], "gy", 1)
    temp_wide = temp_wide[:, 1:-1]
    rate_wide = rate_wide[:, 2:-2]
    (succeeding_order_parameter, succeeding_heat_level), prior_backward_sweep = jax.vjp(
        advance_solver_step, phase_wide, temp_wide, rate_wide
    )
    valid = inside_grid(succeeding_order_parameter, 2)
    succeeding_order_parameter = jnp.where(valid, succeeding_order_parameter, 0.0)
    succeeding_heat_level = jnp.where(valid, succeeding_heat_level, 0.0)
    discarded_result, sensitivity_latest = jax.vjp(
        advance_solver_step,
        succeeding_order_parameter,
        succeeding_heat_level[1:-1, 1:-1],
        rate_wide[2:-2, 2:-2],
    )
    halfway_order_parameter, halfway_heat_level, latest_kinetic_rate = sensitivity_latest(
        (order_parameter_adjoint_seed, heat_level_adjoint_seed)
    )
    halfway_heat_level = ring(halfway_heat_level, 1)
    halfway_order_parameter = jnp.where(valid, halfway_order_parameter, 0.0)
    halfway_heat_level = jnp.where(valid, halfway_heat_level, 0.0)
    sensitivity_order_parameter, sensitivity_heat_level, early_mob = prior_backward_sweep(
        (halfway_order_parameter, halfway_heat_level)
    )
    fields = folded(
        [
            sensitivity_order_parameter,
            jnp.pad(sensitivity_heat_level, ((0, 0), (1, 1), (0, 0))),
            jnp.pad(early_mob, ((0, 0), (2, 2), (0, 0))),
        ],
        [4, 4, 4],
        "gy",
        1,
    )
    start_phase, start_temp, early_mob = folded(fields, [4, 3, 2], "gz", 0)
    return (start_phase, start_temp, latest_kinetic_rate + early_mob)


def solution(mesh):
    return jax.shard_map(
        body,
        mesh=mesh,
        in_specs=(
            P("gz", "gy", None),
            P("gz", "gy", None),
            P("gz", "gy", None),
            P("gz", "gy", None),
            P("gz", "gy", None),
        ),
        out_specs=(P("gz", "gy", None), P("gz", "gy", None), P("gz", "gy", None)),
        check_vma=False,
    )
```

time: 110 us -> 124 us (1.13)
  the two profiles are of different devices: /device:TPU:34 before, /device:TPU:67 now
where the time goes in v3:
time: 124 us; the launch traced here: 123 us
  waiting for transfers between devices  60.7 us (49%)
  starting transfers between devices  28.2 us (23%)
  other arithmetic  26.8 us (22%)
  local copies, waits for them, and re-layouts  6.44 us (5%)
    ppermute x8, waiting for transfers between devices, from_behind(): return lax.ppermute(block, axis, route)  60.7 us
    ppermute x8, starting transfers between devices, from_behind(): return lax.ppermute(block, axis, route)  28.2 us
    neg x2, other arithmetic, advance_solver_step(): grad_x = 0.5 * (padded[1:-1, 1:-1, 2:] - padded[1:-1, 1:-1, :-2])  7.06 us
    unnamed x20, local copies, waits for them, and re-layouts  5.01 us
    neg x2, other arithmetic, advance_solver_step(): grad_y = 0.5 * (padded[1:-1, 2:, 1:-1] - padded[1:-1, :-2, 1:-1])  3.87 us
    mul x2, other arithmetic, advance_solver_step(): ENERGY_SCALE * (aniso_sq * grad_z + factor_a * grad_z * (sq_z - quartic *...  2.66 us
  transfers between devices with their start and end apart: 8, of which 8 were waited for; matrix products, arithmetic and copies ran while one was open for 1% of the time, Pallas kernels for 0%

profile of v3, /device:TPU:67, one launch (start us, length us, event | category | flops | bytes accessed | tf_op | source)
XLA Modules:
  0.0 123.4 jit_solution(12324242113496275766)
XLA Ops:
  0.6 1.2 copy.12
  2.0 0.8 copy-done.6
  3.1 0.3 pad_maximum_fusion.8
  3.3 6.7 %collective-permute-start = (f32[9,16,512]{2,0,1:T(8,128)S(1)}, f32[9,16,512]{2,0,1:T(8,128)S(1)}, u32[]{:S(2)}, u32[]{:S(2)}) collective-permute-start(f32[9,16,512]{2,0,1:T(8,128)S(1)} %get-tuple-element.11), channel_id=1, source_target_pairs={{0,8},{8,16},{16,24},{24,32},{32,40},{40,48},{48,56},{56,64},{64,7... | collective-permute-start | bytes 884744 | tf_op jit(solution)/shard_map/ppermute | solution.py:19
  10.0 1.9 %collective-permute-start.1 = (f32[9,16,512]{2,0,1:T(8,128)S(1)}, f32[9,16,512]{2,0,1:T(8,128)S(1)}, u32[]{:S(2)}, u32[]{:S(2)}) collective-permute-start(f32[9,16,512]{2,0,1:T(8,128)S(1)} %get-tuple-element.12), channel_id=1, source_target_pairs={{8,0},{16,8},{24,16},{32,24},{40,32},{48,40},{56,48},{64,56},{72,6... | collective-permute-start | bytes 884744 | tf_op jit(solution)/shard_map/ppermute | solution.py:19
  12.0 9.5 %collective-permute-done = f32[9,16,512]{2,0,1:T(8,128)S(1)} collective-permute-done((f32[9,16,512]{2,0,1:T(8,128)S(1)}, f32[9,16,512]{2,0,1:T(8,128)S(1)}, u32[]{:S(2)}, u32[]{:S(2)}) %collective-permute-start) | collective-permute-done | bytes 294944 | tf_op jit(solution)/shard_map/ppermute | solution.py:19
  21.6 6.6 %collective-permute-done.1 = f32[9,16,512]{2,0,1:T(8,128)S(1)} collective-permute-done((f32[9,16,512]{2,0,1:T(8,128)S(1)}, f32[9,16,512]{2,0,1:T(8,128)S(1)}, u32[]{:S(2)}, u32[]{:S(2)}) %collective-permute-start.1) | collective-permute-done | bytes 294944 | tf_op jit(solution)/shard_map/ppermute | solution.py:19
  28.4 0.2 fusion.53
  28.5 1.3 %collective-permute-start.2 = (f32[42,4,512]{2,0,1:T(8,128)S(1)}, f32[42,4,512]{2,0,1:T(8,128)S(1)}, u32[]{:S(2)}, u32[]{:S(2)}) collective-permute-start(f32[42,4,512]{2,0,1:T(8,128)S(1)} %get-tuple-element.13), channel_id=1, source_target_pairs={{0,1},{1,2},{2,3},{3,4},{4,5},{5,6},{6,7},{8,9},{9,10},{10,11},{11... | collective-permute-start | bytes 1032200 | tf_op jit(solution)/shard_map/ppermute | solution.py:19
  29.8 1.3 %collective-permute-start.3 = (f32[42,4,512]{2,0,1:T(8,128)S(1)}, f32[42,4,512]{2,0,1:T(8,128)S(1)}, u32[]{:S(2)}, u32[]{:S(2)}) collective-permute-start(f32[42,4,512]{2,0,1:T(8,128)S(1)} %get-tuple-element.14), channel_id=1, source_target_pairs={{1,0},{2,1},{3,2},{4,3},{5,4},{6,5},{7,6},{9,8},{10,9},{11,10},{12... | collective-permute-start | bytes 1032200 | tf_op jit(solution)/shard_map/ppermute | solution.py:19
  31.3 0.2 copy_multiply_fusion
  31.5 3.0 %collective-permute-done.2 = f32[42,4,512]{2,0,1:T(8,128)S(1)} collective-permute-done((f32[42,4,512]{2,0,1:T(8,128)S(1)}, f32[42,4,512]{2,0,1:T(8,128)S(1)}, u32[]{:S(2)}, u32[]{:S(2)}) %collective-permute-start.2) | collective-permute-done | bytes 344096 | tf_op jit(solution)/shard_map/ppermute | solution.py:19
  34.5 11.2 %collective-permute-done.3 = f32[42,4,512]{2,0,1:T(8,128)S(1)} collective-permute-done((f32[42,4,512]{2,0,1:T(8,128)S(1)}, f32[42,4,512]{2,0,1:T(8,128)S(1)}, u32[]{:S(2)}, u32[]{:S(2)}) %collective-permute-start.3) | collective-permute-done | bytes 344096 | tf_op jit(solution)/shard_map/ppermute | solution.py:19
  45.9 1.4 %add_multiply_fusion.5 = (f32[14,22,514]{2,0,1:T(8,128)S(1)}, f32[14,22,514]{2,0,1:T(8,128)S(1)}, f32[14,22,514]{2,0,1:T(8,128)S(1)}, f32[14,22,514]{2,0,1:T(8,1...) fusion(f32[16,24,512]{2,0,1:T(8,128)S(1)} %pad_maximum_fusion), kind=kLoop, calls=%fused_computation.57 | loop fusion | flops 5224296 | bytes 5219168 | tf_op jit(solution)/shard_map/jvp()/mul | solution.py:75
  47.4 0.9 slice-done
  48.4 0.8 add_multiply_fusion.4
  49.2 0.2 copy-done.4
  49.4 1.9 %broadcast_select_fusion = (f32[12,20,512]{2,0,1:T(8,128)S(1)}, f32[12,20,512]{2,0,1:T(8,128)S(1)}, f32[12,20,512]{2,0,1:T(8,128)S(1)}, f32[12,20,512]{2,0,1:T(8,128)S(1)}, f32[12,20,512]{2,0,1:T(8,128)S(1)}) fusion(pred[20]{0:T(512)(128)(4,1)S(1)} %get-tuple-element.113, pred[20]{0:T(512)(128)(4,1)S(1)} %get-tuple-element.114, ...), kind=kLoop, calls=%fused_computation.185 | loop fusion | flops 3072000 | bytes 6979636 | tf_op jit(solution)/shard_map/jit(_where)/select_n | solution.py:130
  51.3 0.4 fusion.36
  51.8 1.2 add_multiply_fusion.8
  53.0 1.1 fusion.79
  54.1 0.2 pad_add_fusion.7
  54.3 0.8 fusion.103
  55.1 3.4 %fusion.97 = (f32[10,18,514]{2,0,1:T(8,128)S(1)}, f32[10,18,514]{2,0,1:T(8,128)S(1)}, f32[10,18,514]{2,0,1:T(8,128)S(1)}, f32[10,18,514]{2,0,1:T(8,128)S(1)}, f32[10,18,514]{2,0,1:T(8,128)S(1)}) fusion(f32[10,18,514]{2,0,1:T(8,128)S(1)} %get-tuple-element.23, f32[8,16,512]{2,0,1:T(8,128)S(1)} %get-tuple-element.47, f32[8,16,512]{2,0,1:T(8,128)S(1)} %get-tuple-element.46, ...), kind=kLoop, calls=%fused_computation.259 | loop fusion | flops 8604360 | bytes 3484928 | tf_op jit(solution)/shard_map/transpose(jvp())/neg | solution.py:66
  58.5 1.9 %fusion.99 = (f32[10,18,514]{2,0,1:T(8,128)S(1)}, f32[10,18,514]{2,0,1:T(8,128)S(1)}, f32[10,18,514]{2,0,1:T(8,128)S(1)}, f32[10,18,514]{2,0,1:T(8,128)S(1)}, f32[10,18,514]{2,0,1:T(8,128)S(1)}) fusion(f32[10,18,514]{2,0,1:T(8,128)S(1)} %get-tuple-element.24, f32[10,18,514]{2,0,1:T(8,128)S(1)} %get-tuple-element.41, ...), kind=kLoop, calls=%fused_computation.260 | loop fusion | flops 5643720 | bytes 4225088 | tf_op jit(solution)/shard_map/transpose(jvp())/neg | solution.py:65
  60.4 1.1 fusion.85
  61.5 1.5 %broadcast_multiply_fusion = (f32[12,20,512]{2,0,1:T(8,128)S(1)}, f32[12,20,512]{2,0,1:T(8,128)S(1)}, f32[12,20,512]{2,0,1:T(8,128)S(1)}, f32[12,20,512]{2,0,1:T(8,128)S(1)}) fusion(f32[12,20,512]{2,0,1:T(8,128)S(1)} %get-tuple-element.35, f32[12,4,512]{2,0,1:T(8,128)S(1)} %slice.437, f32[2,16,512]{2,0,1:T(2,128)S(1)} %slice.432, ...), kind=kLoop, calls=%fused_computation.186 | loop fusion | flops 3686400 | bytes 4890676 | tf_op jit(solution)/shard_map/transpose(jvp())/mul | solution.py:80
  63.0 1.0 fusion.40
  64.0 0.2 pad_add_fusion
  64.3 3.7 %fusion.89 = (f32[14,22,514]{2,0,1:T(8,128)S(1)}, f32[14,22,514]{2,0,1:T(8,128)S(1)}, f32[14,22,514]{2,0,1:T(8,128)S(1)}, f32[14,22,514]{2,0,1:T(8,128)S(1)}) fusion(f32[14,22,514]{2,0,1:T(8,128)S(1)} %get-tuple-element.57, f32[14,22,514]{2,0,1:T(8,128)S(1)} %get-tuple-element.69, f32[14,22,514]{2,0,1:T(8,128)S(1)} %get-tuple-element.53, ...), kind=kLoop, calls=%fused_computation.256 | loop fusion | flops 13298208 | bytes 8582016 | tf_op jit(solution)/shard_map/transpose(jvp())/neg | solution.py:66
  67.9 2.0 %fusion.91 = (f32[14,22,514]{2,0,1:T(8,128)S(1)}, f32[14,22,514]{2,0,1:T(8,128)S(1)}, f32[14,22,514]{2,0,1:T(8,128)S(1)}, f32[14,22,514]{2,0,1:T(8,128)S(1)}) fusion(f32[14,22,514]{2,0,1:T(8,128)S(1)} %get-tuple-element.56, f32[14,22,514]{2,0,1:T(8,128)S(1)} %get-tuple-element.29, f32[14,22,514]{2,0,1:T(8,128)S(1)} %get-tuple-element.28, ...), kind=kLoop, calls=%fused_computation.257 | loop fusion | flops 7598976 | bytes 9215264 | tf_op jit(solution)/shard_map/transpose(jvp())/neg | solution.py:65
  69.9 0.4 pad_add_fusion.16
  70.4 2.3 %collective-permute-start.4 = (f32[42,4,512]{2,0,1:T(8,128)S(1)}, f32[42,4,512]{2,0,1:T(8,128)S(1)}, u32[]{:S(2)}, u32[]{:S(2)}) collective-permute-start(f32[42,4,512]{2,0,1:T(8,128)S(1)} %pad_maximum_fusion.25), channel_id=1, source_target_pairs={{0,1},{1,2},{2,3},{3,4},{4,5},{5,6},{6,7},{8,9},{9,10},{10,11},{11... | collective-permute-start | bytes 1032200 | tf_op jit(solution)/shard_map/ppermute | solution.py:19
  72.6 1.5 %collective-permute-start.5 = (f32[42,4,512]{2,0,1:T(8,128)S(1)}, f32[42,4,512]{2,0,1:T(8,128)S(1)}, u32[]{:S(2)}, u32[]{:S(2)}) collective-permute-start(f32[42,4,512]{2,0,1:T(8,128)S(1)} %pad_maximum_fusion.24), channel_id=1, source_target_pairs={{1,0},{2,1},{3,2},{4,3},{5,4},{6,5},{7,6},{9,8},{10,9},{11,10},{12... | collective-permute-start | bytes 1032200 | tf_op jit(solution)/shard_map/ppermute | solution.py:19
  74.2 0.5 pad_add_fusion.8
  74.7 3.4 %collective-permute-done.4 = f32[42,4,512]{2,0,1:T(8,128)S(1)} collective-permute-done((f32[42,4,512]{2,0,1:T(8,128)S(1)}, f32[42,4,512]{2,0,1:T(8,128)S(1)}, u32[]{:S(2)}, u32[]{:S(2)}) %collective-permute-start.4) | collective-permute-done | bytes 344096 | tf_op jit(solution)/shard_map/ppermute | solution.py:19
  78.1 10.7 %collective-permute-done.5 = f32[42,4,512]{2,0,1:T(8,128)S(1)} collective-permute-done((f32[42,4,512]{2,0,1:T(8,128)S(1)}, f32[42,4,512]{2,0,1:T(8,128)S(1)}, u32[]{:S(2)}, u32[]{:S(2)}) %collective-permute-start.5) | collective-permute-done | bytes 344096 | tf_op jit(solution)/shard_map/ppermute | solution.py:19
  88.7 0.5 slice_add_fusion.13
  89.5 0.2 fusion.51
  89.8 11.3 %collective-permute-start.6 = (f32[9,16,512]{2,0,1:T(8,128)S(1)}, f32[9,16,512]{2,0,1:T(8,128)S(1)}, u32[]{:S(2)}, u32[]{:S(2)}) collective-permute-start(f32[9,16,512]{2,0,1:T(8,128)S(1)} %get-tuple-element.17), channel_id=1, source_target_pairs={{0,8},{8,16},{16,24},{24,32},{32,40},{40,48},{48,56},{56,64},{64,7... | collective-permute-start | bytes 884744 | tf_op jit(solution)/shard_map/ppermute | solution.py:19
  101.1 1.9 %collective-permute-start.7 = (f32[9,16,512]{2,0,1:T(8,128)S(1)}, f32[9,16,512]{2,0,1:T(8,128)S(1)}, u32[]{:S(2)}, u32[]{:S(2)}) collective-permute-start(f32[9,16,512]{2,0,1:T(8,128)S(1)} %get-tuple-element.18), channel_id=1, source_target_pairs={{8,0},{16,8},{24,16},{32,24},{40,32},{48,40},{56,48},{64,56},{72,6... | collective-permute-start | bytes 884744 | tf_op jit(solution)/shard_map/ppermute | solution.py:19
  103.0 9.1 %collective-permute-done.6 = f32[9,16,512]{2,0,1:T(8,128)S(1)} collective-permute-done((f32[9,16,512]{2,0,1:T(8,128)S(1)}, f32[9,16,512]{2,0,1:T(8,128)S(1)}, u32[]{:S(2)}, u32[]{:S(2)}) %collective-permute-start.6) | collective-permute-done | bytes 294944 | tf_op jit(solution)/shard_map/ppermute | solution.py:19
  112.1 7.2 %collective-permute-done.7 = f32[9,16,512]{2,0,1:T(8,128)S(1)} collective-permute-done((f32[9,16,512]{2,0,1:T(8,128)S(1)}, f32[9,16,512]{2,0,1:T(8,128)S(1)}, u32[]{:S(2)}, u32[]{:S(2)}) %collective-permute-start.7) | collective-permute-done | bytes 294944 | tf_op jit(solution)/shard_map/ppermute | solution.py:19
  119.3 0.2 slice_add_fusion.15
  119.5 0.9 fusion.62
  120.4 0.9 copy.24
  121.5 0.9 copy.22
  122.6 0.9 copy.23
  (50 shorter events, 1.9 us)
Async XLA Ops:
  0.6 1.2 copy-start.5
  1.9 1.0 copy-start.6
  3.3 18.2 %collective-permute-start = (f32[9,16,512]{2,0,1:T(8,128)S(1)}, f32[9,16,512]{2,0,1:T(8,128)S(1)}, u32[]{:S(2)}, u32[]{:S(2)}) collective-permute-start(f32[9,16,512]{2,0,1:T(8,128)S(1)} %get-tuple-element.11), channel_id=1, source_target_pairs={{0,8},{8,16},{16,24},{24,32},{32,40},{40,48},{48,56},{56,64},{64,7... | collective-permute-start | bytes 884744 | tf_op jit(solution)/shard_map/ppermute | solution.py:19
  10.0 18.2 %collective-permute-start.1 = (f32[9,16,512]{2,0,1:T(8,128)S(1)}, f32[9,16,512]{2,0,1:T(8,128)S(1)}, u32[]{:S(2)}, u32[]{:S(2)}) collective-permute-start(f32[9,16,512]{2,0,1:T(8,128)S(1)} %get-tuple-element.12), channel_id=1, source_target_pairs={{8,0},{16,8},{24,16},{32,24},{40,32},{48,40},{56,48},{64,56},{72,6... | collective-permute-start | bytes 884744 | tf_op jit(solution)/shard_map/ppermute | solution.py:19
  28.3 2.9 %copy-start = (f32[8,16,512]{2,1,0:T(8,128)S(1)}, f32[8,16,512]{2,1,0:T(8,128)}, u32[]{:S(2)}) copy-start(f32[8,16,512]{2,1,0:T(8,128)} %param.9) | copy-start | bytes 786436
  28.5 6.0 %collective-permute-start.2 = (f32[42,4,512]{2,0,1:T(8,128)S(1)}, f32[42,4,512]{2,0,1:T(8,128)S(1)}, u32[]{:S(2)}, u32[]{:S(2)}) collective-permute-start(f32[42,4,512]{2,0,1:T(8,128)S(1)} %get-tuple-element.13), channel_id=1, source_target_pairs={{0,1},{1,2},{2,3},{3,4},{4,5},{5,6},{6,7},{8,9},{9,10},{10,11},{11... | collective-permute-start | bytes 1032200 | tf_op jit(solution)/shard_map/ppermute | solution.py:19
  29.8 15.9 %collective-permute-start.3 = (f32[42,4,512]{2,0,1:T(8,128)S(1)}, f32[42,4,512]{2,0,1:T(8,128)S(1)}, u32[]{:S(2)}, u32[]{:S(2)}) collective-permute-start(f32[42,4,512]{2,0,1:T(8,128)S(1)} %get-tuple-element.14), channel_id=1, source_target_pairs={{1,0},{2,1},{3,2},{4,3},{5,4},{6,5},{7,6},{9,8},{10,9},{11,10},{12... | collective-permute-start | bytes 1032200 | tf_op jit(solution)/shard_map/ppermute | solution.py:19
  34.5 12.8 %copy-start.3 = (f32[42,4,512]{2,0,1:T(8,128)}, f32[42,4,512]{2,0,1:T(8,128)S(1)}, u32[]{:S(2)}) copy-start(f32[42,4,512]{2,0,1:T(8,128)S(1)} %collective-permute-done.2) | copy-start | bytes 1032196
  47.3 0.9 slice-start
  48.4 1.0 copy-start.4
  51.7 1.3 %copy-start.1 = (f32[8,16,512]{2,1,0:T(8,128)S(1)}, f32[8,16,512]{2,1,0:T(8,128)}, u32[]{:S(2)}) copy-start(f32[8,16,512]{2,1,0:T(8,128)} %param.8) | copy-start | bytes 786436
  51.7 1.2 %copy-start.2 = (f32[8,16,512]{2,1,0:T(8,128)S(1)}, f32[8,16,512]{2,1,0:T(8,128)}, u32[]{:S(2)}) copy-start(f32[8,16,512]{2,1,0:T(8,128)} %param.7) | copy-start | bytes 786436
  70.4 7.7 %collective-permute-start.4 = (f32[42,4,512]{2,0,1:T(8,128)S(1)}, f32[42,4,512]{2,0,1:T(8,128)S(1)}, u32[]{:S(2)}, u32[]{:S(2)}) collective-permute-start(f32[42,4,512]{2,0,1:T(8,128)S(1)} %pad_maximum_fusion.25), channel_id=1, source_target_pairs={{0,1},{1,2},{2,3},{3,4},{4,5},{5,6},{6,7},{8,9},{9,10},{10,11},{11... | collective-permute-start | bytes 1032200 | tf_op jit(solution)/shard_map/ppermute | solution.py:19
  72.6 16.1 %collective-permute-start.5 = (f32[42,4,512]{2,0,1:T(8,128)S(1)}, f32[42,4,512]{2,0,1:T(8,128)S(1)}, u32[]{:S(2)}, u32[]{:S(2)}) collective-permute-start(f32[42,4,512]{2,0,1:T(8,128)S(1)} %pad_maximum_fusion.24), channel_id=1, source_target_pairs={{1,0},{2,1},{3,2},{4,3},{5,4},{6,5},{7,6},{9,8},{10,9},{11,10},{12... | collective-permute-start | bytes 1032200 | tf_op jit(solution)/shard_map/ppermute | solution.py:19
  89.8 22.3 %collective-permute-start.6 = (f32[9,16,512]{2,0,1:T(8,128)S(1)}, f32[9,16,512]{2,0,1:T(8,128)S(1)}, u32[]{:S(2)}, u32[]{:S(2)}) collective-permute-start(f32[9,16,512]{2,0,1:T(8,128)S(1)} %get-tuple-element.17), channel_id=1, source_target_pairs={{0,8},{8,16},{16,24},{24,32},{32,40},{40,48},{48,56},{56,64},{64,7... | collective-permute-start | bytes 884744 | tf_op jit(solution)/shard_map/ppermute | solution.py:19
  101.1 18.2 %collective-permute-start.7 = (f32[9,16,512]{2,0,1:T(8,128)S(1)}, f32[9,16,512]{2,0,1:T(8,128)S(1)}, u32[]{:S(2)}, u32[]{:S(2)}) collective-permute-start(f32[9,16,512]{2,0,1:T(8,128)S(1)} %get-tuple-element.18), channel_id=1, source_target_pairs={{8,0},{16,8},{24,16},{32,24},{40,32},{48,40},{56,48},{64,56},{72,6... | collective-permute-start | bytes 884744 | tf_op jit(solution)/shard_map/ppermute | solution.py:19

commit v4 on v2

--- a/solution.py
+++ b/solution.py
@@ -104,6 +104,34 @@
     return (z >= 0) & (z < total_z) & (y >= 0) & (y < total_y)
 
 
+def adjoint_of_layers(first, last, state, seeds):
+    phase_wide, temp_wide, rate_wide, succeeding_order_parameter, succeeding_heat_level, valid = state
+    discarded_result, sensitivity_latest = jax.vjp(
+        advance_solver_step,
+        succeeding_order_parameter[first : last + 4],
+        succeeding_heat_level[first : last + 4],
+        rate_wide[4 + first : 4 + last, 4:-4],
+    )
+    halfway_order_parameter, halfway_heat_level, latest_kinetic_rate = sensitivity_latest(
+        (seeds[0][first:last], seeds[1][first:last])
+    )
+    inside = valid[first : last + 4]
+    halfway_order_parameter = jnp.where(inside, halfway_order_parameter, 0.0)
+    halfway_heat_level = jnp.where(inside, halfway_heat_level, 0.0)
+    discarded_result, prior_backward_sweep = jax.vjp(
+        advance_solver_step,
+        phase_wide[first : last + 8],
+        temp_wide[first : last + 8],
+        rate_wide[2 + first : 2 + last + 4, 2:-2],
+    )
+    sensitivity_order_parameter, sensitivity_heat_level, early_mob = prior_backward_sweep(
+        (halfway_order_parameter, halfway_heat_level)
+    )
+    early_mob = jnp.pad(early_mob, ((2, 2), (2, 2), (0, 0)))
+    contributions = jnp.stack((sensitivity_order_parameter, sensitivity_heat_level, early_mob))
+    return contributions, latest_kinetic_rate
+
+
 def body(
     saved_order_parameter,
     saved_heat_level,
@@ -123,30 +151,22 @@
     valid = inside_grid(succeeding_order_parameter, 2)
     succeeding_order_parameter = jnp.where(valid, succeeding_order_parameter, 0.0)
     succeeding_heat_level = jnp.where(valid, succeeding_heat_level, 0.0)
-    discarded_result, sensitivity_latest = jax.vjp(
-        advance_solver_step,
-        succeeding_order_parameter,
-        succeeding_heat_level,
-        rate_wide[4:-4, 4:-4],
+    state = (phase_wide, temp_wide, rate_wide, succeeding_order_parameter, succeeding_heat_level, valid)
+    seeds = (order_parameter_adjoint_seed, heat_level_adjoint_seed)
+    half = saved_order_parameter.shape[0] // 2
+    lower, lower_rate = adjoint_of_layers(0, half, state, seeds)
+    state, seeds, lower, lower_rate = lax.optimization_barrier((state, seeds, lower, lower_rate))
+    lower = fold_rims(lower, 4, (("gy", 2),))
+    upper, upper_rate = adjoint_of_layers(half, 2 * half, state, seeds)
+    upper = fold_rims(upper, 4, (("gy", 2),))
+    from_below = from_behind(upper[:, -4:], "gz", 1)
+    from_above = from_behind(lower[:, :4], "gz", -1)
+    total = lower[:, 4:] + upper[:, :-4]
+    total = jnp.concatenate(
+        (total[:, :4] + from_below, total[:, 4:-4], total[:, -4:] + from_above), axis=1
     )
-    halfway_order_parameter, halfway_heat_level, latest_kinetic_rate = sensitivity_latest(
-        (order_parameter_adjoint_seed, heat_level_adjoint_seed)
-    )
-    halfway_order_parameter = jnp.where(valid, halfway_order_parameter, 0.0)
-    halfway_heat_level = jnp.where(valid, halfway_heat_level, 0.0)
-    discarded_result, prior_backward_sweep = jax.vjp(
-        advance_solver_step, phase_wide, temp_wide, rate_wide[2:-2, 2:-2]
-    )
-    sensitivity_order_parameter, sensitivity_heat_level, early_mob = prior_backward_sweep(
-        (halfway_order_parameter, halfway_heat_level)
-    )
-    early_mob = jnp.pad(early_mob, ((2, 2), (2, 2), (0, 0)))
-    folded = fold_rims(
-        jnp.stack((sensitivity_order_parameter, sensitivity_heat_level, early_mob)),
-        4,
-        (("gy", 2), ("gz", 1)),
-    )
-    return (folded[0], folded[1], latest_kinetic_rate + folded[2])
+    latest_kinetic_rate = jnp.concatenate((lower_rate, upper_rate), axis=0)
+    return (total[0], total[1], latest_kinetic_rate + total[2])
 
 
 def solution(mesh):

time: 110 us -> 126 us (1.15)
  the two profiles are of different devices: /device:TPU:34 before, /device:TPU:14 now
where the time goes in v4:
time: 126 us
  waiting for transfers between devices  48.5 us (38%)
  other arithmetic  37.8 us (30%)
  starting transfers between devices  36.3 us (29%)
  local copies, waits for them, and re-layouts  2.04 us (2%)
    ppermute x6, waiting for transfers between devices, from_behind(): return lax.ppermute(block, axis, route)  23.4 us
    ppermute x6, starting transfers between devices, from_behind(): return lax.ppermute(block, axis, route)  19.6 us
    ppermute x2, waiting for transfers between devices, extended(): lax.ppermute(tail, axis, [(i, (i + 1) % count) for i in range(ends)])  12.9 us
    ppermute x2, starting transfers between devices, extended(): lax.ppermute(head, axis, [((i + 1) % count, i) for i in range(ends)])  12.7 us
    ppermute x2, waiting for transfers between devices, extended(): lax.ppermute(head, axis, [((i + 1) % count, i) for i in range(ends)])  12.2 us
    neg x4, other arithmetic, advance_solver_step(): grad_x = 0.5 * (padded[1:-1, 1:-1, 2:] - padded[1:-1, 1:-1, :-2])  9.62 us
    neg x4, other arithmetic, advance_solver_step(): grad_y = 0.5 * (padded[1:-1, 2:, 1:-1] - padded[1:-1, :-2, 1:-1])  5.27 us
    mul x3, other arithmetic, advance_solver_step(): ENERGY_SCALE * (aniso_sq * grad_z + factor_a * grad_z * (sq_z - quartic *...  5.21 us
  transfers between devices with their start and end apart: 10, of which 7 were waited for; matrix products, arithmetic and copies ran while one was open for 12% of the time, Pallas kernels for 0%

profile of v4, /device:TPU:14, one launch (start us, length us, event | category | flops | bytes accessed | tf_op | source)
XLA Modules:
  0.0 125.8 jit_solution(13609902300225776194)
XLA Ops:
  0.6 1.2 pad_maximum_fusion.3
  1.9 2.1 %collective-permute-start = (f32[3,4,16,512]{3,2,1,0:T(8,128)S(1)}, f32[3,4,16,512]{3,2,1,0:T(8,128)S(1)}, u32[]{:S(2)}, u32[]{:S(2)}) collective-permute-start(f32[3,4,16,512]{3,2,1,0:T(8,128)S(1)} %get-tuple-element.145), channel_id=1, source_target_pairs={{0,8},{8,16},{16,24},{24,32},{32,40},{40,48},{48,56},{56,64},{64,7... | collective-permute-start | bytes 1179656 | tf_op jit(solution)/shard_map/ppermute | solution.py:30
  4.0 7.9 %collective-permute-start.1 = (f32[3,4,16,512]{3,2,1,0:T(8,128)S(1)}, f32[3,4,16,512]{3,2,1,0:T(8,128)S(1)}, u32[]{:S(2)}, u32[]{:S(2)}) collective-permute-start(f32[3,4,16,512]{3,2,1,0:T(8,128)S(1)} %get-tuple-element.146), channel_id=1, source_target_pairs={{8,0},{16,8},{24,16},{32,24},{40,32},{48,40},{56,48},{64,56},{72,6... | collective-permute-start | bytes 1179656 | tf_op jit(solution)/shard_map/ppermute | solution.py:32
  11.9 5.1 %collective-permute-done = f32[3,4,16,512]{3,2,1,0:T(8,128)S(1)} collective-permute-done((f32[3,4,16,512]{3,2,1,0:T(8,128)S(1)}, f32[3,4,16,512]{3,2,1,0:T(8,128)S(1)}, u32[]{:S(2)}, u32[]{:S(2)}) %collective-permute-start) | collective-permute-done | bytes 393248 | tf_op jit(solution)/shard_map/ppermute | solution.py:30
  17.0 4.4 %collective-permute-done.1 = f32[3,4,16,512]{3,2,1,0:T(8,128)S(1)} collective-permute-done((f32[3,4,16,512]{3,2,1,0:T(8,128)S(1)}, f32[3,4,16,512]{3,2,1,0:T(8,128)S(1)}, u32[]{:S(2)}, u32[]{:S(2)}) %collective-permute-start.1) | collective-permute-done | bytes 393248 | tf_op jit(solution)/shard_map/ppermute | solution.py:32
  21.6 1.9 %collective-permute-start.2 = (f32[3,16,4,512]{3,2,1,0:T(4,128)S(1)}, f32[3,16,4,512]{3,2,1,0:T(4,128)S(1)}, u32[]{:S(2)}, u32[]{:S(2)}) collective-permute-start(f32[3,16,4,512]{3,2,1,0:T(4,128)S(1)} %get-tuple-element.126), channel_id=1, source_target_pairs={{0,1},{1,2},{2,3},{3,4},{4,5},{5,6},{6,7},{8,9},{9,10},{10,11},{11... | collective-permute-start | bytes 1179656 | tf_op jit(solution)/shard_map/ppermute | solution.py:30
  23.5 4.8 %collective-permute-start.3 = (f32[3,16,4,512]{3,2,1,0:T(4,128)S(1)}, f32[3,16,4,512]{3,2,1,0:T(4,128)S(1)}, u32[]{:S(2)}, u32[]{:S(2)}) collective-permute-start(f32[3,16,4,512]{3,2,1,0:T(4,128)S(1)} %get-tuple-element.127), channel_id=1, source_target_pairs={{1,0},{2,1},{3,2},{4,3},{5,4},{6,5},{7,6},{9,8},{10,9},{11,10},{12... | collective-permute-start | bytes 1179656 | tf_op jit(solution)/shard_map/ppermute | solution.py:32
  28.5 7.9 %collective-permute-done.2 = f32[3,16,4,512]{3,2,1,0:T(4,128)S(1)} collective-permute-done((f32[3,16,4,512]{3,2,1,0:T(4,128)S(1)}, f32[3,16,4,512]{3,2,1,0:T(4,128)S(1)}, u32[]{:S(2)}, u32[]{:S(2)}) %collective-permute-start.2) | collective-permute-done | bytes 393248 | tf_op jit(solution)/shard_map/ppermute | solution.py:30
  36.4 7.7 %collective-permute-done.3 = f32[3,16,4,512]{3,2,1,0:T(4,128)S(1)} collective-permute-done((f32[3,16,4,512]{3,2,1,0:T(4,128)S(1)}, f32[3,16,4,512]{3,2,1,0:T(4,128)S(1)}, u32[]{:S(2)}, u32[]{:S(2)}) %collective-permute-start.3) | collective-permute-done | bytes 393248 | tf_op jit(solution)/shard_map/ppermute | solution.py:32
  44.1 0.4 pad_maximum_fusion
  44.9 3.9 %add_multiply_fusion.2 = (f32[14,22,514]{2,1,0:T(8,128)S(1)}, f32[14,22,514]{2,1,0:T(8,128)S(1)}, f32[14,22,514]{2,1,0:T(8,128)S(1)}) fusion(f32[16,24,512]{2,1,0:T(8,128)S(1)} %get-tuple-element.26), kind=kLoop, calls=%fused_computation.57 | loop fusion | flops 15672888 | bytes 2686176 | tf_op jit(solution)/shard_map/mul | solution.py:52
  48.7 2.1 %fusion.49 = (f32[12,20,512]{2,1,0:T(8,128)S(1)}, f32[12,20,512]{2,1,0:T(8,128)S(1)}) fusion(f32[12,20,512]{2,1,0:T(8,128)S(1)} %slice.520, f32[16,24,512]{2,1,0:T(8,128)S(1)} %get-tuple-element.27, f32[16,24,512]{2,1,0:T(8,128)S(1)} %get-tuple-element.26, pred[20]{0:T(512)(128)(4,1)S(1)} %get-tuple-element.149, pred[20]{0:T(512)(128)(4,1)S(1)} %get-tuple-element.150, ...), kind=kLoop, calls=%fused_computation.149 | loop fusion | flops 4055040 | bytes 7864372 | tf_op jit(solution)/shard_map/jit(_where)/select_n | solution.py:153
  51.0 0.7 add_multiply_fusion.23
  51.7 0.4 add_multiply_fusion.22
  52.1 0.5 copy-done.5
  52.7 0.4 fusion.150
  53.1 0.4 fusion.137
  53.6 1.3 %fusion.194 = (f32[6,18,514]{2,1,0:T(8,128)S(1)}, f32[6,18,514]{2,1,0:T(8,128)S(1)}, f32[6,18,514]{2,1,0:T(8,128)S(1)}, f32[6,18,514]{2,1,0:T(8,128)S(1)}) fusion(f32[6,18,514]{2,1,0:T(8,128)S(1)} %get-tuple-element.65, f32[4,16,512]{2,1,0:T(8,128)S(1)} %get-tuple-element.137, f32[4,16,512]{2,1,0:T(8,128)S(1)} %get-tuple-element.136, ...), kind=kLoop, calls=%fused_computation.429 | loop fusion | flops 4940568 | bytes 1816480 | tf_op jit(solution)/shard_map/transpose(jvp())/neg | solution.py:43
  54.8 0.9 fusion.196
  55.7 1.3 %fusion.65 = (f32[8,20,512]{2,1,0:T(8,128)S(1)}, f32[8,20,512]{2,1,0:T(8,128)S(1)}) fusion(f32[12,24,512]{2,1,0:T(8,128)S(1)} %get-tuple-element.104, f32[12,24,512]{2,1,0:T(8,128)S(1)} %get-tuple-element.103, f32[16,24,512]{2,1,0:T(8,128)S(1)} %get-tuple-element.23, f32[4,16,512]{2,1,0:T(8,128)S(1)} %get-tuple-element.102, ...), kind=kLoop, calls=%fused_computation.214 | loop fusion | flops 2703360 | bytes 3445824 | tf_op jit(solution)/shard_map/transpose(jvp())/add_any | solution.py:62
  57.0 0.5 fusion.193
  57.7 3.6 %fusion.184 = (f32[10,22,514]{2,1,0:T(8,128)S(1)}, f32[10,22,514]{2,1,0:T(8,128)S(1)}, f32[10,22,514]{2,1,0:T(8,128)S(1)}, f32[10,22,514]{2,1,0:T(8,128)S(1)}, f...) fusion(f32[8,20,512]{2,1,0:T(8,128)S(1)} %get-tuple-element.82, ...), kind=kLoop, calls=%fused_computation.425 | loop fusion | flops 10742600 | bytes 4411424 | tf_op jit(solution)/shard_map/transpose(jvp())/neg | solution.py:43
  61.4 1.8 %fusion.189 = (f32[10,22,514]{2,1,0:T(8,128)S(1)}, f32[10,22,514]{2,1,0:T(8,128)S(1)}, f32[10,22,514]{2,1,0:T(8,128)S(1)}, f32[10,22,514]{2,1,0:T(8,128)S(1)}, f...) fusion(f32[10,22,514]{2,1,0:T(8,128)S(1)} %get-tuple-element.75, ...), kind=kLoop, calls=%fused_computation.426 | loop fusion | flops 8028680 | bytes 6083200 | tf_op jit(solution)/shard_map/transpose(jvp())/neg | solution.py:42
  63.1 1.0 fusion.81
  64.2 0.9 fusion.58
  65.5 2.2 %collective-permute-start.4 = (f32[3,12,4,512]{3,2,1,0:T(4,128)S(1)}, f32[3,12,4,512]{3,2,1,0:T(4,128)S(1)}, u32[]{:S(2)}, u32[]{:S(2)}) collective-permute-start(f32[3,12,4,512]{3,2,1,0:T(4,128)S(1)} %get-tuple-element.18), channel_id=1, source_target_pairs={{0,1},{1,2},{2,3},{3,4},{4,5},{5,6},{6,7},{8,9},{9,10},{10,11},{11... | collective-permute-start | bytes 884744 | tf_op jit(solution)/shard_map/ppermute | solution.py:19
  67.7 4.5 %collective-permute-start.5 = (f32[3,12,4,512]{3,2,1,0:T(4,128)S(1)}, f32[3,12,4,512]{3,2,1,0:T(4,128)S(1)}, u32[]{:S(2)}, u32[]{:S(2)}) collective-permute-start(f32[3,12,4,512]{3,2,1,0:T(4,128)S(1)} %get-tuple-element.19), channel_id=1, source_target_pairs={{1,0},{2,1},{3,2},{4,3},{5,4},{6,5},{7,6},{9,8},{10,9},{11,10},{12... | collective-permute-start | bytes 884744 | tf_op jit(solution)/shard_map/ppermute | solution.py:19
  72.3 0.7 add_multiply_fusion.17
  72.9 0.4 add_multiply_fusion.16
  73.4 0.6 copy-done.1
  74.0 0.4 fusion.143
  74.8 1.3 %fusion.173 = (f32[6,18,514]{2,1,0:T(8,128)S(1)}, f32[6,18,514]{2,1,0:T(8,128)S(1)}, f32[6,18,514]{2,1,0:T(8,128)S(1)}, f32[6,18,514]{2,1,0:T(8,128)S(1)}) fusion(f32[6,18,514]{2,1,0:T(8,128)S(1)} %get-tuple-element.34, f32[4,16,512]{2,1,0:T(8,128)S(1)} %get-tuple-element.135, f32[4,16,512]{2,1,0:T(8,128)S(1)} %get-tuple-element.134, ...), kind=kLoop, calls=%fused_computation.421 | loop fusion | flops 4940568 | bytes 1816480 | tf_op jit(solution)/shard_map/transpose(jvp())/neg | solution.py:43
  76.1 0.9 fusion.175
  77.0 1.3 %fusion.67 = (f32[8,20,512]{2,1,0:T(8,128)S(1)}, f32[8,20,512]{2,1,0:T(8,128)S(1)}) fusion(f32[16,24,512]{2,1,0:T(8,128)S(1)} %get-tuple-element.27, f32[16,24,512]{2,1,0:T(8,128)S(1)} %get-tuple-element.26, f32[16,24,512]{2,1,0:T(8,128)S(1)} %get-tuple-element.23, f32[4,16,512]{2,1,0:T(8,128)S(1)} %get-tuple-element.100, ...), kind=kLoop, calls=%fused_computation.216 | loop fusion | flops 2703360 | bytes 3445824 | tf_op jit(solution)/shard_map/transpose(jvp())/add_any | solution.py:62
  78.3 0.5 fusion.172
  79.0 3.4 %fusion.163 = (f32[10,22,514]{2,1,0:T(8,128)S(1)}, f32[10,22,514]{2,1,0:T(8,128)S(1)}, f32[10,22,514]{2,1,0:T(8,128)S(1)}, f32[10,22,514]{2,1,0:T(8,128)S(1)}, f...) fusion(f32[8,20,512]{2,1,0:T(8,128)S(1)} %get-tuple-element.51, ...), kind=kLoop, calls=%fused_computation.417 | loop fusion | flops 10742600 | bytes 4411424 | tf_op jit(solution)/shard_map/transpose(jvp())/neg | solution.py:43
  82.5 1.8 %fusion.168 = (f32[10,22,514]{2,1,0:T(8,128)S(1)}, f32[10,22,514]{2,1,0:T(8,128)S(1)}, f32[10,22,514]{2,1,0:T(8,128)S(1)}, f32[10,22,514]{2,1,0:T(8,128)S(1)}, f...) fusion(f32[10,22,514]{2,1,0:T(8,128)S(1)} %get-tuple-element.44, ...), kind=kLoop, calls=%fused_computation.418 | loop fusion | flops 8028680 | bytes 6083200 | tf_op jit(solution)/shard_map/transpose(jvp())/neg | solution.py:42
  84.2 1.0 fusion.71
  85.4 0.9 fusion.56
  86.4 1.9 %collective-permute-start.6 = (f32[3,12,4,512]{3,2,1,0:T(4,128)S(1)}, f32[3,12,4,512]{3,2,1,0:T(4,128)S(1)}, u32[]{:S(2)}, u32[]{:S(2)}) collective-permute-start(f32[3,12,4,512]{3,2,1,0:T(4,128)S(1)} %get-tuple-element.28), channel_id=1, source_target_pairs={{0,1},{1,2},{2,3},{3,4},{4,5},{5,6},{6,7},{8,9},{9,10},{10,11},{11... | collective-permute-start | bytes 884744 | tf_op jit(solution)/shard_map/ppermute | solution.py:19
  88.3 4.8 %collective-permute-start.7 = (f32[3,12,4,512]{3,2,1,0:T(4,128)S(1)}, f32[3,12,4,512]{3,2,1,0:T(4,128)S(1)}, u32[]{:S(2)}, u32[]{:S(2)}) collective-permute-start(f32[3,12,4,512]{3,2,1,0:T(4,128)S(1)} %get-tuple-element.29), channel_id=1, source_target_pairs={{1,0},{2,1},{3,2},{4,3},{5,4},{6,5},{7,6},{9,8},{10,9},{11,10},{12... | collective-permute-start | bytes 884744 | tf_op jit(solution)/shard_map/ppermute | solution.py:19
  93.5 4.2 %collective-permute-start.9 = (f32[3,4,16,512]{3,2,1,0:T(8,128)S(1)}, f32[3,4,16,512]{3,2,1,0:T(8,128)S(1)}, u32[]{:S(2)}, u32[]{:S(2)}) collective-permute-start(f32[3,4,16,512]{3,2,1,0:T(8,128)S(1)} %pad_maximum_fusion.4), channel_id=1, source_target_pairs={{8,0},{16,8},{24,16},{32,24},{40,32},{48,40},{56,48},{64,56},{72,6... | collective-permute-start | bytes 1179656 | tf_op jit(solution)/shard_map/ppermute | solution.py:19
  97.7 5.6 %collective-permute-done.6 = f32[3,12,4,512]{3,2,1,0:T(4,128)S(1)} collective-permute-done((f32[3,12,4,512]{3,2,1,0:T(4,128)S(1)}, f32[3,12,4,512]{3,2,1,0:T(4,128)S(1)}, u32[]{:S(2)}, u32[]{:S(2)}) %collective-permute-start.6) | collective-permute-done | bytes 294944 | tf_op jit(solution)/shard_map/ppermute | solution.py:19
  103.3 3.9 %collective-permute-done.7 = f32[3,12,4,512]{3,2,1,0:T(4,128)S(1)} collective-permute-done((f32[3,12,4,512]{3,2,1,0:T(4,128)S(1)}, f32[3,12,4,512]{3,2,1,0:T(4,128)S(1)}, u32[]{:S(2)}, u32[]{:S(2)}) %collective-permute-start.7) | collective-permute-done | bytes 294944 | tf_op jit(solution)/shard_map/ppermute | solution.py:19
  107.8 1.9 %collective-permute-start.8 = (f32[3,4,16,512]{3,2,1,0:T(8,128)S(1)}, f32[3,4,16,512]{3,2,1,0:T(8,128)S(1)}, u32[]{:S(2)}, u32[]{:S(2)}) collective-permute-start(f32[3,4,16,512]{3,2,1,0:T(8,128)S(1)} %slice.556), channel_id=1, source_target_pairs={{0,8},{8,16},{16,24},{24,32},{32,40},{40,48},{48,56},{56,64},{64,7... | collective-permute-start | bytes 1179656 | tf_op jit(solution)/shard_map/ppermute | solution.py:19
  110.1 13.9 %collective-permute-done.8 = f32[3,4,16,512]{3,2,1,0:T(8,128)S(1)} collective-permute-done((f32[3,4,16,512]{3,2,1,0:T(8,128)S(1)}, f32[3,4,16,512]{3,2,1,0:T(8,128)S(1)}, u32[]{:S(2)}, u32[]{:S(2)}) %collective-permute-start.8) | collective-permute-done | bytes 393248 | tf_op jit(solution)/shard_map/ppermute | solution.py:19
  124.2 0.8 fusion.131
  125.0 0.7 fusion.135
  (47 shorter events, 4.0 us)
Async XLA Ops:
  1.8 19.6 %copy-start.2 = (f32[8,16,512]{2,1,0:T(8,128)S(1)}, f32[8,16,512]{2,1,0:T(8,128)}, u32[]{:S(2)}) copy-start(f32[8,16,512]{2,1,0:T(8,128)} %param.7) | copy-start | bytes 786436
  1.8 19.6 %copy-start.3 = (f32[8,16,512]{2,1,0:T(8,128)S(1)}, f32[8,16,512]{2,1,0:T(8,128)}, u32[]{:S(2)}) copy-start(f32[8,16,512]{2,1,0:T(8,128)} %param.6) | copy-start | bytes 786436
  1.8 19.6 %copy-start.4 = (f32[8,16,512]{2,1,0:T(8,128)S(1)}, f32[8,16,512]{2,1,0:T(8,128)}, u32[]{:S(2)}) copy-start(f32[8,16,512]{2,1,0:T(8,128)} %param.5) | copy-start | bytes 786436
  1.9 15.1 %collective-permute-start = (f32[3,4,16,512]{3,2,1,0:T(8,128)S(1)}, f32[3,4,16,512]{3,2,1,0:T(8,128)S(1)}, u32[]{:S(2)}, u32[]{:S(2)}) collective-permute-start(f32[3,4,16,512]{3,2,1,0:T(8,128)S(1)} %get-tuple-element.145), channel_id=1, source_target_pairs={{0,8},{8,16},{16,24},{24,32},{32,40},{40,48},{48,56},{56,64},{64,7... | collective-permute-start | bytes 1179656 | tf_op jit(solution)/shard_map/ppermute | solution.py:30
  4.0 17.4 %collective-permute-start.1 = (f32[3,4,16,512]{3,2,1,0:T(8,128)S(1)}, f32[3,4,16,512]{3,2,1,0:T(8,128)S(1)}, u32[]{:S(2)}, u32[]{:S(2)}) collective-permute-start(f32[3,4,16,512]{3,2,1,0:T(8,128)S(1)} %get-tuple-element.146), channel_id=1, source_target_pairs={{8,0},{16,8},{24,16},{32,24},{40,32},{48,40},{56,48},{64,56},{72,6... | collective-permute-start | bytes 1179656 | tf_op jit(solution)/shard_map/ppermute | solution.py:32
  21.6 14.8 %collective-permute-start.2 = (f32[3,16,4,512]{3,2,1,0:T(4,128)S(1)}, f32[3,16,4,512]{3,2,1,0:T(4,128)S(1)}, u32[]{:S(2)}, u32[]{:S(2)}) collective-permute-start(f32[3,16,4,512]{3,2,1,0:T(4,128)S(1)} %get-tuple-element.126), channel_id=1, source_target_pairs={{0,1},{1,2},{2,3},{3,4},{4,5},{5,6},{6,7},{8,9},{9,10},{10,11},{11... | collective-permute-start | bytes 1179656 | tf_op jit(solution)/shard_map/ppermute | solution.py:30
  23.5 20.6 %collective-permute-start.3 = (f32[3,16,4,512]{3,2,1,0:T(4,128)S(1)}, f32[3,16,4,512]{3,2,1,0:T(4,128)S(1)}, u32[]{:S(2)}, u32[]{:S(2)}) collective-permute-start(f32[3,16,4,512]{3,2,1,0:T(4,128)S(1)} %get-tuple-element.127), channel_id=1, source_target_pairs={{1,0},{2,1},{3,2},{4,3},{5,4},{6,5},{7,6},{9,8},{10,9},{11,10},{12... | collective-permute-start | bytes 1179656 | tf_op jit(solution)/shard_map/ppermute | solution.py:32
  51.0 14.3 %copy-start = (f32[12,20,512]{2,1,0:T(8,128)}, f32[12,20,512]{2,1,0:T(8,128)S(1)}, u32[]{:S(2)}) copy-start(f32[12,20,512]{2,1,0:T(8,128)S(1)} %broadcast_select_fusion) | copy-start | bytes 1474564
  51.7 1.0 copy-start.5
  51.7 1.0 copy-start.6
  65.3 7.0 %slice-start = ((f32[12,20,512]{2,1,0:T(8,128)}), f32[8,20,512]{2,1,0:T(8,128)S(1)}, s32[]{:S(2)}) async-start(f32[12,20,512]{2,1,0:T(8,128)} %copy-done), calls=%async_computation | async-start | bytes 786432 | tf_op jit(solution)/shard_map/slice | solution.py:111
  65.5 27.7 %collective-permute-start.4 = (f32[3,12,4,512]{3,2,1,0:T(4,128)S(1)}, f32[3,12,4,512]{3,2,1,0:T(4,128)S(1)}, u32[]{:S(2)}, u32[]{:S(2)}) collective-permute-start(f32[3,12,4,512]{3,2,1,0:T(4,128)S(1)} %get-tuple-element.18), channel_id=1, source_target_pairs={{0,1},{1,2},{2,3},{3,4},{4,5},{5,6},{6,7},{8,9},{9,10},{10,11},{11... | collective-permute-start | bytes 884744 | tf_op jit(solution)/shard_map/ppermute | solution.py:19
  67.7 25.5 %collective-permute-start.5 = (f32[3,12,4,512]{3,2,1,0:T(4,128)S(1)}, f32[3,12,4,512]{3,2,1,0:T(4,128)S(1)}, u32[]{:S(2)}, u32[]{:S(2)}) collective-permute-start(f32[3,12,4,512]{3,2,1,0:T(4,128)S(1)} %get-tuple-element.19), channel_id=1, source_target_pairs={{1,0},{2,1},{3,2},{4,3},{5,4},{6,5},{7,6},{9,8},{10,9},{11,10},{12... | collective-permute-start | bytes 884744 | tf_op jit(solution)/shard_map/ppermute | solution.py:19
  72.9 1.1 copy-start.1
  86.4 16.9 %collective-permute-start.6 = (f32[3,12,4,512]{3,2,1,0:T(4,128)S(1)}, f32[3,12,4,512]{3,2,1,0:T(4,128)S(1)}, u32[]{:S(2)}, u32[]{:S(2)}) collective-permute-start(f32[3,12,4,512]{3,2,1,0:T(4,128)S(1)} %get-tuple-element.28), channel_id=1, source_target_pairs={{0,1},{1,2},{2,3},{3,4},{4,5},{5,6},{6,7},{8,9},{9,10},{10,11},{11... | collective-permute-start | bytes 884744 | tf_op jit(solution)/shard_map/ppermute | solution.py:19
  88.3 18.9 %collective-permute-start.7 = (f32[3,12,4,512]{3,2,1,0:T(4,128)S(1)}, f32[3,12,4,512]{3,2,1,0:T(4,128)S(1)}, u32[]{:S(2)}, u32[]{:S(2)}) collective-permute-start(f32[3,12,4,512]{3,2,1,0:T(4,128)S(1)} %get-tuple-element.29), channel_id=1, source_target_pairs={{1,0},{2,1},{3,2},{4,3},{5,4},{6,5},{7,6},{9,8},{10,9},{11,10},{12... | collective-permute-start | bytes 884744 | tf_op jit(solution)/shard_map/ppermute | solution.py:19
  93.5 16.6 %collective-permute-start.9 = (f32[3,4,16,512]{3,2,1,0:T(8,128)S(1)}, f32[3,4,16,512]{3,2,1,0:T(8,128)S(1)}, u32[]{:S(2)}, u32[]{:S(2)}) collective-permute-start(f32[3,4,16,512]{3,2,1,0:T(8,128)S(1)} %pad_maximum_fusion.4), channel_id=1, source_target_pairs={{8,0},{16,8},{24,16},{32,24},{40,32},{48,40},{56,48},{64,56},{72,6... | collective-permute-start | bytes 1179656 | tf_op jit(solution)/shard_map/ppermute | solution.py:19
  107.8 16.2 %collective-permute-start.8 = (f32[3,4,16,512]{3,2,1,0:T(8,128)S(1)}, f32[3,4,16,512]{3,2,1,0:T(8,128)S(1)}, u32[]{:S(2)}, u32[]{:S(2)}) collective-permute-start(f32[3,4,16,512]{3,2,1,0:T(8,128)S(1)} %slice.556), channel_id=1, source_target_pairs={{0,8},{8,16},{16,24},{24,32},{32,40},{40,48},{48,56},{56,64},{64,7... | collective-permute-start | bytes 1179656 | tf_op jit(solution)/shard_map/ppermute | solution.py:19

commit v5 on v2

--- a/solution.py
+++ b/solution.py
@@ -34,6 +34,64 @@
             axis=dim,
         )
     return cells
+
+
+def packed_z_halo(cells, widths):
+    width, size = max(widths), cells.shape[1]
+    tails = jnp.concatenate([cells[i, size - w :] for i, w in enumerate(widths)], 0)
+    heads = jnp.concatenate([cells[i, :w] for i, w in enumerate(widths)], 0)
+    from_below = from_behind(tails, "gz", 1)
+    from_above = from_behind(heads, "gz", -1)
+    cuts = [sum(widths[:i]) for i in range(len(widths) + 1)]
+    below = jnp.stack(
+        [
+            jnp.pad(from_below[cuts[i] : cuts[i + 1]], ((width - w, 0), (0, 0), (0, 0)))
+            for i, w in enumerate(widths)
+        ]
+    )
+    above = jnp.stack(
+        [
+            jnp.pad(from_above[cuts[i] : cuts[i + 1]], ((0, width - w), (0, 0), (0, 0)))
+            for i, w in enumerate(widths)
+        ]
+    )
+    return jnp.concatenate((below, cells, above), axis=1)
+
+
+def packed_z_fold(contributions, widths):
+    width, size = max(widths), contributions.shape[1]
+    lower = jnp.concatenate(
+        [contributions[i, width - w : width] for i, w in enumerate(widths)], 0
+    )
+    upper = jnp.concatenate(
+        [contributions[i, size - width : size - width + w] for i, w in enumerate(widths)], 0
+    )
+    lower, upper = lax.optimization_barrier((lower, upper))
+    from_above = from_behind(lower, "gz", -1)
+    from_below = from_behind(upper, "gz", 1)
+    cuts = [sum(widths[:i]) for i in range(len(widths) + 1)]
+    below = jnp.stack(
+        [
+            jnp.pad(from_below[cuts[i] : cuts[i + 1]], ((0, width - w), (0, 0), (0, 0)))
+            for i, w in enumerate(widths)
+        ]
+    )
+    above = jnp.stack(
+        [
+            jnp.pad(from_above[cuts[i] : cuts[i + 1]], ((width - w, 0), (0, 0), (0, 0)))
+            for i, w in enumerate(widths)
+        ]
+    )
+    middle = contributions[:, width : size - width]
+    inner = size - 2 * width
+    return jnp.concatenate(
+        (
+            middle[:, :width] + below,
+            middle[:, width : inner - width],
+            middle[:, inner - width :] + above,
+        ),
+        axis=1,
+    )
 
 
 def advance_solver_step(phase_wide, temp_wide, kinetic_rate_field):
@@ -111,11 +169,10 @@
     order_parameter_adjoint_seed,
     heat_level_adjoint_seed,
 ):
-    state = extended(
-        jnp.stack((saved_order_parameter, saved_heat_level, kinetic_rate_field)),
-        (("gz", 1), ("gy", 2)),
-        4,
-    )
+    state = packed_z_halo(
+        jnp.stack((saved_order_parameter, saved_heat_level, kinetic_rate_field)), (4, 3, 2)
+    )
+    state = extended(state, (("gy", 2),), 4)
     phase_wide, temp_wide, rate_wide = state[0], state[1], state[2]
     succeeding_order_parameter, succeeding_heat_level = advance_solver_step(
         phase_wide, temp_wide, rate_wide[2:-2, 2:-2]
@@ -144,8 +201,9 @@
     folded = fold_rims(
         jnp.stack((sensitivity_order_parameter, sensitivity_heat_level, early_mob)),
         4,
-        (("gy", 2), ("gz", 1)),
-    )
+        (("gy", 2),),
+    )
+    folded = packed_z_fold(folded, (4, 3, 2))
     return (folded[0], folded[1], latest_kinetic_rate + folded[2])
 
 

time: 110 us -> 106 us (0.964)
  the two profiles are of different devices: /device:TPU:34 before, /device:TPU:14 now
where the time goes in v5:
time: 106 us
  waiting for transfers between devices  39.2 us (37%)
  starting transfers between devices  36.7 us (35%)
  other arithmetic  25 us (24%)
  local copies, waits for them, and re-layouts  3.73 us (4%)
  between operations  1.1 us (1%)
    ppermute x6, waiting for transfers between devices, from_behind(): return lax.ppermute(block, axis, route)  31.1 us
    ppermute x6, starting transfers between devices, from_behind(): return lax.ppermute(block, axis, route)  30.9 us
    neg x2, other arithmetic, advance_solver_step(): grad_x = 0.5 * (padded[1:-1, 1:-1, 2:] - padded[1:-1, 1:-1, :-2])  6.28 us
    ppermute x1, waiting for transfers between devices, extended(): lax.ppermute(tail, axis, [(i, (i + 1) % count) for i in range(ends)])  4.47 us
    ppermute x1, waiting for transfers between devices, extended(): lax.ppermute(head, axis, [((i + 1) % count, i) for i in range(ends)])  3.63 us
    ppermute x1, starting transfers between devices, extended(): lax.ppermute(head, axis, [((i + 1) % count, i) for i in range(ends)])  3.56 us
    neg x2, other arithmetic, advance_solver_step(): grad_y = 0.5 * (padded[1:-1, 2:, 1:-1] - padded[1:-1, :-2, 1:-1])  3.46 us
    squeeze x3, local copies, waits for them, and re-layouts, packed_z_halo(): cells[i, size - w:]  2.9 us
  transfers between devices with their start and end apart: 8, of which 8 were waited for; matrix products, arithmetic and copies ran while one was open for 0% of the time, Pallas kernels for 0%

profile of v5, /device:TPU:14, one launch (start us, length us, event | category | flops | bytes accessed | tf_op | source)
XLA Modules:
  0.0 105.7 jit_solution(5957569733830039706)
XLA Ops:
  0.6 0.0 copy-start.3
  0.7 0.9 slice_bitcast_fusion.18
  1.6 1.0 slice_bitcast_fusion.14
  2.6 1.0 slice_bitcast_fusion.10
  3.6 7.9 %collective-permute-start.1 = (f32[9,16,512]{2,1,0:T(8,128)S(1)}, f32[9,16,512]{2,1,0:T(8,128)S(1)}, u32[]{:S(2)}, u32[]{:S(2)}) collective-permute-start(f32[9,16,512]{2,1,0:T(8,128)S(1)} %pad_maximum_fusion.12), channel_id=1, source_target_pairs={{8,0},{16,8},{24,16},{32,24},{40,32},{48,40},{56,48},{64,56},{72,6... | collective-permute-start | bytes 884744 | tf_op jit(solution)/shard_map/ppermute | solution.py:19
  11.6 2.1 %collective-permute-start = (f32[9,16,512]{2,1,0:T(8,128)S(1)}, f32[9,16,512]{2,1,0:T(8,128)S(1)}, u32[]{:S(2)}, u32[]{:S(2)}) collective-permute-start(f32[9,16,512]{2,1,0:T(8,128)S(1)} %pad_maximum_fusion.11), channel_id=1, source_target_pairs={{0,8},{8,16},{16,24},{24,32},{32,40},{40,48},{48,56},{56,64},{64,7... | collective-permute-start | bytes 884744 | tf_op jit(solution)/shard_map/ppermute | solution.py:19
  13.7 5.3 %collective-permute-done.1 = f32[9,16,512]{2,1,0:T(8,128)S(1)} collective-permute-done((f32[9,16,512]{2,1,0:T(8,128)S(1)}, f32[9,16,512]{2,1,0:T(8,128)S(1)}, u32[]{:S(2)}, u32[]{:S(2)}) %collective-permute-start.1) | collective-permute-done | bytes 294944 | tf_op jit(solution)/shard_map/ppermute | solution.py:19
  19.0 6.3 %collective-permute-done = f32[9,16,512]{2,1,0:T(8,128)S(1)} collective-permute-done((f32[9,16,512]{2,1,0:T(8,128)S(1)}, f32[9,16,512]{2,1,0:T(8,128)S(1)}, u32[]{:S(2)}, u32[]{:S(2)}) %collective-permute-start) | collective-permute-done | bytes 294944 | tf_op jit(solution)/shard_map/ppermute | solution.py:19
  25.4 0.2 maximum_maximum_fusion
  25.6 3.6 %collective-permute-start.3 = (f32[3,16,4,512]{3,2,1,0:T(4,128)S(1)}, f32[3,16,4,512]{3,2,1,0:T(4,128)S(1)}, u32[]{:S(2)}, u32[]{:S(2)}) collective-permute-start(f32[3,16,4,512]{3,2,1,0:T(4,128)S(1)} %get-tuple-element.76), channel_id=1, source_target_pairs={{1,0},{2,1},{3,2},{4,3},{5,4},{6,5},{7,6},{9,8},{10,9},{11,10},{12... | collective-permute-start | bytes 1179656 | tf_op jit(solution)/shard_map/ppermute | solution.py:32
  29.2 2.3 %collective-permute-start.2 = (f32[3,16,4,512]{3,2,1,0:T(4,128)S(1)}, f32[3,16,4,512]{3,2,1,0:T(4,128)S(1)}, u32[]{:S(2)}, u32[]{:S(2)}) collective-permute-start(f32[3,16,4,512]{3,2,1,0:T(4,128)S(1)} %get-tuple-element.75), channel_id=1, source_target_pairs={{0,1},{1,2},{2,3},{3,4},{4,5},{5,6},{6,7},{8,9},{9,10},{10,11},{11... | collective-permute-start | bytes 1179656 | tf_op jit(solution)/shard_map/ppermute | solution.py:30
  31.5 0.1 and_and_fusion
  31.6 3.6 %collective-permute-done.3 = f32[3,16,4,512]{3,2,1,0:T(4,128)S(1)} collective-permute-done((f32[3,16,4,512]{3,2,1,0:T(4,128)S(1)}, f32[3,16,4,512]{3,2,1,0:T(4,128)S(1)}, u32[]{:S(2)}, u32[]{:S(2)}) %collective-permute-start.3) | collective-permute-done | bytes 393248 | tf_op jit(solution)/shard_map/ppermute | solution.py:32
  35.3 4.5 %collective-permute-done.2 = f32[3,16,4,512]{3,2,1,0:T(4,128)S(1)} collective-permute-done((f32[3,16,4,512]{3,2,1,0:T(4,128)S(1)}, f32[3,16,4,512]{3,2,1,0:T(4,128)S(1)}, u32[]{:S(2)}, u32[]{:S(2)}) %collective-permute-start.2) | collective-permute-done | bytes 393248 | tf_op jit(solution)/shard_map/ppermute | solution.py:30
  39.7 0.6 pad_maximum_fusion
  40.3 0.2 slice_bitcast_fusion
  40.5 1.4 %add_multiply_fusion.5 = (f32[14,22,514]{2,1,0:T(8,128)S(1)}, f32[14,22,514]{2,1,0:T(8,128)S(1)}, f32[14,22,514]{2,1,0:T(8,128)S(1)}, f32[14,22,514]{2,1,0:T(8,1...) fusion(f32[16,24,512]{2,1,0:T(8,128)S(1)} %get-tuple-element.64), kind=kLoop, calls=%fused_computation.67 | loop fusion | flops 5224296 | bytes 5219168 | tf_op jit(solution)/shard_map/mul | solution.py:110
  42.0 0.1 slice.349
  42.0 0.2 pad_slice_fusion.16
  42.3 0.8 add_multiply_fusion.4
  43.1 1.8 %broadcast_select_fusion = (f32[12,20,512]{2,1,0:T(8,128)S(1)}, f32[12,20,512]{2,1,0:T(8,128)S(1)}, f32[12,20,512]{2,1,0:T(8,128)S(1)}, f32[12,20,512]{2,1,0:T(8,128)S(1)}, f32[12,20,512]{2,1,0:T(8,128)S(1)}) fusion(pred[20]{0:T(512)(128)(4,1)S(1)} %get-tuple-element.96, pred[20]{0:T(512)(128)(4,1)S(1)} %get-tuple-element.97, ...), kind=kLoop, calls=%fused_computation.184 | loop fusion | flops 3072000 | bytes 9338932 | tf_op jit(solution)/shard_map/jit(_where)/select_n | solution.py:181
  44.9 1.0 add_multiply_fusion.8
  46.0 0.6 fusion.81
  46.6 0.2 broadcast_multiply_fusion
  46.8 0.5 fusion.60
  47.3 2.8 %fusion.98 = (f32[10,18,514]{2,1,0:T(8,128)S(1)}, f32[10,18,514]{2,1,0:T(8,128)S(1)}, f32[10,18,514]{2,1,0:T(8,128)S(1)}, f32[10,18,514]{2,1,0:T(8,128)S(1)}, f32[10,18,514]{2,1,0:T(8,128)S(1)}) fusion(f32[10,18,514]{2,1,0:T(8,128)S(1)} %get-tuple-element.12, f32[8,16,512]{2,1,0:T(8,128)S(1)} %get-tuple-element.84, f32[8,16,512]{2,1,0:T(8,128)S(1)} %get-tuple-element.85, ...), kind=kLoop, calls=%fused_computation.256 | loop fusion | flops 8604360 | bytes 3484928 | tf_op jit(solution)/shard_map/transpose(jvp())/neg | solution.py:101
  50.1 1.6 %fusion.100 = (f32[10,18,514]{2,1,0:T(8,128)S(1)}, f32[10,18,514]{2,1,0:T(8,128)S(1)}, f32[10,18,514]{2,1,0:T(8,128)S(1)}, f32[10,18,514]{2,1,0:T(8,128)S(1)}, f32[10,18,514]{2,1,0:T(8,128)S(1)}) fusion(f32[10,18,514]{2,1,0:T(8,128)S(1)} %get-tuple-element.13, f32[10,18,514]{2,1,0:T(8,128)S(1)} %get-tuple-element.33, ...), kind=kLoop, calls=%fused_computation.257 | loop fusion | flops 5643720 | bytes 4225088 | tf_op jit(solution)/shard_map/transpose(jvp())/neg | solution.py:100
  51.6 2.2 %fusion.43 = (f32[12,20,512]{2,1,0:T(8,128)S(1)}, f32[12,20,512]{2,1,0:T(8,128)S(1)}) fusion(f32[16,24,512]{2,1,0:T(8,128)S(1)} %get-tuple-element.63, f32[16,24,512]{2,1,0:T(8,128)S(1)} %get-tuple-element.62, f32[16,24,512]{2,1,0:T(8,128)S(1)} %get-tuple-element.64, f32[8,16,512]{2,1,0:T(8,128)S(1)} %get-tuple-element.27, ...), kind=kLoop, calls=%fused_computation.126 | loop fusion | flops 4300800 | bytes 5464564 | tf_op jit(solution)/shard_map/transpose(jvp())/add_any | solution.py:120
  53.8 1.0 fusion.96
  54.8 0.1 pad_bitcast_fusion
  54.9 0.2 add_bitcast_fusion
  55.1 3.5 %fusion.90 = (f32[14,22,514]{2,1,0:T(8,128)S(1)}, f32[14,22,514]{2,1,0:T(8,128)S(1)}, f32[14,22,514]{2,1,0:T(8,128)S(1)}, f32[14,22,514]{2,1,0:T(8,128)S(1)}) fusion(f32[14,22,514]{2,1,0:T(8,128)S(1)} %get-tuple-element.47, f32[14,22,514]{2,1,0:T(8,128)S(1)} %get-tuple-element.55, f32[14,22,514]{2,1,0:T(8,128)S(1)} %get-tuple-element.43, ...), kind=kLoop, calls=%fused_computation.252 | loop fusion | flops 13298208 | bytes 8582016 | tf_op jit(solution)/shard_map/transpose(jvp())/neg | solution.py:101
  58.6 1.9 %fusion.92 = (f32[14,22,514]{2,1,0:T(8,128)S(1)}, f32[14,22,514]{2,1,0:T(8,128)S(1)}, f32[14,22,514]{2,1,0:T(8,128)S(1)}, f32[14,22,514]{2,1,0:T(8,128)S(1)}) fusion(f32[14,22,514]{2,1,0:T(8,128)S(1)} %get-tuple-element.46, f32[14,22,514]{2,1,0:T(8,128)S(1)} %get-tuple-element.20, f32[14,22,514]{2,1,0:T(8,128)S(1)} %get-tuple-element.19, ...), kind=kLoop, calls=%fused_computation.253 | loop fusion | flops 7598976 | bytes 9215264 | tf_op jit(solution)/shard_map/transpose(jvp())/neg | solution.py:100
  60.5 1.2 %fusion.21 = f32[1,16,24,512]{3,2,1,0:T(8,128)S(1)} fusion(f32[14,22,514]{2,1,0:T(8,128)S(1)} %get-tuple-element.53, f32[14,22,514]{2,1,0:T(8,128)S(1)} %get-tuple-element.52, f32[14,22,514]{2,1,0:T(8,128)S(1)} %get-tuple-element.22, f32[14,22,514]{2,1,0:T(8,128)S(1)} %get-tuple-element.21, f32[14,22,514]{2,1,0:T(8,128)S(1)} %get-tuple-element.18, ...), kind=kLoop, calls=%fused_computation.76 | loop fusion | flops 1179648 | bytes 5077440 | tf_op jit(solution)/shard_map/stack | solution.py:202
  61.8 0.2 pad_maximum_fusion.3
  62.0 3.3 %collective-permute-start.4 = (f32[3,16,4,512]{3,2,1,0:T(4,128)S(1)}, f32[3,16,4,512]{3,2,1,0:T(4,128)S(1)}, u32[]{:S(2)}, u32[]{:S(2)}) collective-permute-start(f32[3,16,4,512]{3,2,1,0:T(4,128)S(1)} %get-tuple-element.7), channel_id=1, source_target_pairs={{0,1},{1,2},{2,3},{3,4},{4,5},{5,6},{6,7},{8,9},{9,10},{10,11},{11... | collective-permute-start | bytes 1179656 | tf_op jit(solution)/shard_map/ppermute | solution.py:19
  65.3 3.4 %collective-permute-start.5 = (f32[3,16,4,512]{3,2,1,0:T(4,128)S(1)}, f32[3,16,4,512]{3,2,1,0:T(4,128)S(1)}, u32[]{:S(2)}, u32[]{:S(2)}) collective-permute-start(f32[3,16,4,512]{3,2,1,0:T(4,128)S(1)} %get-tuple-element.8), channel_id=1, source_target_pairs={{1,0},{2,1},{3,2},{4,3},{5,4},{6,5},{7,6},{9,8},{10,9},{11,10},{12... | collective-permute-start | bytes 1179656 | tf_op jit(solution)/shard_map/ppermute | solution.py:19
  68.7 3.8 %collective-permute-done.4 = f32[3,16,4,512]{3,2,1,0:T(4,128)S(1)} collective-permute-done((f32[3,16,4,512]{3,2,1,0:T(4,128)S(1)}, f32[3,16,4,512]{3,2,1,0:T(4,128)S(1)}, u32[]{:S(2)}, u32[]{:S(2)}) %collective-permute-start.4) | collective-permute-done | bytes 393248 | tf_op jit(solution)/shard_map/ppermute | solution.py:19
  72.6 4.3 %collective-permute-done.5 = f32[3,16,4,512]{3,2,1,0:T(4,128)S(1)} collective-permute-done((f32[3,16,4,512]{3,2,1,0:T(4,128)S(1)}, f32[3,16,4,512]{3,2,1,0:T(4,128)S(1)}, u32[]{:S(2)}, u32[]{:S(2)}) %collective-permute-start.5) | collective-permute-done | bytes 393248 | tf_op jit(solution)/shard_map/ppermute | solution.py:19
  76.9 0.3 maximum_add_fusion
  77.1 0.4 fusion.1
  77.7 12.2 %collective-permute-start.7 = (f32[9,16,512]{2,1,0:T(8,128)S(1)}, f32[9,16,512]{2,1,0:T(8,128)S(1)}, u32[]{:S(2)}, u32[]{:S(2)}) collective-permute-start(f32[9,16,512]{2,1,0:T(8,128)S(1)} %pad_maximum_fusion.13), channel_id=1, source_target_pairs={{8,0},{16,8},{24,16},{32,24},{40,32},{48,40},{56,48},{64,56},{72,6... | collective-permute-start | bytes 884744 | tf_op jit(solution)/shard_map/ppermute | solution.py:19
  89.9 1.9 %collective-permute-start.6 = (f32[9,16,512]{2,1,0:T(8,128)S(1)}, f32[9,16,512]{2,1,0:T(8,128)S(1)}, u32[]{:S(2)}, u32[]{:S(2)}) collective-permute-start(f32[9,16,512]{2,1,0:T(8,128)S(1)} %pad_maximum_fusion.14), channel_id=1, source_target_pairs={{0,8},{8,16},{16,24},{24,32},{32,40},{40,48},{48,56},{56,64},{64,7... | collective-permute-start | bytes 884744 | tf_op jit(solution)/shard_map/ppermute | solution.py:19
  91.9 4.8 %collective-permute-done.7 = f32[9,16,512]{2,1,0:T(8,128)S(1)} collective-permute-done((f32[9,16,512]{2,1,0:T(8,128)S(1)}, f32[9,16,512]{2,1,0:T(8,128)S(1)}, u32[]{:S(2)}, u32[]{:S(2)}) %collective-permute-start.7) | collective-permute-done | bytes 294944 | tf_op jit(solution)/shard_map/ppermute | solution.py:19
  96.7 6.6 %collective-permute-done.6 = f32[9,16,512]{2,1,0:T(8,128)S(1)} collective-permute-done((f32[9,16,512]{2,1,0:T(8,128)S(1)}, f32[9,16,512]{2,1,0:T(8,128)S(1)}, u32[]{:S(2)}, u32[]{:S(2)}) %collective-permute-start.6) | collective-permute-done | bytes 294944 | tf_op jit(solution)/shard_map/ppermute | solution.py:19
  103.4 0.1 slice_add_fusion.3
  103.6 0.8 fusion.62
  104.4 1.4 %fusion.66 = f32[8,16,512]{2,1,0:T(8,128)} fusion(f32[3,4,16,512]{3,2,1,0:T(8,128)S(1)} %get-tuple-element.67, f32[3,4,16,512]{3,2,1,0:T(8,128)S(1)} %get-tuple-element.68, f32[10,18,514]{2,1,0:T(8,128)S(1)} %get-tuple-element.66, f32[10,18,514]{2,1,0:T(8,128)S(1)} %get-tuple-element.65, f32[10,18,514]{2,1,0:T(8,128)S(1)} %get-tuple-element.11, ...), kind=kLoop, calls=%fused_computation.195 | loop fusion | flops 1245184 | bytes 3670016 | tf_op jit(solution)/shard_map/add | solution.py:207
  (37 shorter events, 0.4 us)
Async XLA Ops:
  0.6 24.8 %copy-start.4 = (f32[8,16,512]{2,1,0:T(8,128)S(1)}, f32[8,16,512]{2,1,0:T(8,128)}, u32[]{:S(2)}) copy-start(f32[8,16,512]{2,1,0:T(8,128)} %param.7) | copy-start | bytes 786436
  0.6 24.8 %copy-start.3 = (f32[8,16,512]{2,1,0:T(8,128)S(1)}, f32[8,16,512]{2,1,0:T(8,128)}, u32[]{:S(2)}) copy-start(f32[8,16,512]{2,1,0:T(8,128)} %param.6) | copy-start | bytes 786436
  0.7 24.7 %copy-start.1 = (f32[8,16,512]{2,1,0:T(8,128)S(1)}, f32[8,16,512]{2,1,0:T(8,128)}, u32[]{:S(2)}) copy-start(f32[8,16,512]{2,1,0:T(8,128)} %param.5) | copy-start | bytes 786436
  3.6 15.3 %collective-permute-start.1 = (f32[9,16,512]{2,1,0:T(8,128)S(1)}, f32[9,16,512]{2,1,0:T(8,128)S(1)}, u32[]{:S(2)}, u32[]{:S(2)}) collective-permute-start(f32[9,16,512]{2,1,0:T(8,128)S(1)} %pad_maximum_fusion.12), channel_id=1, source_target_pairs={{8,0},{16,8},{24,16},{32,24},{40,32},{48,40},{56,48},{64,56},{72,6... | collective-permute-start | bytes 884744 | tf_op jit(solution)/shard_map/ppermute | solution.py:19
  11.6 20.0 %copy-start = (f32[8,16,512]{2,1,0:T(8,128)S(1)}, f32[8,16,512]{2,1,0:T(8,128)}, u32[]{:S(2)}) copy-start(f32[8,16,512]{2,1,0:T(8,128)} %param.9) | copy-start | bytes 786436
  11.6 13.7 %collective-permute-start = (f32[9,16,512]{2,1,0:T(8,128)S(1)}, f32[9,16,512]{2,1,0:T(8,128)S(1)}, u32[]{:S(2)}, u32[]{:S(2)}) collective-permute-start(f32[9,16,512]{2,1,0:T(8,128)S(1)} %pad_maximum_fusion.11), channel_id=1, source_target_pairs={{0,8},{8,16},{16,24},{24,32},{32,40},{40,48},{48,56},{56,64},{64,7... | collective-permute-start | bytes 884744 | tf_op jit(solution)/shard_map/ppermute | solution.py:19
  25.6 9.7 %collective-permute-start.3 = (f32[3,16,4,512]{3,2,1,0:T(4,128)S(1)}, f32[3,16,4,512]{3,2,1,0:T(4,128)S(1)}, u32[]{:S(2)}, u32[]{:S(2)}) collective-permute-start(f32[3,16,4,512]{3,2,1,0:T(4,128)S(1)} %get-tuple-element.76), channel_id=1, source_target_pairs={{1,0},{2,1},{3,2},{4,3},{5,4},{6,5},{7,6},{9,8},{10,9},{11,10},{12... | collective-permute-start | bytes 1179656 | tf_op jit(solution)/shard_map/ppermute | solution.py:32
  29.2 10.6 %collective-permute-start.2 = (f32[3,16,4,512]{3,2,1,0:T(4,128)S(1)}, f32[3,16,4,512]{3,2,1,0:T(4,128)S(1)}, u32[]{:S(2)}, u32[]{:S(2)}) collective-permute-start(f32[3,16,4,512]{3,2,1,0:T(4,128)S(1)} %get-tuple-element.75), channel_id=1, source_target_pairs={{0,1},{1,2},{2,3},{3,4},{4,5},{5,6},{6,7},{8,9},{9,10},{10,11},{11... | collective-permute-start | bytes 1179656 | tf_op jit(solution)/shard_map/ppermute | solution.py:30
  44.9 1.1 %copy-start.2 = (f32[8,16,512]{2,1,0:T(8,128)S(1)}, f32[8,16,512]{2,1,0:T(8,128)}, u32[]{:S(2)}) copy-start(f32[8,16,512]{2,1,0:T(8,128)} %param.8) | copy-start | bytes 786436
  62.0 10.6 %collective-permute-start.4 = (f32[3,16,4,512]{3,2,1,0:T(4,128)S(1)}, f32[3,16,4,512]{3,2,1,0:T(4,128)S(1)}, u32[]{:S(2)}, u32[]{:S(2)}) collective-permute-start(f32[3,16,4,512]{3,2,1,0:T(4,128)S(1)} %get-tuple-element.7), channel_id=1, source_target_pairs={{0,1},{1,2},{2,3},{3,4},{4,5},{5,6},{6,7},{8,9},{9,10},{10,11},{11... | collective-permute-start | bytes 1179656 | tf_op jit(solution)/shard_map/ppermute | solution.py:19
  65.3 11.6 %collective-permute-start.5 = (f32[3,16,4,512]{3,2,1,0:T(4,128)S(1)}, f32[3,16,4,512]{3,2,1,0:T(4,128)S(1)}, u32[]{:S(2)}, u32[]{:S(2)}) collective-permute-start(f32[3,16,4,512]{3,2,1,0:T(4,128)S(1)} %get-tuple-element.8), channel_id=1, source_target_pairs={{1,0},{2,1},{3,2},{4,3},{5,4},{6,5},{7,6},{9,8},{10,9},{11,10},{12... | collective-permute-start | bytes 1179656 | tf_op jit(solution)/shard_map/ppermute | solution.py:19
  77.7 19.0 %collective-permute-start.7 = (f32[9,16,512]{2,1,0:T(8,128)S(1)}, f32[9,16,512]{2,1,0:T(8,128)S(1)}, u32[]{:S(2)}, u32[]{:S(2)}) collective-permute-start(f32[9,16,512]{2,1,0:T(8,128)S(1)} %pad_maximum_fusion.13), channel_id=1, source_target_pairs={{8,0},{16,8},{24,16},{32,24},{40,32},{48,40},{56,48},{64,56},{72,6... | collective-permute-start | bytes 884744 | tf_op jit(solution)/shard_map/ppermute | solution.py:19
  89.9 13.4 %collective-permute-start.6 = (f32[9,16,512]{2,1,0:T(8,128)S(1)}, f32[9,16,512]{2,1,0:T(8,128)S(1)}, u32[]{:S(2)}, u32[]{:S(2)}) collective-permute-start(f32[9,16,512]{2,1,0:T(8,128)S(1)} %pad_maximum_fusion.14), channel_id=1, source_target_pairs={{0,8},{8,16},{16,24},{24,32},{32,40},{40,48},{48,56},{56,64},{64,7... | collective-permute-start | bytes 884744 | tf_op jit(solution)/shard_map/ppermute | solution.py:19

commit v6 on v5

--- a/solution.py
+++ b/solution.py
@@ -36,10 +36,11 @@
     return cells
 
 
-def packed_z_halo(cells, widths):
-    width, size = max(widths), cells.shape[1]
-    tails = jnp.concatenate([cells[i, size - w :] for i, w in enumerate(widths)], 0)
-    heads = jnp.concatenate([cells[i, :w] for i, w in enumerate(widths)], 0)
+def packed_z_halo(fields, widths):
+    width, size = max(widths), fields[0].shape[0]
+    tails = jnp.concatenate([f[size - w :] for f, w in zip(fields, widths)], 0)
+    heads = jnp.concatenate([f[:w] for f, w in zip(fields, widths)], 0)
+    cells = jnp.stack(fields)
     from_below = from_behind(tails, "gz", 1)
     from_above = from_behind(heads, "gz", -1)
     cuts = [sum(widths[:i]) for i in range(len(widths) + 1)]
@@ -170,7 +171,7 @@
     heat_level_adjoint_seed,
 ):
     state = packed_z_halo(
-        jnp.stack((saved_order_parameter, saved_heat_level, kinetic_rate_field)), (4, 3, 2)
+        (saved_order_parameter, saved_heat_level, kinetic_rate_field), (4, 2, 2)
     )
     state = extended(state, (("gy", 2),), 4)
     phase_wide, temp_wide, rate_wide = state[0], state[1], state[2]

time: 106 us -> 107 us (level); the launches traced: 106 us -> 105 us
    squeeze x3 -> x0, local copies, waits for them, and re-layouts: 2.9 us -> none  [packed_z_halo(): cells[i, size - w:]]
    slice x0 -> x2, local copies, waits for them, and re-layouts: none -> 2.01 us  [packed_z_halo(): tails = jnp.concatenate([f[size - w:] for f, w in zip(fields, widths)], 0)]
where the time goes in v6:
time: 107 us; the launch traced here: 105 us
  waiting for transfers between devices  38.6 us (36%)
  starting transfers between devices  37.5 us (35%)
  other arithmetic  25 us (23%)
  local copies, waits for them, and re-layouts  2.84 us (3%)
  between operations  1.11 us (1%)
    ppermute x6, starting transfers between devices, from_behind(): return lax.ppermute(block, axis, route)  31.7 us
    ppermute x6, waiting for transfers between devices, from_behind(): return lax.ppermute(block, axis, route)  30.4 us
    neg x2, other arithmetic, advance_solver_step(): grad_x = 0.5 * (padded[1:-1, 1:-1, 2:] - padded[1:-1, 1:-1, :-2])  6.28 us
    ppermute x1, waiting for transfers between devices, extended(): lax.ppermute(tail, axis, [(i, (i + 1) % count) for i in range(ends)])  4.51 us
    ppermute x1, waiting for transfers between devices, extended(): lax.ppermute(head, axis, [((i + 1) % count, i) for i in range(ends)])  3.63 us
    ppermute x1, starting transfers between devices, extended(): lax.ppermute(head, axis, [((i + 1) % count, i) for i in range(ends)])  3.6 us
    neg x2, other arithmetic, advance_solver_step(): grad_y = 0.5 * (padded[1:-1, 2:, 1:-1] - padded[1:-1, :-2, 1:-1])  3.46 us
    add_any x2, other arithmetic, advance_solver_step(): 1.0 - phase_now  2.64 us
  transfers between devices with their start and end apart: 8, of which 8 were waited for; matrix products, arithmetic and copies ran while one was open for 0% of the time, Pallas kernels for 0%

profile of v6, /device:TPU:14, one launch (start us, length us, event | category | flops | bytes accessed | tf_op | source)
XLA Modules:
  0.0 105.0 jit_solution(14966880764330249965)
XLA Ops:
  0.6 0.0 copy-start.3
  0.7 0.0 copy-start.4
  0.7 1.1 %fusion.110 = (f32[4,16,512]{2,1,0:T(8,128)S(1)}, f32[4,16,512]{2,1,0:T(8,128)S(1)}) fusion(f32[8,16,512]{2,1,0:T(8,128)} %param.5), kind=kLoop, calls=%fused_computation.254 | loop fusion | bytes 524288 | tf_op jit(solution)/shard_map/slice | solution.py:41
  1.7 1.0 fusion.111
  2.7 7.9 %collective-permute-start.1 = (f32[8,16,512]{2,1,0:T(8,128)S(1)}, f32[8,16,512]{2,1,0:T(8,128)S(1)}, u32[]{:S(2)}, u32[]{:S(2)}) collective-permute-start(f32[8,16,512]{2,1,0:T(8,128)S(1)} %pad_maximum_fusion.15), channel_id=1, source_target_pairs={{8,0},{16,8},{24,16},{32,24},{40,32},{48,40},{56,48},{64,56},{72,6... | collective-permute-start | bytes 786440 | tf_op jit(solution)/shard_map/ppermute | solution.py:19
  10.7 2.1 %collective-permute-start = (f32[8,16,512]{2,1,0:T(8,128)S(1)}, f32[8,16,512]{2,1,0:T(8,128)S(1)}, u32[]{:S(2)}, u32[]{:S(2)}) collective-permute-start(f32[8,16,512]{2,1,0:T(8,128)S(1)} %pad_maximum_fusion.14), channel_id=1, source_target_pairs={{0,8},{8,16},{16,24},{24,32},{32,40},{40,48},{48,56},{56,64},{64,7... | collective-permute-start | bytes 786440 | tf_op jit(solution)/shard_map/ppermute | solution.py:19
  12.8 4.6 %collective-permute-done.1 = f32[8,16,512]{2,1,0:T(8,128)S(1)} collective-permute-done((f32[8,16,512]{2,1,0:T(8,128)S(1)}, f32[8,16,512]{2,1,0:T(8,128)S(1)}, u32[]{:S(2)}, u32[]{:S(2)}) %collective-permute-start.1) | collective-permute-done | bytes 262176 | tf_op jit(solution)/shard_map/ppermute | solution.py:19
  17.4 6.2 %collective-permute-done = f32[8,16,512]{2,1,0:T(8,128)S(1)} collective-permute-done((f32[8,16,512]{2,1,0:T(8,128)S(1)}, f32[8,16,512]{2,1,0:T(8,128)S(1)}, u32[]{:S(2)}, u32[]{:S(2)}) %collective-permute-start) | collective-permute-done | bytes 262176 | tf_op jit(solution)/shard_map/ppermute | solution.py:19
  23.7 0.2 maximum_maximum_fusion
  23.9 3.6 %collective-permute-start.3 = (f32[3,16,4,512]{3,2,1,0:T(4,128)S(1)}, f32[3,16,4,512]{3,2,1,0:T(4,128)S(1)}, u32[]{:S(2)}, u32[]{:S(2)}) collective-permute-start(f32[3,16,4,512]{3,2,1,0:T(4,128)S(1)} %get-tuple-element.76), channel_id=1, source_target_pairs={{1,0},{2,1},{3,2},{4,3},{5,4},{6,5},{7,6},{9,8},{10,9},{11,10},{12... | collective-permute-start | bytes 1179656 | tf_op jit(solution)/shard_map/ppermute | solution.py:32
  27.5 2.2 %collective-permute-start.2 = (f32[3,16,4,512]{3,2,1,0:T(4,128)S(1)}, f32[3,16,4,512]{3,2,1,0:T(4,128)S(1)}, u32[]{:S(2)}, u32[]{:S(2)}) collective-permute-start(f32[3,16,4,512]{3,2,1,0:T(4,128)S(1)} %get-tuple-element.75), channel_id=1, source_target_pairs={{0,1},{1,2},{2,3},{3,4},{4,5},{5,6},{6,7},{8,9},{9,10},{10,11},{11... | collective-permute-start | bytes 1179656 | tf_op jit(solution)/shard_map/ppermute | solution.py:30
  29.8 0.1 and_and_fusion
  30.0 3.6 %collective-permute-done.3 = f32[3,16,4,512]{3,2,1,0:T(4,128)S(1)} collective-permute-done((f32[3,16,4,512]{3,2,1,0:T(4,128)S(1)}, f32[3,16,4,512]{3,2,1,0:T(4,128)S(1)}, u32[]{:S(2)}, u32[]{:S(2)}) %collective-permute-start.3) | collective-permute-done | bytes 393248 | tf_op jit(solution)/shard_map/ppermute | solution.py:32
  33.6 4.5 %collective-permute-done.2 = f32[3,16,4,512]{3,2,1,0:T(4,128)S(1)} collective-permute-done((f32[3,16,4,512]{3,2,1,0:T(4,128)S(1)}, f32[3,16,4,512]{3,2,1,0:T(4,128)S(1)}, u32[]{:S(2)}, u32[]{:S(2)}) %collective-permute-start.2) | collective-permute-done | bytes 393248 | tf_op jit(solution)/shard_map/ppermute | solution.py:30
  38.1 0.6 pad_maximum_fusion
  38.7 0.2 slice_bitcast_fusion
  38.9 1.4 %add_multiply_fusion.5 = (f32[14,22,514]{2,1,0:T(8,128)S(1)}, f32[14,22,514]{2,1,0:T(8,128)S(1)}, f32[14,22,514]{2,1,0:T(8,128)S(1)}, f32[14,22,514]{2,1,0:T(8,1...) fusion(f32[16,24,512]{2,1,0:T(8,128)S(1)} %get-tuple-element.64), kind=kLoop, calls=%fused_computation.67 | loop fusion | flops 5224296 | bytes 5219168 | tf_op jit(solution)/shard_map/mul | solution.py:111
  40.3 0.1 slice.343
  40.4 0.2 pad_slice_fusion.16
  40.7 0.8 add_multiply_fusion.4
  41.4 1.8 %broadcast_select_fusion = (f32[12,20,512]{2,1,0:T(8,128)S(1)}, f32[12,20,512]{2,1,0:T(8,128)S(1)}, f32[12,20,512]{2,1,0:T(8,128)S(1)}, f32[12,20,512]{2,1,0:T(8,128)S(1)}, f32[12,20,512]{2,1,0:T(8,128)S(1)}) fusion(pred[20]{0:T(512)(128)(4,1)S(1)} %get-tuple-element.98, pred[20]{0:T(512)(128)(4,1)S(1)} %get-tuple-element.99, ...), kind=kLoop, calls=%fused_computation.182 | loop fusion | flops 3072000 | bytes 9338932 | tf_op jit(solution)/shard_map/jit(_where)/select_n | solution.py:182
  43.3 1.0 add_multiply_fusion.8
  44.3 0.6 fusion.81
  45.0 0.2 broadcast_multiply_fusion
  45.2 0.5 fusion.60
  45.7 2.8 %fusion.98 = (f32[10,18,514]{2,1,0:T(8,128)S(1)}, f32[10,18,514]{2,1,0:T(8,128)S(1)}, f32[10,18,514]{2,1,0:T(8,128)S(1)}, f32[10,18,514]{2,1,0:T(8,128)S(1)}, f32[10,18,514]{2,1,0:T(8,128)S(1)}) fusion(f32[10,18,514]{2,1,0:T(8,128)S(1)} %get-tuple-element.12, f32[8,16,512]{2,1,0:T(8,128)S(1)} %get-tuple-element.84, f32[8,16,512]{2,1,0:T(8,128)S(1)} %get-tuple-element.85, ...), kind=kLoop, calls=%fused_computation.250 | loop fusion | flops 8604360 | bytes 3484928 | tf_op jit(solution)/shard_map/transpose(jvp())/neg | solution.py:102
  48.5 1.6 %fusion.100 = (f32[10,18,514]{2,1,0:T(8,128)S(1)}, f32[10,18,514]{2,1,0:T(8,128)S(1)}, f32[10,18,514]{2,1,0:T(8,128)S(1)}, f32[10,18,514]{2,1,0:T(8,128)S(1)}, f32[10,18,514]{2,1,0:T(8,128)S(1)}) fusion(f32[10,18,514]{2,1,0:T(8,128)S(1)} %get-tuple-element.13, f32[10,18,514]{2,1,0:T(8,128)S(1)} %get-tuple-element.33, ...), kind=kLoop, calls=%fused_computation.251 | loop fusion | flops 5643720 | bytes 4225088 | tf_op jit(solution)/shard_map/transpose(jvp())/neg | solution.py:101
  50.0 2.2 %fusion.43 = (f32[12,20,512]{2,1,0:T(8,128)S(1)}, f32[12,20,512]{2,1,0:T(8,128)S(1)}) fusion(f32[16,24,512]{2,1,0:T(8,128)S(1)} %get-tuple-element.63, f32[16,24,512]{2,1,0:T(8,128)S(1)} %get-tuple-element.62, f32[16,24,512]{2,1,0:T(8,128)S(1)} %get-tuple-element.64, f32[8,16,512]{2,1,0:T(8,128)S(1)} %get-tuple-element.27, ...), kind=kLoop, calls=%fused_computation.126 | loop fusion | flops 4300800 | bytes 5464564 | tf_op jit(solution)/shard_map/transpose(jvp())/add_any | solution.py:121
  52.2 1.0 fusion.96
  53.1 0.1 pad_bitcast_fusion
  53.2 0.2 add_bitcast_fusion
  53.5 3.5 %fusion.90 = (f32[14,22,514]{2,1,0:T(8,128)S(1)}, f32[14,22,514]{2,1,0:T(8,128)S(1)}, f32[14,22,514]{2,1,0:T(8,128)S(1)}, f32[14,22,514]{2,1,0:T(8,128)S(1)}) fusion(f32[14,22,514]{2,1,0:T(8,128)S(1)} %get-tuple-element.47, f32[14,22,514]{2,1,0:T(8,128)S(1)} %get-tuple-element.55, f32[14,22,514]{2,1,0:T(8,128)S(1)} %get-tuple-element.43, ...), kind=kLoop, calls=%fused_computation.246 | loop fusion | flops 13298208 | bytes 8582016 | tf_op jit(solution)/shard_map/transpose(jvp())/neg | solution.py:102
  57.0 1.9 %fusion.92 = (f32[14,22,514]{2,1,0:T(8,128)S(1)}, f32[14,22,514]{2,1,0:T(8,128)S(1)}, f32[14,22,514]{2,1,0:T(8,128)S(1)}, f32[14,22,514]{2,1,0:T(8,128)S(1)}) fusion(f32[14,22,514]{2,1,0:T(8,128)S(1)} %get-tuple-element.46, f32[14,22,514]{2,1,0:T(8,128)S(1)} %get-tuple-element.20, f32[14,22,514]{2,1,0:T(8,128)S(1)} %get-tuple-element.19, ...), kind=kLoop, calls=%fused_computation.247 | loop fusion | flops 7598976 | bytes 9215264 | tf_op jit(solution)/shard_map/transpose(jvp())/neg | solution.py:101
  58.9 1.2 %fusion.21 = f32[1,16,24,512]{3,2,1,0:T(8,128)S(1)} fusion(f32[14,22,514]{2,1,0:T(8,128)S(1)} %get-tuple-element.53, f32[14,22,514]{2,1,0:T(8,128)S(1)} %get-tuple-element.52, f32[14,22,514]{2,1,0:T(8,128)S(1)} %get-tuple-element.22, f32[14,22,514]{2,1,0:T(8,128)S(1)} %get-tuple-element.21, f32[14,22,514]{2,1,0:T(8,128)S(1)} %get-tuple-element.18, ...), kind=kLoop, calls=%fused_computation.76 | loop fusion | flops 1179648 | bytes 5077440 | tf_op jit(solution)/shard_map/stack | solution.py:203
  60.2 0.2 pad_maximum_fusion.3
  60.4 3.3 %collective-permute-start.4 = (f32[3,16,4,512]{3,2,1,0:T(4,128)S(1)}, f32[3,16,4,512]{3,2,1,0:T(4,128)S(1)}, u32[]{:S(2)}, u32[]{:S(2)}) collective-permute-start(f32[3,16,4,512]{3,2,1,0:T(4,128)S(1)} %get-tuple-element.7), channel_id=1, source_target_pairs={{0,1},{1,2},{2,3},{3,4},{4,5},{5,6},{6,7},{8,9},{9,10},{10,11},{11... | collective-permute-start | bytes 1179656 | tf_op jit(solution)/shard_map/ppermute | solution.py:19
  63.7 3.4 %collective-permute-start.5 = (f32[3,16,4,512]{3,2,1,0:T(4,128)S(1)}, f32[3,16,4,512]{3,2,1,0:T(4,128)S(1)}, u32[]{:S(2)}, u32[]{:S(2)}) collective-permute-start(f32[3,16,4,512]{3,2,1,0:T(4,128)S(1)} %get-tuple-element.8), channel_id=1, source_target_pairs={{1,0},{2,1},{3,2},{4,3},{5,4},{6,5},{7,6},{9,8},{10,9},{11,10},{12... | collective-permute-start | bytes 1179656 | tf_op jit(solution)/shard_map/ppermute | solution.py:19
  67.1 3.8 %collective-permute-done.4 = f32[3,16,4,512]{3,2,1,0:T(4,128)S(1)} collective-permute-done((f32[3,16,4,512]{3,2,1,0:T(4,128)S(1)}, f32[3,16,4,512]{3,2,1,0:T(4,128)S(1)}, u32[]{:S(2)}, u32[]{:S(2)}) %collective-permute-start.4) | collective-permute-done | bytes 393248 | tf_op jit(solution)/shard_map/ppermute | solution.py:19
  70.9 4.3 %collective-permute-done.5 = f32[3,16,4,512]{3,2,1,0:T(4,128)S(1)} collective-permute-done((f32[3,16,4,512]{3,2,1,0:T(4,128)S(1)}, f32[3,16,4,512]{3,2,1,0:T(4,128)S(1)}, u32[]{:S(2)}, u32[]{:S(2)}) %collective-permute-start.5) | collective-permute-done | bytes 393248 | tf_op jit(solution)/shard_map/ppermute | solution.py:19
  75.3 0.3 maximum_add_fusion
  75.5 0.4 fusion.1
  76.1 13.1 %collective-permute-start.7 = (f32[9,16,512]{2,1,0:T(8,128)S(1)}, f32[9,16,512]{2,1,0:T(8,128)S(1)}, u32[]{:S(2)}, u32[]{:S(2)}) collective-permute-start(f32[9,16,512]{2,1,0:T(8,128)S(1)} %pad_maximum_fusion.11), channel_id=1, source_target_pairs={{8,0},{16,8},{24,16},{32,24},{40,32},{48,40},{56,48},{64,56},{72,6... | collective-permute-start | bytes 884744 | tf_op jit(solution)/shard_map/ppermute | solution.py:19
  89.1 1.9 %collective-permute-start.6 = (f32[9,16,512]{2,1,0:T(8,128)S(1)}, f32[9,16,512]{2,1,0:T(8,128)S(1)}, u32[]{:S(2)}, u32[]{:S(2)}) collective-permute-start(f32[9,16,512]{2,1,0:T(8,128)S(1)} %pad_maximum_fusion.12), channel_id=1, source_target_pairs={{0,8},{8,16},{16,24},{24,32},{32,40},{40,48},{48,56},{56,64},{64,7... | collective-permute-start | bytes 884744 | tf_op jit(solution)/shard_map/ppermute | solution.py:19
  91.1 2.4 %collective-permute-done.7 = f32[9,16,512]{2,1,0:T(8,128)S(1)} collective-permute-done((f32[9,16,512]{2,1,0:T(8,128)S(1)}, f32[9,16,512]{2,1,0:T(8,128)S(1)}, u32[]{:S(2)}, u32[]{:S(2)}) %collective-permute-start.7) | collective-permute-done | bytes 294944 | tf_op jit(solution)/shard_map/ppermute | solution.py:19
  93.5 9.1 %collective-permute-done.6 = f32[9,16,512]{2,1,0:T(8,128)S(1)} collective-permute-done((f32[9,16,512]{2,1,0:T(8,128)S(1)}, f32[9,16,512]{2,1,0:T(8,128)S(1)}, u32[]{:S(2)}, u32[]{:S(2)}) %collective-permute-start.6) | collective-permute-done | bytes 294944 | tf_op jit(solution)/shard_map/ppermute | solution.py:19
  102.7 0.1 slice_add_fusion.3
  102.8 0.8 fusion.62
  103.7 1.4 %fusion.66 = f32[8,16,512]{2,1,0:T(8,128)} fusion(f32[3,4,16,512]{3,2,1,0:T(8,128)S(1)} %get-tuple-element.67, f32[3,4,16,512]{3,2,1,0:T(8,128)S(1)} %get-tuple-element.68, f32[10,18,514]{2,1,0:T(8,128)S(1)} %get-tuple-element.66, f32[10,18,514]{2,1,0:T(8,128)S(1)} %get-tuple-element.65, f32[10,18,514]{2,1,0:T(8,128)S(1)} %get-tuple-element.11, ...), kind=kLoop, calls=%fused_computation.193 | loop fusion | flops 1245184 | bytes 3670016 | tf_op jit(solution)/shard_map/add | solution.py:208
  (36 shorter events, 0.4 us)
Async XLA Ops:
  0.6 23.1 %copy-start.1 = (f32[8,16,512]{2,1,0:T(8,128)S(1)}, f32[8,16,512]{2,1,0:T(8,128)}, u32[]{:S(2)}) copy-start(f32[8,16,512]{2,1,0:T(8,128)} %param.5) | copy-start | bytes 786436
  0.6 23.1 %copy-start.3 = (f32[8,16,512]{2,1,0:T(8,128)S(1)}, f32[8,16,512]{2,1,0:T(8,128)}, u32[]{:S(2)}) copy-start(f32[8,16,512]{2,1,0:T(8,128)} %param.6) | copy-start | bytes 786436
  0.7 23.1 %copy-start.4 = (f32[8,16,512]{2,1,0:T(8,128)S(1)}, f32[8,16,512]{2,1,0:T(8,128)}, u32[]{:S(2)}) copy-start(f32[8,16,512]{2,1,0:T(8,128)} %param.7) | copy-start | bytes 786436
  2.7 14.6 %collective-permute-start.1 = (f32[8,16,512]{2,1,0:T(8,128)S(1)}, f32[8,16,512]{2,1,0:T(8,128)S(1)}, u32[]{:S(2)}, u32[]{:S(2)}) collective-permute-start(f32[8,16,512]{2,1,0:T(8,128)S(1)} %pad_maximum_fusion.15), channel_id=1, source_target_pairs={{8,0},{16,8},{24,16},{32,24},{40,32},{48,40},{56,48},{64,56},{72,6... | collective-permute-start | bytes 786440 | tf_op jit(solution)/shard_map/ppermute | solution.py:19
  10.6 19.3 %copy-start = (f32[8,16,512]{2,1,0:T(8,128)S(1)}, f32[8,16,512]{2,1,0:T(8,128)}, u32[]{:S(2)}) copy-start(f32[8,16,512]{2,1,0:T(8,128)} %param.9) | copy-start | bytes 786436
  10.7 13.0 %collective-permute-start = (f32[8,16,512]{2,1,0:T(8,128)S(1)}, f32[8,16,512]{2,1,0:T(8,128)S(1)}, u32[]{:S(2)}, u32[]{:S(2)}) collective-permute-start(f32[8,16,512]{2,1,0:T(8,128)S(1)} %pad_maximum_fusion.14), channel_id=1, source_target_pairs={{0,8},{8,16},{16,24},{24,32},{32,40},{40,48},{48,56},{56,64},{64,7... | collective-permute-start | bytes 786440 | tf_op jit(solution)/shard_map/ppermute | solution.py:19
  23.9 9.7 %collective-permute-start.3 = (f32[3,16,4,512]{3,2,1,0:T(4,128)S(1)}, f32[3,16,4,512]{3,2,1,0:T(4,128)S(1)}, u32[]{:S(2)}, u32[]{:S(2)}) collective-permute-start(f32[3,16,4,512]{3,2,1,0:T(4,128)S(1)} %get-tuple-element.76), channel_id=1, source_target_pairs={{1,0},{2,1},{3,2},{4,3},{5,4},{6,5},{7,6},{9,8},{10,9},{11,10},{12... | collective-permute-start | bytes 1179656 | tf_op jit(solution)/shard_map/ppermute | solution.py:32
  27.5 10.6 %collective-permute-start.2 = (f32[3,16,4,512]{3,2,1,0:T(4,128)S(1)}, f32[3,16,4,512]{3,2,1,0:T(4,128)S(1)}, u32[]{:S(2)}, u32[]{:S(2)}) collective-permute-start(f32[3,16,4,512]{3,2,1,0:T(4,128)S(1)} %get-tuple-element.75), channel_id=1, source_target_pairs={{0,1},{1,2},{2,3},{3,4},{4,5},{5,6},{6,7},{8,9},{9,10},{10,11},{11... | collective-permute-start | bytes 1179656 | tf_op jit(solution)/shard_map/ppermute | solution.py:30
  43.3 1.1 %copy-start.2 = (f32[8,16,512]{2,1,0:T(8,128)S(1)}, f32[8,16,512]{2,1,0:T(8,128)}, u32[]{:S(2)}) copy-start(f32[8,16,512]{2,1,0:T(8,128)} %param.8) | copy-start | bytes 786436
  60.4 10.6 %collective-permute-start.4 = (f32[3,16,4,512]{3,2,1,0:T(4,128)S(1)}, f32[3,16,4,512]{3,2,1,0:T(4,128)S(1)}, u32[]{:S(2)}, u32[]{:S(2)}) collective-permute-start(f32[3,16,4,512]{3,2,1,0:T(4,128)S(1)} %get-tuple-element.7), channel_id=1, source_target_pairs={{0,1},{1,2},{2,3},{3,4},{4,5},{5,6},{6,7},{8,9},{9,10},{10,11},{11... | collective-permute-start | bytes 1179656 | tf_op jit(solution)/shard_map/ppermute | solution.py:19
  63.7 11.6 %collective-permute-start.5 = (f32[3,16,4,512]{3,2,1,0:T(4,128)S(1)}, f32[3,16,4,512]{3,2,1,0:T(4,128)S(1)}, u32[]{:S(2)}, u32[]{:S(2)}) collective-permute-start(f32[3,16,4,512]{3,2,1,0:T(4,128)S(1)} %get-tuple-element.8), channel_id=1, source_target_pairs={{1,0},{2,1},{3,2},{4,3},{5,4},{6,5},{7,6},{9,8},{10,9},{11,10},{12... | collective-permute-start | bytes 1179656 | tf_op jit(solution)/shard_map/ppermute | solution.py:19
  76.1 17.3 %collective-permute-start.7 = (f32[9,16,512]{2,1,0:T(8,128)S(1)}, f32[9,16,512]{2,1,0:T(8,128)S(1)}, u32[]{:S(2)}, u32[]{:S(2)}) collective-permute-start(f32[9,16,512]{2,1,0:T(8,128)S(1)} %pad_maximum_fusion.11), channel_id=1, source_target_pairs={{8,0},{16,8},{24,16},{32,24},{40,32},{48,40},{56,48},{64,56},{72,6... | collective-permute-start | bytes 884744 | tf_op jit(solution)/shard_map/ppermute | solution.py:19
  89.1 13.5 %collective-permute-start.6 = (f32[9,16,512]{2,1,0:T(8,128)S(1)}, f32[9,16,512]{2,1,0:T(8,128)S(1)}, u32[]{:S(2)}, u32[]{:S(2)}) collective-permute-start(f32[9,16,512]{2,1,0:T(8,128)S(1)} %pad_maximum_fusion.12), channel_id=1, source_target_pairs={{0,8},{8,16},{16,24},{24,32},{32,40},{40,48},{48,56},{56,64},{64,7... | collective-permute-start | bytes 884744 | tf_op jit(solution)/shard_map/ppermute | solution.py:19

commit v7 on v6

--- a/solution.py
+++ b/solution.py
@@ -92,6 +92,81 @@
             middle[:, inner - width :] + above,
         ),
         axis=1,
+    )
+
+
+def packed_y_halo(cells):
+    depth, rows = cells.shape[1], cells.shape[2]
+
+    def rims(lo, hi, narrow):
+        return jnp.concatenate(
+            (
+                cells[0, :, lo:hi],
+                jnp.concatenate(
+                    (cells[1, 2 : depth - 2, narrow], cells[2, 2 : depth - 2, narrow]), axis=1
+                ),
+            ),
+            axis=0,
+        )
+
+    lower = rims(0, 4, slice(0, 2))
+    upper = rims(rows - 4, rows, slice(rows - 2, rows))
+    lower, upper = lax.optimization_barrier((lower, upper))
+    from_above = from_behind(lower, "gy", -1)
+    from_below = from_behind(upper, "gy", 1)
+
+    def unpack(arrived, outer):
+        narrow = arrived[depth:]
+        spread = ((2, 2), outer, (0, 0))
+        return jnp.stack(
+            (
+                arrived[:depth],
+                jnp.pad(narrow[:, :2], spread),
+                jnp.pad(narrow[:, 2:], spread),
+            )
+        )
+
+    return jnp.concatenate(
+        (unpack(from_below, (2, 0)), cells, unpack(from_above, (0, 2))), axis=2
+    )
+
+
+def packed_y_fold(contributions):
+    depth, rows = contributions.shape[1], contributions.shape[2]
+
+    def rims(lo, hi):
+        return jnp.concatenate(
+            (
+                contributions[0, :, lo:hi],
+                contributions[1, 1 : depth - 1, lo:hi],
+                contributions[2, 2 : depth - 2, lo:hi],
+            ),
+            axis=0,
+        )
+
+    lower = rims(0, 4)
+    upper = rims(rows - 4, rows)
+    lower, upper = lax.optimization_barrier((lower, upper))
+    from_above = from_behind(lower, "gy", -1)
+    from_below = from_behind(upper, "gy", 1)
+
+    def unpack(arrived):
+        return jnp.stack(
+            (
+                arrived[:depth],
+                jnp.pad(arrived[depth : 2 * depth - 2], ((1, 1), (0, 0), (0, 0))),
+                jnp.pad(arrived[2 * depth - 2 :], ((2, 2), (0, 0), (0, 0))),
+            )
+        )
+
+    middle = contributions[:, :, 4 : rows - 4]
+    return jnp.concatenate(
+        (
+            middle[:, :, :4] + unpack(from_below),
+            middle[:, :, 4:-4],
+            middle[:, :, -4:] + unpack(from_above),
+        ),
+        axis=2,
     )
 
 
@@ -173,7 +248,7 @@
     state = packed_z_halo(
         (saved_order_parameter, saved_heat_level, kinetic_rate_field), (4, 2, 2)
     )
-    state = extended(state, (("gy", 2),), 4)
+    state = packed_y_halo(state)
     phase_wide, temp_wide, rate_wide = state[0], state[1], state[2]
     succeeding_order_parameter, succeeding_heat_level = advance_solver_step(
         phase_wide, temp_wide, rate_wide[2:-2, 2:-2]
@@ -199,10 +274,8 @@
         (halfway_order_parameter, halfway_heat_level)
     )
     early_mob = jnp.pad(early_mob, ((2, 2), (2, 2), (0, 0)))
-    folded = fold_rims(
-        jnp.stack((sensitivity_order_parameter, sensitivity_heat_level, early_mob)),
-        4,
-        (("gy", 2),),
+    folded = packed_y_fold(
+        jnp.stack((sensitivity_order_parameter, sensitivity_heat_level, early_mob))
     )
     folded = packed_z_fold(folded, (4, 3, 2))
     return (folded[0], folded[1], latest_kinetic_rate + folded[2])

time: 107 us -> 98.3 us (0.919); the launches traced: 105 us -> 97.5 us
  starting transfers between devices: 37.5 us -> 31.9 us
  waiting for transfers between devices: 38.6 us -> 34.9 us
  other arithmetic: 25 us -> 26.1 us
    ppermute x2 -> x0, waiting for transfers between devices: 8.14 us -> none  [the longest x1 4.51 us: extended(): lax.ppermute(tail, axis, [(i, (i + 1) % count) for i in range(ends)])]
    ppermute x2 -> x0, starting transfers between devices: 5.84 us -> none  [the longest x1 3.6 us: extended(): lax.ppermute(head, axis, [((i + 1) % count, i) for i in range(ends)])]
    ppermute x6 -> x8, waiting for transfers between devices: 30.4 us -> 34.9 us  [from_behind(): return lax.ppermute(block, axis, route)]
    ppermute x6 -> x8, starting transfers between devices: 31.7 us -> 31.9 us  [from_behind(): return lax.ppermute(block, axis, route)]
  transfers between devices with their start and end apart: 8 -> 8, of which waited for: 8 -> 8; matrix products, arithmetic and copies ran while one was open for 0% -> 1% of each run, Pallas kernels for 0% -> 0%
where the time goes in v7:
time: 98.3 us; the launch traced here: 97.5 us
  waiting for transfers between devices  34.9 us (36%)
  starting transfers between devices  31.9 us (32%)
  other arithmetic  26.1 us (27%)
  local copies, waits for them, and re-layouts  3.29 us (3%)
  between operations  1.28 us (1%)
    ppermute x8, waiting for transfers between devices, from_behind(): return lax.ppermute(block, axis, route)  34.9 us
    ppermute x8, starting transfers between devices, from_behind(): return lax.ppermute(block, axis, route)  31.9 us
    neg x2, other arithmetic, advance_solver_step(): grad_x = 0.5 * (padded[1:-1, 1:-1, 2:] - padded[1:-1, 1:-1, :-2])  6.28 us
    neg x2, other arithmetic, advance_solver_step(): grad_y = 0.5 * (padded[1:-1, 2:, 1:-1] - padded[1:-1, :-2, 1:-1])  3.47 us
    add_any x2, other arithmetic, advance_solver_step(): 1.0 - phase_now  2.63 us
    mul x2, other arithmetic, advance_solver_step(): ENERGY_SCALE * (aniso_sq * grad_z + factor_a * grad_z * (sq_z - quartic *...  2.47 us
    slice x2, local copies, waits for them, and re-layouts, packed_z_halo(): tails = jnp.concatenate([f[size - w:] for f, w in zip(fields, widths)], 0)  2.01 us
  transfers between devices with their start and end apart: 8, of which 8 were waited for; matrix products, arithmetic and copies ran while one was open for 1% of the time, Pallas kernels for 0%

profile of v7, /device:TPU:14, one launch (start us, length us, event | category | flops | bytes accessed | tf_op | source)
XLA Modules:
  0.0 97.5 jit_solution(6730020945017292518)
XLA Ops:
  0.7 1.1 %fusion.111 = (f32[4,16,512]{2,1,0:T(8,128)S(1)}, f32[4,16,512]{2,1,0:T(8,128)S(1)}) fusion(f32[8,16,512]{2,1,0:T(8,128)} %param.5), kind=kLoop, calls=%fused_computation.279 | loop fusion | bytes 524288 | tf_op jit(solution)/shard_map/slice | solution.py:41
  1.7 1.0 fusion.112
  2.7 7.9 %collective-permute-start.1 = (f32[8,16,512]{2,1,0:T(8,128)S(1)}, f32[8,16,512]{2,1,0:T(8,128)S(1)}, u32[]{:S(2)}, u32[]{:S(2)}) collective-permute-start(f32[8,16,512]{2,1,0:T(8,128)S(1)} %pad_maximum_fusion.8), channel_id=1, source_target_pairs={{8,0},{16,8},{24,16},{32,24},{40,32},{48,40},{56,48},{64,56},{72,6... | collective-permute-start | bytes 786440 | tf_op jit(solution)/shard_map/ppermute | solution.py:19
  10.7 1.9 %collective-permute-start = (f32[8,16,512]{2,1,0:T(8,128)S(1)}, f32[8,16,512]{2,1,0:T(8,128)S(1)}, u32[]{:S(2)}, u32[]{:S(2)}) collective-permute-start(f32[8,16,512]{2,1,0:T(8,128)S(1)} %pad_maximum_fusion.7), channel_id=1, source_target_pairs={{0,8},{8,16},{16,24},{24,32},{32,40},{40,48},{48,56},{56,64},{64,7... | collective-permute-start | bytes 786440 | tf_op jit(solution)/shard_map/ppermute | solution.py:19
  12.6 1.0 %broadcast_multiply_fusion.3 = f32[8,16,512]{2,1,0:T(8,128)S(1)} fusion(f32[8,16,512]{2,1,0:T(8,128)} %param.9), kind=kLoop, calls=%fused_computation.245 | loop fusion | flops 65536 | bytes 524288 | tf_op jit(solution)/shard_map/transpose(jvp())/mul | solution.py:207
  13.6 3.7 %collective-permute-done.1 = f32[8,16,512]{2,1,0:T(8,128)S(1)} collective-permute-done((f32[8,16,512]{2,1,0:T(8,128)S(1)}, f32[8,16,512]{2,1,0:T(8,128)S(1)}, u32[]{:S(2)}, u32[]{:S(2)}) %collective-permute-start.1) | collective-permute-done | bytes 262176 | tf_op jit(solution)/shard_map/ppermute | solution.py:19
  17.4 6.1 %collective-permute-done = f32[8,16,512]{2,1,0:T(8,128)S(1)} collective-permute-done((f32[8,16,512]{2,1,0:T(8,128)S(1)}, f32[8,16,512]{2,1,0:T(8,128)S(1)}, u32[]{:S(2)}, u32[]{:S(2)}) %collective-permute-start) | collective-permute-done | bytes 262176 | tf_op jit(solution)/shard_map/ppermute | solution.py:19
  23.8 0.1 maximum_maximum_fusion.1
  23.9 0.1 maximum_maximum_fusion.2
  23.9 3.6 %collective-permute-start.3 = (f32[28,4,512]{2,1,0:T(4,128)S(1)}, f32[28,4,512]{2,1,0:T(4,128)S(1)}, u32[]{:S(2)}, u32[]{:S(2)}) collective-permute-start(f32[28,4,512]{2,1,0:T(4,128)S(1)} %maximum_maximum_fusion.1), channel_id=1, source_target_pairs={{1,0},{2,1},{3,2},{4,3},{5,4},{6,5},{7,6},{9,8},{10,9},{11,10},{12... | collective-permute-start | bytes 688136 | tf_op jit(solution)/shard_map/ppermute | solution.py:19
  27.6 0.1 and_and_fusion
  27.7 2.2 %collective-permute-start.2 = (f32[28,4,512]{2,1,0:T(4,128)S(1)}, f32[28,4,512]{2,1,0:T(4,128)S(1)}, u32[]{:S(2)}, u32[]{:S(2)}) collective-permute-start(f32[28,4,512]{2,1,0:T(4,128)S(1)} %maximum_maximum_fusion.2), channel_id=1, source_target_pairs={{0,1},{1,2},{2,3},{3,4},{4,5},{5,6},{6,7},{8,9},{9,10},{10,11},{11... | collective-permute-start | bytes 688136 | tf_op jit(solution)/shard_map/ppermute | solution.py:19
  29.9 1.9 %collective-permute-done.3 = f32[28,4,512]{2,1,0:T(4,128)S(1)} collective-permute-done((f32[28,4,512]{2,1,0:T(4,128)S(1)}, f32[28,4,512]{2,1,0:T(4,128)S(1)}, u32[]{:S(2)}, u32[]{:S(2)}) %collective-permute-start.3) | collective-permute-done | bytes 229408 | tf_op jit(solution)/shard_map/ppermute | solution.py:19
  32.0 4.6 %collective-permute-done.2 = f32[28,4,512]{2,1,0:T(4,128)S(1)} collective-permute-done((f32[28,4,512]{2,1,0:T(4,128)S(1)}, f32[28,4,512]{2,1,0:T(4,128)S(1)}, u32[]{:S(2)}, u32[]{:S(2)}) %collective-permute-start.2) | collective-permute-done | bytes 229408 | tf_op jit(solution)/shard_map/ppermute | solution.py:19
  36.7 0.7 maximum_maximum_fusion
  37.3 0.2 slice_bitcast_fusion
  37.5 1.4 %add_multiply_fusion.5 = (f32[14,22,514]{2,1,0:T(8,128)S(1)}, f32[14,22,514]{2,1,0:T(8,128)S(1)}, f32[14,22,514]{2,1,0:T(8,128)S(1)}, f32[14,22,514]{2,1,0:T(8,1...) fusion(f32[16,24,512]{2,1,0:T(8,128)S(1)} %get-tuple-element.66), kind=kLoop, calls=%fused_computation.67 | loop fusion | flops 5224296 | bytes 5219168 | tf_op jit(solution)/shard_map/mul | solution.py:186
  39.1 0.2 pad_slice_fusion.16
  39.3 0.8 add_multiply_fusion.4
  40.1 1.8 %broadcast_select_fusion = (f32[12,20,512]{2,1,0:T(8,128)S(1)}, f32[12,20,512]{2,1,0:T(8,128)S(1)}, f32[12,20,512]{2,1,0:T(8,128)S(1)}, f32[12,20,512]{2,1,0:T(8,128)S(1)}, f32[12,20,512]{2,1,0:T(8,128)S(1)}) fusion(pred[20]{0:T(512)(128)(4,1)S(1)} %get-tuple-element.114, pred[20]{0:T(512)(128)(4,1)S(1)} %get-tuple-element.115, ...), kind=kLoop, calls=%fused_computation.173 | loop fusion | flops 3072000 | bytes 9338932 | tf_op jit(solution)/shard_map/jit(_where)/select_n | solution.py:257
  41.9 1.0 %add_multiply_fusion.8 = (f32[10,18,514]{2,1,0:T(8,128)S(1)}, f32[10,18,514]{2,1,0:T(8,128)S(1)}, f32[10,18,514]{2,1,0:T(8,128)S(1)}, f32[10,18,514]{2,1,0:T(8,128)S(1)}) fusion(f32[12,20,512]{2,1,0:T(8,128)S(1)} %get-tuple-element.42), kind=kLoop, calls=%fused_computation.114 | loop fusion | flops 3053160 | bytes 1971840 | tf_op jit(solution)/shard_map/jvp()/mul | solution.py:186
  43.0 0.6 fusion.79
  43.6 0.2 broadcast_multiply_fusion
  43.8 0.5 fusion.58
  44.3 2.8 %fusion.99 = (f32[10,18,514]{2,1,0:T(8,128)S(1)}, f32[10,18,514]{2,1,0:T(8,128)S(1)}, f32[10,18,514]{2,1,0:T(8,128)S(1)}, f32[10,18,514]{2,1,0:T(8,128)S(1)}, f32[10,18,514]{2,1,0:T(8,128)S(1)}) fusion(f32[10,18,514]{2,1,0:T(8,128)S(1)} %get-tuple-element.16, f32[8,16,512]{2,1,0:T(8,128)S(1)} %get-tuple-element.96, f32[8,16,512]{2,1,0:T(8,128)S(1)} %get-tuple-element.97, ...), kind=kLoop, calls=%fused_computation.275 | loop fusion | flops 8604360 | bytes 3484928 | tf_op jit(solution)/shard_map/transpose(jvp())/neg | solution.py:177
  47.1 1.6 %fusion.101 = (f32[10,18,514]{2,1,0:T(8,128)S(1)}, f32[10,18,514]{2,1,0:T(8,128)S(1)}, f32[10,18,514]{2,1,0:T(8,128)S(1)}, f32[10,18,514]{2,1,0:T(8,128)S(1)}, f32[10,18,514]{2,1,0:T(8,128)S(1)}) fusion(f32[10,18,514]{2,1,0:T(8,128)S(1)} %get-tuple-element.17, f32[10,18,514]{2,1,0:T(8,128)S(1)} %get-tuple-element.37, ...), kind=kLoop, calls=%fused_computation.276 | loop fusion | flops 5643720 | bytes 4225088 | tf_op jit(solution)/shard_map/transpose(jvp())/neg | solution.py:176
  48.6 2.1 %fusion.43 = (f32[12,20,512]{2,1,0:T(8,128)S(1)}, f32[12,20,512]{2,1,0:T(8,128)S(1)}) fusion(f32[16,24,512]{2,1,0:T(8,128)S(1)} %get-tuple-element.65, f32[16,24,512]{2,1,0:T(8,128)S(1)} %get-tuple-element.64, f32[16,24,512]{2,1,0:T(8,128)S(1)} %get-tuple-element.66, f32[8,16,512]{2,1,0:T(8,128)S(1)} %get-tuple-element.31, ...), kind=kLoop, calls=%fused_computation.126 | loop fusion | flops 4300800 | bytes 5464564 | tf_op jit(solution)/shard_map/transpose(jvp())/add_any | solution.py:196
  50.8 1.0 %fusion.97 = (f32[12,20,512]{2,1,0:T(8,128)S(1)}, f32[12,20,512]{2,1,0:T(8,128)S(1)}, f32[12,20,512]{2,1,0:T(8,128)S(1)}, f32[12,20,512]{2,1,0:T(8,128)S(1)}) fusion(f32[12,20,512]{2,1,0:T(8,128)S(1)} %get-tuple-element.20, f32[16,24,512]{2,1,0:T(8,128)S(1)} %get-tuple-element.65, f32[16,24,512]{2,1,0:T(8,128)S(1)} %get-tuple-element.64, ...), kind=kLoop, calls=%fused_computation.274 | loop fusion | flops 3563520 | bytes 5439540 | tf_op jit(solution)/shard_map/transpose(jvp())/neg | solution.py:191
  51.8 0.1 pad_bitcast_fusion
  51.9 0.2 add_bitcast_fusion
  52.2 3.5 %fusion.91 = (f32[14,22,514]{2,1,0:T(8,128)S(1)}, f32[14,22,514]{2,1,0:T(8,128)S(1)}, f32[14,22,514]{2,1,0:T(8,128)S(1)}, f32[14,22,514]{2,1,0:T(8,128)S(1)}) fusion(f32[14,22,514]{2,1,0:T(8,128)S(1)} %get-tuple-element.51, f32[14,22,514]{2,1,0:T(8,128)S(1)} %get-tuple-element.59, f32[14,22,514]{2,1,0:T(8,128)S(1)} %get-tuple-element.47, ...), kind=kLoop, calls=%fused_computation.271 | loop fusion | flops 13298208 | bytes 8582016 | tf_op jit(solution)/shard_map/transpose(jvp())/neg | solution.py:177
  55.7 1.9 %fusion.93 = (f32[14,22,514]{2,1,0:T(8,128)S(1)}, f32[14,22,514]{2,1,0:T(8,128)S(1)}, f32[14,22,514]{2,1,0:T(8,128)S(1)}, f32[14,22,514]{2,1,0:T(8,128)S(1)}) fusion(f32[14,22,514]{2,1,0:T(8,128)S(1)} %get-tuple-element.50, f32[14,22,514]{2,1,0:T(8,128)S(1)} %get-tuple-element.24, f32[14,22,514]{2,1,0:T(8,128)S(1)} %get-tuple-element.23, ...), kind=kLoop, calls=%fused_computation.272 | loop fusion | flops 7598976 | bytes 9215264 | tf_op jit(solution)/shard_map/transpose(jvp())/neg | solution.py:176
  57.7 1.2 %fusion.21 = f32[1,16,24,512]{3,2,1,0:T(8,128)S(1)} fusion(f32[14,22,514]{2,1,0:T(8,128)S(1)} %get-tuple-element.57, f32[14,22,514]{2,1,0:T(8,128)S(1)} %get-tuple-element.56, f32[14,22,514]{2,1,0:T(8,128)S(1)} %get-tuple-element.26, f32[14,22,514]{2,1,0:T(8,128)S(1)} %get-tuple-element.25, f32[14,22,514]{2,1,0:T(8,128)S(1)} %get-tuple-element.22, ...), kind=kLoop, calls=%fused_computation.76 | loop fusion | flops 1179648 | bytes 5077440 | tf_op jit(solution)/shard_map/stack | solution.py:278
  59.0 0.1 pad_maximum_fusion.2
  59.1 0.1 pad_maximum_fusion.3
  59.1 1.9 %collective-permute-start.4 = (f32[42,4,512]{2,1,0:T(4,128)S(1)}, f32[42,4,512]{2,1,0:T(4,128)S(1)}, u32[]{:S(2)}, u32[]{:S(2)}) collective-permute-start(f32[42,4,512]{2,1,0:T(4,128)S(1)} %pad_maximum_fusion.3), channel_id=1, source_target_pairs={{0,1},{1,2},{2,3},{3,4},{4,5},{5,6},{6,7},{8,9},{9,10},{10,11},{11... | collective-permute-start | bytes 1032200 | tf_op jit(solution)/shard_map/ppermute | solution.py:19
  61.1 4.8 %collective-permute-start.5 = (f32[42,4,512]{2,1,0:T(4,128)S(1)}, f32[42,4,512]{2,1,0:T(4,128)S(1)}, u32[]{:S(2)}, u32[]{:S(2)}) collective-permute-start(f32[42,4,512]{2,1,0:T(4,128)S(1)} %pad_maximum_fusion.2), channel_id=1, source_target_pairs={{1,0},{2,1},{3,2},{4,3},{5,4},{6,5},{7,6},{9,8},{10,9},{11,10},{12... | collective-permute-start | bytes 1032200 | tf_op jit(solution)/shard_map/ppermute | solution.py:19
  65.9 3.3 %collective-permute-done.4 = f32[42,4,512]{2,1,0:T(4,128)S(1)} collective-permute-done((f32[42,4,512]{2,1,0:T(4,128)S(1)}, f32[42,4,512]{2,1,0:T(4,128)S(1)}, u32[]{:S(2)}, u32[]{:S(2)}) %collective-permute-start.4) | collective-permute-done | bytes 344096 | tf_op jit(solution)/shard_map/ppermute | solution.py:19
  69.2 3.7 %collective-permute-done.5 = f32[42,4,512]{2,1,0:T(4,128)S(1)} collective-permute-done((f32[42,4,512]{2,1,0:T(4,128)S(1)}, f32[42,4,512]{2,1,0:T(4,128)S(1)}, u32[]{:S(2)}, u32[]{:S(2)}) %collective-permute-start.5) | collective-permute-done | bytes 344096 | tf_op jit(solution)/shard_map/ppermute | solution.py:19
  73.1 0.3 maximum_add_fusion
  73.4 0.4 fusion.1
  73.9 7.6 %collective-permute-start.7 = (f32[9,16,512]{2,1,0:T(8,128)S(1)}, f32[9,16,512]{2,1,0:T(8,128)S(1)}, u32[]{:S(2)}, u32[]{:S(2)}) collective-permute-start(f32[9,16,512]{2,1,0:T(8,128)S(1)} %pad_maximum_fusion.4), channel_id=1, source_target_pairs={{8,0},{16,8},{24,16},{32,24},{40,32},{48,40},{56,48},{64,56},{72,6... | collective-permute-start | bytes 884744 | tf_op jit(solution)/shard_map/ppermute | solution.py:19
  81.5 1.9 %collective-permute-start.6 = (f32[9,16,512]{2,1,0:T(8,128)S(1)}, f32[9,16,512]{2,1,0:T(8,128)S(1)}, u32[]{:S(2)}, u32[]{:S(2)}) collective-permute-start(f32[9,16,512]{2,1,0:T(8,128)S(1)} %pad_maximum_fusion.5), channel_id=1, source_target_pairs={{0,8},{8,16},{16,24},{24,32},{32,40},{40,48},{48,56},{56,64},{64,7... | collective-permute-start | bytes 884744 | tf_op jit(solution)/shard_map/ppermute | solution.py:19
  83.4 2.4 %collective-permute-done.7 = f32[9,16,512]{2,1,0:T(8,128)S(1)} collective-permute-done((f32[9,16,512]{2,1,0:T(8,128)S(1)}, f32[9,16,512]{2,1,0:T(8,128)S(1)}, u32[]{:S(2)}, u32[]{:S(2)}) %collective-permute-start.7) | collective-permute-done | bytes 294944 | tf_op jit(solution)/shard_map/ppermute | solution.py:19
  85.9 9.2 %collective-permute-done.6 = f32[9,16,512]{2,1,0:T(8,128)S(1)} collective-permute-done((f32[9,16,512]{2,1,0:T(8,128)S(1)}, f32[9,16,512]{2,1,0:T(8,128)S(1)}, u32[]{:S(2)}, u32[]{:S(2)}) %collective-permute-start.6) | collective-permute-done | bytes 294944 | tf_op jit(solution)/shard_map/ppermute | solution.py:19
  95.2 0.1 slice_add_fusion.3
  95.3 0.8 fusion.60
  96.1 1.4 %fusion.64 = f32[8,16,512]{2,1,0:T(8,128)} fusion(f32[3,4,16,512]{3,2,1,0:T(8,128)S(1)} %get-tuple-element.69, f32[3,4,16,512]{3,2,1,0:T(8,128)S(1)} %get-tuple-element.70, f32[10,18,514]{2,1,0:T(8,128)S(1)} %get-tuple-element.68, f32[10,18,514]{2,1,0:T(8,128)S(1)} %get-tuple-element.67, f32[10,18,514]{2,1,0:T(8,128)S(1)} %get-tuple-element.15, ...), kind=kLoop, calls=%fused_computation.184 | loop fusion | flops 1245184 | bytes 3670016 | tf_op jit(solution)/shard_map/add | solution.py:281
  (62 shorter events, 1.0 us)
Async XLA Ops:
  0.6 22.9 %copy-start = (f32[8,16,512]{2,1,0:T(8,128)S(1)}, f32[8,16,512]{2,1,0:T(8,128)}, u32[]{:S(2)}) copy-start(f32[8,16,512]{2,1,0:T(8,128)} %param.5) | copy-start | bytes 786436
  0.6 22.9 %copy-start.1 = (f32[8,16,512]{2,1,0:T(8,128)S(1)}, f32[8,16,512]{2,1,0:T(8,128)}, u32[]{:S(2)}) copy-start(f32[8,16,512]{2,1,0:T(8,128)} %param.6) | copy-start | bytes 786436
  0.7 22.9 %copy-start.2 = (f32[8,16,512]{2,1,0:T(8,128)S(1)}, f32[8,16,512]{2,1,0:T(8,128)}, u32[]{:S(2)}) copy-start(f32[8,16,512]{2,1,0:T(8,128)} %param.7) | copy-start | bytes 786436
  2.7 14.6 %collective-permute-start.1 = (f32[8,16,512]{2,1,0:T(8,128)S(1)}, f32[8,16,512]{2,1,0:T(8,128)S(1)}, u32[]{:S(2)}, u32[]{:S(2)}) collective-permute-start(f32[8,16,512]{2,1,0:T(8,128)S(1)} %pad_maximum_fusion.8), channel_id=1, source_target_pairs={{8,0},{16,8},{24,16},{32,24},{40,32},{48,40},{56,48},{64,56},{72,6... | collective-permute-start | bytes 786440 | tf_op jit(solution)/shard_map/ppermute | solution.py:19
  10.7 12.8 %collective-permute-start = (f32[8,16,512]{2,1,0:T(8,128)S(1)}, f32[8,16,512]{2,1,0:T(8,128)S(1)}, u32[]{:S(2)}, u32[]{:S(2)}) collective-permute-start(f32[8,16,512]{2,1,0:T(8,128)S(1)} %pad_maximum_fusion.7), channel_id=1, source_target_pairs={{0,8},{8,16},{16,24},{24,32},{32,40},{40,48},{48,56},{56,64},{64,7... | collective-permute-start | bytes 786440 | tf_op jit(solution)/shard_map/ppermute | solution.py:19
  23.9 7.9 %collective-permute-start.3 = (f32[28,4,512]{2,1,0:T(4,128)S(1)}, f32[28,4,512]{2,1,0:T(4,128)S(1)}, u32[]{:S(2)}, u32[]{:S(2)}) collective-permute-start(f32[28,4,512]{2,1,0:T(4,128)S(1)} %maximum_maximum_fusion.1), channel_id=1, source_target_pairs={{1,0},{2,1},{3,2},{4,3},{5,4},{6,5},{7,6},{9,8},{10,9},{11,10},{12... | collective-permute-start | bytes 688136 | tf_op jit(solution)/shard_map/ppermute | solution.py:19
  27.7 8.8 %collective-permute-start.2 = (f32[28,4,512]{2,1,0:T(4,128)S(1)}, f32[28,4,512]{2,1,0:T(4,128)S(1)}, u32[]{:S(2)}, u32[]{:S(2)}) collective-permute-start(f32[28,4,512]{2,1,0:T(4,128)S(1)} %maximum_maximum_fusion.2), channel_id=1, source_target_pairs={{0,1},{1,2},{2,3},{3,4},{4,5},{5,6},{6,7},{8,9},{9,10},{10,11},{11... | collective-permute-start | bytes 688136 | tf_op jit(solution)/shard_map/ppermute | solution.py:19
  41.9 1.1 %copy-start.3 = (f32[8,16,512]{2,1,0:T(8,128)S(1)}, f32[8,16,512]{2,1,0:T(8,128)}, u32[]{:S(2)}) copy-start(f32[8,16,512]{2,1,0:T(8,128)} %param.9) | copy-start | bytes 786436
  41.9 1.1 %copy-start.4 = (f32[8,16,512]{2,1,0:T(8,128)S(1)}, f32[8,16,512]{2,1,0:T(8,128)}, u32[]{:S(2)}) copy-start(f32[8,16,512]{2,1,0:T(8,128)} %param.8) | copy-start | bytes 786436
  59.1 10.0 %collective-permute-start.4 = (f32[42,4,512]{2,1,0:T(4,128)S(1)}, f32[42,4,512]{2,1,0:T(4,128)S(1)}, u32[]{:S(2)}, u32[]{:S(2)}) collective-permute-start(f32[42,4,512]{2,1,0:T(4,128)S(1)} %pad_maximum_fusion.3), channel_id=1, source_target_pairs={{0,1},{1,2},{2,3},{3,4},{4,5},{5,6},{6,7},{8,9},{9,10},{10,11},{11... | collective-permute-start | bytes 1032200 | tf_op jit(solution)/shard_map/ppermute | solution.py:19
  61.1 11.9 %collective-permute-start.5 = (f32[42,4,512]{2,1,0:T(4,128)S(1)}, f32[42,4,512]{2,1,0:T(4,128)S(1)}, u32[]{:S(2)}, u32[]{:S(2)}) collective-permute-start(f32[42,4,512]{2,1,0:T(4,128)S(1)} %pad_maximum_fusion.2), channel_id=1, source_target_pairs={{1,0},{2,1},{3,2},{4,3},{5,4},{6,5},{7,6},{9,8},{10,9},{11,10},{12... | collective-permute-start | bytes 1032200 | tf_op jit(solution)/shard_map/ppermute | solution.py:19
  73.9 11.9 %collective-permute-start.7 = (f32[9,16,512]{2,1,0:T(8,128)S(1)}, f32[9,16,512]{2,1,0:T(8,128)S(1)}, u32[]{:S(2)}, u32[]{:S(2)}) collective-permute-start(f32[9,16,512]{2,1,0:T(8,128)S(1)} %pad_maximum_fusion.4), channel_id=1, source_target_pairs={{8,0},{16,8},{24,16},{32,24},{40,32},{48,40},{56,48},{64,56},{72,6... | collective-permute-start | bytes 884744 | tf_op jit(solution)/shard_map/ppermute | solution.py:19
  81.5 13.6 %collective-permute-start.6 = (f32[9,16,512]{2,1,0:T(8,128)S(1)}, f32[9,16,512]{2,1,0:T(8,128)S(1)}, u32[]{:S(2)}, u32[]{:S(2)}) collective-permute-start(f32[9,16,512]{2,1,0:T(8,128)S(1)} %pad_maximum_fusion.5), channel_id=1, source_target_pairs={{0,8},{8,16},{16,24},{24,32},{32,40},{40,48},{48,56},{56,64},{64,7... | collective-permute-start | bytes 884744 | tf_op jit(solution)/shard_map/ppermute | solution.py:19

commit v8 on v7

--- a/solution.py
+++ b/solution.py
@@ -134,37 +134,40 @@
 def packed_y_fold(contributions):
     depth, rows = contributions.shape[1], contributions.shape[2]
 
-    def rims(lo, hi):
+    lanes = contributions.shape[3]
+
+    def rims(lo, hi, narrow):
         return jnp.concatenate(
             (
                 contributions[0, :, lo:hi],
                 contributions[1, 1 : depth - 1, lo:hi],
-                contributions[2, 2 : depth - 2, lo:hi],
+                contributions[2, 2 : depth - 2, narrow].reshape(-1, 4, lanes),
             ),
             axis=0,
         )
 
-    lower = rims(0, 4)
-    upper = rims(rows - 4, rows)
+    lower = rims(0, 4, slice(2, 4))
+    upper = rims(rows - 4, rows, slice(rows - 4, rows - 2))
     lower, upper = lax.optimization_barrier((lower, upper))
     from_above = from_behind(lower, "gy", -1)
     from_below = from_behind(upper, "gy", 1)
 
-    def unpack(arrived):
+    def unpack(arrived, outer):
+        narrow = arrived[2 * depth - 2 :].reshape(depth - 4, 2, lanes)
         return jnp.stack(
             (
                 arrived[:depth],
                 jnp.pad(arrived[depth : 2 * depth - 2], ((1, 1), (0, 0), (0, 0))),
-                jnp.pad(arrived[2 * depth - 2 :], ((2, 2), (0, 0), (0, 0))),
+                jnp.pad(narrow, ((2, 2), outer, (0, 0))),
             )
         )
 
     middle = contributions[:, :, 4 : rows - 4]
     return jnp.concatenate(
         (
-            middle[:, :, :4] + unpack(from_below),
+            middle[:, :, :4] + unpack(from_below, (0, 2)),
             middle[:, :, 4:-4],
-            middle[:, :, -4:] + unpack(from_above),
+            middle[:, :, -4:] + unpack(from_above, (2, 0)),
         ),
         axis=2,
     )

time: 98.3 us -> 114 us (1.16)
  other arithmetic: 26.1 us -> 36.7 us
  local copies, waits for them, and re-layouts: 3.29 us -> 9.85 us
    neg x2, other arithmetic: 6.28 us -> 9.36 us  [advance_solver_step(): grad_x = 0.5 * (padded[1:-1, 1:-1, 2:] - padded[1:-1, 1:-1, :-2])]
    mul x2, other arithmetic: 2.47 us -> 4.28 us  [advance_solver_step(): ENERGY_SCALE * (aniso_sq * grad_z + factor_a * grad_z * (sq_z - quartic *...]
    squeeze x1, local copies, waits for them, and re-layouts: 0.05 us -> 1.74 us  [rims(): contributions[1, 1:depth - 1, lo:hi]]
    slice x2 -> x3, local copies, waits for them, and re-layouts: 0.01 us -> 1.47 us  [the longest x2 0.81 us: unpack(): narrow = arrived[2 * depth - 2:].reshape(depth - 4, 2, lanes)]
    mul x1, other arithmetic: 0.78 us -> 1.99 us  [advance_solver_step(): ENERGY_SCALE * (aniso_sq * grad_y + factor_a * grad_y * (sq_y - quartic *...]
where the time goes in v8:
time: 114 us; the launch traced here: 113 us
  other arithmetic  36.7 us (32%)
  waiting for transfers between devices  33.9 us (30%)
  starting transfers between devices  31 us (27%)
  local copies, waits for them, and re-layouts  9.85 us (9%)
  between operations  1.45 us (1%)
    ppermute x8, waiting for transfers between devices, from_behind(): return lax.ppermute(block, axis, route)  33.9 us
    ppermute x8, starting transfers between devices, from_behind(): return lax.ppermute(block, axis, route)  31 us
    neg x2, other arithmetic, advance_solver_step(): grad_x = 0.5 * (padded[1:-1, 1:-1, 2:] - padded[1:-1, 1:-1, :-2])  9.36 us
    mul x2, other arithmetic, advance_solver_step(): ENERGY_SCALE * (aniso_sq * grad_z + factor_a * grad_z * (sq_z - quartic *...  4.28 us
    neg x2, other arithmetic, advance_solver_step(): grad_y = 0.5 * (padded[1:-1, 2:, 1:-1] - padded[1:-1, :-2, 1:-1])  4.24 us
    add_any x2, other arithmetic, advance_solver_step(): 1.0 - phase_now  3.45 us
    another operation x2, other arithmetic, body(): jnp.stack((sensitivity_order_parameter, sensitivity_heat_level, early_mob))  2.43 us
    add x1, other arithmetic, body(): return (folded[0], folded[1], latest_kinetic_rate + folded[2])  2.36 us
  transfers between devices with their start and end apart: 8, of which 8 were waited for; matrix products, arithmetic and copies ran while one was open for 1% of the time, Pallas kernels for 0%

profile of v8, /device:TPU:14, one launch (start us, length us, event | category | flops | bytes accessed | tf_op | source)
XLA Modules:
  0.0 113.0 jit_solution(11902763686984837452)
XLA Ops:
  0.7 1.1 fusion.112
  1.7 1.0 fusion.113
  2.7 7.9 %collective-permute-start.1 = (f32[8,16,512]{2,1,0:T(8,128)S(1)}, f32[8,16,512]{2,1,0:T(8,128)S(1)}, u32[]{:S(2)}, u32[]{:S(2)}) collective-permute-start(f32[8,16,512]{2,1,0:T(8,128)S(1)} %pad_maximum_fusion.8), channel_id=1, source_target_pairs={{8,0},{16,8},{24,16},{32,24},{40,32},{48,40},{56,48},{64,56},{72,6... | collective-permute-start | bytes 786440 | tf_op jit(solution)/shard_map/ppermute | solution.py:19
  10.7 1.9 %collective-permute-start = (f32[8,16,512]{2,1,0:T(8,128)S(1)}, f32[8,16,512]{2,1,0:T(8,128)S(1)}, u32[]{:S(2)}, u32[]{:S(2)}) collective-permute-start(f32[8,16,512]{2,1,0:T(8,128)S(1)} %pad_maximum_fusion.7), channel_id=1, source_target_pairs={{0,8},{8,16},{16,24},{24,32},{32,40},{40,48},{48,56},{56,64},{64,7... | collective-permute-start | bytes 786440 | tf_op jit(solution)/shard_map/ppermute | solution.py:19
  12.6 1.0 broadcast_multiply_fusion.3
  13.6 3.7 %collective-permute-done.1 = f32[8,16,512]{2,1,0:T(8,128)S(1)} collective-permute-done((f32[8,16,512]{2,1,0:T(8,128)S(1)}, f32[8,16,512]{2,1,0:T(8,128)S(1)}, u32[]{:S(2)}, u32[]{:S(2)}) %collective-permute-start.1) | collective-permute-done | bytes 262176 | tf_op jit(solution)/shard_map/ppermute | solution.py:19
  17.4 6.1 %collective-permute-done = f32[8,16,512]{2,1,0:T(8,128)S(1)} collective-permute-done((f32[8,16,512]{2,1,0:T(8,128)S(1)}, f32[8,16,512]{2,1,0:T(8,128)S(1)}, u32[]{:S(2)}, u32[]{:S(2)}) %collective-permute-start) | collective-permute-done | bytes 262176 | tf_op jit(solution)/shard_map/ppermute | solution.py:19
  23.9 3.6 %collective-permute-start.3 = (f32[28,4,512]{2,1,0:T(4,128)S(1)}, f32[28,4,512]{2,1,0:T(4,128)S(1)}, u32[]{:S(2)}, u32[]{:S(2)}) collective-permute-start(f32[28,4,512]{2,1,0:T(4,128)S(1)} %maximum_maximum_fusion.1), channel_id=1, source_target_pairs={{1,0},{2,1},{3,2},{4,3},{5,4},{6,5},{7,6},{9,8},{10,9},{11,10},{12... | collective-permute-start | bytes 688136 | tf_op jit(solution)/shard_map/ppermute | solution.py:19
  27.7 2.2 %collective-permute-start.2 = (f32[28,4,512]{2,1,0:T(4,128)S(1)}, f32[28,4,512]{2,1,0:T(4,128)S(1)}, u32[]{:S(2)}, u32[]{:S(2)}) collective-permute-start(f32[28,4,512]{2,1,0:T(4,128)S(1)} %maximum_maximum_fusion.2), channel_id=1, source_target_pairs={{0,1},{1,2},{2,3},{3,4},{4,5},{5,6},{6,7},{8,9},{9,10},{10,11},{11... | collective-permute-start | bytes 688136 | tf_op jit(solution)/shard_map/ppermute | solution.py:19
  29.9 1.9 %collective-permute-done.3 = f32[28,4,512]{2,1,0:T(4,128)S(1)} collective-permute-done((f32[28,4,512]{2,1,0:T(4,128)S(1)}, f32[28,4,512]{2,1,0:T(4,128)S(1)}, u32[]{:S(2)}, u32[]{:S(2)}) %collective-permute-start.3) | collective-permute-done | bytes 229408 | tf_op jit(solution)/shard_map/ppermute | solution.py:19
  32.0 4.6 %collective-permute-done.2 = f32[28,4,512]{2,1,0:T(4,128)S(1)} collective-permute-done((f32[28,4,512]{2,1,0:T(4,128)S(1)}, f32[28,4,512]{2,1,0:T(4,128)S(1)}, u32[]{:S(2)}, u32[]{:S(2)}) %collective-permute-start.2) | collective-permute-done | bytes 229408 | tf_op jit(solution)/shard_map/ppermute | solution.py:19
  36.7 0.7 maximum_maximum_fusion
  37.5 2.4 %add_multiply_fusion.5 = (f32[14,22,514]{2,1,0:T(8,128)S(1)}, f32[14,22,514]{2,1,0:T(8,128)}, f32[14,22,514]{2,1,0:T(8,128)S(1)}, f32[14,22,514]{2,1,0:T(8,128)S...) fusion(f32[16,24,512]{2,1,0:T(8,128)S(1)} %get-tuple-element.66), kind=kLoop, calls=%fused_computation.67 | loop fusion | flops 5224296 | bytes 5219168 | tf_op jit(solution)/shard_map/mul | solution.py:189
  40.0 0.2 pad_slice_fusion.16
  40.2 2.0 %add_multiply_fusion.4 = (f32[14,22,514]{2,1,0:T(8,128)S(1)}, f32[14,22,514]{2,1,0:T(8,128)}, f32[14,22,514]{2,1,0:T(8,128)S(1)}, f32[14,22,514]{2,1,0:T(8,128)}) fusion(f32[14,22,514]{2,1,0:T(8,128)S(1)} %get-tuple-element.47, f32[14,22,514]{2,1,0:T(8,128)S(1)} %get-tuple-element.50, f32[14,22,514]{2,1,0:T(8,128)S(1)} %get-tuple-element.51, ...), kind=kLoop, calls=%fused_computation.66 | loop fusion | flops 4116112 | bytes 5699232 | tf_op jit(solution)/shard_map/mul | solution.py:190
  42.2 1.8 %broadcast_select_fusion = (f32[12,20,512]{2,1,0:T(8,128)S(1)}, f32[12,20,512]{2,1,0:T(8,128)S(1)}, f32[12,20,512]{2,1,0:T(8,128)S(1)}, f32[12,20,512]{2,1,0:T(8,128)S(1)}, f32[12,20,512]{2,1,0:T(8,128)S(1)}) fusion(pred[20]{0:T(512)(128)(4,1)S(1)} %get-tuple-element.114, pred[20]{0:T(512)(128)(4,1)S(1)} %get-tuple-element.115, ...), kind=kLoop, calls=%fused_computation.173 | loop fusion | flops 3072000 | bytes 9338932 | tf_op jit(solution)/shard_map/jit(_where)/select_n | solution.py:260
  44.1 1.9 %add_multiply_fusion.8 = (f32[10,18,514]{2,1,0:T(8,128)}, f32[10,18,514]{2,1,0:T(8,128)S(1)}, f32[10,18,514]{2,1,0:T(8,128)S(1)}, f32[10,18,514]{2,1,0:T(8,128)S(1)}) fusion(f32[12,20,512]{2,1,0:T(8,128)S(1)} %get-tuple-element.42), kind=kLoop, calls=%fused_computation.114 | loop fusion | flops 3053160 | bytes 1971840 | tf_op jit(solution)/shard_map/jvp()/mul | solution.py:189
  46.0 0.6 fusion.79
  46.6 0.2 broadcast_multiply_fusion
  46.9 0.5 fusion.58
  47.4 3.3 %fusion.99 = (f32[10,18,514]{2,1,0:T(8,128)S(1)}, f32[10,18,514]{2,1,0:T(8,128)S(1)}, f32[10,18,514]{2,1,0:T(8,128)S(1)}, f32[10,18,514]{2,1,0:T(8,128)S(1)}, f32[10,18,514]{2,1,0:T(8,128)}) fusion(f32[10,18,514]{2,1,0:T(8,128)S(1)} %get-tuple-element.16, f32[8,16,512]{2,1,0:T(8,128)S(1)} %get-tuple-element.96, f32[8,16,512]{2,1,0:T(8,128)S(1)} %get-tuple-element.97, ...), kind=kLoop, calls=%fused_computation.273 | loop fusion | flops 8604360 | bytes 3484928 | tf_op jit(solution)/shard_map/transpose(jvp())/neg | solution.py:180
  50.6 2.3 %fusion.101 = (f32[10,18,514]{2,1,0:T(8,128)S(1)}, f32[10,18,514]{2,1,0:T(8,128)S(1)}, f32[10,18,514]{2,1,0:T(8,128)S(1)}, f32[10,18,514]{2,1,0:T(8,128)S(1)}, f32[10,18,514]{2,1,0:T(8,128)}) fusion(f32[10,18,514]{2,1,0:T(8,128)S(1)} %get-tuple-element.17, f32[10,18,514]{2,1,0:T(8,128)S(1)} %get-tuple-element.37, f32[10,18,514]{2,1,0:T(8,128)S(1)} %get-tuple-element.36, ...), kind=kLoop, calls=%fused_computation.274 | loop fusion | flops 5643720 | bytes 4225088 | tf_op jit(solution)/shard_map/transpose(jvp())/neg | solution.py:179
  52.9 3.0 %fusion.43 = (f32[12,20,512]{2,1,0:T(8,128)}, f32[12,20,512]{2,1,0:T(8,128)S(1)}) fusion(f32[16,24,512]{2,1,0:T(8,128)S(1)} %get-tuple-element.65, f32[16,24,512]{2,1,0:T(8,128)S(1)} %get-tuple-element.64, f32[16,24,512]{2,1,0:T(8,128)S(1)} %get-tuple-element.66, f32[8,16,512]{2,1,0:T(8,128)S(1)} %get-tuple-element.31, ...), kind=kLoop, calls=%fused_computation.126 | loop fusion | flops 4300800 | bytes 5464564 | tf_op jit(solution)/shard_map/transpose(jvp())/add_any | solution.py:199
  55.9 1.9 %fusion.97 = (f32[12,20,512]{2,1,0:T(8,128)}, f32[12,20,512]{2,1,0:T(8,128)}, f32[12,20,512]{2,1,0:T(8,128)S(1)}, f32[12,20,512]{2,1,0:T(8,128)S(1)}) fusion(f32[12,20,512]{2,1,0:T(8,128)S(1)} %get-tuple-element.20, f32[16,24,512]{2,1,0:T(8,128)S(1)} %get-tuple-element.65, f32[16,24,512]{2,1,0:T(8,128)S(1)} %get-tuple-element.64, ...), kind=kLoop, calls=%fused_computation.272 | loop fusion | flops 3563520 | bytes 5439540 | tf_op jit(solution)/shard_map/transpose(jvp())/neg | solution.py:194
  57.9 1.2 %add_bitcast_fusion = f32[1,16,24,512]{3,2,1,0:T(8,128)} fusion(f32[12,20,512]{2,1,0:T(8,128)S(1)} %get-tuple-element.83, f32[12,20,512]{2,1,0:T(8,128)S(1)} %broadcast_multiply_fusion), kind=kLoop, calls=%fused_computation.85 | loop fusion | flops 786432 | bytes 1769472 | tf_op jit(solution)/shard_map/stack | solution.py:281
  59.1 0.7 fusion.110
  59.8 0.7 reshape_squeeze.6
  60.5 1.7 %slice_bitcast_fusion.15 = (f32[14,4,512]{2,1,0:T(4,128)S(1)}, f32[14,4,512]{2,1,0:T(4,128)}) fusion(f32[1,16,24,512]{3,2,1,0:T(8,128)} %add_bitcast_fusion), kind=kLoop, calls=%fused_computation.246 | loop fusion | bytes 458752 | tf_op jit(solution)/shard_map/squeeze | solution.py:143
  62.2 6.1 %fusion.91 = (f32[14,22,514]{2,1,0:T(8,128)S(1)}, f32[14,22,514]{2,1,0:T(8,128)S(1)}, f32[14,22,514]{2,1,0:T(8,128)S(1)}, f32[14,22,514]{2,1,0:T(8,128)S(1)}) fusion(f32[14,22,514]{2,1,0:T(8,128)} %copy-done, f32[14,22,514]{2,1,0:T(8,128)} %get-tuple-element.59, f32[14,22,514]{2,1,0:T(8,128)S(1)} %get-tuple-element.47, ...), kind=kLoop, calls=%fused_computation.269 | loop fusion | flops 13298208 | bytes 8582016 | tf_op jit(solution)/shard_map/transpose(jvp())/neg | solution.py:180
  68.4 1.9 %fusion.93 = (f32[14,22,514]{2,1,0:T(8,128)S(1)}, f32[14,22,514]{2,1,0:T(8,128)S(1)}, f32[14,22,514]{2,1,0:T(8,128)S(1)}, f32[14,22,514]{2,1,0:T(8,128)S(1)}) fusion(f32[14,22,514]{2,1,0:T(8,128)S(1)} %get-tuple-element.50, f32[14,22,514]{2,1,0:T(8,128)S(1)} %get-tuple-element.24, f32[14,22,514]{2,1,0:T(8,128)S(1)} %get-tuple-element.23, ...), kind=kLoop, calls=%fused_computation.270 | loop fusion | flops 7598976 | bytes 9215264 | tf_op jit(solution)/shard_map/transpose(jvp())/neg | solution.py:179
  70.3 1.2 %fusion.21 = f32[1,16,24,512]{3,2,1,0:T(8,128)S(1)} fusion(f32[14,22,514]{2,1,0:T(8,128)S(1)} %get-tuple-element.57, f32[14,22,514]{2,1,0:T(8,128)S(1)} %get-tuple-element.56, f32[14,22,514]{2,1,0:T(8,128)S(1)} %get-tuple-element.26, f32[14,22,514]{2,1,0:T(8,128)S(1)} %get-tuple-element.25, f32[14,22,514]{2,1,0:T(8,128)S(1)} %get-tuple-element.22, ...), kind=kLoop, calls=%fused_computation.76 | loop fusion | flops 1179648 | bytes 5077440 | tf_op jit(solution)/shard_map/stack | solution.py:281
  71.9 2.1 %collective-permute-start.4 = (f32[36,4,512]{2,1,0:T(4,128)S(1)}, f32[36,4,512]{2,1,0:T(4,128)S(1)}, u32[]{:S(2)}, u32[]{:S(2)}) collective-permute-start(f32[36,4,512]{2,1,0:T(4,128)S(1)} %pad_maximum_fusion.3), channel_id=1, source_target_pairs={{0,1},{1,2},{2,3},{3,4},{4,5},{5,6},{6,7},{8,9},{9,10},{10,11},{11... | collective-permute-start | bytes 884744 | tf_op jit(solution)/shard_map/ppermute | solution.py:19
  74.0 4.8 %collective-permute-start.5 = (f32[36,4,512]{2,1,0:T(4,128)S(1)}, f32[36,4,512]{2,1,0:T(4,128)}, u32[]{:S(2)}, u32[]{:S(2)}) collective-permute-start(f32[36,4,512]{2,1,0:T(4,128)S(1)} %pad_maximum_fusion.2), channel_id=1, source_target_pairs={{1,0},{2,1},{3,2},{4,3},{5,4},{6,5},{7,6},{9,8},{10,9},{11,10},{12... | collective-permute-start | bytes 884744 | tf_op jit(solution)/shard_map/ppermute | solution.py:19
  78.8 2.8 %collective-permute-done.4 = f32[36,4,512]{2,1,0:T(4,128)S(1)} collective-permute-done((f32[36,4,512]{2,1,0:T(4,128)S(1)}, f32[36,4,512]{2,1,0:T(4,128)S(1)}, u32[]{:S(2)}, u32[]{:S(2)}) %collective-permute-start.4) | collective-permute-done | bytes 294944 | tf_op jit(solution)/shard_map/ppermute | solution.py:19
  81.7 3.3 %collective-permute-done.5 = f32[36,4,512]{2,1,0:T(4,128)} collective-permute-done((f32[36,4,512]{2,1,0:T(4,128)S(1)}, f32[36,4,512]{2,1,0:T(4,128)}, u32[]{:S(2)}, u32[]{:S(2)}) %collective-permute-start.5) | collective-permute-done | bytes 294944 | tf_op jit(solution)/shard_map/ppermute | solution.py:19
  84.9 0.8 slice.459
  85.8 0.9 slice.458
  86.8 0.9 slice_bitcast_fusion.7
  87.7 0.3 maximum_add_fusion
  88.0 0.4 fusion.1
  88.6 6.5 %collective-permute-start.7 = (f32[9,16,512]{2,1,0:T(8,128)S(1)}, f32[9,16,512]{2,1,0:T(8,128)S(1)}, u32[]{:S(2)}, u32[]{:S(2)}) collective-permute-start(f32[9,16,512]{2,1,0:T(8,128)S(1)} %pad_maximum_fusion.4), channel_id=1, source_target_pairs={{8,0},{16,8},{24,16},{32,24},{40,32},{48,40},{56,48},{64,56},{72,6... | collective-permute-start | bytes 884744 | tf_op jit(solution)/shard_map/ppermute | solution.py:19
  95.1 1.9 %collective-permute-start.6 = (f32[9,16,512]{2,1,0:T(8,128)S(1)}, f32[9,16,512]{2,1,0:T(8,128)S(1)}, u32[]{:S(2)}, u32[]{:S(2)}) collective-permute-start(f32[9,16,512]{2,1,0:T(8,128)S(1)} %pad_maximum_fusion.5), channel_id=1, source_target_pairs={{0,8},{8,16},{16,24},{24,32},{32,40},{40,48},{48,56},{56,64},{64,7... | collective-permute-start | bytes 884744 | tf_op jit(solution)/shard_map/ppermute | solution.py:19
  97.0 2.4 %collective-permute-done.7 = f32[9,16,512]{2,1,0:T(8,128)S(1)} collective-permute-done((f32[9,16,512]{2,1,0:T(8,128)S(1)}, f32[9,16,512]{2,1,0:T(8,128)S(1)}, u32[]{:S(2)}, u32[]{:S(2)}) %collective-permute-start.7) | collective-permute-done | bytes 294944 | tf_op jit(solution)/shard_map/ppermute | solution.py:19
  99.5 9.2 %collective-permute-done.6 = f32[9,16,512]{2,1,0:T(8,128)S(1)} collective-permute-done((f32[9,16,512]{2,1,0:T(8,128)S(1)}, f32[9,16,512]{2,1,0:T(8,128)S(1)}, u32[]{:S(2)}, u32[]{:S(2)}) %collective-permute-start.6) | collective-permute-done | bytes 294944 | tf_op jit(solution)/shard_map/ppermute | solution.py:19
  109.0 0.8 fusion.60
  109.8 0.3 copy-done.20
  110.2 0.2 copy-done.21
  110.6 2.4 %fusion.64 = f32[8,16,512]{2,1,0:T(8,128)} fusion(f32[3,4,16,512]{3,2,1,0:T(8,128)S(1)} %get-tuple-element.69, f32[3,4,16,512]{3,2,1,0:T(8,128)S(1)} %get-tuple-element.70, f32[10,18,514]{2,1,0:T(8,128)S(1)} %copy-done.22, f32[10,18,514]{2,1,0:T(8,128)S(1)} %copy-done.21, f32[10,18,514]{2,1,0:T(8,128)S(1)} %copy-done.20, f32[12,20,512]{2,1,0:T(8,128)} %copy-done.8, ...), kind=kLoop, calls=%fused_computation.184 | loop fusion | flops 1245184 | bytes 3670016 | tf_op jit(solution)/shard_map/add | solution.py:284
  (108 shorter events, 2.2 us)
Async XLA Ops:
  0.6 22.9 %copy-start.7 = (f32[8,16,512]{2,1,0:T(8,128)S(1)}, f32[8,16,512]{2,1,0:T(8,128)}, u32[]{:S(2)}) copy-start(f32[8,16,512]{2,1,0:T(8,128)} %param.5) | copy-start | bytes 786436
  0.6 22.9 %copy-start.9 = (f32[8,16,512]{2,1,0:T(8,128)S(1)}, f32[8,16,512]{2,1,0:T(8,128)}, u32[]{:S(2)}) copy-start(f32[8,16,512]{2,1,0:T(8,128)} %param.6) | copy-start | bytes 786436
  0.7 22.9 %copy-start.10 = (f32[8,16,512]{2,1,0:T(8,128)S(1)}, f32[8,16,512]{2,1,0:T(8,128)}, u32[]{:S(2)}) copy-start(f32[8,16,512]{2,1,0:T(8,128)} %param.7) | copy-start | bytes 786436
  2.7 14.6 %collective-permute-start.1 = (f32[8,16,512]{2,1,0:T(8,128)S(1)}, f32[8,16,512]{2,1,0:T(8,128)S(1)}, u32[]{:S(2)}, u32[]{:S(2)}) collective-permute-start(f32[8,16,512]{2,1,0:T(8,128)S(1)} %pad_maximum_fusion.8), channel_id=1, source_target_pairs={{8,0},{16,8},{24,16},{32,24},{40,32},{48,40},{56,48},{64,56},{72,6... | collective-permute-start | bytes 786440 | tf_op jit(solution)/shard_map/ppermute | solution.py:19
  10.7 12.8 %collective-permute-start = (f32[8,16,512]{2,1,0:T(8,128)S(1)}, f32[8,16,512]{2,1,0:T(8,128)S(1)}, u32[]{:S(2)}, u32[]{:S(2)}) collective-permute-start(f32[8,16,512]{2,1,0:T(8,128)S(1)} %pad_maximum_fusion.7), channel_id=1, source_target_pairs={{0,8},{8,16},{16,24},{24,32},{32,40},{40,48},{48,56},{56,64},{64,7... | collective-permute-start | bytes 786440 | tf_op jit(solution)/shard_map/ppermute | solution.py:19
  23.9 7.9 %collective-permute-start.3 = (f32[28,4,512]{2,1,0:T(4,128)S(1)}, f32[28,4,512]{2,1,0:T(4,128)S(1)}, u32[]{:S(2)}, u32[]{:S(2)}) collective-permute-start(f32[28,4,512]{2,1,0:T(4,128)S(1)} %maximum_maximum_fusion.1), channel_id=1, source_target_pairs={{1,0},{2,1},{3,2},{4,3},{5,4},{6,5},{7,6},{9,8},{10,9},{11,10},{12... | collective-permute-start | bytes 688136 | tf_op jit(solution)/shard_map/ppermute | solution.py:19
  27.7 8.8 %collective-permute-start.2 = (f32[28,4,512]{2,1,0:T(4,128)S(1)}, f32[28,4,512]{2,1,0:T(4,128)S(1)}, u32[]{:S(2)}, u32[]{:S(2)}) collective-permute-start(f32[28,4,512]{2,1,0:T(4,128)S(1)} %maximum_maximum_fusion.2), channel_id=1, source_target_pairs={{0,1},{1,2},{2,3},{3,4},{4,5},{5,6},{6,7},{8,9},{9,10},{10,11},{11... | collective-permute-start | bytes 688136 | tf_op jit(solution)/shard_map/ppermute | solution.py:19
  39.9 2.3 %copy-start = (f32[14,22,514]{2,1,0:T(8,128)}, f32[14,22,514]{2,1,0:T(8,128)S(1)}, u32[]{:S(2)}) copy-start(f32[14,22,514]{2,1,0:T(8,128)S(1)} %get-tuple-element.51) | copy-start | bytes 1899748
  44.0 2.8 %copy-start.8 = (f32[12,20,512]{2,1,0:T(8,128)}, f32[12,20,512]{2,1,0:T(8,128)S(1)}, u32[]{:S(2)}) copy-start(f32[12,20,512]{2,1,0:T(8,128)S(1)} %get-tuple-element.42) | copy-start | bytes 1474564
  44.0 1.9 %copy-start.13 = (f32[8,16,512]{2,1,0:T(8,128)S(1)}, f32[8,16,512]{2,1,0:T(8,128)}, u32[]{:S(2)}) copy-start(f32[8,16,512]{2,1,0:T(8,128)} %param.9) | copy-start | bytes 786436
  44.0 1.9 %copy-start.16 = (f32[8,16,512]{2,1,0:T(8,128)S(1)}, f32[8,16,512]{2,1,0:T(8,128)}, u32[]{:S(2)}) copy-start(f32[8,16,512]{2,1,0:T(8,128)} %param.8) | copy-start | bytes 786436
  46.6 0.8 copy-start.18
  57.9 1.2 %copy-start.5 = (f32[1,16,24,512]{3,2,1,0:T(8,128)}, f32[1,16,24,512]{3,2,1,0:T(8,128)S(1)}, u32[]{:S(2)}) copy-start(f32[1,16,24,512]{3,2,1,0:T(8,128)S(1)} %pad_bitcast_fusion) | copy-start | bytes 2359300
  62.2 6.1 %copy-start.1 = (f32[14,22,514]{2,1,0:T(8,128)S(1)}, f32[14,22,514]{2,1,0:T(8,128)}, u32[]{:S(2)}) copy-start(f32[14,22,514]{2,1,0:T(8,128)} %copy-done) | copy-start | bytes 1899748
  62.2 6.1 %copy-start.3 = (f32[14,22,514]{2,1,0:T(8,128)S(1)}, f32[14,22,514]{2,1,0:T(8,128)}, u32[]{:S(2)}) copy-start(f32[14,22,514]{2,1,0:T(8,128)} %get-tuple-element.53) | copy-start | bytes 1899748
  62.2 6.2 %copy-start.4 = (f32[14,22,514]{2,1,0:T(8,128)S(1)}, f32[14,22,514]{2,1,0:T(8,128)}, u32[]{:S(2)}) copy-start(f32[14,22,514]{2,1,0:T(8,128)} %get-tuple-element.46) | copy-start | bytes 1899748
  62.2 6.2 %copy-start.11 = (f32[12,20,512]{2,1,0:T(8,128)S(1)}, f32[12,20,512]{2,1,0:T(8,128)}, u32[]{:S(2)}) copy-start(f32[12,20,512]{2,1,0:T(8,128)} %get-tuple-element.29) | copy-start | bytes 1474564
  62.2 6.2 %copy-start.12 = (f32[12,20,512]{2,1,0:T(8,128)S(1)}, f32[12,20,512]{2,1,0:T(8,128)}, u32[]{:S(2)}) copy-start(f32[12,20,512]{2,1,0:T(8,128)} %get-tuple-element.30) | copy-start | bytes 1474564
  68.4 1.9 %copy-start.15 = (f32[12,20,512]{2,1,0:T(8,128)S(1)}, f32[12,20,512]{2,1,0:T(8,128)}, u32[]{:S(2)}) copy-start(f32[12,20,512]{2,1,0:T(8,128)} %get-tuple-element.19) | copy-start | bytes 1474564
  70.3 1.4 %copy-start.25 = (f32[1,12,2,512]{3,2,1,0:T(2,128)S(1)}, f32[1,12,2,512]{3,2,1,0:T(2,128)}, u32[]{:S(2)}) copy-start(f32[1,12,2,512]{3,2,1,0:T(2,128)} %get-tuple-element.90) | copy-start | bytes 147460
  70.3 1.4 %copy-start.23 = (f32[14,4,512]{2,1,0:T(4,128)S(1)}, f32[14,4,512]{2,1,0:T(4,128)}, u32[]{:S(2)}) copy-start(f32[14,4,512]{2,1,0:T(4,128)} %get-tuple-element.89) | copy-start | bytes 344068
  70.3 1.4 %copy-start.24 = (f32[6,4,512]{2,1,0:T(4,128)S(1)}, f32[6,4,512]{2,1,0:T(4,128)}, u32[]{:S(2)}) copy-start(f32[6,4,512]{2,1,0:T(4,128)} %reshape_squeeze.6) | copy-start | bytes 147460
  71.6 16.1 %copy-start.2 = (f32[1,16,24,512]{3,2,1,0:T(8,128)S(1)}, f32[1,16,24,512]{3,2,1,0:T(8,128)}, u32[]{:S(2)}) copy-start(f32[1,16,24,512]{3,2,1,0:T(8,128)} %add_bitcast_fusion) | copy-start | bytes 2359300
  71.6 16.1 %copy-start.6 = (f32[1,16,24,512]{3,2,1,0:T(8,128)S(1)}, f32[1,16,24,512]{3,2,1,0:T(8,128)}, u32[]{:S(2)}) copy-start(f32[1,16,24,512]{3,2,1,0:T(8,128)} %copy-done.5) | copy-start | bytes 2359300
  71.9 9.6 %collective-permute-start.4 = (f32[36,4,512]{2,1,0:T(4,128)S(1)}, f32[36,4,512]{2,1,0:T(4,128)S(1)}, u32[]{:S(2)}, u32[]{:S(2)}) collective-permute-start(f32[36,4,512]{2,1,0:T(4,128)S(1)} %pad_maximum_fusion.3), channel_id=1, source_target_pairs={{0,1},{1,2},{2,3},{3,4},{4,5},{5,6},{6,7},{8,9},{9,10},{10,11},{11... | collective-permute-start | bytes 884744 | tf_op jit(solution)/shard_map/ppermute | solution.py:19
  74.0 11.0 %collective-permute-start.5 = (f32[36,4,512]{2,1,0:T(4,128)S(1)}, f32[36,4,512]{2,1,0:T(4,128)}, u32[]{:S(2)}, u32[]{:S(2)}) collective-permute-start(f32[36,4,512]{2,1,0:T(4,128)S(1)} %pad_maximum_fusion.2), channel_id=1, source_target_pairs={{1,0},{2,1},{3,2},{4,3},{5,4},{6,5},{7,6},{9,8},{10,9},{11,10},{12... | collective-permute-start | bytes 884744 | tf_op jit(solution)/shard_map/ppermute | solution.py:19
  88.6 10.9 %collective-permute-start.7 = (f32[9,16,512]{2,1,0:T(8,128)S(1)}, f32[9,16,512]{2,1,0:T(8,128)S(1)}, u32[]{:S(2)}, u32[]{:S(2)}) collective-permute-start(f32[9,16,512]{2,1,0:T(8,128)S(1)} %pad_maximum_fusion.4), channel_id=1, source_target_pairs={{8,0},{16,8},{24,16},{32,24},{40,32},{48,40},{56,48},{64,56},{72,6... | collective-permute-start | bytes 884744 | tf_op jit(solution)/shard_map/ppermute | solution.py:19
  95.1 13.6 %collective-permute-start.6 = (f32[9,16,512]{2,1,0:T(8,128)S(1)}, f32[9,16,512]{2,1,0:T(8,128)S(1)}, u32[]{:S(2)}, u32[]{:S(2)}) collective-permute-start(f32[9,16,512]{2,1,0:T(8,128)S(1)} %pad_maximum_fusion.5), channel_id=1, source_target_pairs={{0,8},{8,16},{16,24},{24,32},{32,40},{40,48},{48,56},{56,64},{64,7... | collective-permute-start | bytes 884744 | tf_op jit(solution)/shard_map/ppermute | solution.py:19
  108.7 1.1 %copy-start.14 = (f32[8,16,512]{2,1,0:T(8,128)S(1)}, f32[8,16,512]{2,1,0:T(8,128)}, u32[]{:S(2)}) copy-start(f32[8,16,512]{2,1,0:T(8,128)} %param.9) | copy-start | bytes 786436
  108.7 1.1 copy-start.17
  108.7 1.1 copy-start.19
  108.7 1.4 %copy-start.20 = (f32[10,18,514]{2,1,0:T(8,128)S(1)}, f32[10,18,514]{2,1,0:T(8,128)}, u32[]{:S(2)}) copy-start(f32[10,18,514]{2,1,0:T(8,128)} %get-tuple-element.15) | copy-start | bytes 1110244
  108.7 1.7 %copy-start.21 = (f32[10,18,514]{2,1,0:T(8,128)S(1)}, f32[10,18,514]{2,1,0:T(8,128)}, u32[]{:S(2)}) copy-start(f32[10,18,514]{2,1,0:T(8,128)} %get-tuple-element.67) | copy-start | bytes 1110244
  108.8 1.8 %copy-start.22 = (f32[10,18,514]{2,1,0:T(8,128)S(1)}, f32[10,18,514]{2,1,0:T(8,128)}, u32[]{:S(2)}) copy-start(f32[10,18,514]{2,1,0:T(8,128)} %get-tuple-element.68) | copy-start | bytes 1110244

commit v9 on v7

--- a/solution.py
+++ b/solution.py
@@ -179,13 +179,15 @@
     sq_y = grad_y * grad_y
     sq_x = grad_x * grad_x
     squared = sq_z + sq_y + sq_x + GRAD_FLOOR
-    quartic = (sq_z * sq_z + sq_y * sq_y + sq_x * sq_x) / (squared * squared)
+    inverse = 1.0 / squared
+    quartic_times_squared = (sq_z * sq_z + sq_y * sq_y + sq_x * sq_x) * inverse
+    quartic = quartic_times_squared * inverse
     anisotropy = 1.0 + ANISOTROPY * (4.0 * quartic - 3.0)
     aniso_sq = anisotropy * anisotropy
-    factor_a = 16.0 * ANISOTROPY * anisotropy / squared
-    flux_z = ENERGY_SCALE * (aniso_sq * grad_z + factor_a * grad_z * (sq_z - quartic * squared))
-    flux_y = ENERGY_SCALE * (aniso_sq * grad_y + factor_a * grad_y * (sq_y - quartic * squared))
-    flux_x = ENERGY_SCALE * (aniso_sq * grad_x + factor_a * grad_x * (sq_x - quartic * squared))
+    factor_a = 16.0 * ANISOTROPY * anisotropy * inverse
+    flux_z = ENERGY_SCALE * (aniso_sq * grad_z + factor_a * grad_z * (sq_z - quartic_times_squared))
+    flux_y = ENERGY_SCALE * (aniso_sq * grad_y + factor_a * grad_y * (sq_y - quartic_times_squared))
+    flux_x = ENERGY_SCALE * (aniso_sq * grad_x + factor_a * grad_x * (sq_x - quartic_times_squared))
     divergence = 0.5 * (flux_z[2:, 1:-1, 1:-1] - flux_z[:-2, 1:-1, 1:-1])
     divergence = divergence + 0.5 * (flux_y[1:-1, 2:, 1:-1] - flux_y[1:-1, :-2, 1:-1])
     divergence = divergence + 0.5 * (flux_x[1:-1, 1:-1, 2:] - flux_x[1:-1, 1:-1, :-2])

time: 98.3 us -> 101 us (1.027)
  other arithmetic: 26.1 us -> 28.6 us
    mul x3 -> x4, other arithmetic: 3.26 us -> 6.32 us  [the longest x2 3.94 us: advance_solver_step(): ENERGY_SCALE * (aniso_sq * grad_y + factor_a * grad_y * (sq_y - quartic_t...]
    neg x2 -> x1, other arithmetic: 6.28 us -> 3.83 us  [advance_solver_step(): grad_x = 0.5 * (padded[1:-1, 1:-1, 2:] - padded[1:-1, 1:-1, :-2])]
    neg x2, other arithmetic: 3.47 us -> 5.35 us  [advance_solver_step(): grad_z = 0.5 * (padded[2:, 1:-1, 1:-1] - padded[:-2, 1:-1, 1:-1])]
where the time goes in v9:
time: 101 us; the launch traced here: 100 us
  waiting for transfers between devices  34.9 us (35%)
  starting transfers between devices  31.9 us (32%)
  other arithmetic  28.6 us (28%)
  local copies, waits for them, and re-layouts  3.28 us (3%)
  between operations  1.29 us (1%)
    ppermute x8, waiting for transfers between devices, from_behind(): return lax.ppermute(block, axis, route)  34.9 us
    ppermute x8, starting transfers between devices, from_behind(): return lax.ppermute(block, axis, route)  31.9 us
    neg x2, other arithmetic, advance_solver_step(): grad_z = 0.5 * (padded[2:, 1:-1, 1:-1] - padded[:-2, 1:-1, 1:-1])  5.35 us
    mul x2, other arithmetic, advance_solver_step(): ENERGY_SCALE * (aniso_sq * grad_y + factor_a * grad_y * (sq_y - quartic_t...  3.94 us
    neg x1, other arithmetic, advance_solver_step(): grad_x = 0.5 * (padded[1:-1, 1:-1, 2:] - padded[1:-1, 1:-1, :-2])  3.83 us
    add_any x2, other arithmetic, advance_solver_step(): 1.0 - phase_now  2.62 us
    mul x2, other arithmetic, advance_solver_step(): ENERGY_SCALE * (aniso_sq * grad_z + factor_a * grad_z * (sq_z - quartic_t...  2.38 us
  transfers between devices with their start and end apart: 8, of which 8 were waited for; matrix products, arithmetic and copies ran while one was open for 1% of the time, Pallas kernels for 0%

profile of v9, /device:TPU:14, one launch (start us, length us, event | category | flops | bytes accessed | tf_op | source)
XLA Modules:
  0.0 100.0 jit_solution(3536574092192316056)
XLA Ops:
  0.7 1.1 %fusion.126 = (f32[4,16,512]{2,1,0:T(8,128)S(1)}, f32[4,16,512]{2,1,0:T(8,128)S(1)}) fusion(f32[8,16,512]{2,1,0:T(8,128)} %param.5), kind=kLoop, calls=%fused_computation.282 | loop fusion | bytes 524288 | tf_op jit(solution)/shard_map/slice | solution.py:41
  1.7 1.0 fusion.127
  2.7 7.9 %collective-permute-start.1 = (f32[8,16,512]{2,1,0:T(8,128)S(1)}, f32[8,16,512]{2,1,0:T(8,128)S(1)}, u32[]{:S(2)}, u32[]{:S(2)}) collective-permute-start(f32[8,16,512]{2,1,0:T(8,128)S(1)} %pad_maximum_fusion.8), channel_id=1, source_target_pairs={{8,0},{16,8},{24,16},{32,24},{40,32},{48,40},{56,48},{64,56},{72,6... | collective-permute-start | bytes 786440 | tf_op jit(solution)/shard_map/ppermute | solution.py:19
  10.7 1.9 %collective-permute-start = (f32[8,16,512]{2,1,0:T(8,128)S(1)}, f32[8,16,512]{2,1,0:T(8,128)S(1)}, u32[]{:S(2)}, u32[]{:S(2)}) collective-permute-start(f32[8,16,512]{2,1,0:T(8,128)S(1)} %pad_maximum_fusion.7), channel_id=1, source_target_pairs={{0,8},{8,16},{16,24},{24,32},{32,40},{40,48},{48,56},{56,64},{64,7... | collective-permute-start | bytes 786440 | tf_op jit(solution)/shard_map/ppermute | solution.py:19
  12.6 1.0 broadcast_multiply_fusion.3
  13.6 3.7 %collective-permute-done.1 = f32[8,16,512]{2,1,0:T(8,128)S(1)} collective-permute-done((f32[8,16,512]{2,1,0:T(8,128)S(1)}, f32[8,16,512]{2,1,0:T(8,128)S(1)}, u32[]{:S(2)}, u32[]{:S(2)}) %collective-permute-start.1) | collective-permute-done | bytes 262176 | tf_op jit(solution)/shard_map/ppermute | solution.py:19
  17.4 6.1 %collective-permute-done = f32[8,16,512]{2,1,0:T(8,128)S(1)} collective-permute-done((f32[8,16,512]{2,1,0:T(8,128)S(1)}, f32[8,16,512]{2,1,0:T(8,128)S(1)}, u32[]{:S(2)}, u32[]{:S(2)}) %collective-permute-start) | collective-permute-done | bytes 262176 | tf_op jit(solution)/shard_map/ppermute | solution.py:19
  23.8 0.1 maximum_maximum_fusion.1
  23.8 0.1 maximum_maximum_fusion.2
  23.9 3.6 %collective-permute-start.3 = (f32[28,4,512]{2,1,0:T(4,128)S(1)}, f32[28,4,512]{2,1,0:T(4,128)S(1)}, u32[]{:S(2)}, u32[]{:S(2)}) collective-permute-start(f32[28,4,512]{2,1,0:T(4,128)S(1)} %maximum_maximum_fusion.1), channel_id=1, source_target_pairs={{1,0},{2,1},{3,2},{4,3},{5,4},{6,5},{7,6},{9,8},{10,9},{11,10},{12... | collective-permute-start | bytes 688136 | tf_op jit(solution)/shard_map/ppermute | solution.py:19
  27.6 0.1 and_and_fusion
  27.7 2.2 %collective-permute-start.2 = (f32[28,4,512]{2,1,0:T(4,128)S(1)}, f32[28,4,512]{2,1,0:T(4,128)S(1)}, u32[]{:S(2)}, u32[]{:S(2)}) collective-permute-start(f32[28,4,512]{2,1,0:T(4,128)S(1)} %maximum_maximum_fusion.2), channel_id=1, source_target_pairs={{0,1},{1,2},{2,3},{3,4},{4,5},{5,6},{6,7},{8,9},{9,10},{10,11},{11... | collective-permute-start | bytes 688136 | tf_op jit(solution)/shard_map/ppermute | solution.py:19
  29.9 1.9 %collective-permute-done.3 = f32[28,4,512]{2,1,0:T(4,128)S(1)} collective-permute-done((f32[28,4,512]{2,1,0:T(4,128)S(1)}, f32[28,4,512]{2,1,0:T(4,128)S(1)}, u32[]{:S(2)}, u32[]{:S(2)}) %collective-permute-start.3) | collective-permute-done | bytes 229408 | tf_op jit(solution)/shard_map/ppermute | solution.py:19
  31.9 4.6 %collective-permute-done.2 = f32[28,4,512]{2,1,0:T(4,128)S(1)} collective-permute-done((f32[28,4,512]{2,1,0:T(4,128)S(1)}, f32[28,4,512]{2,1,0:T(4,128)S(1)}, u32[]{:S(2)}, u32[]{:S(2)}) %collective-permute-start.2) | collective-permute-done | bytes 229408 | tf_op jit(solution)/shard_map/ppermute | solution.py:19
  36.7 0.7 maximum_maximum_fusion
  37.3 0.2 slice_bitcast_fusion
  37.5 1.4 %add_multiply_fusion.5 = (f32[14,22,514]{2,1,0:T(8,128)S(1)}, f32[14,22,514]{2,1,0:T(8,128)S(1)}, f32[14,22,514]{2,1,0:T(8,128)S(1)}, f32[14,22,514]{2,1,0:T(8,128)S(1)}) fusion(f32[16,24,512]{2,1,0:T(8,128)S(1)} %get-tuple-element.55), kind=kLoop, calls=%fused_computation.63 | loop fusion | flops 5224296 | bytes 3319424 | tf_op jit(solution)/shard_map/mul | solution.py:188
  39.0 0.2 pad_slice_fusion.16
  39.2 0.9 add_multiply_fusion.4
  40.2 1.8 %broadcast_select_fusion = (f32[12,20,512]{2,1,0:T(8,128)S(1)}, f32[12,20,512]{2,1,0:T(8,128)S(1)}, f32[12,20,512]{2,1,0:T(8,128)S(1)}, f32[12,20,512]{2,1,0:T(8,128)S(1)}, f32[12,20,512]{2,1,0:T(8,128)S(1)}) fusion(pred[20]{0:T(512)(128)(4,1)S(1)} %get-tuple-element.107, pred[20]{0:T(512)(128)(4,1)S(1)} %get-tuple-element.108, ...), kind=kLoop, calls=%fused_computation.176 | loop fusion | flops 3072000 | bytes 9338932 | tf_op jit(solution)/shard_map/jit(_where)/select_n | solution.py:259
  42.0 1.0 %add_multiply_fusion.8 = (f32[10,18,514]{2,1,0:T(8,128)S(1)}, f32[10,18,514]{2,1,0:T(8,128)S(1)}, f32[10,18,514]{2,1,0:T(8,128)S(1)}, f32[10,18,514]{2,1,0:T(8,128)S(1)}) fusion(f32[12,20,512]{2,1,0:T(8,128)S(1)} %get-tuple-element.38), kind=kLoop, calls=%fused_computation.110 | loop fusion | flops 3053160 | bytes 1971840 | tf_op jit(solution)/shard_map/jvp()/mul | solution.py:188
  43.0 0.6 fusion.95
  43.6 0.5 fusion.74
  44.1 2.0 %fusion.119 = (f32[10,18,514]{2,1,0:T(8,128)S(1)}, f32[10,18,514]{2,1,0:T(8,128)S(1)}) fusion(f32[10,18,514]{2,1,0:T(8,128)S(1)} %get-tuple-element.18, f32[10,18,514]{2,1,0:T(8,128)S(1)} %get-tuple-element.17, f32[10,18,514]{2,1,0:T(8,128)S(1)} %get-tuple-element.16, f32[8,16,512]{2,1,0:T(8,128)S(1)} %get-tuple-element.89, ...), kind=kLoop, calls=%fused_computation.280 | loop fusion | flops 7771680 | bytes 2374688 | tf_op jit(solution)/shard_map/transpose(jvp())/neg | solution.py:175
  46.1 3.0 %add_multiply_fusion.7 = (f32[10,18,514]{2,1,0:T(8,128)S(1)}, f32[10,18,514]{2,1,0:T(8,128)S(1)}, f32[10,18,514]{2,1,0:T(8,128)S(1)}, f32[10,18,514]{2,1,0:T(8,1...) fusion(f32[10,18,514]{2,1,0:T(8,128)S(1)} %get-tuple-element.17, ...), kind=kLoop, calls=%fused_computation.109 | loop fusion | flops 9622080 | bytes 3855008 | tf_op jit(solution)/shard_map/jvp()/mul | solution.py:189
  49.1 0.2 broadcast_multiply_fusion
  49.3 2.1 %fusion.50 = (f32[12,20,512]{2,1,0:T(8,128)S(1)}, f32[12,20,512]{2,1,0:T(8,128)S(1)}) fusion(f32[16,24,512]{2,1,0:T(8,128)S(1)} %get-tuple-element.54, f32[16,24,512]{2,1,0:T(8,128)S(1)} %get-tuple-element.53, f32[16,24,512]{2,1,0:T(8,128)S(1)} %get-tuple-element.55, f32[8,16,512]{2,1,0:T(8,128)S(1)} %get-tuple-element.29, ...), kind=kLoop, calls=%fused_computation.123 | loop fusion | flops 4300800 | bytes 5464564 | tf_op jit(solution)/shard_map/transpose(jvp())/add_any | solution.py:198
  51.5 1.0 fusion.113
  52.5 3.4 %fusion.111 = (f32[14,22,514]{2,1,0:T(8,128)S(1)}, f32[14,22,514]{2,1,0:T(8,128)S(1)}) fusion(f32[14,22,514]{2,1,0:T(8,128)S(1)} %get-tuple-element.42, f32[14,22,514]{2,1,0:T(8,128)S(1)} %get-tuple-element.43, f32[14,22,514]{2,1,0:T(8,128)S(1)} %get-tuple-element.44, f32[12,20,512]{2,1,0:T(8,128)S(1)} %get-tuple-element.28, ...), kind=kLoop, calls=%fused_computation.276 | loop fusion | flops 13298208 | bytes 4149280 | tf_op jit(solution)/shard_map/transpose(jvp())/neg | solution.py:175
  55.9 3.8 %fusion.107 = (f32[14,22,514]{2,1,0:T(8,128)S(1)}, f32[14,22,514]{2,1,0:T(8,128)S(1)}, f32[14,22,514]{2,1,0:T(8,128)S(1)}, f32[14,22,514]{2,1,0:T(8,128)S(1)}) fusion(f32[14,22,514]{2,1,0:T(8,128)S(1)} %get-tuple-element.44, f32[14,22,514]{2,1,0:T(8,128)S(1)} %get-tuple-element.42, f32[14,22,514]{2,1,0:T(8,128)S(1)} %get-tuple-element.43, ...), kind=kLoop, calls=%fused_computation.274 | loop fusion | flops 15197952 | bytes 5415776 | tf_op jit(solution)/shard_map/transpose(jvp())/neg | solution.py:177
  59.7 0.1 pad_bitcast_fusion
  59.8 0.2 add_bitcast_fusion
  60.1 1.3 %fusion.30 = f32[1,16,24,512]{3,2,1,0:T(8,128)S(1)} fusion(f32[14,22,514]{2,1,0:T(8,128)S(1)} %get-tuple-element.26, f32[14,22,514]{2,1,0:T(8,128)S(1)} %get-tuple-element.25, f32[14,22,514]{2,1,0:T(8,128)S(1)} %get-tuple-element.46, f32[14,22,514]{2,1,0:T(8,128)S(1)} %get-tuple-element.45, f32[14,22,514]{2,1,0:T(8,128)S(1)} %get-tuple-element.22, ...), kind=kLoop, calls=%fused_computation.80 | loop fusion | flops 1179648 | bytes 5077440 | tf_op jit(solution)/shard_map/stack | solution.py:280
  61.5 0.1 pad_maximum_fusion.2
  61.6 0.1 pad_maximum_fusion.3
  61.6 1.9 %collective-permute-start.4 = (f32[42,4,512]{2,1,0:T(4,128)S(1)}, f32[42,4,512]{2,1,0:T(4,128)S(1)}, u32[]{:S(2)}, u32[]{:S(2)}) collective-permute-start(f32[42,4,512]{2,1,0:T(4,128)S(1)} %pad_maximum_fusion.3), channel_id=1, source_target_pairs={{0,1},{1,2},{2,3},{3,4},{4,5},{5,6},{6,7},{8,9},{9,10},{10,11},{11... | collective-permute-start | bytes 1032200 | tf_op jit(solution)/shard_map/ppermute | solution.py:19
  63.6 4.8 %collective-permute-start.5 = (f32[42,4,512]{2,1,0:T(4,128)S(1)}, f32[42,4,512]{2,1,0:T(4,128)S(1)}, u32[]{:S(2)}, u32[]{:S(2)}) collective-permute-start(f32[42,4,512]{2,1,0:T(4,128)S(1)} %pad_maximum_fusion.2), channel_id=1, source_target_pairs={{1,0},{2,1},{3,2},{4,3},{5,4},{6,5},{7,6},{9,8},{10,9},{11,10},{12... | collective-permute-start | bytes 1032200 | tf_op jit(solution)/shard_map/ppermute | solution.py:19
  68.4 3.3 %collective-permute-done.4 = f32[42,4,512]{2,1,0:T(4,128)S(1)} collective-permute-done((f32[42,4,512]{2,1,0:T(4,128)S(1)}, f32[42,4,512]{2,1,0:T(4,128)S(1)}, u32[]{:S(2)}, u32[]{:S(2)}) %collective-permute-start.4) | collective-permute-done | bytes 344096 | tf_op jit(solution)/shard_map/ppermute | solution.py:19
  71.8 3.7 %collective-permute-done.5 = f32[42,4,512]{2,1,0:T(4,128)S(1)} collective-permute-done((f32[42,4,512]{2,1,0:T(4,128)S(1)}, f32[42,4,512]{2,1,0:T(4,128)S(1)}, u32[]{:S(2)}, u32[]{:S(2)}) %collective-permute-start.5) | collective-permute-done | bytes 344096 | tf_op jit(solution)/shard_map/ppermute | solution.py:19
  75.6 0.3 maximum_add_fusion
  75.9 0.4 fusion.1
  76.4 7.6 %collective-permute-start.7 = (f32[9,16,512]{2,1,0:T(8,128)S(1)}, f32[9,16,512]{2,1,0:T(8,128)S(1)}, u32[]{:S(2)}, u32[]{:S(2)}) collective-permute-start(f32[9,16,512]{2,1,0:T(8,128)S(1)} %pad_maximum_fusion.4), channel_id=1, source_target_pairs={{8,0},{16,8},{24,16},{32,24},{40,32},{48,40},{56,48},{64,56},{72,6... | collective-permute-start | bytes 884744 | tf_op jit(solution)/shard_map/ppermute | solution.py:19
  84.0 1.9 %collective-permute-start.6 = (f32[9,16,512]{2,1,0:T(8,128)S(1)}, f32[9,16,512]{2,1,0:T(8,128)S(1)}, u32[]{:S(2)}, u32[]{:S(2)}) collective-permute-start(f32[9,16,512]{2,1,0:T(8,128)S(1)} %pad_maximum_fusion.5), channel_id=1, source_target_pairs={{0,8},{8,16},{16,24},{24,32},{32,40},{40,48},{48,56},{56,64},{64,7... | collective-permute-start | bytes 884744 | tf_op jit(solution)/shard_map/ppermute | solution.py:19
  85.9 2.4 %collective-permute-done.7 = f32[9,16,512]{2,1,0:T(8,128)S(1)} collective-permute-done((f32[9,16,512]{2,1,0:T(8,128)S(1)}, f32[9,16,512]{2,1,0:T(8,128)S(1)}, u32[]{:S(2)}, u32[]{:S(2)}) %collective-permute-start.7) | collective-permute-done | bytes 294944 | tf_op jit(solution)/shard_map/ppermute | solution.py:19
  88.4 9.2 %collective-permute-done.6 = f32[9,16,512]{2,1,0:T(8,128)S(1)} collective-permute-done((f32[9,16,512]{2,1,0:T(8,128)S(1)}, f32[9,16,512]{2,1,0:T(8,128)S(1)}, u32[]{:S(2)}, u32[]{:S(2)}) %collective-permute-start.6) | collective-permute-done | bytes 294944 | tf_op jit(solution)/shard_map/ppermute | solution.py:19
  97.7 0.2 slice_add_fusion.3
  97.8 0.8 fusion.76
  98.7 1.4 %fusion.80 = f32[8,16,512]{2,1,0:T(8,128)} fusion(f32[3,4,16,512]{3,2,1,0:T(8,128)S(1)} %get-tuple-element.62, f32[3,4,16,512]{3,2,1,0:T(8,128)S(1)} %get-tuple-element.63, f32[10,18,514]{2,1,0:T(8,128)S(1)} %get-tuple-element.57, f32[10,18,514]{2,1,0:T(8,128)S(1)} %get-tuple-element.56, f32[10,18,514]{2,1,0:T(8,128)S(1)} %get-tuple-element.15, ...), kind=kLoop, calls=%fused_computation.187 | loop fusion | flops 1245184 | bytes 3670016 | tf_op jit(solution)/shard_map/add | solution.py:283
  (62 shorter events, 1.0 us)
Async XLA Ops:
  0.6 22.9 %copy-start = (f32[8,16,512]{2,1,0:T(8,128)S(1)}, f32[8,16,512]{2,1,0:T(8,128)}, u32[]{:S(2)}) copy-start(f32[8,16,512]{2,1,0:T(8,128)} %param.5) | copy-start | bytes 786436
  0.6 22.9 %copy-start.1 = (f32[8,16,512]{2,1,0:T(8,128)S(1)}, f32[8,16,512]{2,1,0:T(8,128)}, u32[]{:S(2)}) copy-start(f32[8,16,512]{2,1,0:T(8,128)} %param.6) | copy-start | bytes 786436
  0.7 22.9 %copy-start.2 = (f32[8,16,512]{2,1,0:T(8,128)S(1)}, f32[8,16,512]{2,1,0:T(8,128)}, u32[]{:S(2)}) copy-start(f32[8,16,512]{2,1,0:T(8,128)} %param.7) | copy-start | bytes 786436
  2.7 14.6 %collective-permute-start.1 = (f32[8,16,512]{2,1,0:T(8,128)S(1)}, f32[8,16,512]{2,1,0:T(8,128)S(1)}, u32[]{:S(2)}, u32[]{:S(2)}) collective-permute-start(f32[8,16,512]{2,1,0:T(8,128)S(1)} %pad_maximum_fusion.8), channel_id=1, source_target_pairs={{8,0},{16,8},{24,16},{32,24},{40,32},{48,40},{56,48},{64,56},{72,6... | collective-permute-start | bytes 786440 | tf_op jit(solution)/shard_map/ppermute | solution.py:19
  10.7 12.8 %collective-permute-start = (f32[8,16,512]{2,1,0:T(8,128)S(1)}, f32[8,16,512]{2,1,0:T(8,128)S(1)}, u32[]{:S(2)}, u32[]{:S(2)}) collective-permute-start(f32[8,16,512]{2,1,0:T(8,128)S(1)} %pad_maximum_fusion.7), channel_id=1, source_target_pairs={{0,8},{8,16},{16,24},{24,32},{32,40},{40,48},{48,56},{56,64},{64,7... | collective-permute-start | bytes 786440 | tf_op jit(solution)/shard_map/ppermute | solution.py:19
  23.9 7.9 %collective-permute-start.3 = (f32[28,4,512]{2,1,0:T(4,128)S(1)}, f32[28,4,512]{2,1,0:T(4,128)S(1)}, u32[]{:S(2)}, u32[]{:S(2)}) collective-permute-start(f32[28,4,512]{2,1,0:T(4,128)S(1)} %maximum_maximum_fusion.1), channel_id=1, source_target_pairs={{1,0},{2,1},{3,2},{4,3},{5,4},{6,5},{7,6},{9,8},{10,9},{11,10},{12... | collective-permute-start | bytes 688136 | tf_op jit(solution)/shard_map/ppermute | solution.py:19
  27.7 8.8 %collective-permute-start.2 = (f32[28,4,512]{2,1,0:T(4,128)S(1)}, f32[28,4,512]{2,1,0:T(4,128)S(1)}, u32[]{:S(2)}, u32[]{:S(2)}) collective-permute-start(f32[28,4,512]{2,1,0:T(4,128)S(1)} %maximum_maximum_fusion.2), channel_id=1, source_target_pairs={{0,1},{1,2},{2,3},{3,4},{4,5},{5,6},{6,7},{8,9},{9,10},{10,11},{11... | collective-permute-start | bytes 688136 | tf_op jit(solution)/shard_map/ppermute | solution.py:19
  42.0 1.0 %copy-start.3 = (f32[8,16,512]{2,1,0:T(8,128)S(1)}, f32[8,16,512]{2,1,0:T(8,128)}, u32[]{:S(2)}) copy-start(f32[8,16,512]{2,1,0:T(8,128)} %param.9) | copy-start | bytes 786436
  42.0 1.0 %copy-start.4 = (f32[8,16,512]{2,1,0:T(8,128)S(1)}, f32[8,16,512]{2,1,0:T(8,128)}, u32[]{:S(2)}) copy-start(f32[8,16,512]{2,1,0:T(8,128)} %param.8) | copy-start | bytes 786436
  61.6 10.0 %collective-permute-start.4 = (f32[42,4,512]{2,1,0:T(4,128)S(1)}, f32[42,4,512]{2,1,0:T(4,128)S(1)}, u32[]{:S(2)}, u32[]{:S(2)}) collective-permute-start(f32[42,4,512]{2,1,0:T(4,128)S(1)} %pad_maximum_fusion.3), channel_id=1, source_target_pairs={{0,1},{1,2},{2,3},{3,4},{4,5},{5,6},{6,7},{8,9},{9,10},{10,11},{11... | collective-permute-start | bytes 1032200 | tf_op jit(solution)/shard_map/ppermute | solution.py:19
  63.6 11.9 %collective-permute-start.5 = (f32[42,4,512]{2,1,0:T(4,128)S(1)}, f32[42,4,512]{2,1,0:T(4,128)S(1)}, u32[]{:S(2)}, u32[]{:S(2)}) collective-permute-start(f32[42,4,512]{2,1,0:T(4,128)S(1)} %pad_maximum_fusion.2), channel_id=1, source_target_pairs={{1,0},{2,1},{3,2},{4,3},{5,4},{6,5},{7,6},{9,8},{10,9},{11,10},{12... | collective-permute-start | bytes 1032200 | tf_op jit(solution)/shard_map/ppermute | solution.py:19
  76.4 11.9 %collective-permute-start.7 = (f32[9,16,512]{2,1,0:T(8,128)S(1)}, f32[9,16,512]{2,1,0:T(8,128)S(1)}, u32[]{:S(2)}, u32[]{:S(2)}) collective-permute-start(f32[9,16,512]{2,1,0:T(8,128)S(1)} %pad_maximum_fusion.4), channel_id=1, source_target_pairs={{8,0},{16,8},{24,16},{32,24},{40,32},{48,40},{56,48},{64,56},{72,6... | collective-permute-start | bytes 884744 | tf_op jit(solution)/shard_map/ppermute | solution.py:19
  84.0 13.6 %collective-permute-start.6 = (f32[9,16,512]{2,1,0:T(8,128)S(1)}, f32[9,16,512]{2,1,0:T(8,128)S(1)}, u32[]{:S(2)}, u32[]{:S(2)}) collective-permute-start(f32[9,16,512]{2,1,0:T(8,128)S(1)} %pad_maximum_fusion.5), channel_id=1, source_target_pairs={{0,8},{8,16},{16,24},{24,32},{32,40},{40,48},{48,56},{56,64},{64,7... | collective-permute-start | bytes 884744 | tf_op jit(solution)/shard_map/ppermute | solution.py:19

commit v10 on v8

--- a/solution.py
+++ b/solution.py
@@ -134,14 +134,15 @@
 def packed_y_fold(contributions):
     depth, rows = contributions.shape[1], contributions.shape[2]
 
-    lanes = contributions.shape[3]
+    half = (depth - 4) // 2
 
     def rims(lo, hi, narrow):
+        third = contributions[2, 2 : depth - 2, narrow]
         return jnp.concatenate(
             (
                 contributions[0, :, lo:hi],
                 contributions[1, 1 : depth - 1, lo:hi],
-                contributions[2, 2 : depth - 2, narrow].reshape(-1, 4, lanes),
+                jnp.concatenate((third[:half], third[half:]), axis=1),
             ),
             axis=0,
         )
@@ -153,12 +154,13 @@
     from_below = from_behind(upper, "gy", 1)
 
     def unpack(arrived, outer):
-        narrow = arrived[2 * depth - 2 :].reshape(depth - 4, 2, lanes)
+        third = arrived[2 * depth - 2 :]
+        third = jnp.concatenate((third[:, :2], third[:, 2:]), axis=0)
         return jnp.stack(
             (
                 arrived[:depth],
                 jnp.pad(arrived[depth : 2 * depth - 2], ((1, 1), (0, 0), (0, 0))),
-                jnp.pad(narrow, ((2, 2), outer, (0, 0))),
+                jnp.pad(third, ((2, 2), outer, (0, 0))),
             )
         )
 
@@ -257,8 +259,6 @@
         phase_wide, temp_wide, rate_wide[2:-2, 2:-2]
     )
     valid = inside_grid(succeeding_order_parameter, 2)
-    succeeding_order_parameter = jnp.where(valid, succeeding_order_parameter, 0.0)
-    succeeding_heat_level = jnp.where(valid, succeeding_heat_level, 0.0)
     discarded_result, sensitivity_latest = jax.vjp(
         advance_solver_step,
         succeeding_order_parameter,

time: 114 us -> 97.5 us (0.86)
  other arithmetic: 36.7 us -> 25.1 us
  local copies, waits for them, and re-layouts: 9.85 us -> 3.37 us
  waiting for transfers between devices: 33.9 us -> 37.2 us
    ppermute x8, waiting for transfers between devices: 33.9 us -> 37.2 us  [from_behind(): return lax.ppermute(block, axis, route)]
    neg x2, other arithmetic: 9.36 us -> 6.28 us  [advance_solver_step(): grad_x = 0.5 * (padded[1:-1, 1:-1, 2:] - padded[1:-1, 1:-1, :-2])]
    select_n x1 -> x0, other arithmetic: 1.81 us -> none  [body(): jnp.where(valid, succeeding_order_parameter, 0.0)]
    mul x2, other arithmetic: 4.28 us -> 2.47 us  [advance_solver_step(): ENERGY_SCALE * (aniso_sq * grad_z + factor_a * grad_z * (sq_z - quartic *...]
    add x0 -> x1, other arithmetic: none -> 1.78 us  [advance_solver_step(): new_phase = phase_now + TIME_STEP * growth]
    squeeze x1, local copies, waits for them, and re-layouts: 1.74 us -> 0.05 us  [rims(): contributions[1, 1:depth - 1, lo:hi]]
    slice x5 -> x4, local copies, waits for them, and re-layouts: 1.77 us -> 0.46 us  [the longest x1 0.37 us: advance_solver_step(): temp_x[:, :, 2:]]
    mul x1, other arithmetic: 1.99 us -> 0.79 us  [advance_solver_step(): ENERGY_SCALE * (aniso_sq * grad_y + factor_a * grad_y * (sq_y - quartic *...]
  transfers between devices with their start and end apart: 8 -> 8, of which waited for: 8 -> 8; matrix products, arithmetic and copies ran while one was open for 1% -> 0% of each run, Pallas kernels for 0% -> 0%
where the time goes in v10:
time: 97.5 us; the launch traced here: 97.1 us
  waiting for transfers between devices  37.2 us (38%)
  starting transfers between devices  30.2 us (31%)
  other arithmetic  25.1 us (26%)
  local copies, waits for them, and re-layouts  3.37 us (3%)
  between operations  1.27 us (1%)
    ppermute x8, waiting for transfers between devices, from_behind(): return lax.ppermute(block, axis, route)  37.2 us
    ppermute x8, starting transfers between devices, from_behind(): return lax.ppermute(block, axis, route)  30.2 us
    neg x2, other arithmetic, advance_solver_step(): grad_x = 0.5 * (padded[1:-1, 1:-1, 2:] - padded[1:-1, 1:-1, :-2])  6.28 us
    neg x2, other arithmetic, advance_solver_step(): grad_y = 0.5 * (padded[1:-1, 2:, 1:-1] - padded[1:-1, :-2, 1:-1])  3.45 us
    add_any x2, other arithmetic, advance_solver_step(): 1.0 - phase_now  2.62 us
    mul x2, other arithmetic, advance_solver_step(): ENERGY_SCALE * (aniso_sq * grad_z + factor_a * grad_z * (sq_z - quartic *...  2.47 us
    slice x2, local copies, waits for them, and re-layouts, packed_z_halo(): tails = jnp.concatenate([f[size - w:] for f, w in zip(fields, widths)], 0)  2.01 us
  transfers between devices with their start and end apart: 8, of which 8 were waited for; matrix products, arithmetic and copies ran while one was open for 0% of the time, Pallas kernels for 0%

profile of v10, /device:TPU:14, one launch (start us, length us, event | category | flops | bytes accessed | tf_op | source)
XLA Modules:
  0.0 97.1 jit_solution(6763105904529953914)
XLA Ops:
  0.7 1.1 %fusion.114 = (f32[4,16,512]{2,1,0:T(8,128)S(1)}, f32[4,16,512]{2,1,0:T(8,128)S(1)}) fusion(f32[8,16,512]{2,1,0:T(8,128)} %param.5), kind=kLoop, calls=%fused_computation.288 | loop fusion | bytes 524288 | tf_op jit(solution)/shard_map/slice | solution.py:41
  1.7 1.0 fusion.115
  2.7 1.9 %collective-permute-start = (f32[8,16,512]{2,1,0:T(8,128)S(1)}, f32[8,16,512]{2,1,0:T(8,128)S(1)}, u32[]{:S(2)}, u32[]{:S(2)}) collective-permute-start(f32[8,16,512]{2,1,0:T(8,128)S(1)} %pad_maximum_fusion.5), channel_id=1, source_target_pairs={{0,8},{8,16},{16,24},{24,32},{32,40},{40,48},{48,56},{56,64},{64,7... | collective-permute-start | bytes 786440 | tf_op jit(solution)/shard_map/ppermute | solution.py:19
  4.7 7.9 %collective-permute-start.1 = (f32[8,16,512]{2,1,0:T(8,128)S(1)}, f32[8,16,512]{2,1,0:T(8,128)S(1)}, u32[]{:S(2)}, u32[]{:S(2)}) collective-permute-start(f32[8,16,512]{2,1,0:T(8,128)S(1)} %pad_maximum_fusion.6), channel_id=1, source_target_pairs={{8,0},{16,8},{24,16},{32,24},{40,32},{48,40},{56,48},{64,56},{72,6... | collective-permute-start | bytes 786440 | tf_op jit(solution)/shard_map/ppermute | solution.py:19
  12.6 2.6 %collective-permute-done = f32[8,16,512]{2,1,0:T(8,128)S(1)} collective-permute-done((f32[8,16,512]{2,1,0:T(8,128)S(1)}, f32[8,16,512]{2,1,0:T(8,128)S(1)}, u32[]{:S(2)}, u32[]{:S(2)}) %collective-permute-start) | collective-permute-done | bytes 262176 | tf_op jit(solution)/shard_map/ppermute | solution.py:19
  15.3 4.0 %collective-permute-done.1 = f32[8,16,512]{2,1,0:T(8,128)S(1)} collective-permute-done((f32[8,16,512]{2,1,0:T(8,128)S(1)}, f32[8,16,512]{2,1,0:T(8,128)S(1)}, u32[]{:S(2)}, u32[]{:S(2)}) %collective-permute-start.1) | collective-permute-done | bytes 262176 | tf_op jit(solution)/shard_map/ppermute | solution.py:19
  19.4 0.1 maximum_bitcast_fusion
  19.6 0.1 maximum_maximum_fusion.4
  19.6 0.1 maximum_maximum_fusion.3
  19.7 1.9 %collective-permute-start.2 = (f32[28,4,512]{2,1,0:T(4,128)S(1)}, f32[28,4,512]{2,1,0:T(4,128)S(1)}, u32[]{:S(2)}, u32[]{:S(2)}) collective-permute-start(f32[28,4,512]{2,1,0:T(4,128)S(1)} %maximum_maximum_fusion.4), channel_id=1, source_target_pairs={{0,1},{1,2},{2,3},{3,4},{4,5},{5,6},{6,7},{8,9},{9,10},{10,11},{11... | collective-permute-start | bytes 688136 | tf_op jit(solution)/shard_map/ppermute | solution.py:19
  21.7 4.8 %collective-permute-start.3 = (f32[28,4,512]{2,1,0:T(4,128)S(1)}, f32[28,4,512]{2,1,0:T(4,128)S(1)}, u32[]{:S(2)}, u32[]{:S(2)}) collective-permute-start(f32[28,4,512]{2,1,0:T(4,128)S(1)} %maximum_maximum_fusion.3), channel_id=1, source_target_pairs={{1,0},{2,1},{3,2},{4,3},{5,4},{6,5},{7,6},{9,8},{10,9},{11,10},{12... | collective-permute-start | bytes 688136 | tf_op jit(solution)/shard_map/ppermute | solution.py:19
  26.5 4.5 %collective-permute-done.2 = f32[28,4,512]{2,1,0:T(4,128)S(1)} collective-permute-done((f32[28,4,512]{2,1,0:T(4,128)S(1)}, f32[28,4,512]{2,1,0:T(4,128)S(1)}, u32[]{:S(2)}, u32[]{:S(2)}) %collective-permute-start.2) | collective-permute-done | bytes 229408 | tf_op jit(solution)/shard_map/ppermute | solution.py:19
  31.1 4.2 %collective-permute-done.3 = f32[28,4,512]{2,1,0:T(4,128)S(1)} collective-permute-done((f32[28,4,512]{2,1,0:T(4,128)S(1)}, f32[28,4,512]{2,1,0:T(4,128)S(1)}, u32[]{:S(2)}, u32[]{:S(2)}) %collective-permute-start.3) | collective-permute-done | bytes 229408 | tf_op jit(solution)/shard_map/ppermute | solution.py:19
  35.5 0.7 maximum_maximum_fusion
  36.1 0.2 slice_bitcast_fusion
  36.3 1.4 %add_multiply_fusion.5 = (f32[14,22,514]{2,1,0:T(8,128)S(1)}, f32[14,22,514]{2,1,0:T(8,128)S(1)}, f32[14,22,514]{2,1,0:T(8,128)S(1)}, f32[14,22,514]{2,1,0:T(8,1...) fusion(f32[16,24,512]{2,1,0:T(8,128)S(1)} %get-tuple-element.65), kind=kLoop, calls=%fused_computation.67 | loop fusion | flops 5224296 | bytes 5219168 | tf_op jit(solution)/shard_map/mul | solution.py:191
  37.8 0.8 add_multiply_fusion.4
  38.5 1.8 %multiply_add_fusion.8 = (f32[12,20,512]{2,1,0:T(8,128)S(1)}, f32[12,20,512]{2,1,0:T(8,128)S(1)}, f32[12,20,512]{2,1,0:T(8,128)S(1)}, f32[12,20,512]{2,1,0:T(8,128)S(1)}, f32[12,20,512]{2,1,0:T(8,128)S(1)}) fusion(f32[16,24,512]{2,1,0:T(8,128)S(1)} %get-tuple-element.64, f32[16,24,512]{2,1,0:T(8,128)S(1)} %get-tuple-element.65, ...), kind=kLoop, calls=%fused_computation.148 | loop fusion | flops 2580480 | bytes 8847360 | tf_op jit(solution)/shard_map/add | solution.py:203
  40.3 0.4 pad_slice_fusion.17
  40.7 1.1 %add_multiply_fusion.8 = (f32[10,18,514]{2,1,0:T(8,128)S(1)}, f32[10,18,514]{2,1,0:T(8,128)S(1)}, f32[10,18,514]{2,1,0:T(8,128)S(1)}, f32[10,18,514]{2,1,0:T(8,128)S(1)}) fusion(f32[12,20,512]{2,1,0:T(8,128)S(1)} %get-tuple-element.42), kind=kLoop, calls=%fused_computation.114 | loop fusion | flops 3053160 | bytes 1971840 | tf_op jit(solution)/shard_map/jvp()/mul | solution.py:191
  41.8 0.6 fusion.77
  42.4 0.5 fusion.57
  42.8 2.8 %fusion.100 = (f32[10,18,514]{2,1,0:T(8,128)S(1)}, f32[10,18,514]{2,1,0:T(8,128)S(1)}, f32[10,18,514]{2,1,0:T(8,128)S(1)}, f32[10,18,514]{2,1,0:T(8,128)S(1)}, f32[10,18,514]{2,1,0:T(8,128)S(1)}) fusion(f32[10,18,514]{2,1,0:T(8,128)S(1)} %get-tuple-element.16, f32[8,16,512]{2,1,0:T(8,128)S(1)} %get-tuple-element.104, ...), kind=kLoop, calls=%fused_computation.282 | loop fusion | flops 8604360 | bytes 3484928 | tf_op jit(solution)/shard_map/transpose(jvp())/neg | solution.py:182
  45.6 1.5 %fusion.102 = (f32[10,18,514]{2,1,0:T(8,128)S(1)}, f32[10,18,514]{2,1,0:T(8,128)S(1)}, f32[10,18,514]{2,1,0:T(8,128)S(1)}, f32[10,18,514]{2,1,0:T(8,128)S(1)}, f32[10,18,514]{2,1,0:T(8,128)S(1)}) fusion(f32[10,18,514]{2,1,0:T(8,128)S(1)} %get-tuple-element.17, f32[10,18,514]{2,1,0:T(8,128)S(1)} %get-tuple-element.37, ...), kind=kLoop, calls=%fused_computation.283 | loop fusion | flops 5643720 | bytes 4225088 | tf_op jit(solution)/shard_map/transpose(jvp())/neg | solution.py:181
  47.1 0.2 broadcast_multiply_fusion
  47.4 2.1 %fusion.42 = (f32[12,20,512]{2,1,0:T(8,128)S(1)}, f32[12,20,512]{2,1,0:T(8,128)S(1)}) fusion(f32[16,24,512]{2,1,0:T(8,128)S(1)} %get-tuple-element.64, f32[16,24,512]{2,1,0:T(8,128)S(1)} %get-tuple-element.63, f32[16,24,512]{2,1,0:T(8,128)S(1)} %get-tuple-element.65, f32[8,16,512]{2,1,0:T(8,128)S(1)} %get-tuple-element.31, ...), kind=kLoop, calls=%fused_computation.125 | loop fusion | flops 4300800 | bytes 5464564 | tf_op jit(solution)/shard_map/transpose(jvp())/add_any | solution.py:201
  49.5 1.0 %fusion.98 = (f32[12,20,512]{2,1,0:T(8,128)S(1)}, f32[12,20,512]{2,1,0:T(8,128)S(1)}, f32[12,20,512]{2,1,0:T(8,128)S(1)}, f32[12,20,512]{2,1,0:T(8,128)S(1)}) fusion(f32[12,20,512]{2,1,0:T(8,128)S(1)} %get-tuple-element.20, f32[16,24,512]{2,1,0:T(8,128)S(1)} %get-tuple-element.64, f32[16,24,512]{2,1,0:T(8,128)S(1)} %get-tuple-element.63, ...), kind=kLoop, calls=%fused_computation.281 | loop fusion | flops 3563520 | bytes 5439540 | tf_op jit(solution)/shard_map/transpose(jvp())/neg | solution.py:196
  50.5 3.5 %fusion.92 = (f32[14,22,514]{2,1,0:T(8,128)S(1)}, f32[14,22,514]{2,1,0:T(8,128)S(1)}, f32[14,22,514]{2,1,0:T(8,128)S(1)}, f32[14,22,514]{2,1,0:T(8,128)S(1)}) fusion(f32[14,22,514]{2,1,0:T(8,128)S(1)} %get-tuple-element.50, f32[14,22,514]{2,1,0:T(8,128)S(1)} %get-tuple-element.58, f32[14,22,514]{2,1,0:T(8,128)S(1)} %get-tuple-element.46, ...), kind=kLoop, calls=%fused_computation.278 | loop fusion | flops 13298208 | bytes 8582016 | tf_op jit(solution)/shard_map/transpose(jvp())/neg | solution.py:182
  54.1 1.9 %fusion.94 = (f32[14,22,514]{2,1,0:T(8,128)S(1)}, f32[14,22,514]{2,1,0:T(8,128)S(1)}, f32[14,22,514]{2,1,0:T(8,128)S(1)}, f32[14,22,514]{2,1,0:T(8,128)S(1)}) fusion(f32[14,22,514]{2,1,0:T(8,128)S(1)} %get-tuple-element.49, f32[14,22,514]{2,1,0:T(8,128)S(1)} %get-tuple-element.24, f32[14,22,514]{2,1,0:T(8,128)S(1)} %get-tuple-element.23, ...), kind=kLoop, calls=%fused_computation.279 | loop fusion | flops 7598976 | bytes 9215264 | tf_op jit(solution)/shard_map/transpose(jvp())/neg | solution.py:181
  56.0 1.2 %fusion.21 = f32[1,16,24,512]{3,2,1,0:T(8,128)S(1)} fusion(f32[14,22,514]{2,1,0:T(8,128)S(1)} %get-tuple-element.56, f32[14,22,514]{2,1,0:T(8,128)S(1)} %get-tuple-element.55, f32[14,22,514]{2,1,0:T(8,128)S(1)} %get-tuple-element.26, f32[14,22,514]{2,1,0:T(8,128)S(1)} %get-tuple-element.25, f32[14,22,514]{2,1,0:T(8,128)S(1)} %get-tuple-element.22, ...), kind=kLoop, calls=%fused_computation.76 | loop fusion | flops 1179648 | bytes 5077440 | tf_op jit(solution)/shard_map/stack | solution.py:281
  57.2 0.1 slice_bitcast_fusion.9
  57.3 0.2 add_bitcast_fusion
  57.6 0.1 pad_bitcast_fusion
  57.7 0.1 maximum_maximum_fusion.2
  57.8 0.1 maximum_maximum_fusion.1
  57.9 2.1 %collective-permute-start.5 = (f32[36,4,512]{2,1,0:T(4,128)S(1)}, f32[36,4,512]{2,1,0:T(4,128)S(1)}, u32[]{:S(2)}, u32[]{:S(2)}) collective-permute-start(f32[36,4,512]{2,1,0:T(4,128)S(1)} %maximum_maximum_fusion.1), channel_id=1, source_target_pairs={{1,0},{2,1},{3,2},{4,3},{5,4},{6,5},{7,6},{9,8},{10,9},{11,10},{12... | collective-permute-start | bytes 884744 | tf_op jit(solution)/shard_map/ppermute | solution.py:19
  60.0 3.8 %collective-permute-start.4 = (f32[36,4,512]{2,1,0:T(4,128)S(1)}, f32[36,4,512]{2,1,0:T(4,128)S(1)}, u32[]{:S(2)}, u32[]{:S(2)}) collective-permute-start(f32[36,4,512]{2,1,0:T(4,128)S(1)} %maximum_maximum_fusion.2), channel_id=1, source_target_pairs={{0,1},{1,2},{2,3},{3,4},{4,5},{5,6},{6,7},{8,9},{9,10},{10,11},{11... | collective-permute-start | bytes 884744 | tf_op jit(solution)/shard_map/ppermute | solution.py:19
  63.8 5.9 %collective-permute-done.5 = f32[36,4,512]{2,1,0:T(4,128)S(1)} collective-permute-done((f32[36,4,512]{2,1,0:T(4,128)S(1)}, f32[36,4,512]{2,1,0:T(4,128)S(1)}, u32[]{:S(2)}, u32[]{:S(2)}) %collective-permute-start.5) | collective-permute-done | bytes 294944 | tf_op jit(solution)/shard_map/ppermute | solution.py:19
  69.7 4.6 %collective-permute-done.4 = f32[36,4,512]{2,1,0:T(4,128)S(1)} collective-permute-done((f32[36,4,512]{2,1,0:T(4,128)S(1)}, f32[36,4,512]{2,1,0:T(4,128)S(1)}, u32[]{:S(2)}, u32[]{:S(2)}) %collective-permute-start.4) | collective-permute-done | bytes 294944 | tf_op jit(solution)/shard_map/ppermute | solution.py:19
  74.5 0.3 maximum_add_fusion
  74.8 0.4 fusion.1
  75.3 5.9 %collective-permute-start.7 = (f32[9,16,512]{2,1,0:T(8,128)S(1)}, f32[9,16,512]{2,1,0:T(8,128)S(1)}, u32[]{:S(2)}, u32[]{:S(2)}) collective-permute-start(f32[9,16,512]{2,1,0:T(8,128)S(1)} %pad_maximum_fusion.2), channel_id=1, source_target_pairs={{8,0},{16,8},{24,16},{32,24},{40,32},{48,40},{56,48},{64,56},{72,6... | collective-permute-start | bytes 884744 | tf_op jit(solution)/shard_map/ppermute | solution.py:19
  81.2 1.9 %collective-permute-start.6 = (f32[9,16,512]{2,1,0:T(8,128)S(1)}, f32[9,16,512]{2,1,0:T(8,128)S(1)}, u32[]{:S(2)}, u32[]{:S(2)}) collective-permute-start(f32[9,16,512]{2,1,0:T(8,128)S(1)} %pad_maximum_fusion.3), channel_id=1, source_target_pairs={{0,8},{8,16},{16,24},{24,32},{32,40},{40,48},{48,56},{56,64},{64,7... | collective-permute-start | bytes 884744 | tf_op jit(solution)/shard_map/ppermute | solution.py:19
  83.2 5.2 %collective-permute-done.7 = f32[9,16,512]{2,1,0:T(8,128)S(1)} collective-permute-done((f32[9,16,512]{2,1,0:T(8,128)S(1)}, f32[9,16,512]{2,1,0:T(8,128)S(1)}, u32[]{:S(2)}, u32[]{:S(2)}) %collective-permute-start.7) | collective-permute-done | bytes 294944 | tf_op jit(solution)/shard_map/ppermute | solution.py:19
  88.4 6.3 %collective-permute-done.6 = f32[9,16,512]{2,1,0:T(8,128)S(1)} collective-permute-done((f32[9,16,512]{2,1,0:T(8,128)S(1)}, f32[9,16,512]{2,1,0:T(8,128)S(1)}, u32[]{:S(2)}, u32[]{:S(2)}) %collective-permute-start.6) | collective-permute-done | bytes 294944 | tf_op jit(solution)/shard_map/ppermute | solution.py:19
  94.8 0.1 slice_add_fusion.3
  94.9 0.8 fusion.59
  95.8 1.4 %fusion.63 = f32[8,16,512]{2,1,0:T(8,128)} fusion(f32[3,4,16,512]{3,2,1,0:T(8,128)S(1)} %get-tuple-element.68, f32[3,4,16,512]{3,2,1,0:T(8,128)S(1)} %get-tuple-element.69, f32[10,18,514]{2,1,0:T(8,128)S(1)} %get-tuple-element.67, f32[10,18,514]{2,1,0:T(8,128)S(1)} %get-tuple-element.66, f32[10,18,514]{2,1,0:T(8,128)S(1)} %get-tuple-element.15, ...), kind=kLoop, calls=%fused_computation.182 | loop fusion | flops 1245184 | bytes 3670016 | tf_op jit(solution)/shard_map/add | solution.py:284
  (60 shorter events, 0.9 us)
Async XLA Ops:
  0.6 18.7 %copy-start = (f32[8,16,512]{2,1,0:T(8,128)S(1)}, f32[8,16,512]{2,1,0:T(8,128)}, u32[]{:S(2)}) copy-start(f32[8,16,512]{2,1,0:T(8,128)} %param.5) | copy-start | bytes 786436
  0.6 18.7 %copy-start.1 = (f32[8,16,512]{2,1,0:T(8,128)S(1)}, f32[8,16,512]{2,1,0:T(8,128)}, u32[]{:S(2)}) copy-start(f32[8,16,512]{2,1,0:T(8,128)} %param.6) | copy-start | bytes 786436
  0.7 18.7 %copy-start.2 = (f32[8,16,512]{2,1,0:T(8,128)S(1)}, f32[8,16,512]{2,1,0:T(8,128)}, u32[]{:S(2)}) copy-start(f32[8,16,512]{2,1,0:T(8,128)} %param.7) | copy-start | bytes 786436
  2.7 12.6 %collective-permute-start = (f32[8,16,512]{2,1,0:T(8,128)S(1)}, f32[8,16,512]{2,1,0:T(8,128)S(1)}, u32[]{:S(2)}, u32[]{:S(2)}) collective-permute-start(f32[8,16,512]{2,1,0:T(8,128)S(1)} %pad_maximum_fusion.5), channel_id=1, source_target_pairs={{0,8},{8,16},{16,24},{24,32},{32,40},{40,48},{48,56},{56,64},{64,7... | collective-permute-start | bytes 786440 | tf_op jit(solution)/shard_map/ppermute | solution.py:19
  4.7 14.6 %collective-permute-start.1 = (f32[8,16,512]{2,1,0:T(8,128)S(1)}, f32[8,16,512]{2,1,0:T(8,128)S(1)}, u32[]{:S(2)}, u32[]{:S(2)}) collective-permute-start(f32[8,16,512]{2,1,0:T(8,128)S(1)} %pad_maximum_fusion.6), channel_id=1, source_target_pairs={{8,0},{16,8},{24,16},{32,24},{40,32},{48,40},{56,48},{64,56},{72,6... | collective-permute-start | bytes 786440 | tf_op jit(solution)/shard_map/ppermute | solution.py:19
  19.4 2.2 %copy-start.3 = (f32[8,16,512]{2,1,0:T(8,128)S(1)}, f32[8,16,512]{2,1,0:T(8,128)}, u32[]{:S(2)}) copy-start(f32[8,16,512]{2,1,0:T(8,128)} %param.9) | copy-start | bytes 786436
  19.7 11.3 %collective-permute-start.2 = (f32[28,4,512]{2,1,0:T(4,128)S(1)}, f32[28,4,512]{2,1,0:T(4,128)S(1)}, u32[]{:S(2)}, u32[]{:S(2)}) collective-permute-start(f32[28,4,512]{2,1,0:T(4,128)S(1)} %maximum_maximum_fusion.4), channel_id=1, source_target_pairs={{0,1},{1,2},{2,3},{3,4},{4,5},{5,6},{6,7},{8,9},{9,10},{10,11},{11... | collective-permute-start | bytes 688136 | tf_op jit(solution)/shard_map/ppermute | solution.py:19
  21.7 13.6 %collective-permute-start.3 = (f32[28,4,512]{2,1,0:T(4,128)S(1)}, f32[28,4,512]{2,1,0:T(4,128)S(1)}, u32[]{:S(2)}, u32[]{:S(2)}) collective-permute-start(f32[28,4,512]{2,1,0:T(4,128)S(1)} %maximum_maximum_fusion.3), channel_id=1, source_target_pairs={{1,0},{2,1},{3,2},{4,3},{5,4},{6,5},{7,6},{9,8},{10,9},{11,10},{12... | collective-permute-start | bytes 688136 | tf_op jit(solution)/shard_map/ppermute | solution.py:19
  40.3 1.4 %copy-start.4 = (f32[8,16,512]{2,1,0:T(8,128)S(1)}, f32[8,16,512]{2,1,0:T(8,128)}, u32[]{:S(2)}) copy-start(f32[8,16,512]{2,1,0:T(8,128)} %param.8) | copy-start | bytes 786436
  57.9 11.8 %collective-permute-start.5 = (f32[36,4,512]{2,1,0:T(4,128)S(1)}, f32[36,4,512]{2,1,0:T(4,128)S(1)}, u32[]{:S(2)}, u32[]{:S(2)}) collective-permute-start(f32[36,4,512]{2,1,0:T(4,128)S(1)} %maximum_maximum_fusion.1), channel_id=1, source_target_pairs={{1,0},{2,1},{3,2},{4,3},{5,4},{6,5},{7,6},{9,8},{10,9},{11,10},{12... | collective-permute-start | bytes 884744 | tf_op jit(solution)/shard_map/ppermute | solution.py:19
  60.0 14.3 %collective-permute-start.4 = (f32[36,4,512]{2,1,0:T(4,128)S(1)}, f32[36,4,512]{2,1,0:T(4,128)S(1)}, u32[]{:S(2)}, u32[]{:S(2)}) collective-permute-start(f32[36,4,512]{2,1,0:T(4,128)S(1)} %maximum_maximum_fusion.2), channel_id=1, source_target_pairs={{0,1},{1,2},{2,3},{3,4},{4,5},{5,6},{6,7},{8,9},{9,10},{10,11},{11... | collective-permute-start | bytes 884744 | tf_op jit(solution)/shard_map/ppermute | solution.py:19
  75.3 13.0 %collective-permute-start.7 = (f32[9,16,512]{2,1,0:T(8,128)S(1)}, f32[9,16,512]{2,1,0:T(8,128)S(1)}, u32[]{:S(2)}, u32[]{:S(2)}) collective-permute-start(f32[9,16,512]{2,1,0:T(8,128)S(1)} %pad_maximum_fusion.2), channel_id=1, source_target_pairs={{8,0},{16,8},{24,16},{32,24},{40,32},{48,40},{56,48},{64,56},{72,6... | collective-permute-start | bytes 884744 | tf_op jit(solution)/shard_map/ppermute | solution.py:19
  81.2 13.4 %collective-permute-start.6 = (f32[9,16,512]{2,1,0:T(8,128)S(1)}, f32[9,16,512]{2,1,0:T(8,128)S(1)}, u32[]{:S(2)}, u32[]{:S(2)}) collective-permute-start(f32[9,16,512]{2,1,0:T(8,128)S(1)} %pad_maximum_fusion.3), channel_id=1, source_target_pairs={{0,8},{8,16},{16,24},{24,32},{32,40},{40,48},{48,56},{56,64},{64,7... | collective-permute-start | bytes 884744 | tf_op jit(solution)/shard_map/ppermute | solution.py:19

commit v11 on v10

--- a/solution.py
+++ b/solution.py
@@ -175,11 +175,7 @@
     )
 
 
-def advance_solver_step(phase_wide, temp_wide, kinetic_rate_field):
-    padded = jnp.pad(phase_wide, ((0, 0), (0, 0), (2, 2)))
-    grad_z = 0.5 * (padded[2:, 1:-1, 1:-1] - padded[:-2, 1:-1, 1:-1])
-    grad_y = 0.5 * (padded[1:-1, 2:, 1:-1] - padded[1:-1, :-2, 1:-1])
-    grad_x = 0.5 * (padded[1:-1, 1:-1, 2:] - padded[1:-1, 1:-1, :-2])
+def fluxes(grad_z, grad_y, grad_x):
     sq_z = grad_z * grad_z
     sq_y = grad_y * grad_y
     sq_x = grad_x * grad_x
@@ -191,10 +187,29 @@
     flux_z = ENERGY_SCALE * (aniso_sq * grad_z + factor_a * grad_z * (sq_z - quartic * squared))
     flux_y = ENERGY_SCALE * (aniso_sq * grad_y + factor_a * grad_y * (sq_y - quartic * squared))
     flux_x = ENERGY_SCALE * (aniso_sq * grad_x + factor_a * grad_x * (sq_x - quartic * squared))
-    divergence = 0.5 * (flux_z[2:, 1:-1, 1:-1] - flux_z[:-2, 1:-1, 1:-1])
-    divergence = divergence + 0.5 * (flux_y[1:-1, 2:, 1:-1] - flux_y[1:-1, :-2, 1:-1])
-    divergence = divergence + 0.5 * (flux_x[1:-1, 1:-1, 2:] - flux_x[1:-1, 1:-1, :-2])
+    return flux_z, flux_y, flux_x
+
+
+def advance_solver_step(phase_wide, temp_wide, kinetic_rate_field):
+    cells = phase_wide[1:-1, 1:-1]
+    none = jnp.zeros_like(cells[:, :, :1])
+    grad_z = 0.5 * (phase_wide[2:, 1:-1] - phase_wide[:-2, 1:-1])
+    grad_y = 0.5 * (phase_wide[1:-1, 2:] - phase_wide[1:-1, :-2])
+    grad_x = 0.5 * (
+        jnp.concatenate((cells[:, :, 1:], none), axis=2)
+        - jnp.concatenate((none, cells[:, :, :-1]), axis=2)
+    )
+    flux_z, flux_y, flux_x = fluxes(grad_z, grad_y, grad_x)
     phase_now = phase_wide[2:-2, 2:-2]
+    edge_x = jnp.stack((0.5 * (phase_now[:, :, 0] - 0.0), 0.5 * (0.0 - phase_now[:, :, -1])))
+    edge_zero = jnp.zeros_like(edge_x)
+    edge_flux = fluxes(edge_zero, edge_zero, edge_x)[2]
+    inner_x = flux_x[1:-1, 1:-1]
+    ahead = jnp.concatenate((inner_x[:, :, 1:], edge_flux[1][:, :, None]), axis=2)
+    behind = jnp.concatenate((edge_flux[0][:, :, None], inner_x[:, :, :-1]), axis=2)
+    divergence = 0.5 * (flux_z[2:, 1:-1] - flux_z[:-2, 1:-1])
+    divergence = divergence + 0.5 * (flux_y[1:-1, 2:] - flux_y[1:-1, :-2])
+    divergence = divergence + 0.5 * (ahead - behind)
     temp_now = temp_wide[2:-2, 2:-2]
     driving = DRIVE_SCALE / jnp.pi * jnp.arctan(DRIVE_SHARP * (MELT_POINT - temp_now))
     growth = kinetic_rate_field * (

time: 97.5 us -> 129 us (1.32)
  other arithmetic: 25.1 us -> 44.2 us
  local copies, waits for them, and re-layouts: 3.37 us -> 19.2 us
  waiting for transfers between devices: 37.2 us -> 32.5 us
    mul x3 -> x7, other arithmetic: 3.26 us -> 9.16 us  [the longest x4 5.1 us: fluxes(): ENERGY_SCALE * (aniso_sq * grad_x + factor_a * grad_x * (sq_x - quartic *...]
    ppermute x8, waiting for transfers between devices: 37.2 us -> 32.5 us  [from_behind(): return lax.ppermute(block, axis, route)]
    add_any x2 -> x7, other arithmetic: 2.62 us -> 7.31 us  [the longest x2 5.06 us: advance_solver_step(): phase_now[:, :, 0] - 0.0]
    unnamed x10 -> x86, local copies, waits for them, and re-layouts: 0.03 us -> 4.2 us
    neg x5 -> x10, other arithmetic: 10.7 us -> 13.9 us  [the longest x2 4.94 us: advance_solver_step(): grad_y = 0.5 * (phase_wide[1:-1, 2:] - phase_wide[1:-1, :-2])]
    neg x0 -> x2, local copies, waits for them, and re-layouts: none -> 2.24 us  [advance_solver_step(): 0.0 - phase_now[:, :, -1]]
    slice x0 -> x4, local copies, waits for them, and re-layouts: none -> 1.99 us  [the longest x1 1.32 us: advance_solver_step(): inner_x[:, :, 1:]]
    split x0 -> x6, local copies, waits for them, and re-layouts: none -> 1.7 us  [the longest x4 1.35 us: advance_solver_step(): jnp.concatenate((edge_flux[0][:, :, None], inner_x[:, :, :-1]), axis=2)]
  transfers between devices with their start and end apart: 8 -> 8, of which waited for: 8 -> 8; matrix products, arithmetic and copies ran while one was open for 0% -> 2% of each run, Pallas kernels for 0% -> 0%
where the time goes in v11:
time: 129 us; the launch traced here: 128 us
  other arithmetic  44.2 us (34%)
  waiting for transfers between devices  32.5 us (25%)
  starting transfers between devices  30.7 us (24%)
  local copies, waits for them, and re-layouts  19.2 us (15%)
  between operations  1.69 us (1%)
    ppermute x8, waiting for transfers between devices, from_behind(): return lax.ppermute(block, axis, route)  32.5 us
    ppermute x8, starting transfers between devices, from_behind(): return lax.ppermute(block, axis, route)  30.7 us
    mul x4, other arithmetic, fluxes(): ENERGY_SCALE * (aniso_sq * grad_x + factor_a * grad_x * (sq_x - quartic *...  5.1 us
    add_any x2, other arithmetic, advance_solver_step(): phase_now[:, :, 0] - 0.0  5.06 us
    neg x2, other arithmetic, advance_solver_step(): grad_y = 0.5 * (phase_wide[1:-1, 2:] - phase_wide[1:-1, :-2])  4.94 us
    unnamed x86, local copies, waits for them, and re-layouts  4.2 us
    mul x1, other arithmetic, fluxes(): ENERGY_SCALE * (aniso_sq * grad_z + factor_a * grad_z * (sq_z - quartic *...  3.69 us
    neg x2, other arithmetic, advance_solver_step(): divergence = divergence + 0.5 * (ahead - behind)  3.53 us
  transfers between devices with their start and end apart: 8, of which 8 were waited for; matrix products, arithmetic and copies ran while one was open for 2% of the time, Pallas kernels for 0%

profile of v11, /device:TPU:14, one launch (start us, length us, event | category | flops | bytes accessed | tf_op | source)
XLA Modules:
  0.0 128.3 jit_solution(13850870683050439923)
XLA Ops:
  0.7 1.1 fusion.133
  1.7 1.0 fusion.134
  2.7 7.9 %collective-permute-start.1 = (f32[8,16,512]{2,1,0:T(8,128)S(1)}, f32[8,16,512]{2,1,0:T(8,128)S(1)}, u32[]{:S(2)}, u32[]{:S(2)}) collective-permute-start(f32[8,16,512]{2,1,0:T(8,128)S(1)} %pad_maximum_fusion.6), channel_id=1, source_target_pairs={{8,0},{16,8},{24,16},{32,24},{40,32},{48,40},{56,48},{64,56},{72,6... | collective-permute-start | bytes 786440 | tf_op jit(solution)/shard_map/ppermute | solution.py:19
  10.7 1.9 %collective-permute-start = (f32[8,16,512]{2,1,0:T(8,128)S(1)}, f32[8,16,512]{2,1,0:T(8,128)S(1)}, u32[]{:S(2)}, u32[]{:S(2)}) collective-permute-start(f32[8,16,512]{2,1,0:T(8,128)S(1)} %pad_maximum_fusion.5), channel_id=1, source_target_pairs={{0,8},{8,16},{16,24},{24,32},{32,40},{40,48},{48,56},{56,64},{64,7... | collective-permute-start | bytes 786440 | tf_op jit(solution)/shard_map/ppermute | solution.py:19
  13.8 3.6 %collective-permute-done.1 = f32[8,16,512]{2,1,0:T(8,128)S(1)} collective-permute-done((f32[8,16,512]{2,1,0:T(8,128)S(1)}, f32[8,16,512]{2,1,0:T(8,128)S(1)}, u32[]{:S(2)}, u32[]{:S(2)}) %collective-permute-start.1) | collective-permute-done | bytes 262176 | tf_op jit(solution)/shard_map/ppermute | solution.py:19
  17.4 6.1 %collective-permute-done = f32[8,16,512]{2,1,0:T(8,128)S(1)} collective-permute-done((f32[8,16,512]{2,1,0:T(8,128)S(1)}, f32[8,16,512]{2,1,0:T(8,128)S(1)}, u32[]{:S(2)}, u32[]{:S(2)}) %collective-permute-start) | collective-permute-done | bytes 262176 | tf_op jit(solution)/shard_map/ppermute | solution.py:19
  23.9 3.6 %collective-permute-start.3 = (f32[28,4,512]{2,1,0:T(4,128)S(1)}, f32[28,4,512]{2,1,0:T(4,128)S(1)}, u32[]{:S(2)}, u32[]{:S(2)}) collective-permute-start(f32[28,4,512]{2,1,0:T(4,128)S(1)} %maximum_maximum_fusion.3), channel_id=1, source_target_pairs={{1,0},{2,1},{3,2},{4,3},{5,4},{6,5},{7,6},{9,8},{10,9},{11,10},{12... | collective-permute-start | bytes 688136 | tf_op jit(solution)/shard_map/ppermute | solution.py:19
  27.6 2.2 %collective-permute-start.2 = (f32[28,4,512]{2,1,0:T(4,128)S(1)}, f32[28,4,512]{2,1,0:T(4,128)S(1)}, u32[]{:S(2)}, u32[]{:S(2)}) collective-permute-start(f32[28,4,512]{2,1,0:T(4,128)S(1)} %maximum_maximum_fusion.4), channel_id=1, source_target_pairs={{0,1},{1,2},{2,3},{3,4},{4,5},{5,6},{6,7},{8,9},{9,10},{10,11},{11... | collective-permute-start | bytes 688136 | tf_op jit(solution)/shard_map/ppermute | solution.py:19
  29.9 2.0 %collective-permute-done.3 = f32[28,4,512]{2,1,0:T(4,128)S(1)} collective-permute-done((f32[28,4,512]{2,1,0:T(4,128)S(1)}, f32[28,4,512]{2,1,0:T(4,128)S(1)}, u32[]{:S(2)}, u32[]{:S(2)}) %collective-permute-start.3) | collective-permute-done | bytes 229408 | tf_op jit(solution)/shard_map/ppermute | solution.py:19
  32.0 4.5 %collective-permute-done.2 = f32[28,4,512]{2,1,0:T(4,128)S(1)} collective-permute-done((f32[28,4,512]{2,1,0:T(4,128)S(1)}, f32[28,4,512]{2,1,0:T(4,128)S(1)}, u32[]{:S(2)}, u32[]{:S(2)}) %collective-permute-start.2) | collective-permute-done | bytes 229408 | tf_op jit(solution)/shard_map/ppermute | solution.py:19
  38.0 2.9 %add_multiply_fusion.2 = (f32[14,22,512]{2,1,0:T(8,128)S(1)}, f32[14,22,512]{2,1,0:T(8,128)}, f32[14,22,512]{2,1,0:T(8,128)}, f32[14,22,512]{2,1,0:T(8,128)}, f3...) fusion(f32[16,24,512]{2,1,0:T(8,128)S(1)} %get-tuple-element.71, ...), kind=kLoop, calls=%fused_computation.63 | loop fusion | flops 5203968 | bytes 8197728 | tf_op jit(solution)/shard_map/mul | solution.py:189
  40.9 1.3 %fusion.127 = (f32[12,20,511]{2,1,0:T(8,128)}, f32[12,20,511]{2,1,0:T(8,128)}) fusion(f32[14,22,512]{2,1,0:T(8,128)S(1)} %get-tuple-element.52), kind=kLoop, calls=%fused_computation.342 | loop fusion | bytes 1962240 | tf_op jit(solution)/shard_map/slice | solution.py:208
  42.7 3.7 %add_multiply_fusion.4 = (f32[14,22,512]{2,1,0:T(8,128)S(1)}, f32[14,22,512]{2,1,0:T(8,128)}, f32[14,22,512]{2,1,0:T(8,128)S(1)}, f32[14,22,512]{2,1,0:T(8,128)}) fusion(f32[14,22,512]{2,1,0:T(8,128)} %get-tuple-element.54, f32[14,22,512]{2,1,0:T(8,128)} %get-tuple-element.56, f32[14,22,512]{2,1,0:T(8,128)} %get-tuple-element.58, ...), kind=kLoop, calls=%fused_computation.65 | loop fusion | flops 4100096 | bytes 5677056 | tf_op jit(solution)/shard_map/mul | solution.py:187
  46.4 2.2 %multiply_add_fusion.4 = (f32[12,20,512]{2,1,0:T(8,128)S(1)}, f32[12,20,512]{2,1,0:T(8,128)}, f32[12,20,512]{2,1,0:T(8,128)S(1)}, f32[12,20,512]{2,1,0:T(8,128)S(1)}, f32[12,20,512]{2,1,0:T(8,128)S(1)}) fusion(f32[16,24,512]{2,1,0:T(8,128)S(1)} %get-tuple-element.70, f32[16,24,512]{2,1,0:T(8,128)S(1)} %get-tuple-element.71, ...), kind=kLoop, calls=%fused_computation.96 | loop fusion | flops 2826240 | bytes 8847360 | tf_op jit(solution)/shard_map/add | solution.py:218
  49.7 1.3 fusion.69
  51.4 1.5 %add_multiply_fusion.5 = (f32[10,18,512]{2,1,0:T(8,128)}, f32[10,18,512]{2,1,0:T(8,128)S(1)}, f32[10,18,512]{2,1,0:T(8,128)S(1)}, f32[10,18,512]{2,1,0:T(8,128)S(1)}) fusion(f32[12,20,512]{2,1,0:T(8,128)S(1)} %get-tuple-element.50, f32[10,18,511]{2,1,0:T(8,128)S(1)} %get-tuple-element.110, f32[10,18,511]{2,1,0:T(8,128)S(1)} %get-tuple-element.109), kind=kLoop, calls=%fused_computation.121 | loop fusion | flops 3041280 | bytes 3684960 | tf_op jit(solution)/shard_map/jvp()/mul | solution.py:189
  53.0 2.9 %fusion.118 = (f32[10,18,512]{2,1,0:T(8,128)}, f32[10,18,512]{2,1,0:T(8,128)}, f32[10,18,512]{2,1,0:T(8,128)S(1)}, f32[10,18,512]{2,1,0:T(8,128)S(1)}, f32[10,18,512]{2,1,0:T(8,128)}) fusion(f32[10,18,512]{2,1,0:T(8,128)S(1)} %get-tuple-element.29, f32[8,16,512]{2,1,0:T(8,128)S(1)} %get-tuple-element.122, f32[8,16,512]{2,1,0:T(8,128)S(1)} %get-tuple-element.121, ...), kind=kLoop, calls=%fused_computation.339 | loop fusion | flops 8478720 | bytes 3735552 | tf_op jit(solution)/shard_map/transpose(jvp())/neg | solution.py:197
  55.9 2.2 %fusion.120 = (f32[10,18,512]{2,1,0:T(8,128)}, f32[10,18,512]{2,1,0:T(8,128)}, f32[10,18,512]{2,1,0:T(8,128)S(1)}, f32[10,18,512]{2,1,0:T(8,128)}) fusion(f32[10,18,512]{2,1,0:T(8,128)S(1)} %get-tuple-element.30, f32[10,18,512]{2,1,0:T(8,128)S(1)} %get-tuple-element.47, f32[10,18,512]{2,1,0:T(8,128)S(1)} %get-tuple-element.46, ...), kind=kLoop, calls=%fused_computation.340 | loop fusion | flops 5437440 | bytes 4104192 | tf_op jit(solution)/shard_map/transpose(jvp())/neg | solution.py:196
  58.1 1.1 slice_negate_fusion.1
  60.4 0.8 copy.344
  61.2 1.4 %copy.343 = f32[8,16,1]{2,1,0:T(8,128)} copy(f32[8,16,1]{1,0,2:T(8,128)} %get-tuple-element.145) | data formatting | bytes 1024 | tf_op jit(solution)/shard_map/transpose(jvp())/neg | solution.py:204
  62.7 1.5 %pad_add_fusion.3 = f32[10,18,512]{2,1,0:T(8,128)S(1)} fusion(f32[10,18,511]{2,1,0:T(8,128)} %get-tuple-element.116, f32[10,18,511]{2,1,0:T(8,128)} %get-tuple-element.115), kind=kLoop, calls=%fused_computation.124 | loop fusion | flops 92160 | bytes 1104480 | tf_op jit(solution)/shard_map/transpose(jvp())/add_any | solution.py:199
  64.2 1.7 %fusion.49 = f32[8,16,512]{2,1,0:T(8,128)S(1)} fusion(f32[8,16,1]{2,1,0:T(8,128)S(1)} %copy.344, f32[8,16,1]{2,1,0:T(8,128)} %copy.343, f32[8,16,512]{2,1,0:T(8,128)} %copy-done.23, f32[8,16,512]{2,1,0:T(8,128)} %param.9, f32[8,16,512]{2,1,0:T(8,128)} %get-tuple-element.42, f32[12,20,512]{2,1,0:T(8,128)S(1)} %get-tuple-element.50, f32[8,16,512]{2,1,0:T(8,128)} %param.8), kind=kLoop, calls=%fused_computation.158 | loop fusion | flops 1245184 | bytes 1573888 | tf_op jit(solution)/shard_map/transpose(jvp())/add_any | solution.py:204
  65.9 1.7 %broadcast_multiply_fusion = f32[12,20,512]{2,1,0:T(8,128)} fusion(f32[8,16,512]{2,1,0:T(8,128)S(1)} %get-tuple-element.41, f32[8,16,512]{2,1,0:T(8,128)S(1)} %broadcast_multiply_fusion.3, pred[20]{0:T(512)(128)(4,1)} %get-tuple-element.149, pred[20]{0:T(512)(128)(4,1)} %get-tuple-element.150, pred[12]{0:T(512)(128)(4,1)} %compare_and_fusion), kind=kLoop, calls=%fused_computation.153 | loop fusion | flops 983040 | bytes 1015860 | tf_op jit(solution)/shard_map/transpose(jvp())/mul | solution.py:227
  67.6 3.5 %fusion.116 = (f32[12,20,512]{2,1,0:T(8,128)S(1)}, f32[12,20,512]{2,1,0:T(8,128)S(1)}, f32[12,20,512]{2,1,0:T(8,128)}) fusion(f32[16,24,512]{2,1,0:T(8,128)S(1)} %get-tuple-element.70, f32[8,16,512]{2,1,0:T(8,128)} %copy-done.10, f32[8,16,512]{2,1,0:T(8,128)} %copy-done.7, f32[10,18,512]{2,1,0:T(8,128)S(1)} %pad_add_fusion.3, ...), kind=kLoop, calls=%fused_computation.338 | loop fusion | flops 2334720 | bytes 4595764 | tf_op jit(solution)/shard_map/transpose(jvp())/neg | solution.py:212
  71.2 0.8 copy-done.5
  72.0 1.0 split.56
  73.4 0.8 copy.346
  74.2 0.8 copy.345
  75.1 3.4 %fusion.21 = (f32[12,20,512]{2,1,0:T(8,128)S(1)}, f32[12,20,512]{2,1,0:T(8,128)S(1)}) fusion(f32[12,20,1]{2,1,0:T(8,128)} %copy.346, f32[12,20,1]{2,1,0:T(8,128)} %copy.345, f32[12,20,512]{2,1,0:T(8,128)} %get-tuple-element.40, f32[16,24,512]{2,1,0:T(8,128)S(1)} %get-tuple-element.70, f32[16,24,512]{2,1,0:T(8,128)S(1)} %get-tuple-element.69, ...), kind=kLoop, calls=%fused_computation.79 | loop fusion | flops 3686400 | bytes 3966900 | tf_op jit(solution)/shard_map/transpose(jvp())/add_any | solution.py:204
  78.7 0.9 fusion.23
  81.7 2.1 %fusion.112 = (f32[14,22,512]{2,1,0:T(8,128)S(1)}, f32[14,22,512]{2,1,0:T(8,128)S(1)}, f32[14,22,512]{2,1,0:T(8,128)S(1)}, f32[14,22,512]{2,1,0:T(8,128)S(1)}) fusion(f32[14,22,512]{2,1,0:T(8,128)S(1)} %copy-done.3, f32[14,22,512]{2,1,0:T(8,128)S(1)} %copy-done.21, f32[14,22,512]{2,1,0:T(8,128)S(1)} %copy-done, f32[14,22,512]{2,1,0:T(8,128)S(1)} %copy-done.1, ...), kind=kLoop, calls=%fused_computation.336 | loop fusion | flops 13088768 | bytes 9043968 | tf_op jit(solution)/shard_map/transpose(jvp())/neg | solution.py:197
  83.8 1.2 fusion.114
  86.5 1.9 %collective-permute-start.4 = (f32[36,4,512]{2,1,0:T(4,128)S(1)}, f32[36,4,512]{2,1,0:T(4,128)S(1)}, u32[]{:S(2)}, u32[]{:S(2)}) collective-permute-start(f32[36,4,512]{2,1,0:T(4,128)S(1)} %maximum_maximum_fusion.2), channel_id=1, source_target_pairs={{0,1},{1,2},{2,3},{3,4},{4,5},{5,6},{6,7},{8,9},{9,10},{10,11},{11... | collective-permute-start | bytes 884744 | tf_op jit(solution)/shard_map/ppermute | solution.py:19
  88.4 4.8 %collective-permute-start.5 = (f32[36,4,512]{2,1,0:T(4,128)S(1)}, f32[36,4,512]{2,1,0:T(4,128)S(1)}, u32[]{:S(2)}, u32[]{:S(2)}) collective-permute-start(f32[36,4,512]{2,1,0:T(4,128)S(1)} %maximum_maximum_fusion.1), channel_id=1, source_target_pairs={{1,0},{2,1},{3,2},{4,3},{5,4},{6,5},{7,6},{9,8},{10,9},{11,10},{12... | collective-permute-start | bytes 884744 | tf_op jit(solution)/shard_map/ppermute | solution.py:19
  93.2 2.8 %collective-permute-done.4 = f32[36,4,512]{2,1,0:T(4,128)S(1)} collective-permute-done((f32[36,4,512]{2,1,0:T(4,128)S(1)}, f32[36,4,512]{2,1,0:T(4,128)S(1)}, u32[]{:S(2)}, u32[]{:S(2)}) %collective-permute-start.4) | collective-permute-done | bytes 294944 | tf_op jit(solution)/shard_map/ppermute | solution.py:19
  96.0 3.2 %collective-permute-done.5 = f32[36,4,512]{2,1,0:T(4,128)S(1)} collective-permute-done((f32[36,4,512]{2,1,0:T(4,128)S(1)}, f32[36,4,512]{2,1,0:T(4,128)S(1)}, u32[]{:S(2)}, u32[]{:S(2)}) %collective-permute-start.5) | collective-permute-done | bytes 294944 | tf_op jit(solution)/shard_map/ppermute | solution.py:19
  100.3 0.8 pad_maximum_fusion.2
  101.1 0.8 pad_maximum_fusion.3
  101.8 6.4 %collective-permute-start.7 = (f32[9,16,512]{2,1,0:T(8,128)}, f32[9,16,512]{2,1,0:T(8,128)S(1)}, u32[]{:S(2)}, u32[]{:S(2)}) collective-permute-start(f32[9,16,512]{2,1,0:T(8,128)} %pad_maximum_fusion.2), channel_id=1, source_target_pairs={{8,0},{16,8},{24,16},{32,24},{40,32},{48,40},{56,48},{64,56},{72,6... | collective-permute-start | bytes 884744 | tf_op jit(solution)/shard_map/ppermute | solution.py:19
  108.4 1.9 %collective-permute-start.6 = (f32[9,16,512]{2,1,0:T(8,128)}, f32[9,16,512]{2,1,0:T(8,128)S(1)}, u32[]{:S(2)}, u32[]{:S(2)}) collective-permute-start(f32[9,16,512]{2,1,0:T(8,128)} %pad_maximum_fusion.3), channel_id=1, source_target_pairs={{0,8},{8,16},{16,24},{24,32},{32,40},{40,48},{48,56},{56,64},{64,7... | collective-permute-start | bytes 884744 | tf_op jit(solution)/shard_map/ppermute | solution.py:19
  111.2 1.7 %collective-permute-done.7 = f32[9,16,512]{2,1,0:T(8,128)S(1)} collective-permute-done((f32[9,16,512]{2,1,0:T(8,128)}, f32[9,16,512]{2,1,0:T(8,128)S(1)}, u32[]{:S(2)}, u32[]{:S(2)}) %collective-permute-start.7) | collective-permute-done | bytes 294944 | tf_op jit(solution)/shard_map/ppermute | solution.py:19
  113.7 8.7 %collective-permute-done.6 = f32[9,16,512]{2,1,0:T(8,128)S(1)} collective-permute-done((f32[9,16,512]{2,1,0:T(8,128)}, f32[9,16,512]{2,1,0:T(8,128)S(1)}, u32[]{:S(2)}, u32[]{:S(2)}) %collective-permute-start.6) | collective-permute-done | bytes 294944 | tf_op jit(solution)/shard_map/ppermute | solution.py:19
  123.1 1.0 slice.586
  124.2 0.9 slice_bitcast_fusion.3
  125.1 0.9 slice_bitcast_fusion.4
  126.2 0.8 fusion.51
  127.0 1.3 fusion.55
  (175 shorter events, 14.1 us)
Async XLA Ops:
  0.6 22.9 %copy-start.9 = (f32[8,16,512]{2,1,0:T(8,128)S(1)}, f32[8,16,512]{2,1,0:T(8,128)}, u32[]{:S(2)}) copy-start(f32[8,16,512]{2,1,0:T(8,128)} %param.5) | copy-start | bytes 786436
  0.6 22.9 %copy-start.16 = (f32[8,16,512]{2,1,0:T(8,128)S(1)}, f32[8,16,512]{2,1,0:T(8,128)}, u32[]{:S(2)}) copy-start(f32[8,16,512]{2,1,0:T(8,128)} %param.6) | copy-start | bytes 786436
  0.7 22.9 %copy-start.17 = (f32[8,16,512]{2,1,0:T(8,128)S(1)}, f32[8,16,512]{2,1,0:T(8,128)}, u32[]{:S(2)}) copy-start(f32[8,16,512]{2,1,0:T(8,128)} %param.7) | copy-start | bytes 786436
  2.7 14.6 %collective-permute-start.1 = (f32[8,16,512]{2,1,0:T(8,128)S(1)}, f32[8,16,512]{2,1,0:T(8,128)S(1)}, u32[]{:S(2)}, u32[]{:S(2)}) collective-permute-start(f32[8,16,512]{2,1,0:T(8,128)S(1)} %pad_maximum_fusion.6), channel_id=1, source_target_pairs={{8,0},{16,8},{24,16},{32,24},{40,32},{48,40},{56,48},{64,56},{72,6... | collective-permute-start | bytes 786440 | tf_op jit(solution)/shard_map/ppermute | solution.py:19
  10.7 12.8 %collective-permute-start = (f32[8,16,512]{2,1,0:T(8,128)S(1)}, f32[8,16,512]{2,1,0:T(8,128)S(1)}, u32[]{:S(2)}, u32[]{:S(2)}) collective-permute-start(f32[8,16,512]{2,1,0:T(8,128)S(1)} %pad_maximum_fusion.5), channel_id=1, source_target_pairs={{0,8},{8,16},{16,24},{24,32},{32,40},{40,48},{48,56},{56,64},{64,7... | collective-permute-start | bytes 786440 | tf_op jit(solution)/shard_map/ppermute | solution.py:19
  23.7 3.9 %copy-start.18 = (f32[8,16,512]{2,1,0:T(8,128)S(1)}, f32[8,16,512]{2,1,0:T(8,128)}, u32[]{:S(2)}) copy-start(f32[8,16,512]{2,1,0:T(8,128)} %param.9) | copy-start | bytes 786436
  23.9 7.9 %collective-permute-start.3 = (f32[28,4,512]{2,1,0:T(4,128)S(1)}, f32[28,4,512]{2,1,0:T(4,128)S(1)}, u32[]{:S(2)}, u32[]{:S(2)}) collective-permute-start(f32[28,4,512]{2,1,0:T(4,128)S(1)} %maximum_maximum_fusion.3), channel_id=1, source_target_pairs={{1,0},{2,1},{3,2},{4,3},{5,4},{6,5},{7,6},{9,8},{10,9},{11,10},{12... | collective-permute-start | bytes 688136 | tf_op jit(solution)/shard_map/ppermute | solution.py:19
  27.6 38.3 %copy-start.7 = (f32[8,16,512]{2,1,0:T(8,128)}, f32[8,16,512]{2,1,0:T(8,128)S(1)}, u32[]{:S(2)}) copy-start(f32[8,16,512]{2,1,0:T(8,128)S(1)} %broadcast_multiply_fusion.3) | copy-start | bytes 786436
  27.6 8.8 %collective-permute-start.2 = (f32[28,4,512]{2,1,0:T(4,128)S(1)}, f32[28,4,512]{2,1,0:T(4,128)S(1)}, u32[]{:S(2)}, u32[]{:S(2)}) collective-permute-start(f32[28,4,512]{2,1,0:T(4,128)S(1)} %maximum_maximum_fusion.4), channel_id=1, source_target_pairs={{0,1},{1,2},{2,3},{3,4},{4,5},{5,6},{6,7},{8,9},{9,10},{10,11},{11... | collective-permute-start | bytes 688136 | tf_op jit(solution)/shard_map/ppermute | solution.py:19
  42.7 3.7 %copy-start.24 = (f32[12,20,511]{2,1,0:T(8,128)S(1)}, f32[12,20,511]{2,1,0:T(8,128)}, u32[]{:S(2)}) copy-start(f32[12,20,511]{2,1,0:T(8,128)} %get-tuple-element.105) | copy-start | bytes 1471684
  42.7 3.7 %copy-start.25 = (f32[12,20,511]{2,1,0:T(8,128)S(1)}, f32[12,20,511]{2,1,0:T(8,128)}, u32[]{:S(2)}) copy-start(f32[12,20,511]{2,1,0:T(8,128)} %get-tuple-element.106) | copy-start | bytes 1471684
  48.6 0.9 copy-start.19
  48.6 1.0 copy-start.26
  50.9 2.0 %copy-start.23 = (f32[8,16,512]{2,1,0:T(8,128)}, f32[8,16,512]{2,1,0:T(8,128)S(1)}, u32[]{:S(2)}) copy-start(f32[8,16,512]{2,1,0:T(8,128)S(1)} %get-tuple-element.43) | copy-start | bytes 786436
  50.9 14.9 %copy-start.10 = (f32[8,16,512]{2,1,0:T(8,128)}, f32[8,16,512]{2,1,0:T(8,128)S(1)}, u32[]{:S(2)}) copy-start(f32[8,16,512]{2,1,0:T(8,128)S(1)} %get-tuple-element.41) | copy-start | bytes 786436
  62.6 5.0 %copy-start.32 = (f32[10,18,512]{2,1,0:T(8,128)S(1)}, f32[10,18,512]{2,1,0:T(8,128)}, u32[]{:S(2)}) copy-start(f32[10,18,512]{2,1,0:T(8,128)} %get-tuple-element.44) | copy-start | bytes 1105924
  62.6 5.0 %copy-start.33 = (f32[10,18,512]{2,1,0:T(8,128)S(1)}, f32[10,18,512]{2,1,0:T(8,128)}, u32[]{:S(2)}) copy-start(f32[10,18,512]{2,1,0:T(8,128)} %get-tuple-element.45) | copy-start | bytes 1105924
  62.6 5.0 %copy-start.34 = (f32[10,18,512]{2,1,0:T(8,128)S(1)}, f32[10,18,512]{2,1,0:T(8,128)}, u32[]{:S(2)}) copy-start(f32[10,18,512]{2,1,0:T(8,128)} %get-tuple-element.48) | copy-start | bytes 1105924
  62.6 5.0 %copy-start.35 = (f32[10,18,512]{2,1,0:T(8,128)S(1)}, f32[10,18,512]{2,1,0:T(8,128)}, u32[]{:S(2)}) copy-start(f32[10,18,512]{2,1,0:T(8,128)} %get-tuple-element.49) | copy-start | bytes 1105924
  75.0 3.5 %copy-start.8 = (f32[8,16,512]{2,1,0:T(8,128)S(1)}, f32[8,16,512]{2,1,0:T(8,128)}, u32[]{:S(2)}) copy-start(f32[8,16,512]{2,1,0:T(8,128)} %copy-done.7) | copy-start | bytes 786436
  75.0 3.5 %copy-start.11 = (f32[8,16,512]{2,1,0:T(8,128)S(1)}, f32[8,16,512]{2,1,0:T(8,128)}, u32[]{:S(2)}) copy-start(f32[8,16,512]{2,1,0:T(8,128)} %copy-done.10) | copy-start | bytes 786436
  75.0 3.5 %copy-start.14 = (f32[12,20,512]{2,1,0:T(8,128)S(1)}, f32[12,20,512]{2,1,0:T(8,128)}, u32[]{:S(2)}) copy-start(f32[12,20,512]{2,1,0:T(8,128)} %get-tuple-element.40) | copy-start | bytes 1474564
  75.0 3.5 %copy-start.15 = (f32[12,20,512]{2,1,0:T(8,128)S(1)}, f32[12,20,512]{2,1,0:T(8,128)}, u32[]{:S(2)}) copy-start(f32[12,20,512]{2,1,0:T(8,128)} %broadcast_multiply_fusion) | copy-start | bytes 1474564
  75.1 3.5 %copy-start.40 = (pred[12]{0:T(512)(128)(4,1)S(1)}, pred[12]{0:T(512)(128)(4,1)}, u32[]{:S(2)}) copy-start(pred[12]{0:T(512)(128)(4,1)} %compare_and_fusion) | copy-start | bytes 40
  75.1 3.5 %copy-start.41 = (pred[20]{0:T(512)(128)(4,1)S(1)}, pred[20]{0:T(512)(128)(4,1)}, u32[]{:S(2)}) copy-start(pred[20]{0:T(512)(128)(4,1)} %get-tuple-element.149) | copy-start | bytes 64
  75.1 3.5 %copy-start.42 = (pred[20]{0:T(512)(128)(4,1)S(1)}, pred[20]{0:T(512)(128)(4,1)}, u32[]{:S(2)}) copy-start(pred[20]{0:T(512)(128)(4,1)} %get-tuple-element.150) | copy-start | bytes 64
  78.6 1.3 copy-start.22
  78.6 1.5 %copy-start.6 = (f32[12,20,512]{2,1,0:T(8,128)S(1)}, f32[12,20,512]{2,1,0:T(8,128)}, u32[]{:S(2)}) copy-start(f32[12,20,512]{2,1,0:T(8,128)} %copy-done.5) | copy-start | bytes 1474564
  78.6 1.5 %copy-start.12 = (f32[14,22,512]{2,1,0:T(8,128)S(1)}, f32[14,22,512]{2,1,0:T(8,128)}, u32[]{:S(2)}) copy-start(f32[14,22,512]{2,1,0:T(8,128)} %get-tuple-element.60) | copy-start | bytes 1892356
  78.6 1.6 %copy-start.13 = (f32[14,22,512]{2,1,0:T(8,128)S(1)}, f32[14,22,512]{2,1,0:T(8,128)}, u32[]{:S(2)}) copy-start(f32[14,22,512]{2,1,0:T(8,128)} %get-tuple-element.53) | copy-start | bytes 1892356
  78.7 1.8 %copy-start.21 = (f32[14,22,512]{2,1,0:T(8,128)S(1)}, f32[14,22,512]{2,1,0:T(8,128)}, u32[]{:S(2)}) copy-start(f32[14,22,512]{2,1,0:T(8,128)} %get-tuple-element.65) | copy-start | bytes 1892356
  79.6 1.3 %copy-start = (f32[14,22,512]{2,1,0:T(8,128)S(1)}, f32[14,22,512]{2,1,0:T(8,128)}, u32[]{:S(2)}) copy-start(f32[14,22,512]{2,1,0:T(8,128)} %get-tuple-element.54) | copy-start | bytes 1892356
  79.6 1.5 %copy-start.1 = (f32[14,22,512]{2,1,0:T(8,128)S(1)}, f32[14,22,512]{2,1,0:T(8,128)}, u32[]{:S(2)}) copy-start(f32[14,22,512]{2,1,0:T(8,128)} %get-tuple-element.55) | copy-start | bytes 1892356
  79.6 1.7 %copy-start.2 = (f32[14,22,512]{2,1,0:T(8,128)S(1)}, f32[14,22,512]{2,1,0:T(8,128)}, u32[]{:S(2)}) copy-start(f32[14,22,512]{2,1,0:T(8,128)} %get-tuple-element.56) | copy-start | bytes 1892356
  79.6 1.9 %copy-start.3 = (f32[14,22,512]{2,1,0:T(8,128)S(1)}, f32[14,22,512]{2,1,0:T(8,128)}, u32[]{:S(2)}) copy-start(f32[14,22,512]{2,1,0:T(8,128)} %get-tuple-element.57) | copy-start | bytes 1892356
  79.6 2.1 %copy-start.4 = (f32[14,22,512]{2,1,0:T(8,128)S(1)}, f32[14,22,512]{2,1,0:T(8,128)}, u32[]{:S(2)}) copy-start(f32[14,22,512]{2,1,0:T(8,128)} %get-tuple-element.58) | copy-start | bytes 1892356
  86.5 9.5 %collective-permute-start.4 = (f32[36,4,512]{2,1,0:T(4,128)S(1)}, f32[36,4,512]{2,1,0:T(4,128)S(1)}, u32[]{:S(2)}, u32[]{:S(2)}) collective-permute-start(f32[36,4,512]{2,1,0:T(4,128)S(1)} %maximum_maximum_fusion.2), channel_id=1, source_target_pairs={{0,1},{1,2},{2,3},{3,4},{4,5},{5,6},{6,7},{8,9},{9,10},{10,11},{11... | collective-permute-start | bytes 884744 | tf_op jit(solution)/shard_map/ppermute | solution.py:19
  88.4 10.9 %collective-permute-start.5 = (f32[36,4,512]{2,1,0:T(4,128)S(1)}, f32[36,4,512]{2,1,0:T(4,128)S(1)}, u32[]{:S(2)}, u32[]{:S(2)}) collective-permute-start(f32[36,4,512]{2,1,0:T(4,128)S(1)} %maximum_maximum_fusion.1), channel_id=1, source_target_pairs={{1,0},{2,1},{3,2},{4,3},{5,4},{6,5},{7,6},{9,8},{10,9},{11,10},{12... | collective-permute-start | bytes 884744 | tf_op jit(solution)/shard_map/ppermute | solution.py:19
  100.2 8.0 %copy-start.29 = (f32[10,18,512]{2,1,0:T(8,128)S(1)}, f32[10,18,512]{2,1,0:T(8,128)}, u32[]{:S(2)}) copy-start(f32[10,18,512]{2,1,0:T(8,128)} %get-tuple-element.28) | copy-start | bytes 1105924
  100.2 10.1 %copy-start.39 = (f32[2,8,16]{2,1,0:T(8,128)S(1)}, f32[2,8,16]{2,1,0:T(8,128)}, u32[]{:S(2)}) copy-start(f32[2,8,16]{2,1,0:T(8,128)} %get-tuple-element.143) | copy-start | bytes 3076
  101.8 11.1 %collective-permute-start.7 = (f32[9,16,512]{2,1,0:T(8,128)}, f32[9,16,512]{2,1,0:T(8,128)S(1)}, u32[]{:S(2)}, u32[]{:S(2)}) collective-permute-start(f32[9,16,512]{2,1,0:T(8,128)} %pad_maximum_fusion.2), channel_id=1, source_target_pairs={{8,0},{16,8},{24,16},{32,24},{40,32},{48,40},{56,48},{64,56},{72,6... | collective-permute-start | bytes 884744 | tf_op jit(solution)/shard_map/ppermute | solution.py:19
  108.4 14.0 %collective-permute-start.6 = (f32[9,16,512]{2,1,0:T(8,128)}, f32[9,16,512]{2,1,0:T(8,128)S(1)}, u32[]{:S(2)}, u32[]{:S(2)}) collective-permute-start(f32[9,16,512]{2,1,0:T(8,128)} %pad_maximum_fusion.3), channel_id=1, source_target_pairs={{0,8},{8,16},{16,24},{24,32},{32,40},{40,48},{48,56},{56,64},{64,7... | collective-permute-start | bytes 884744 | tf_op jit(solution)/shard_map/ppermute | solution.py:19
  123.1 3.9 %copy-start.20 = (f32[8,16,512]{2,1,0:T(8,128)S(1)}, f32[8,16,512]{2,1,0:T(8,128)}, u32[]{:S(2)}) copy-start(f32[8,16,512]{2,1,0:T(8,128)} %param.9) | copy-start | bytes 786436
  123.1 3.9 %copy-start.27 = (f32[8,16,512]{2,1,0:T(8,128)S(1)}, f32[8,16,512]{2,1,0:T(8,128)}, u32[]{:S(2)}) copy-start(f32[8,16,512]{2,1,0:T(8,128)} %param.8) | copy-start | bytes 786436
  123.1 3.9 %copy-start.28 = (f32[8,16,512]{2,1,0:T(8,128)S(1)}, f32[8,16,512]{2,1,0:T(8,128)}, u32[]{:S(2)}) copy-start(f32[8,16,512]{2,1,0:T(8,128)} %get-tuple-element.42) | copy-start | bytes 786436
  123.1 3.9 %copy-start.30 = (f32[10,18,512]{2,1,0:T(8,128)S(1)}, f32[10,18,512]{2,1,0:T(8,128)}, u32[]{:S(2)}) copy-start(f32[10,18,512]{2,1,0:T(8,128)} %get-tuple-element.87) | copy-start | bytes 1105924
  123.1 3.9 %copy-start.31 = (f32[10,18,512]{2,1,0:T(8,128)S(1)}, f32[10,18,512]{2,1,0:T(8,128)}, u32[]{:S(2)}) copy-start(f32[10,18,512]{2,1,0:T(8,128)} %get-tuple-element.86) | copy-start | bytes 1105924
  123.1 3.9 %copy-start.38 = (f32[8,16,1]{2,1,0:T(8,128)S(1)}, f32[8,16,1]{2,1,0:T(8,128)}, u32[]{:S(2)}) copy-start(f32[8,16,1]{2,1,0:T(8,128)} %copy.348) | copy-start | bytes 1540
  (3 other events, 2.4 us)

commit v12 on v7

--- a/solution.py
+++ b/solution.py
@@ -133,38 +133,49 @@
 
 def packed_y_fold(contributions):
     depth, rows = contributions.shape[1], contributions.shape[2]
-
-    def rims(lo, hi):
+    quarter = (depth - 4) // 4
+
+    def rims(second_rows, third_first, third_second):
+        second = contributions[1, 1 : depth - 1, second_rows]
+        third = contributions[2, 2 : depth - 2]
+        first_row = third[:, third_first : third_first + 1]
+        second_row = jnp.pad(third[:, third_second : third_second + 1], ((1, 1), (0, 0), (0, 0)))
         return jnp.concatenate(
             (
-                contributions[0, :, lo:hi],
-                contributions[1, 1 : depth - 1, lo:hi],
-                contributions[2, 2 : depth - 2, lo:hi],
+                jnp.concatenate((second, second_row), axis=1),
+                jnp.concatenate(
+                    [first_row[k * quarter : (k + 1) * quarter] for k in range(4)], axis=1
+                ),
             ),
             axis=0,
         )
 
-    lower = rims(0, 4)
-    upper = rims(rows - 4, rows)
+    lower = jnp.concatenate(
+        (contributions[0, :, 0:4], rims(slice(1, 4), 2, 3)), axis=0
+    )
+    upper = jnp.concatenate(
+        (contributions[0, :, rows - 4 :], rims(slice(rows - 4, rows - 1), rows - 4, rows - 3)),
+        axis=0,
+    )
     lower, upper = lax.optimization_barrier((lower, upper))
     from_above = from_behind(lower, "gy", -1)
     from_below = from_behind(upper, "gy", 1)
 
-    def unpack(arrived):
-        return jnp.stack(
-            (
-                arrived[:depth],
-                jnp.pad(arrived[depth : 2 * depth - 2], ((1, 1), (0, 0), (0, 0))),
-                jnp.pad(arrived[2 * depth - 2 :], ((2, 2), (0, 0), (0, 0))),
-            )
-        )
+    def unpack(arrived, second_side, third_side):
+        block = arrived[depth : 2 * depth - 2]
+        spread = arrived[2 * depth - 2 :]
+        second = jnp.pad(block[:, 0:3], ((1, 1), second_side, (0, 0)))
+        first_row = jnp.concatenate([spread[:, k : k + 1] for k in range(4)], axis=0)
+        third = jnp.concatenate((first_row, block[1 : depth - 3, 3:4]), axis=1)
+        third = jnp.pad(third, ((2, 2), third_side, (0, 0)))
+        return jnp.stack((arrived[:depth], second, third))
 
     middle = contributions[:, :, 4 : rows - 4]
     return jnp.concatenate(
         (
-            middle[:, :, :4] + unpack(from_below),
+            middle[:, :, :4] + unpack(from_below, (0, 1), (0, 2)),
             middle[:, :, 4:-4],
-            middle[:, :, -4:] + unpack(from_above),
+            middle[:, :, -4:] + unpack(from_above, (1, 0), (2, 0)),
         ),
         axis=2,
     )
@@ -254,8 +265,6 @@
         phase_wide, temp_wide, rate_wide[2:-2, 2:-2]
     )
     valid = inside_grid(succeeding_order_parameter, 2)
-    succeeding_order_parameter = jnp.where(valid, succeeding_order_parameter, 0.0)
-    succeeding_heat_level = jnp.where(valid, succeeding_heat_level, 0.0)
     discarded_result, sensitivity_latest = jax.vjp(
         advance_solver_step,
         succeeding_order_parameter,

time: 98.3 us -> 96.7 us (0.984)
  starting transfers between devices: 31.9 us -> 30.4 us
  waiting for transfers between devices: 34.9 us -> 35.9 us
    select_n x1 -> x0, other arithmetic: 1.82 us -> none  [body(): jnp.where(valid, succeeding_order_parameter, 0.0)]
    add x1 -> x2, other arithmetic: 0.28 us -> 2.06 us  [the longest x1 1.78 us: advance_solver_step(): new_phase = phase_now + TIME_STEP * growth]
    ppermute x8, starting transfers between devices: 31.9 us -> 30.4 us  [from_behind(): return lax.ppermute(block, axis, route)]
    ppermute x8, waiting for transfers between devices: 34.9 us -> 35.9 us  [from_behind(): return lax.ppermute(block, axis, route)]
  transfers between devices with their start and end apart: 8 -> 8, of which waited for: 8 -> 8; matrix products, arithmetic and copies ran while one was open for 1% -> 0% of each run, Pallas kernels for 0% -> 0%
where the time goes in v12:
time: 96.7 us; the launch traced here: 96.4 us
  waiting for transfers between devices  35.9 us (37%)
  starting transfers between devices  30.4 us (31%)
  other arithmetic  25.2 us (26%)
  local copies, waits for them, and re-layouts  3.56 us (4%)
  between operations  1.29 us (1%)
    ppermute x8, waiting for transfers between devices, from_behind(): return lax.ppermute(block, axis, route)  35.9 us
    ppermute x8, starting transfers between devices, from_behind(): return lax.ppermute(block, axis, route)  30.4 us
    neg x2, other arithmetic, advance_solver_step(): grad_x = 0.5 * (padded[1:-1, 1:-1, 2:] - padded[1:-1, 1:-1, :-2])  6.27 us
    neg x2, other arithmetic, advance_solver_step(): grad_y = 0.5 * (padded[1:-1, 2:, 1:-1] - padded[1:-1, :-2, 1:-1])  3.46 us
    add_any x2, other arithmetic, advance_solver_step(): 1.0 - phase_now  2.62 us
    mul x2, other arithmetic, advance_solver_step(): ENERGY_SCALE * (aniso_sq * grad_z + factor_a * grad_z * (sq_z - quartic *...  2.47 us
    slice x2, local copies, waits for them, and re-layouts, packed_z_halo(): tails = jnp.concatenate([f[size - w:] for f, w in zip(fields, widths)], 0)  2.01 us
  transfers between devices with their start and end apart: 8, of which 8 were waited for; matrix products, arithmetic and copies ran while one was open for 0% of the time, Pallas kernels for 0%

profile of v12, /device:TPU:14, one launch (start us, length us, event | category | flops | bytes accessed | tf_op | source)
XLA Modules:
  0.0 96.4 jit_solution(7804557883422386816)
XLA Ops:
  0.7 1.1 %fusion.122 = (f32[4,16,512]{2,1,0:T(8,128)S(1)}, f32[4,16,512]{2,1,0:T(8,128)S(1)}) fusion(f32[8,16,512]{2,1,0:T(8,128)} %param.5), kind=kLoop, calls=%fused_computation.302 | loop fusion | bytes 524288 | tf_op jit(solution)/shard_map/slice | solution.py:41
  1.7 1.0 fusion.123
  2.7 1.9 %collective-permute-start = (f32[8,16,512]{2,1,0:T(8,128)S(1)}, f32[8,16,512]{2,1,0:T(8,128)S(1)}, u32[]{:S(2)}, u32[]{:S(2)}) collective-permute-start(f32[8,16,512]{2,1,0:T(8,128)S(1)} %pad_maximum_fusion.5), channel_id=1, source_target_pairs={{0,8},{8,16},{16,24},{24,32},{32,40},{40,48},{48,56},{56,64},{64,7... | collective-permute-start | bytes 786440 | tf_op jit(solution)/shard_map/ppermute | solution.py:19
  4.7 7.9 %collective-permute-start.1 = (f32[8,16,512]{2,1,0:T(8,128)S(1)}, f32[8,16,512]{2,1,0:T(8,128)S(1)}, u32[]{:S(2)}, u32[]{:S(2)}) collective-permute-start(f32[8,16,512]{2,1,0:T(8,128)S(1)} %pad_maximum_fusion.6), channel_id=1, source_target_pairs={{8,0},{16,8},{24,16},{32,24},{40,32},{48,40},{56,48},{64,56},{72,6... | collective-permute-start | bytes 786440 | tf_op jit(solution)/shard_map/ppermute | solution.py:19
  12.6 2.6 %collective-permute-done = f32[8,16,512]{2,1,0:T(8,128)S(1)} collective-permute-done((f32[8,16,512]{2,1,0:T(8,128)S(1)}, f32[8,16,512]{2,1,0:T(8,128)S(1)}, u32[]{:S(2)}, u32[]{:S(2)}) %collective-permute-start) | collective-permute-done | bytes 262176 | tf_op jit(solution)/shard_map/ppermute | solution.py:19
  15.3 4.0 %collective-permute-done.1 = f32[8,16,512]{2,1,0:T(8,128)S(1)} collective-permute-done((f32[8,16,512]{2,1,0:T(8,128)S(1)}, f32[8,16,512]{2,1,0:T(8,128)S(1)}, u32[]{:S(2)}, u32[]{:S(2)}) %collective-permute-start.1) | collective-permute-done | bytes 262176 | tf_op jit(solution)/shard_map/ppermute | solution.py:19
  19.6 0.1 maximum_maximum_fusion.2
  19.6 0.1 maximum_maximum_fusion.1
  19.7 1.9 %collective-permute-start.2 = (f32[28,4,512]{2,1,0:T(4,128)S(1)}, f32[28,4,512]{2,1,0:T(4,128)S(1)}, u32[]{:S(2)}, u32[]{:S(2)}) collective-permute-start(f32[28,4,512]{2,1,0:T(4,128)S(1)} %maximum_maximum_fusion.2), channel_id=1, source_target_pairs={{0,1},{1,2},{2,3},{3,4},{4,5},{5,6},{6,7},{8,9},{9,10},{10,11},{11... | collective-permute-start | bytes 688136 | tf_op jit(solution)/shard_map/ppermute | solution.py:19
  21.7 4.8 %collective-permute-start.3 = (f32[28,4,512]{2,1,0:T(4,128)S(1)}, f32[28,4,512]{2,1,0:T(4,128)S(1)}, u32[]{:S(2)}, u32[]{:S(2)}) collective-permute-start(f32[28,4,512]{2,1,0:T(4,128)S(1)} %maximum_maximum_fusion.1), channel_id=1, source_target_pairs={{1,0},{2,1},{3,2},{4,3},{5,4},{6,5},{7,6},{9,8},{10,9},{11,10},{12... | collective-permute-start | bytes 688136 | tf_op jit(solution)/shard_map/ppermute | solution.py:19
  26.5 4.5 %collective-permute-done.2 = f32[28,4,512]{2,1,0:T(4,128)S(1)} collective-permute-done((f32[28,4,512]{2,1,0:T(4,128)S(1)}, f32[28,4,512]{2,1,0:T(4,128)S(1)}, u32[]{:S(2)}, u32[]{:S(2)}) %collective-permute-start.2) | collective-permute-done | bytes 229408 | tf_op jit(solution)/shard_map/ppermute | solution.py:19
  31.1 4.2 %collective-permute-done.3 = f32[28,4,512]{2,1,0:T(4,128)S(1)} collective-permute-done((f32[28,4,512]{2,1,0:T(4,128)S(1)}, f32[28,4,512]{2,1,0:T(4,128)S(1)}, u32[]{:S(2)}, u32[]{:S(2)}) %collective-permute-start.3) | collective-permute-done | bytes 229408 | tf_op jit(solution)/shard_map/ppermute | solution.py:19
  35.5 0.7 maximum_maximum_fusion
  36.1 0.2 slice_bitcast_fusion
  36.3 1.4 %add_multiply_fusion.5 = (f32[14,22,514]{2,1,0:T(8,128)S(1)}, f32[14,22,514]{2,1,0:T(8,128)S(1)}, f32[14,22,514]{2,1,0:T(8,128)S(1)}, f32[14,22,514]{2,1,0:T(8,1...) fusion(f32[16,24,512]{2,1,0:T(8,128)S(1)} %get-tuple-element.65), kind=kLoop, calls=%fused_computation.67 | loop fusion | flops 5224296 | bytes 5219168 | tf_op jit(solution)/shard_map/mul | solution.py:197
  37.8 0.8 add_multiply_fusion.4
  38.5 1.8 %multiply_add_fusion.8 = (f32[12,20,512]{2,1,0:T(8,128)S(1)}, f32[12,20,512]{2,1,0:T(8,128)S(1)}, f32[12,20,512]{2,1,0:T(8,128)S(1)}, f32[12,20,512]{2,1,0:T(8,128)S(1)}, f32[12,20,512]{2,1,0:T(8,128)S(1)}) fusion(f32[16,24,512]{2,1,0:T(8,128)S(1)} %get-tuple-element.64, f32[16,24,512]{2,1,0:T(8,128)S(1)} %get-tuple-element.65, ...), kind=kLoop, calls=%fused_computation.149 | loop fusion | flops 2580480 | bytes 8847360 | tf_op jit(solution)/shard_map/add | solution.py:209
  40.3 0.4 pad_slice_fusion.17
  40.7 1.1 %add_multiply_fusion.8 = (f32[10,18,514]{2,1,0:T(8,128)S(1)}, f32[10,18,514]{2,1,0:T(8,128)S(1)}, f32[10,18,514]{2,1,0:T(8,128)S(1)}, f32[10,18,514]{2,1,0:T(8,128)S(1)}) fusion(f32[12,20,512]{2,1,0:T(8,128)S(1)} %get-tuple-element.42), kind=kLoop, calls=%fused_computation.114 | loop fusion | flops 3053160 | bytes 1971840 | tf_op jit(solution)/shard_map/jvp()/mul | solution.py:197
  41.8 0.6 fusion.83
  42.3 0.5 fusion.63
  42.8 2.7 %fusion.106 = (f32[10,18,514]{2,1,0:T(8,128)S(1)}, f32[10,18,514]{2,1,0:T(8,128)S(1)}, f32[10,18,514]{2,1,0:T(8,128)S(1)}, f32[10,18,514]{2,1,0:T(8,128)S(1)}, f32[10,18,514]{2,1,0:T(8,128)S(1)}) fusion(f32[10,18,514]{2,1,0:T(8,128)S(1)} %get-tuple-element.16, f32[8,16,512]{2,1,0:T(8,128)S(1)} %get-tuple-element.114, ...), kind=kLoop, calls=%fused_computation.294 | loop fusion | flops 8604360 | bytes 3484928 | tf_op jit(solution)/shard_map/transpose(jvp())/neg | solution.py:188
  45.6 1.5 %fusion.108 = (f32[10,18,514]{2,1,0:T(8,128)S(1)}, f32[10,18,514]{2,1,0:T(8,128)S(1)}, f32[10,18,514]{2,1,0:T(8,128)S(1)}, f32[10,18,514]{2,1,0:T(8,128)S(1)}, f32[10,18,514]{2,1,0:T(8,128)S(1)}) fusion(f32[10,18,514]{2,1,0:T(8,128)S(1)} %get-tuple-element.17, f32[10,18,514]{2,1,0:T(8,128)S(1)} %get-tuple-element.37, ...), kind=kLoop, calls=%fused_computation.295 | loop fusion | flops 5643720 | bytes 4225088 | tf_op jit(solution)/shard_map/transpose(jvp())/neg | solution.py:187
  47.1 0.2 broadcast_multiply_fusion
  47.4 2.1 %fusion.42 = (f32[12,20,512]{2,1,0:T(8,128)S(1)}, f32[12,20,512]{2,1,0:T(8,128)S(1)}) fusion(f32[16,24,512]{2,1,0:T(8,128)S(1)} %get-tuple-element.64, f32[16,24,512]{2,1,0:T(8,128)S(1)} %get-tuple-element.63, f32[16,24,512]{2,1,0:T(8,128)S(1)} %get-tuple-element.65, f32[8,16,512]{2,1,0:T(8,128)S(1)} %get-tuple-element.31, ...), kind=kLoop, calls=%fused_computation.125 | loop fusion | flops 4300800 | bytes 5464564 | tf_op jit(solution)/shard_map/transpose(jvp())/add_any | solution.py:207
  49.5 1.0 %fusion.104 = (f32[12,20,512]{2,1,0:T(8,128)S(1)}, f32[12,20,512]{2,1,0:T(8,128)S(1)}, f32[12,20,512]{2,1,0:T(8,128)S(1)}, f32[12,20,512]{2,1,0:T(8,128)S(1)}) fusion(f32[12,20,512]{2,1,0:T(8,128)S(1)} %get-tuple-element.20, f32[16,24,512]{2,1,0:T(8,128)S(1)} %get-tuple-element.64, f32[16,24,512]{2,1,0:T(8,128)S(1)} %get-tuple-element.63, ...), kind=kLoop, calls=%fused_computation.293 | loop fusion | flops 3563520 | bytes 5439540 | tf_op jit(solution)/shard_map/transpose(jvp())/neg | solution.py:202
  50.5 0.1 pad_bitcast_fusion
  50.8 3.5 %fusion.98 = (f32[14,22,514]{2,1,0:T(8,128)S(1)}, f32[14,22,514]{2,1,0:T(8,128)S(1)}, f32[14,22,514]{2,1,0:T(8,128)S(1)}, f32[14,22,514]{2,1,0:T(8,128)S(1)}) fusion(f32[14,22,514]{2,1,0:T(8,128)S(1)} %get-tuple-element.50, f32[14,22,514]{2,1,0:T(8,128)S(1)} %get-tuple-element.58, f32[14,22,514]{2,1,0:T(8,128)S(1)} %get-tuple-element.46, ...), kind=kLoop, calls=%fused_computation.290 | loop fusion | flops 13298208 | bytes 8582016 | tf_op jit(solution)/shard_map/transpose(jvp())/neg | solution.py:188
  54.3 1.9 %fusion.100 = (f32[14,22,514]{2,1,0:T(8,128)S(1)}, f32[14,22,514]{2,1,0:T(8,128)S(1)}, f32[14,22,514]{2,1,0:T(8,128)S(1)}, f32[14,22,514]{2,1,0:T(8,128)S(1)}) fusion(f32[14,22,514]{2,1,0:T(8,128)S(1)} %get-tuple-element.49, f32[14,22,514]{2,1,0:T(8,128)S(1)} %get-tuple-element.24, f32[14,22,514]{2,1,0:T(8,128)S(1)} %get-tuple-element.23, ...), kind=kLoop, calls=%fused_computation.291 | loop fusion | flops 7598976 | bytes 9215264 | tf_op jit(solution)/shard_map/transpose(jvp())/neg | solution.py:187
  56.2 1.2 %fusion.21 = f32[1,16,24,512]{3,2,1,0:T(8,128)S(1)} fusion(f32[14,22,514]{2,1,0:T(8,128)S(1)} %get-tuple-element.56, f32[14,22,514]{2,1,0:T(8,128)S(1)} %get-tuple-element.55, f32[14,22,514]{2,1,0:T(8,128)S(1)} %get-tuple-element.26, f32[14,22,514]{2,1,0:T(8,128)S(1)} %get-tuple-element.25, f32[14,22,514]{2,1,0:T(8,128)S(1)} %get-tuple-element.22, ...), kind=kLoop, calls=%fused_computation.76 | loop fusion | flops 1179648 | bytes 5077440 | tf_op jit(solution)/shard_map/stack | solution.py:287
  57.5 0.2 add_bitcast_fusion
  57.8 0.1 fusion.57
  57.9 0.1 fusion.59
  58.1 2.1 %collective-permute-start.5 = (f32[33,4,512]{2,1,0:T(4,128)S(1)}, f32[33,4,512]{2,1,0:T(4,128)S(1)}, u32[]{:S(2)}, u32[]{:S(2)}) collective-permute-start(f32[33,4,512]{2,1,0:T(4,128)S(1)} %fusion.59), channel_id=1, source_target_pairs={{1,0},{2,1},{3,2},{4,3},{5,4},{6,5},{7,6},{9,8},{10,9},{11,10},{12... | collective-permute-start | bytes 811016 | tf_op jit(solution)/shard_map/ppermute | solution.py:19
  60.2 4.0 %collective-permute-start.4 = (f32[33,4,512]{2,1,0:T(4,128)S(1)}, f32[33,4,512]{2,1,0:T(4,128)S(1)}, u32[]{:S(2)}, u32[]{:S(2)}) collective-permute-start(f32[33,4,512]{2,1,0:T(4,128)S(1)} %fusion.57), channel_id=1, source_target_pairs={{0,1},{1,2},{2,3},{3,4},{4,5},{5,6},{6,7},{8,9},{9,10},{10,11},{11... | collective-permute-start | bytes 811016 | tf_op jit(solution)/shard_map/ppermute | solution.py:19
  64.1 5.2 %collective-permute-done.5 = f32[33,4,512]{2,1,0:T(4,128)S(1)} collective-permute-done((f32[33,4,512]{2,1,0:T(4,128)S(1)}, f32[33,4,512]{2,1,0:T(4,128)S(1)}, u32[]{:S(2)}, u32[]{:S(2)}) %collective-permute-start.5) | collective-permute-done | bytes 270368 | tf_op jit(solution)/shard_map/ppermute | solution.py:19
  69.4 4.0 %collective-permute-done.4 = f32[33,4,512]{2,1,0:T(4,128)S(1)} collective-permute-done((f32[33,4,512]{2,1,0:T(4,128)S(1)}, f32[33,4,512]{2,1,0:T(4,128)S(1)}, u32[]{:S(2)}, u32[]{:S(2)}) %collective-permute-start.4) | collective-permute-done | bytes 270368 | tf_op jit(solution)/shard_map/ppermute | solution.py:19
  73.5 0.1 fusion.85
  73.6 0.1 fusion.86
  73.8 0.3 maximum_add_fusion
  74.0 0.4 fusion.1
  74.6 5.9 %collective-permute-start.7 = (f32[9,16,512]{2,1,0:T(8,128)S(1)}, f32[9,16,512]{2,1,0:T(8,128)S(1)}, u32[]{:S(2)}, u32[]{:S(2)}) collective-permute-start(f32[9,16,512]{2,1,0:T(8,128)S(1)} %pad_maximum_fusion.2), channel_id=1, source_target_pairs={{8,0},{16,8},{24,16},{32,24},{40,32},{48,40},{56,48},{64,56},{72,6... | collective-permute-start | bytes 884744 | tf_op jit(solution)/shard_map/ppermute | solution.py:19
  80.5 1.9 %collective-permute-start.6 = (f32[9,16,512]{2,1,0:T(8,128)S(1)}, f32[9,16,512]{2,1,0:T(8,128)S(1)}, u32[]{:S(2)}, u32[]{:S(2)}) collective-permute-start(f32[9,16,512]{2,1,0:T(8,128)S(1)} %pad_maximum_fusion.3), channel_id=1, source_target_pairs={{0,8},{8,16},{16,24},{24,32},{32,40},{40,48},{48,56},{56,64},{64,7... | collective-permute-start | bytes 884744 | tf_op jit(solution)/shard_map/ppermute | solution.py:19
  82.4 5.2 %collective-permute-done.7 = f32[9,16,512]{2,1,0:T(8,128)S(1)} collective-permute-done((f32[9,16,512]{2,1,0:T(8,128)S(1)}, f32[9,16,512]{2,1,0:T(8,128)S(1)}, u32[]{:S(2)}, u32[]{:S(2)}) %collective-permute-start.7) | collective-permute-done | bytes 294944 | tf_op jit(solution)/shard_map/ppermute | solution.py:19
  87.6 6.3 %collective-permute-done.6 = f32[9,16,512]{2,1,0:T(8,128)S(1)} collective-permute-done((f32[9,16,512]{2,1,0:T(8,128)S(1)}, f32[9,16,512]{2,1,0:T(8,128)S(1)}, u32[]{:S(2)}, u32[]{:S(2)}) %collective-permute-start.6) | collective-permute-done | bytes 294944 | tf_op jit(solution)/shard_map/ppermute | solution.py:19
  94.0 0.2 slice_add_fusion.3
  94.2 0.8 fusion.65
  95.0 1.4 %fusion.69 = f32[8,16,512]{2,1,0:T(8,128)} fusion(f32[3,4,16,512]{3,2,1,0:T(8,128)S(1)} %get-tuple-element.68, f32[3,4,16,512]{3,2,1,0:T(8,128)S(1)} %get-tuple-element.69, f32[10,18,514]{2,1,0:T(8,128)S(1)} %get-tuple-element.67, f32[10,18,514]{2,1,0:T(8,128)S(1)} %get-tuple-element.66, f32[10,18,514]{2,1,0:T(8,128)S(1)} %get-tuple-element.15, ...), kind=kLoop, calls=%fused_computation.192 | loop fusion | flops 1245184 | bytes 3670016 | tf_op jit(solution)/shard_map/add | solution.py:290
  (64 shorter events, 1.2 us)
Async XLA Ops:
  0.6 18.7 %copy-start = (f32[8,16,512]{2,1,0:T(8,128)S(1)}, f32[8,16,512]{2,1,0:T(8,128)}, u32[]{:S(2)}) copy-start(f32[8,16,512]{2,1,0:T(8,128)} %param.5) | copy-start | bytes 786436
  0.6 18.7 %copy-start.1 = (f32[8,16,512]{2,1,0:T(8,128)S(1)}, f32[8,16,512]{2,1,0:T(8,128)}, u32[]{:S(2)}) copy-start(f32[8,16,512]{2,1,0:T(8,128)} %param.6) | copy-start | bytes 786436
  0.7 18.7 %copy-start.2 = (f32[8,16,512]{2,1,0:T(8,128)S(1)}, f32[8,16,512]{2,1,0:T(8,128)}, u32[]{:S(2)}) copy-start(f32[8,16,512]{2,1,0:T(8,128)} %param.7) | copy-start | bytes 786436
  2.7 12.6 %collective-permute-start = (f32[8,16,512]{2,1,0:T(8,128)S(1)}, f32[8,16,512]{2,1,0:T(8,128)S(1)}, u32[]{:S(2)}, u32[]{:S(2)}) collective-permute-start(f32[8,16,512]{2,1,0:T(8,128)S(1)} %pad_maximum_fusion.5), channel_id=1, source_target_pairs={{0,8},{8,16},{16,24},{24,32},{32,40},{40,48},{48,56},{56,64},{64,7... | collective-permute-start | bytes 786440 | tf_op jit(solution)/shard_map/ppermute | solution.py:19
  4.7 14.6 %collective-permute-start.1 = (f32[8,16,512]{2,1,0:T(8,128)S(1)}, f32[8,16,512]{2,1,0:T(8,128)S(1)}, u32[]{:S(2)}, u32[]{:S(2)}) collective-permute-start(f32[8,16,512]{2,1,0:T(8,128)S(1)} %pad_maximum_fusion.6), channel_id=1, source_target_pairs={{8,0},{16,8},{24,16},{32,24},{40,32},{48,40},{56,48},{64,56},{72,6... | collective-permute-start | bytes 786440 | tf_op jit(solution)/shard_map/ppermute | solution.py:19
  19.4 2.2 %copy-start.3 = (f32[8,16,512]{2,1,0:T(8,128)S(1)}, f32[8,16,512]{2,1,0:T(8,128)}, u32[]{:S(2)}) copy-start(f32[8,16,512]{2,1,0:T(8,128)} %param.9) | copy-start | bytes 786436
  19.7 11.3 %collective-permute-start.2 = (f32[28,4,512]{2,1,0:T(4,128)S(1)}, f32[28,4,512]{2,1,0:T(4,128)S(1)}, u32[]{:S(2)}, u32[]{:S(2)}) collective-permute-start(f32[28,4,512]{2,1,0:T(4,128)S(1)} %maximum_maximum_fusion.2), channel_id=1, source_target_pairs={{0,1},{1,2},{2,3},{3,4},{4,5},{5,6},{6,7},{8,9},{9,10},{10,11},{11... | collective-permute-start | bytes 688136 | tf_op jit(solution)/shard_map/ppermute | solution.py:19
  21.7 13.6 %collective-permute-start.3 = (f32[28,4,512]{2,1,0:T(4,128)S(1)}, f32[28,4,512]{2,1,0:T(4,128)S(1)}, u32[]{:S(2)}, u32[]{:S(2)}) collective-permute-start(f32[28,4,512]{2,1,0:T(4,128)S(1)} %maximum_maximum_fusion.1), channel_id=1, source_target_pairs={{1,0},{2,1},{3,2},{4,3},{5,4},{6,5},{7,6},{9,8},{10,9},{11,10},{12... | collective-permute-start | bytes 688136 | tf_op jit(solution)/shard_map/ppermute | solution.py:19
  40.3 1.4 %copy-start.4 = (f32[8,16,512]{2,1,0:T(8,128)S(1)}, f32[8,16,512]{2,1,0:T(8,128)}, u32[]{:S(2)}) copy-start(f32[8,16,512]{2,1,0:T(8,128)} %param.8) | copy-start | bytes 786436
  58.1 11.2 %collective-permute-start.5 = (f32[33,4,512]{2,1,0:T(4,128)S(1)}, f32[33,4,512]{2,1,0:T(4,128)S(1)}, u32[]{:S(2)}, u32[]{:S(2)}) collective-permute-start(f32[33,4,512]{2,1,0:T(4,128)S(1)} %fusion.59), channel_id=1, source_target_pairs={{1,0},{2,1},{3,2},{4,3},{5,4},{6,5},{7,6},{9,8},{10,9},{11,10},{12... | collective-permute-start | bytes 811016 | tf_op jit(solution)/shard_map/ppermute | solution.py:19
  60.2 13.2 %collective-permute-start.4 = (f32[33,4,512]{2,1,0:T(4,128)S(1)}, f32[33,4,512]{2,1,0:T(4,128)S(1)}, u32[]{:S(2)}, u32[]{:S(2)}) collective-permute-start(f32[33,4,512]{2,1,0:T(4,128)S(1)} %fusion.57), channel_id=1, source_target_pairs={{0,1},{1,2},{2,3},{3,4},{4,5},{5,6},{6,7},{8,9},{9,10},{10,11},{11... | collective-permute-start | bytes 811016 | tf_op jit(solution)/shard_map/ppermute | solution.py:19
  74.6 13.0 %collective-permute-start.7 = (f32[9,16,512]{2,1,0:T(8,128)S(1)}, f32[9,16,512]{2,1,0:T(8,128)S(1)}, u32[]{:S(2)}, u32[]{:S(2)}) collective-permute-start(f32[9,16,512]{2,1,0:T(8,128)S(1)} %pad_maximum_fusion.2), channel_id=1, source_target_pairs={{8,0},{16,8},{24,16},{32,24},{40,32},{48,40},{56,48},{64,56},{72,6... | collective-permute-start | bytes 884744 | tf_op jit(solution)/shard_map/ppermute | solution.py:19
  80.5 13.4 %collective-permute-start.6 = (f32[9,16,512]{2,1,0:T(8,128)S(1)}, f32[9,16,512]{2,1,0:T(8,128)S(1)}, u32[]{:S(2)}, u32[]{:S(2)}) collective-permute-start(f32[9,16,512]{2,1,0:T(8,128)S(1)} %pad_maximum_fusion.3), channel_id=1, source_target_pairs={{0,8},{8,16},{16,24},{24,32},{32,40},{40,48},{48,56},{56,64},{64,7... | collective-permute-start | bytes 884744 | tf_op jit(solution)/shard_map/ppermute | solution.py:19

commit v13 on v12

--- a/solution.py
+++ b/solution.py
@@ -274,7 +274,6 @@
     halfway_order_parameter, halfway_heat_level, latest_kinetic_rate = sensitivity_latest(
         (order_parameter_adjoint_seed, heat_level_adjoint_seed)
     )
-    halfway_order_parameter = jnp.where(valid, halfway_order_parameter, 0.0)
     halfway_heat_level = jnp.where(valid, halfway_heat_level, 0.0)
     discarded_result, prior_backward_sweep = jax.vjp(
         advance_solver_step, phase_wide, temp_wide, rate_wide[2:-2, 2:-2]

time: 96.7 us -> 96.7 us (level)
  no operation moved by 1% of the time
where the time goes in v13:
time: 96.7 us; the launch traced here: 96.3 us
  waiting for transfers between devices  35.9 us (37%)
  starting transfers between devices  30.4 us (31%)
  other arithmetic  25.1 us (26%)
  local copies, waits for them, and re-layouts  3.56 us (4%)
  between operations  1.29 us (1%)
    ppermute x8, waiting for transfers between devices, from_behind(): return lax.ppermute(block, axis, route)  35.9 us
    ppermute x8, starting transfers between devices, from_behind(): return lax.ppermute(block, axis, route)  30.4 us
    neg x2, other arithmetic, advance_solver_step(): grad_x = 0.5 * (padded[1:-1, 1:-1, 2:] - padded[1:-1, 1:-1, :-2])  6.27 us
    neg x2, other arithmetic, advance_solver_step(): grad_y = 0.5 * (padded[1:-1, 2:, 1:-1] - padded[1:-1, :-2, 1:-1])  3.46 us
    add_any x2, other arithmetic, advance_solver_step(): 1.0 - phase_now  2.58 us
    mul x2, other arithmetic, advance_solver_step(): ENERGY_SCALE * (aniso_sq * grad_z + factor_a * grad_z * (sq_z - quartic *...  2.47 us
    slice x2, local copies, waits for them, and re-layouts, packed_z_halo(): tails = jnp.concatenate([f[size - w:] for f, w in zip(fields, widths)], 0)  2.01 us
  transfers between devices with their start and end apart: 8, of which 8 were waited for; matrix products, arithmetic and copies ran while one was open for 0% of the time, Pallas kernels for 0%

profile of v13, /device:TPU:14, one launch (start us, length us, event | category | flops | bytes accessed | tf_op | source)
XLA Modules:
  0.0 96.3 jit_solution(14327080303906718951)
XLA Ops:
  0.7 1.1 %fusion.121 = (f32[4,16,512]{2,1,0:T(8,128)S(1)}, f32[4,16,512]{2,1,0:T(8,128)S(1)}) fusion(f32[8,16,512]{2,1,0:T(8,128)} %param.5), kind=kLoop, calls=%fused_computation.300 | loop fusion | bytes 524288 | tf_op jit(solution)/shard_map/slice | solution.py:41
  1.7 1.0 fusion.122
  2.7 1.9 %collective-permute-start = (f32[8,16,512]{2,1,0:T(8,128)S(1)}, f32[8,16,512]{2,1,0:T(8,128)S(1)}, u32[]{:S(2)}, u32[]{:S(2)}) collective-permute-start(f32[8,16,512]{2,1,0:T(8,128)S(1)} %pad_maximum_fusion.5), channel_id=1, source_target_pairs={{0,8},{8,16},{16,24},{24,32},{32,40},{40,48},{48,56},{56,64},{64,7... | collective-permute-start | bytes 786440 | tf_op jit(solution)/shard_map/ppermute | solution.py:19
  4.7 7.9 %collective-permute-start.1 = (f32[8,16,512]{2,1,0:T(8,128)S(1)}, f32[8,16,512]{2,1,0:T(8,128)S(1)}, u32[]{:S(2)}, u32[]{:S(2)}) collective-permute-start(f32[8,16,512]{2,1,0:T(8,128)S(1)} %pad_maximum_fusion.6), channel_id=1, source_target_pairs={{8,0},{16,8},{24,16},{32,24},{40,32},{48,40},{56,48},{64,56},{72,6... | collective-permute-start | bytes 786440 | tf_op jit(solution)/shard_map/ppermute | solution.py:19
  12.6 2.6 %collective-permute-done = f32[8,16,512]{2,1,0:T(8,128)S(1)} collective-permute-done((f32[8,16,512]{2,1,0:T(8,128)S(1)}, f32[8,16,512]{2,1,0:T(8,128)S(1)}, u32[]{:S(2)}, u32[]{:S(2)}) %collective-permute-start) | collective-permute-done | bytes 262176 | tf_op jit(solution)/shard_map/ppermute | solution.py:19
  15.3 4.0 %collective-permute-done.1 = f32[8,16,512]{2,1,0:T(8,128)S(1)} collective-permute-done((f32[8,16,512]{2,1,0:T(8,128)S(1)}, f32[8,16,512]{2,1,0:T(8,128)S(1)}, u32[]{:S(2)}, u32[]{:S(2)}) %collective-permute-start.1) | collective-permute-done | bytes 262176 | tf_op jit(solution)/shard_map/ppermute | solution.py:19
  19.6 0.1 maximum_maximum_fusion.2
  19.6 0.1 maximum_maximum_fusion.1
  19.7 1.9 %collective-permute-start.2 = (f32[28,4,512]{2,1,0:T(4,128)S(1)}, f32[28,4,512]{2,1,0:T(4,128)S(1)}, u32[]{:S(2)}, u32[]{:S(2)}) collective-permute-start(f32[28,4,512]{2,1,0:T(4,128)S(1)} %maximum_maximum_fusion.2), channel_id=1, source_target_pairs={{0,1},{1,2},{2,3},{3,4},{4,5},{5,6},{6,7},{8,9},{9,10},{10,11},{11... | collective-permute-start | bytes 688136 | tf_op jit(solution)/shard_map/ppermute | solution.py:19
  21.7 4.8 %collective-permute-start.3 = (f32[28,4,512]{2,1,0:T(4,128)S(1)}, f32[28,4,512]{2,1,0:T(4,128)S(1)}, u32[]{:S(2)}, u32[]{:S(2)}) collective-permute-start(f32[28,4,512]{2,1,0:T(4,128)S(1)} %maximum_maximum_fusion.1), channel_id=1, source_target_pairs={{1,0},{2,1},{3,2},{4,3},{5,4},{6,5},{7,6},{9,8},{10,9},{11,10},{12... | collective-permute-start | bytes 688136 | tf_op jit(solution)/shard_map/ppermute | solution.py:19
  26.5 4.5 %collective-permute-done.2 = f32[28,4,512]{2,1,0:T(4,128)S(1)} collective-permute-done((f32[28,4,512]{2,1,0:T(4,128)S(1)}, f32[28,4,512]{2,1,0:T(4,128)S(1)}, u32[]{:S(2)}, u32[]{:S(2)}) %collective-permute-start.2) | collective-permute-done | bytes 229408 | tf_op jit(solution)/shard_map/ppermute | solution.py:19
  31.1 4.2 %collective-permute-done.3 = f32[28,4,512]{2,1,0:T(4,128)S(1)} collective-permute-done((f32[28,4,512]{2,1,0:T(4,128)S(1)}, f32[28,4,512]{2,1,0:T(4,128)S(1)}, u32[]{:S(2)}, u32[]{:S(2)}) %collective-permute-start.3) | collective-permute-done | bytes 229408 | tf_op jit(solution)/shard_map/ppermute | solution.py:19
  35.5 0.7 maximum_maximum_fusion
  36.1 0.2 slice_bitcast_fusion
  36.3 1.4 %add_multiply_fusion.5 = (f32[14,22,514]{2,1,0:T(8,128)S(1)}, f32[14,22,514]{2,1,0:T(8,128)S(1)}, f32[14,22,514]{2,1,0:T(8,128)S(1)}, f32[14,22,514]{2,1,0:T(8,1...) fusion(f32[16,24,512]{2,1,0:T(8,128)S(1)} %get-tuple-element.65), kind=kLoop, calls=%fused_computation.67 | loop fusion | flops 5224296 | bytes 5219168 | tf_op jit(solution)/shard_map/mul | solution.py:197
  37.8 0.8 add_multiply_fusion.4
  38.5 1.8 %multiply_add_fusion.8 = (f32[12,20,512]{2,1,0:T(8,128)S(1)}, f32[12,20,512]{2,1,0:T(8,128)S(1)}, f32[12,20,512]{2,1,0:T(8,128)S(1)}, f32[12,20,512]{2,1,0:T(8,128)S(1)}, f32[12,20,512]{2,1,0:T(8,128)S(1)}) fusion(f32[16,24,512]{2,1,0:T(8,128)S(1)} %get-tuple-element.64, f32[16,24,512]{2,1,0:T(8,128)S(1)} %get-tuple-element.65, ...), kind=kLoop, calls=%fused_computation.148 | loop fusion | flops 2580480 | bytes 8847360 | tf_op jit(solution)/shard_map/add | solution.py:209
  40.3 0.4 pad_slice_fusion.17
  40.7 1.1 %add_multiply_fusion.8 = (f32[10,18,514]{2,1,0:T(8,128)S(1)}, f32[10,18,514]{2,1,0:T(8,128)S(1)}, f32[10,18,514]{2,1,0:T(8,128)S(1)}, f32[10,18,514]{2,1,0:T(8,128)S(1)}) fusion(f32[12,20,512]{2,1,0:T(8,128)S(1)} %get-tuple-element.42), kind=kLoop, calls=%fused_computation.114 | loop fusion | flops 3053160 | bytes 1971840 | tf_op jit(solution)/shard_map/jvp()/mul | solution.py:197
  41.8 0.6 fusion.82
  42.3 0.5 fusion.62
  42.8 2.7 %fusion.105 = (f32[10,18,514]{2,1,0:T(8,128)S(1)}, f32[10,18,514]{2,1,0:T(8,128)S(1)}, f32[10,18,514]{2,1,0:T(8,128)S(1)}, f32[10,18,514]{2,1,0:T(8,128)S(1)}, f32[10,18,514]{2,1,0:T(8,128)S(1)}) fusion(f32[10,18,514]{2,1,0:T(8,128)S(1)} %get-tuple-element.16, f32[8,16,512]{2,1,0:T(8,128)S(1)} %get-tuple-element.114, ...), kind=kLoop, calls=%fused_computation.292 | loop fusion | flops 8604360 | bytes 3484928 | tf_op jit(solution)/shard_map/transpose(jvp())/neg | solution.py:188
  45.6 1.5 %fusion.107 = (f32[10,18,514]{2,1,0:T(8,128)S(1)}, f32[10,18,514]{2,1,0:T(8,128)S(1)}, f32[10,18,514]{2,1,0:T(8,128)S(1)}, f32[10,18,514]{2,1,0:T(8,128)S(1)}, f32[10,18,514]{2,1,0:T(8,128)S(1)}) fusion(f32[10,18,514]{2,1,0:T(8,128)S(1)} %get-tuple-element.17, f32[10,18,514]{2,1,0:T(8,128)S(1)} %get-tuple-element.37, ...), kind=kLoop, calls=%fused_computation.293 | loop fusion | flops 5643720 | bytes 4225088 | tf_op jit(solution)/shard_map/transpose(jvp())/neg | solution.py:187
  47.1 0.2 broadcast_multiply_fusion
  47.4 2.1 %fusion.42 = (f32[12,20,512]{2,1,0:T(8,128)S(1)}, f32[12,20,512]{2,1,0:T(8,128)S(1)}) fusion(f32[16,24,512]{2,1,0:T(8,128)S(1)} %get-tuple-element.64, f32[16,24,512]{2,1,0:T(8,128)S(1)} %get-tuple-element.63, f32[16,24,512]{2,1,0:T(8,128)S(1)} %get-tuple-element.65, f32[8,16,512]{2,1,0:T(8,128)S(1)} %get-tuple-element.31, ...), kind=kLoop, calls=%fused_computation.125 | loop fusion | flops 4177920 | bytes 5464564 | tf_op jit(solution)/shard_map/transpose(jvp())/add_any | solution.py:207
  49.5 1.0 %fusion.103 = (f32[12,20,512]{2,1,0:T(8,128)S(1)}, f32[12,20,512]{2,1,0:T(8,128)S(1)}, f32[12,20,512]{2,1,0:T(8,128)S(1)}, f32[12,20,512]{2,1,0:T(8,128)S(1)}) fusion(f32[12,20,512]{2,1,0:T(8,128)S(1)} %get-tuple-element.20, f32[16,24,512]{2,1,0:T(8,128)S(1)} %get-tuple-element.64, f32[16,24,512]{2,1,0:T(8,128)S(1)} %get-tuple-element.63, ...), kind=kLoop, calls=%fused_computation.291 | loop fusion | flops 3563520 | bytes 5439540 | tf_op jit(solution)/shard_map/transpose(jvp())/neg | solution.py:202
  50.5 0.1 pad_bitcast_fusion
  50.7 3.5 %fusion.97 = (f32[14,22,514]{2,1,0:T(8,128)S(1)}, f32[14,22,514]{2,1,0:T(8,128)S(1)}, f32[14,22,514]{2,1,0:T(8,128)S(1)}, f32[14,22,514]{2,1,0:T(8,128)S(1)}) fusion(f32[14,22,514]{2,1,0:T(8,128)S(1)} %get-tuple-element.50, f32[14,22,514]{2,1,0:T(8,128)S(1)} %get-tuple-element.58, f32[14,22,514]{2,1,0:T(8,128)S(1)} %get-tuple-element.46, ...), kind=kLoop, calls=%fused_computation.288 | loop fusion | flops 13298208 | bytes 8582016 | tf_op jit(solution)/shard_map/transpose(jvp())/neg | solution.py:188
  54.2 1.9 %fusion.99 = (f32[14,22,514]{2,1,0:T(8,128)S(1)}, f32[14,22,514]{2,1,0:T(8,128)S(1)}, f32[14,22,514]{2,1,0:T(8,128)S(1)}, f32[14,22,514]{2,1,0:T(8,128)S(1)}) fusion(f32[14,22,514]{2,1,0:T(8,128)S(1)} %get-tuple-element.49, f32[14,22,514]{2,1,0:T(8,128)S(1)} %get-tuple-element.24, f32[14,22,514]{2,1,0:T(8,128)S(1)} %get-tuple-element.23, ...), kind=kLoop, calls=%fused_computation.289 | loop fusion | flops 7598976 | bytes 9215264 | tf_op jit(solution)/shard_map/transpose(jvp())/neg | solution.py:187
  56.2 1.2 %fusion.21 = f32[1,16,24,512]{3,2,1,0:T(8,128)S(1)} fusion(f32[14,22,514]{2,1,0:T(8,128)S(1)} %get-tuple-element.56, f32[14,22,514]{2,1,0:T(8,128)S(1)} %get-tuple-element.55, f32[14,22,514]{2,1,0:T(8,128)S(1)} %get-tuple-element.26, f32[14,22,514]{2,1,0:T(8,128)S(1)} %get-tuple-element.25, f32[14,22,514]{2,1,0:T(8,128)S(1)} %get-tuple-element.22, ...), kind=kLoop, calls=%fused_computation.76 | loop fusion | flops 1179648 | bytes 5077440 | tf_op jit(solution)/shard_map/stack | solution.py:286
  57.5 0.2 add_bitcast_fusion
  57.8 0.1 fusion.56
  57.9 0.1 fusion.58
  58.0 2.1 %collective-permute-start.5 = (f32[33,4,512]{2,1,0:T(4,128)S(1)}, f32[33,4,512]{2,1,0:T(4,128)S(1)}, u32[]{:S(2)}, u32[]{:S(2)}) collective-permute-start(f32[33,4,512]{2,1,0:T(4,128)S(1)} %fusion.58), channel_id=1, source_target_pairs={{1,0},{2,1},{3,2},{4,3},{5,4},{6,5},{7,6},{9,8},{10,9},{11,10},{12... | collective-permute-start | bytes 811016 | tf_op jit(solution)/shard_map/ppermute | solution.py:19
  60.1 4.0 %collective-permute-start.4 = (f32[33,4,512]{2,1,0:T(4,128)S(1)}, f32[33,4,512]{2,1,0:T(4,128)S(1)}, u32[]{:S(2)}, u32[]{:S(2)}) collective-permute-start(f32[33,4,512]{2,1,0:T(4,128)S(1)} %fusion.56), channel_id=1, source_target_pairs={{0,1},{1,2},{2,3},{3,4},{4,5},{5,6},{6,7},{8,9},{9,10},{10,11},{11... | collective-permute-start | bytes 811016 | tf_op jit(solution)/shard_map/ppermute | solution.py:19
  64.1 5.2 %collective-permute-done.5 = f32[33,4,512]{2,1,0:T(4,128)S(1)} collective-permute-done((f32[33,4,512]{2,1,0:T(4,128)S(1)}, f32[33,4,512]{2,1,0:T(4,128)S(1)}, u32[]{:S(2)}, u32[]{:S(2)}) %collective-permute-start.5) | collective-permute-done | bytes 270368 | tf_op jit(solution)/shard_map/ppermute | solution.py:19
  69.3 4.0 %collective-permute-done.4 = f32[33,4,512]{2,1,0:T(4,128)S(1)} collective-permute-done((f32[33,4,512]{2,1,0:T(4,128)S(1)}, f32[33,4,512]{2,1,0:T(4,128)S(1)}, u32[]{:S(2)}, u32[]{:S(2)}) %collective-permute-start.4) | collective-permute-done | bytes 270368 | tf_op jit(solution)/shard_map/ppermute | solution.py:19
  73.4 0.1 fusion.84
  73.6 0.1 fusion.85
  73.7 0.3 maximum_add_fusion
  74.0 0.4 fusion.1
  74.5 5.9 %collective-permute-start.7 = (f32[9,16,512]{2,1,0:T(8,128)S(1)}, f32[9,16,512]{2,1,0:T(8,128)S(1)}, u32[]{:S(2)}, u32[]{:S(2)}) collective-permute-start(f32[9,16,512]{2,1,0:T(8,128)S(1)} %pad_maximum_fusion.2), channel_id=1, source_target_pairs={{8,0},{16,8},{24,16},{32,24},{40,32},{48,40},{56,48},{64,56},{72,6... | collective-permute-start | bytes 884744 | tf_op jit(solution)/shard_map/ppermute | solution.py:19
  80.4 1.9 %collective-permute-start.6 = (f32[9,16,512]{2,1,0:T(8,128)S(1)}, f32[9,16,512]{2,1,0:T(8,128)S(1)}, u32[]{:S(2)}, u32[]{:S(2)}) collective-permute-start(f32[9,16,512]{2,1,0:T(8,128)S(1)} %pad_maximum_fusion.3), channel_id=1, source_target_pairs={{0,8},{8,16},{16,24},{24,32},{32,40},{40,48},{48,56},{56,64},{64,7... | collective-permute-start | bytes 884744 | tf_op jit(solution)/shard_map/ppermute | solution.py:19
  82.4 5.2 %collective-permute-done.7 = f32[9,16,512]{2,1,0:T(8,128)S(1)} collective-permute-done((f32[9,16,512]{2,1,0:T(8,128)S(1)}, f32[9,16,512]{2,1,0:T(8,128)S(1)}, u32[]{:S(2)}, u32[]{:S(2)}) %collective-permute-start.7) | collective-permute-done | bytes 294944 | tf_op jit(solution)/shard_map/ppermute | solution.py:19
  87.6 6.3 %collective-permute-done.6 = f32[9,16,512]{2,1,0:T(8,128)S(1)} collective-permute-done((f32[9,16,512]{2,1,0:T(8,128)S(1)}, f32[9,16,512]{2,1,0:T(8,128)S(1)}, u32[]{:S(2)}, u32[]{:S(2)}) %collective-permute-start.6) | collective-permute-done | bytes 294944 | tf_op jit(solution)/shard_map/ppermute | solution.py:19
  94.0 0.2 slice_add_fusion.3
  94.2 0.8 fusion.64
  95.0 1.4 %fusion.68 = f32[8,16,512]{2,1,0:T(8,128)} fusion(f32[3,4,16,512]{3,2,1,0:T(8,128)S(1)} %get-tuple-element.68, f32[3,4,16,512]{3,2,1,0:T(8,128)S(1)} %get-tuple-element.69, f32[10,18,514]{2,1,0:T(8,128)S(1)} %get-tuple-element.67, f32[10,18,514]{2,1,0:T(8,128)S(1)} %get-tuple-element.66, f32[10,18,514]{2,1,0:T(8,128)S(1)} %get-tuple-element.15, ...), kind=kLoop, calls=%fused_computation.190 | loop fusion | flops 1245184 | bytes 3670016 | tf_op jit(solution)/shard_map/add | solution.py:289
  (64 shorter events, 1.2 us)
Async XLA Ops:
  0.6 18.7 %copy-start = (f32[8,16,512]{2,1,0:T(8,128)S(1)}, f32[8,16,512]{2,1,0:T(8,128)}, u32[]{:S(2)}) copy-start(f32[8,16,512]{2,1,0:T(8,128)} %param.5) | copy-start | bytes 786436
  0.6 18.7 %copy-start.1 = (f32[8,16,512]{2,1,0:T(8,128)S(1)}, f32[8,16,512]{2,1,0:T(8,128)}, u32[]{:S(2)}) copy-start(f32[8,16,512]{2,1,0:T(8,128)} %param.6) | copy-start | bytes 786436
  0.7 18.7 %copy-start.2 = (f32[8,16,512]{2,1,0:T(8,128)S(1)}, f32[8,16,512]{2,1,0:T(8,128)}, u32[]{:S(2)}) copy-start(f32[8,16,512]{2,1,0:T(8,128)} %param.7) | copy-start | bytes 786436
  2.7 12.6 %collective-permute-start = (f32[8,16,512]{2,1,0:T(8,128)S(1)}, f32[8,16,512]{2,1,0:T(8,128)S(1)}, u32[]{:S(2)}, u32[]{:S(2)}) collective-permute-start(f32[8,16,512]{2,1,0:T(8,128)S(1)} %pad_maximum_fusion.5), channel_id=1, source_target_pairs={{0,8},{8,16},{16,24},{24,32},{32,40},{40,48},{48,56},{56,64},{64,7... | collective-permute-start | bytes 786440 | tf_op jit(solution)/shard_map/ppermute | solution.py:19
  4.7 14.6 %collective-permute-start.1 = (f32[8,16,512]{2,1,0:T(8,128)S(1)}, f32[8,16,512]{2,1,0:T(8,128)S(1)}, u32[]{:S(2)}, u32[]{:S(2)}) collective-permute-start(f32[8,16,512]{2,1,0:T(8,128)S(1)} %pad_maximum_fusion.6), channel_id=1, source_target_pairs={{8,0},{16,8},{24,16},{32,24},{40,32},{48,40},{56,48},{64,56},{72,6... | collective-permute-start | bytes 786440 | tf_op jit(solution)/shard_map/ppermute | solution.py:19
  19.4 2.2 %copy-start.3 = (f32[8,16,512]{2,1,0:T(8,128)S(1)}, f32[8,16,512]{2,1,0:T(8,128)}, u32[]{:S(2)}) copy-start(f32[8,16,512]{2,1,0:T(8,128)} %param.9) | copy-start | bytes 786436
  19.7 11.3 %collective-permute-start.2 = (f32[28,4,512]{2,1,0:T(4,128)S(1)}, f32[28,4,512]{2,1,0:T(4,128)S(1)}, u32[]{:S(2)}, u32[]{:S(2)}) collective-permute-start(f32[28,4,512]{2,1,0:T(4,128)S(1)} %maximum_maximum_fusion.2), channel_id=1, source_target_pairs={{0,1},{1,2},{2,3},{3,4},{4,5},{5,6},{6,7},{8,9},{9,10},{10,11},{11... | collective-permute-start | bytes 688136 | tf_op jit(solution)/shard_map/ppermute | solution.py:19
  21.7 13.6 %collective-permute-start.3 = (f32[28,4,512]{2,1,0:T(4,128)S(1)}, f32[28,4,512]{2,1,0:T(4,128)S(1)}, u32[]{:S(2)}, u32[]{:S(2)}) collective-permute-start(f32[28,4,512]{2,1,0:T(4,128)S(1)} %maximum_maximum_fusion.1), channel_id=1, source_target_pairs={{1,0},{2,1},{3,2},{4,3},{5,4},{6,5},{7,6},{9,8},{10,9},{11,10},{12... | collective-permute-start | bytes 688136 | tf_op jit(solution)/shard_map/ppermute | solution.py:19
  40.3 1.4 %copy-start.4 = (f32[8,16,512]{2,1,0:T(8,128)S(1)}, f32[8,16,512]{2,1,0:T(8,128)}, u32[]{:S(2)}) copy-start(f32[8,16,512]{2,1,0:T(8,128)} %param.8) | copy-start | bytes 786436
  58.0 11.2 %collective-permute-start.5 = (f32[33,4,512]{2,1,0:T(4,128)S(1)}, f32[33,4,512]{2,1,0:T(4,128)S(1)}, u32[]{:S(2)}, u32[]{:S(2)}) collective-permute-start(f32[33,4,512]{2,1,0:T(4,128)S(1)} %fusion.58), channel_id=1, source_target_pairs={{1,0},{2,1},{3,2},{4,3},{5,4},{6,5},{7,6},{9,8},{10,9},{11,10},{12... | collective-permute-start | bytes 811016 | tf_op jit(solution)/shard_map/ppermute | solution.py:19
  60.1 13.2 %collective-permute-start.4 = (f32[33,4,512]{2,1,0:T(4,128)S(1)}, f32[33,4,512]{2,1,0:T(4,128)S(1)}, u32[]{:S(2)}, u32[]{:S(2)}) collective-permute-start(f32[33,4,512]{2,1,0:T(4,128)S(1)} %fusion.56), channel_id=1, source_target_pairs={{0,1},{1,2},{2,3},{3,4},{4,5},{5,6},{6,7},{8,9},{9,10},{10,11},{11... | collective-permute-start | bytes 811016 | tf_op jit(solution)/shard_map/ppermute | solution.py:19
  74.5 13.0 %collective-permute-start.7 = (f32[9,16,512]{2,1,0:T(8,128)S(1)}, f32[9,16,512]{2,1,0:T(8,128)S(1)}, u32[]{:S(2)}, u32[]{:S(2)}) collective-permute-start(f32[9,16,512]{2,1,0:T(8,128)S(1)} %pad_maximum_fusion.2), channel_id=1, source_target_pairs={{8,0},{16,8},{24,16},{32,24},{40,32},{48,40},{56,48},{64,56},{72,6... | collective-permute-start | bytes 884744 | tf_op jit(solution)/shard_map/ppermute | solution.py:19
  80.4 13.4 %collective-permute-start.6 = (f32[9,16,512]{2,1,0:T(8,128)S(1)}, f32[9,16,512]{2,1,0:T(8,128)S(1)}, u32[]{:S(2)}, u32[]{:S(2)}) collective-permute-start(f32[9,16,512]{2,1,0:T(8,128)S(1)} %pad_maximum_fusion.3), channel_id=1, source_target_pairs={{0,8},{8,16},{16,24},{24,32},{32,40},{40,48},{48,56},{56,64},{64,7... | collective-permute-start | bytes 884744 | tf_op jit(solution)/shard_map/ppermute | solution.py:19

commit v14 on v13

--- a/solution.py
+++ b/solution.py
@@ -281,12 +281,13 @@
     sensitivity_order_parameter, sensitivity_heat_level, early_mob = prior_backward_sweep(
         (halfway_order_parameter, halfway_heat_level)
     )
+    early_mob = early_mob.at[2:-2, 2:-2].add(latest_kinetic_rate)
     early_mob = jnp.pad(early_mob, ((2, 2), (2, 2), (0, 0)))
     folded = packed_y_fold(
         jnp.stack((sensitivity_order_parameter, sensitivity_heat_level, early_mob))
     )
     folded = packed_z_fold(folded, (4, 3, 2))
-    return (folded[0], folded[1], latest_kinetic_rate + folded[2])
+    return (folded[0], folded[1], folded[2])
 
 
 def solution(mesh):

time: 96.7 us -> 107 us (1.11)
  other arithmetic: 25.1 us -> 31.4 us
  local copies, waits for them, and re-layouts: 3.56 us -> 7.81 us
    neg x2, other arithmetic: 6.27 us -> 8.28 us  [advance_solver_step(): grad_x = 0.5 * (padded[1:-1, 1:-1, 2:] - padded[1:-1, 1:-1, :-2])]
    scatter-add x0 -> x1, local copies, waits for them, and re-layouts: none -> 1.82 us  [body(): early_mob = early_mob.at[2:-2, 2:-2].add(latest_kinetic_rate)]
    another operation x1, local copies, waits for them, and re-layouts: 0.08 us -> 1.31 us  [body(): jnp.stack((sensitivity_order_parameter, sensitivity_heat_level, early_mob))]
    unnamed x10 -> x32, local copies, waits for them, and re-layouts: 0.03 us -> 1.22 us
    mul x1, other arithmetic: 0.79 us -> 1.96 us  [advance_solver_step(): ENERGY_SCALE * (aniso_sq * grad_y + factor_a * grad_y * (sq_y - quartic *...]
    neg x1, other arithmetic: 0.98 us -> 2.12 us  [advance_solver_step(): flux_x[1:-1, 1:-1, 2:] - flux_x[1:-1, 1:-1, :-2]]
where the time goes in v14:
time: 107 us
  waiting for transfers between devices  36.1 us (34%)
  other arithmetic  31.4 us (29%)
  starting transfers between devices  30.2 us (28%)
  local copies, waits for them, and re-layouts  7.81 us (7%)
  between operations  1.38 us (1%)
    ppermute x8, waiting for transfers between devices, from_behind(): return lax.ppermute(block, axis, route)  36.1 us
    ppermute x8, starting transfers between devices, from_behind(): return lax.ppermute(block, axis, route)  30.2 us
    neg x2, other arithmetic, advance_solver_step(): grad_x = 0.5 * (padded[1:-1, 1:-1, 2:] - padded[1:-1, 1:-1, :-2])  8.28 us
    neg x2, other arithmetic, advance_solver_step(): grad_y = 0.5 * (padded[1:-1, 2:, 1:-1] - padded[1:-1, :-2, 1:-1])  3.46 us
    mul x2, other arithmetic, advance_solver_step(): ENERGY_SCALE * (aniso_sq * grad_z + factor_a * grad_z * (sq_z - quartic *...  3.43 us
    add_any x2, other arithmetic, advance_solver_step(): 1.0 - phase_now  3.38 us
  transfers between devices with their start and end apart: 8, of which 8 were waited for; matrix products, arithmetic and copies ran while one was open for 0% of the time, Pallas kernels for 0%

profile of v14, /device:TPU:14, one launch (start us, length us, event | category | flops | bytes accessed | tf_op | source)
XLA Modules:
  0.0 106.9 jit_solution(7564003564608286462)
XLA Ops:
  0.7 1.1 fusion.121
  1.7 1.0 fusion.122
  2.7 1.9 %collective-permute-start = (f32[8,16,512]{2,1,0:T(8,128)S(1)}, f32[8,16,512]{2,1,0:T(8,128)S(1)}, u32[]{:S(2)}, u32[]{:S(2)}) collective-permute-start(f32[8,16,512]{2,1,0:T(8,128)S(1)} %pad_maximum_fusion.5), channel_id=1, source_target_pairs={{0,8},{8,16},{16,24},{24,32},{32,40},{40,48},{48,56},{56,64},{64,7... | collective-permute-start | bytes 786440 | tf_op jit(solution)/shard_map/ppermute | solution.py:19
  4.7 7.9 %collective-permute-start.1 = (f32[8,16,512]{2,1,0:T(8,128)S(1)}, f32[8,16,512]{2,1,0:T(8,128)S(1)}, u32[]{:S(2)}, u32[]{:S(2)}) collective-permute-start(f32[8,16,512]{2,1,0:T(8,128)S(1)} %pad_maximum_fusion.6), channel_id=1, source_target_pairs={{8,0},{16,8},{24,16},{32,24},{40,32},{48,40},{56,48},{64,56},{72,6... | collective-permute-start | bytes 786440 | tf_op jit(solution)/shard_map/ppermute | solution.py:19
  12.6 2.6 %collective-permute-done = f32[8,16,512]{2,1,0:T(8,128)S(1)} collective-permute-done((f32[8,16,512]{2,1,0:T(8,128)S(1)}, f32[8,16,512]{2,1,0:T(8,128)S(1)}, u32[]{:S(2)}, u32[]{:S(2)}) %collective-permute-start) | collective-permute-done | bytes 262176 | tf_op jit(solution)/shard_map/ppermute | solution.py:19
  15.3 4.0 %collective-permute-done.1 = f32[8,16,512]{2,1,0:T(8,128)S(1)} collective-permute-done((f32[8,16,512]{2,1,0:T(8,128)S(1)}, f32[8,16,512]{2,1,0:T(8,128)S(1)}, u32[]{:S(2)}, u32[]{:S(2)}) %collective-permute-start.1) | collective-permute-done | bytes 262176 | tf_op jit(solution)/shard_map/ppermute | solution.py:19
  19.7 1.9 %collective-permute-start.2 = (f32[28,4,512]{2,1,0:T(4,128)S(1)}, f32[28,4,512]{2,1,0:T(4,128)S(1)}, u32[]{:S(2)}, u32[]{:S(2)}) collective-permute-start(f32[28,4,512]{2,1,0:T(4,128)S(1)} %maximum_maximum_fusion.2), channel_id=1, source_target_pairs={{0,1},{1,2},{2,3},{3,4},{4,5},{5,6},{6,7},{8,9},{9,10},{10,11},{11... | collective-permute-start | bytes 688136 | tf_op jit(solution)/shard_map/ppermute | solution.py:19
  21.7 4.8 %collective-permute-start.3 = (f32[28,4,512]{2,1,0:T(4,128)S(1)}, f32[28,4,512]{2,1,0:T(4,128)S(1)}, u32[]{:S(2)}, u32[]{:S(2)}) collective-permute-start(f32[28,4,512]{2,1,0:T(4,128)S(1)} %maximum_maximum_fusion.1), channel_id=1, source_target_pairs={{1,0},{2,1},{3,2},{4,3},{5,4},{6,5},{7,6},{9,8},{10,9},{11,10},{12... | collective-permute-start | bytes 688136 | tf_op jit(solution)/shard_map/ppermute | solution.py:19
  26.5 4.5 %collective-permute-done.2 = f32[28,4,512]{2,1,0:T(4,128)S(1)} collective-permute-done((f32[28,4,512]{2,1,0:T(4,128)S(1)}, f32[28,4,512]{2,1,0:T(4,128)S(1)}, u32[]{:S(2)}, u32[]{:S(2)}) %collective-permute-start.2) | collective-permute-done | bytes 229408 | tf_op jit(solution)/shard_map/ppermute | solution.py:19
  31.1 4.2 %collective-permute-done.3 = f32[28,4,512]{2,1,0:T(4,128)S(1)} collective-permute-done((f32[28,4,512]{2,1,0:T(4,128)S(1)}, f32[28,4,512]{2,1,0:T(4,128)S(1)}, u32[]{:S(2)}, u32[]{:S(2)}) %collective-permute-start.3) | collective-permute-done | bytes 229408 | tf_op jit(solution)/shard_map/ppermute | solution.py:19
  35.5 0.7 maximum_maximum_fusion
  36.1 0.2 slice_bitcast_fusion
  36.3 2.4 %add_multiply_fusion.5 = (f32[14,22,514]{2,1,0:T(8,128)S(1)}, f32[14,22,514]{2,1,0:T(8,128)}, f32[14,22,514]{2,1,0:T(8,128)S(1)}, f32[14,22,514]{2,1,0:T(8,128)S...) fusion(f32[16,24,512]{2,1,0:T(8,128)S(1)} %get-tuple-element.77), kind=kLoop, calls=%fused_computation.67 | loop fusion | flops 5224296 | bytes 5219168 | tf_op jit(solution)/shard_map/mul | solution.py:197
  38.7 2.0 %add_multiply_fusion.4 = (f32[14,22,514]{2,1,0:T(8,128)S(1)}, f32[14,22,514]{2,1,0:T(8,128)}, f32[14,22,514]{2,1,0:T(8,128)S(1)}, f32[14,22,514]{2,1,0:T(8,128)}) fusion(f32[14,22,514]{2,1,0:T(8,128)S(1)} %get-tuple-element.58, f32[14,22,514]{2,1,0:T(8,128)S(1)} %get-tuple-element.61, f32[14,22,514]{2,1,0:T(8,128)S(1)} %get-tuple-element.62, ...), kind=kLoop, calls=%fused_computation.66 | loop fusion | flops 4116112 | bytes 5699232 | tf_op jit(solution)/shard_map/mul | solution.py:198
  40.7 1.8 %multiply_add_fusion.8 = (f32[12,20,512]{2,1,0:T(8,128)S(1)}, f32[12,20,512]{2,1,0:T(8,128)S(1)}, f32[12,20,512]{2,1,0:T(8,128)S(1)}, f32[12,20,512]{2,1,0:T(8,128)S(1)}, f32[12,20,512]{2,1,0:T(8,128)S(1)}) fusion(f32[16,24,512]{2,1,0:T(8,128)S(1)} %get-tuple-element.76, f32[16,24,512]{2,1,0:T(8,128)S(1)} %get-tuple-element.77, ...), kind=kLoop, calls=%fused_computation.148 | loop fusion | flops 2580480 | bytes 8847360 | tf_op jit(solution)/shard_map/add | solution.py:209
  42.5 0.4 pad_slice_fusion.17
  42.8 1.1 add_multiply_fusion.8
  43.9 0.6 fusion.82
  44.5 0.5 fusion.62
  45.0 2.8 %fusion.105 = (f32[10,18,514]{2,1,0:T(8,128)S(1)}, f32[10,18,514]{2,1,0:T(8,128)S(1)}, f32[10,18,514]{2,1,0:T(8,128)S(1)}, f32[10,18,514]{2,1,0:T(8,128)S(1)}, f32[10,18,514]{2,1,0:T(8,128)S(1)}) fusion(f32[10,18,514]{2,1,0:T(8,128)S(1)} %get-tuple-element.40, f32[8,16,512]{2,1,0:T(8,128)S(1)} %get-tuple-element.127, ...), kind=kLoop, calls=%fused_computation.292 | loop fusion | flops 8604360 | bytes 3484928 | tf_op jit(solution)/shard_map/transpose(jvp())/neg | solution.py:188
  47.7 1.6 %fusion.107 = (f32[10,18,514]{2,1,0:T(8,128)S(1)}, f32[10,18,514]{2,1,0:T(8,128)S(1)}, f32[10,18,514]{2,1,0:T(8,128)S(1)}, f32[10,18,514]{2,1,0:T(8,128)S(1)}, f32[10,18,514]{2,1,0:T(8,128)S(1)}) fusion(f32[10,18,514]{2,1,0:T(8,128)S(1)} %get-tuple-element.41, f32[10,18,514]{2,1,0:T(8,128)S(1)} %get-tuple-element.49, ...), kind=kLoop, calls=%fused_computation.293 | loop fusion | flops 5643720 | bytes 4225088 | tf_op jit(solution)/shard_map/transpose(jvp())/neg | solution.py:187
  49.3 0.2 broadcast_multiply_fusion
  49.5 2.9 %fusion.42 = (f32[12,20,512]{2,1,0:T(8,128)}, f32[12,20,512]{2,1,0:T(8,128)S(1)}) fusion(f32[16,24,512]{2,1,0:T(8,128)S(1)} %get-tuple-element.76, f32[16,24,512]{2,1,0:T(8,128)S(1)} %get-tuple-element.75, f32[16,24,512]{2,1,0:T(8,128)S(1)} %get-tuple-element.77, f32[8,16,512]{2,1,0:T(8,128)S(1)} %get-tuple-element.43, ...), kind=kLoop, calls=%fused_computation.125 | loop fusion | flops 4177920 | bytes 5464564 | tf_op jit(solution)/shard_map/transpose(jvp())/add_any | solution.py:207
  52.4 2.1 %fusion.100 = (f32[12,20,512]{2,1,0:T(8,128)}, f32[12,20,512]{2,1,0:T(8,128)}, f32[12,20,512]{2,1,0:T(8,128)}, f32[12,20,512]{2,1,0:T(8,128)S(1)}) fusion(f32[12,20,512]{2,1,0:T(8,128)S(1)} %get-tuple-element.28, f32[16,24,512]{2,1,0:T(8,128)S(1)} %get-tuple-element.76, f32[16,24,512]{2,1,0:T(8,128)S(1)} %get-tuple-element.75, ...), kind=kLoop, calls=%fused_computation.291 | loop fusion | flops 3563520 | bytes 5439540 | tf_op jit(solution)/shard_map/transpose(jvp())/neg | solution.py:202
  54.6 0.8 copy-done.12
  55.4 1.4 %fusion.72 = f32[8,16,512]{2,1,0:T(8,128)} fusion(f32[10,18,514]{2,1,0:T(8,128)S(1)} %get-tuple-element.79, f32[10,18,514]{2,1,0:T(8,128)S(1)} %get-tuple-element.78, f32[10,18,514]{2,1,0:T(8,128)S(1)} %get-tuple-element.39, f32[12,20,512]{2,1,0:T(8,128)S(1)} %get-tuple-element.115, f32[8,16,512]{2,1,0:T(8,128)S(1)} %get-tuple-element.44, ...), kind=kLoop, calls=%fused_computation.195 | loop fusion | flops 1179648 | bytes 3145728 | tf_op jit(solution)/shard_map/add | solution.py:284
  56.8 1.8 %scatter-add.4 = f32[12,20,512]{2,1,0:T(8,128)} dynamic-update-slice(f32[12,20,512]{2,1,0:T(8,128)} %copy-done.12, f32[8,16,512]{2,1,0:T(8,128)} %fusion.72, s32[]{:T(128)} %constant.112.clone.1, s32[]{:T(128)} %constant.112.clone.1, s32[]{:T(128)} %constant.92.clone.1) | dynamic-update-slice | bytes 524292 | tf_op jit(solution)/shard_map/scatter-add | solution.py:284
  58.6 1.3 %pad_bitcast_fusion = f32[1,16,24,512]{3,2,1,0:T(8,128)S(1)} fusion(f32[12,20,512]{2,1,0:T(8,128)} %scatter-add.4), kind=kLoop, calls=%fused_computation.84 | loop fusion | bytes 1277952 | tf_op jit(solution)/shard_map/stack | solution.py:287
  60.1 0.1 copy-done.2
  60.2 0.3 copy-done.3
  60.4 5.5 %fusion.94 = (f32[14,22,514]{2,1,0:T(8,128)S(1)}, f32[14,22,514]{2,1,0:T(8,128)S(1)}, f32[14,22,514]{2,1,0:T(8,128)S(1)}, f32[14,22,514]{2,1,0:T(8,128)S(1)}) fusion(f32[14,22,514]{2,1,0:T(8,128)S(1)} %copy-done.1, f32[14,22,514]{2,1,0:T(8,128)} %get-tuple-element.70, f32[14,22,514]{2,1,0:T(8,128)S(1)} %get-tuple-element.58, ...), kind=kLoop, calls=%fused_computation.288 | loop fusion | flops 13298208 | bytes 8582016 | tf_op jit(solution)/shard_map/transpose(jvp())/neg | solution.py:188
  66.0 1.9 %fusion.96 = (f32[14,22,514]{2,1,0:T(8,128)S(1)}, f32[14,22,514]{2,1,0:T(8,128)S(1)}, f32[14,22,514]{2,1,0:T(8,128)S(1)}, f32[14,22,514]{2,1,0:T(8,128)S(1)}) fusion(f32[14,22,514]{2,1,0:T(8,128)S(1)} %get-tuple-element.61, f32[14,22,514]{2,1,0:T(8,128)S(1)} %get-tuple-element.32, f32[14,22,514]{2,1,0:T(8,128)S(1)} %get-tuple-element.31, ...), kind=kLoop, calls=%fused_computation.289 | loop fusion | flops 7598976 | bytes 9215264 | tf_op jit(solution)/shard_map/transpose(jvp())/neg | solution.py:187
  67.9 1.2 %fusion.21 = f32[1,16,24,512]{3,2,1,0:T(8,128)S(1)} fusion(f32[14,22,514]{2,1,0:T(8,128)S(1)} %get-tuple-element.68, f32[14,22,514]{2,1,0:T(8,128)S(1)} %get-tuple-element.67, f32[14,22,514]{2,1,0:T(8,128)S(1)} %get-tuple-element.34, f32[14,22,514]{2,1,0:T(8,128)S(1)} %get-tuple-element.33, f32[14,22,514]{2,1,0:T(8,128)S(1)} %get-tuple-element.30, ...), kind=kLoop, calls=%fused_computation.76 | loop fusion | flops 1179648 | bytes 5077440 | tf_op jit(solution)/shard_map/stack | solution.py:287
  69.3 0.2 add_bitcast_fusion
  69.6 0.1 fusion.56
  69.7 0.1 fusion.58
  69.8 2.1 %collective-permute-start.5 = (f32[33,4,512]{2,1,0:T(4,128)S(1)}, f32[33,4,512]{2,1,0:T(4,128)S(1)}, u32[]{:S(2)}, u32[]{:S(2)}) collective-permute-start(f32[33,4,512]{2,1,0:T(4,128)S(1)} %fusion.58), channel_id=1, source_target_pairs={{1,0},{2,1},{3,2},{4,3},{5,4},{6,5},{7,6},{9,8},{10,9},{11,10},{12... | collective-permute-start | bytes 811016 | tf_op jit(solution)/shard_map/ppermute | solution.py:19
  71.9 3.8 %collective-permute-start.4 = (f32[33,4,512]{2,1,0:T(4,128)S(1)}, f32[33,4,512]{2,1,0:T(4,128)S(1)}, u32[]{:S(2)}, u32[]{:S(2)}) collective-permute-start(f32[33,4,512]{2,1,0:T(4,128)S(1)} %fusion.56), channel_id=1, source_target_pairs={{0,1},{1,2},{2,3},{3,4},{4,5},{5,6},{6,7},{8,9},{9,10},{10,11},{11... | collective-permute-start | bytes 811016 | tf_op jit(solution)/shard_map/ppermute | solution.py:19
  75.7 5.4 %collective-permute-done.5 = f32[33,4,512]{2,1,0:T(4,128)S(1)} collective-permute-done((f32[33,4,512]{2,1,0:T(4,128)S(1)}, f32[33,4,512]{2,1,0:T(4,128)S(1)}, u32[]{:S(2)}, u32[]{:S(2)}) %collective-permute-start.5) | collective-permute-done | bytes 270368 | tf_op jit(solution)/shard_map/ppermute | solution.py:19
  81.1 4.0 %collective-permute-done.4 = f32[33,4,512]{2,1,0:T(4,128)S(1)} collective-permute-done((f32[33,4,512]{2,1,0:T(4,128)S(1)}, f32[33,4,512]{2,1,0:T(4,128)S(1)}, u32[]{:S(2)}, u32[]{:S(2)}) %collective-permute-start.4) | collective-permute-done | bytes 270368 | tf_op jit(solution)/shard_map/ppermute | solution.py:19
  85.5 0.3 maximum_add_fusion
  85.8 0.4 fusion.1
  86.4 5.9 %collective-permute-start.7 = (f32[9,16,512]{2,1,0:T(8,128)S(1)}, f32[9,16,512]{2,1,0:T(8,128)S(1)}, u32[]{:S(2)}, u32[]{:S(2)}) collective-permute-start(f32[9,16,512]{2,1,0:T(8,128)S(1)} %pad_maximum_fusion.2), channel_id=1, source_target_pairs={{8,0},{16,8},{24,16},{32,24},{40,32},{48,40},{56,48},{64,56},{72,6... | collective-permute-start | bytes 884744 | tf_op jit(solution)/shard_map/ppermute | solution.py:19
  92.3 1.9 %collective-permute-start.6 = (f32[9,16,512]{2,1,0:T(8,128)S(1)}, f32[9,16,512]{2,1,0:T(8,128)S(1)}, u32[]{:S(2)}, u32[]{:S(2)}) collective-permute-start(f32[9,16,512]{2,1,0:T(8,128)S(1)} %pad_maximum_fusion.3), channel_id=1, source_target_pairs={{0,8},{8,16},{16,24},{24,32},{32,40},{40,48},{48,56},{56,64},{64,7... | collective-permute-start | bytes 884744 | tf_op jit(solution)/shard_map/ppermute | solution.py:19
  94.2 5.2 %collective-permute-done.7 = f32[9,16,512]{2,1,0:T(8,128)S(1)} collective-permute-done((f32[9,16,512]{2,1,0:T(8,128)S(1)}, f32[9,16,512]{2,1,0:T(8,128)S(1)}, u32[]{:S(2)}, u32[]{:S(2)}) %collective-permute-start.7) | collective-permute-done | bytes 294944 | tf_op jit(solution)/shard_map/ppermute | solution.py:19
  99.4 6.3 %collective-permute-done.6 = f32[9,16,512]{2,1,0:T(8,128)S(1)} collective-permute-done((f32[9,16,512]{2,1,0:T(8,128)S(1)}, f32[9,16,512]{2,1,0:T(8,128)S(1)}, u32[]{:S(2)}, u32[]{:S(2)}) %collective-permute-start.6) | collective-permute-done | bytes 294944 | tf_op jit(solution)/shard_map/ppermute | solution.py:19
  105.8 0.2 slice_add_fusion.3
  106.0 0.9 fusion.67
  (87 shorter events, 1.5 us)
Async XLA Ops:
  0.6 18.7 %copy-start.4 = (f32[8,16,512]{2,1,0:T(8,128)S(1)}, f32[8,16,512]{2,1,0:T(8,128)}, u32[]{:S(2)}) copy-start(f32[8,16,512]{2,1,0:T(8,128)} %param.7) | copy-start | bytes 786436
  0.6 18.7 %copy-start.5 = (f32[8,16,512]{2,1,0:T(8,128)S(1)}, f32[8,16,512]{2,1,0:T(8,128)}, u32[]{:S(2)}) copy-start(f32[8,16,512]{2,1,0:T(8,128)} %param.8) | copy-start | bytes 786436
  0.7 18.7 %copy-start.6 = (f32[8,16,512]{2,1,0:T(8,128)S(1)}, f32[8,16,512]{2,1,0:T(8,128)}, u32[]{:S(2)}) copy-start(f32[8,16,512]{2,1,0:T(8,128)} %param.9) | copy-start | bytes 786436
  2.7 12.6 %collective-permute-start = (f32[8,16,512]{2,1,0:T(8,128)S(1)}, f32[8,16,512]{2,1,0:T(8,128)S(1)}, u32[]{:S(2)}, u32[]{:S(2)}) collective-permute-start(f32[8,16,512]{2,1,0:T(8,128)S(1)} %pad_maximum_fusion.5), channel_id=1, source_target_pairs={{0,8},{8,16},{16,24},{24,32},{32,40},{40,48},{48,56},{56,64},{64,7... | collective-permute-start | bytes 786440 | tf_op jit(solution)/shard_map/ppermute | solution.py:19
  4.7 14.6 %collective-permute-start.1 = (f32[8,16,512]{2,1,0:T(8,128)S(1)}, f32[8,16,512]{2,1,0:T(8,128)S(1)}, u32[]{:S(2)}, u32[]{:S(2)}) collective-permute-start(f32[8,16,512]{2,1,0:T(8,128)S(1)} %pad_maximum_fusion.6), channel_id=1, source_target_pairs={{8,0},{16,8},{24,16},{32,24},{40,32},{48,40},{56,48},{64,56},{72,6... | collective-permute-start | bytes 786440 | tf_op jit(solution)/shard_map/ppermute | solution.py:19
  19.4 2.2 %copy-start.11 = (f32[8,16,512]{2,1,0:T(8,128)S(1)}, f32[8,16,512]{2,1,0:T(8,128)}, u32[]{:S(2)}) copy-start(f32[8,16,512]{2,1,0:T(8,128)} %param.11) | copy-start | bytes 786436
  19.7 11.3 %collective-permute-start.2 = (f32[28,4,512]{2,1,0:T(4,128)S(1)}, f32[28,4,512]{2,1,0:T(4,128)S(1)}, u32[]{:S(2)}, u32[]{:S(2)}) collective-permute-start(f32[28,4,512]{2,1,0:T(4,128)S(1)} %maximum_maximum_fusion.2), channel_id=1, source_target_pairs={{0,1},{1,2},{2,3},{3,4},{4,5},{5,6},{6,7},{8,9},{9,10},{10,11},{11... | collective-permute-start | bytes 688136 | tf_op jit(solution)/shard_map/ppermute | solution.py:19
  21.7 13.6 %collective-permute-start.3 = (f32[28,4,512]{2,1,0:T(4,128)S(1)}, f32[28,4,512]{2,1,0:T(4,128)S(1)}, u32[]{:S(2)}, u32[]{:S(2)}) collective-permute-start(f32[28,4,512]{2,1,0:T(4,128)S(1)} %maximum_maximum_fusion.1), channel_id=1, source_target_pairs={{1,0},{2,1},{3,2},{4,3},{5,4},{6,5},{7,6},{9,8},{10,9},{11,10},{12... | collective-permute-start | bytes 688136 | tf_op jit(solution)/shard_map/ppermute | solution.py:19
  38.7 2.0 %copy-start = (f32[14,22,514]{2,1,0:T(8,128)}, f32[14,22,514]{2,1,0:T(8,128)S(1)}, u32[]{:S(2)}) copy-start(f32[14,22,514]{2,1,0:T(8,128)S(1)} %get-tuple-element.62) | copy-start | bytes 1899748
  42.5 1.4 %copy-start.15 = (f32[8,16,512]{2,1,0:T(8,128)S(1)}, f32[8,16,512]{2,1,0:T(8,128)}, u32[]{:S(2)}) copy-start(f32[8,16,512]{2,1,0:T(8,128)} %param.10) | copy-start | bytes 786436
  49.5 2.9 %copy-start.7 = (f32[12,20,512]{2,1,0:T(8,128)}, f32[12,20,512]{2,1,0:T(8,128)S(1)}, u32[]{:S(2)}) copy-start(f32[12,20,512]{2,1,0:T(8,128)S(1)} %broadcast_multiply_fusion) | copy-start | bytes 1474564
  54.6 0.8 copy-start.12
  58.6 1.5 %copy-start.1 = (f32[14,22,514]{2,1,0:T(8,128)S(1)}, f32[14,22,514]{2,1,0:T(8,128)}, u32[]{:S(2)}) copy-start(f32[14,22,514]{2,1,0:T(8,128)} %copy-done) | copy-start | bytes 1899748
  58.6 1.6 %copy-start.2 = (f32[14,22,514]{2,1,0:T(8,128)S(1)}, f32[14,22,514]{2,1,0:T(8,128)}, u32[]{:S(2)}) copy-start(f32[14,22,514]{2,1,0:T(8,128)} %get-tuple-element.64) | copy-start | bytes 1899748
  58.6 1.9 %copy-start.3 = (f32[14,22,514]{2,1,0:T(8,128)S(1)}, f32[14,22,514]{2,1,0:T(8,128)}, u32[]{:S(2)}) copy-start(f32[14,22,514]{2,1,0:T(8,128)} %get-tuple-element.57) | copy-start | bytes 1899748
  60.4 5.5 %copy-start.9 = (f32[12,20,512]{2,1,0:T(8,128)S(1)}, f32[12,20,512]{2,1,0:T(8,128)}, u32[]{:S(2)}) copy-start(f32[12,20,512]{2,1,0:T(8,128)} %get-tuple-element.37) | copy-start | bytes 1474564
  60.4 5.5 %copy-start.10 = (f32[12,20,512]{2,1,0:T(8,128)S(1)}, f32[12,20,512]{2,1,0:T(8,128)}, u32[]{:S(2)}) copy-start(f32[12,20,512]{2,1,0:T(8,128)} %get-tuple-element.38) | copy-start | bytes 1474564
  66.0 1.9 %copy-start.13 = (f32[12,20,512]{2,1,0:T(8,128)S(1)}, f32[12,20,512]{2,1,0:T(8,128)}, u32[]{:S(2)}) copy-start(f32[12,20,512]{2,1,0:T(8,128)} %get-tuple-element.27) | copy-start | bytes 1474564
  67.9 1.3 %copy-start.8 = (f32[12,20,512]{2,1,0:T(8,128)S(1)}, f32[12,20,512]{2,1,0:T(8,128)}, u32[]{:S(2)}) copy-start(f32[12,20,512]{2,1,0:T(8,128)} %copy-done.7) | copy-start | bytes 1474564
  67.9 1.3 %copy-start.14 = (f32[12,20,512]{2,1,0:T(8,128)S(1)}, f32[12,20,512]{2,1,0:T(8,128)}, u32[]{:S(2)}) copy-start(f32[12,20,512]{2,1,0:T(8,128)} %get-tuple-element.94) | copy-start | bytes 1474564
  69.8 11.2 %collective-permute-start.5 = (f32[33,4,512]{2,1,0:T(4,128)S(1)}, f32[33,4,512]{2,1,0:T(4,128)S(1)}, u32[]{:S(2)}, u32[]{:S(2)}) collective-permute-start(f32[33,4,512]{2,1,0:T(4,128)S(1)} %fusion.58), channel_id=1, source_target_pairs={{1,0},{2,1},{3,2},{4,3},{5,4},{6,5},{7,6},{9,8},{10,9},{11,10},{12... | collective-permute-start | bytes 811016 | tf_op jit(solution)/shard_map/ppermute | solution.py:19
  71.9 13.2 %collective-permute-start.4 = (f32[33,4,512]{2,1,0:T(4,128)S(1)}, f32[33,4,512]{2,1,0:T(4,128)S(1)}, u32[]{:S(2)}, u32[]{:S(2)}) collective-permute-start(f32[33,4,512]{2,1,0:T(4,128)S(1)} %fusion.56), channel_id=1, source_target_pairs={{0,1},{1,2},{2,3},{3,4},{4,5},{5,6},{6,7},{8,9},{9,10},{10,11},{11... | collective-permute-start | bytes 811016 | tf_op jit(solution)/shard_map/ppermute | solution.py:19
  86.4 13.0 %collective-permute-start.7 = (f32[9,16,512]{2,1,0:T(8,128)S(1)}, f32[9,16,512]{2,1,0:T(8,128)S(1)}, u32[]{:S(2)}, u32[]{:S(2)}) collective-permute-start(f32[9,16,512]{2,1,0:T(8,128)S(1)} %pad_maximum_fusion.2), channel_id=1, source_target_pairs={{8,0},{16,8},{24,16},{32,24},{40,32},{48,40},{56,48},{64,56},{72,6... | collective-permute-start | bytes 884744 | tf_op jit(solution)/shard_map/ppermute | solution.py:19
  92.3 13.4 %collective-permute-start.6 = (f32[9,16,512]{2,1,0:T(8,128)S(1)}, f32[9,16,512]{2,1,0:T(8,128)S(1)}, u32[]{:S(2)}, u32[]{:S(2)}) collective-permute-start(f32[9,16,512]{2,1,0:T(8,128)S(1)} %pad_maximum_fusion.3), channel_id=1, source_target_pairs={{0,8},{8,16},{16,24},{24,32},{32,40},{40,48},{48,56},{56,64},{64,7... | collective-permute-start | bytes 884744 | tf_op jit(solution)/shard_map/ppermute | solution.py:19

commit v15 on v13

--- a/solution.py
+++ b/solution.py
@@ -111,7 +111,6 @@
 
     lower = rims(0, 4, slice(0, 2))
     upper = rims(rows - 4, rows, slice(rows - 2, rows))
-    lower, upper = lax.optimization_barrier((lower, upper))
     from_above = from_behind(lower, "gy", -1)
     from_below = from_behind(upper, "gy", 1)
 

time: 96.7 us -> 96.6 us (level)
  waiting for transfers between devices: 35.9 us -> 34.8 us
  other arithmetic: 25.1 us -> 26.1 us
    ppermute x8, waiting for transfers between devices: 35.9 us -> 34.8 us  [from_behind(): return lax.ppermute(block, axis, route)]
  transfers between devices with their start and end apart: 8 -> 8, of which waited for: 8 -> 8; matrix products, arithmetic and copies ran while one was open for 0% -> 1% of each run, Pallas kernels for 0% -> 0%
where the time goes in v15:
time: 96.6 us; the launch traced here: 96.2 us
  waiting for transfers between devices  34.8 us (36%)
  starting transfers between devices  30.4 us (31%)
  other arithmetic  26.1 us (27%)
  local copies, waits for them, and re-layouts  3.56 us (4%)
  between operations  1.29 us (1%)
    ppermute x8, waiting for transfers between devices, from_behind(): return lax.ppermute(block, axis, route)  34.8 us
    ppermute x8, starting transfers between devices, from_behind(): return lax.ppermute(block, axis, route)  30.4 us
    neg x2, other arithmetic, advance_solver_step(): grad_x = 0.5 * (padded[1:-1, 1:-1, 2:] - padded[1:-1, 1:-1, :-2])  6.27 us
    neg x2, other arithmetic, advance_solver_step(): grad_y = 0.5 * (padded[1:-1, 2:, 1:-1] - padded[1:-1, :-2, 1:-1])  3.46 us
    add_any x2, other arithmetic, advance_solver_step(): 1.0 - phase_now  2.58 us
    mul x2, other arithmetic, advance_solver_step(): ENERGY_SCALE * (aniso_sq * grad_z + factor_a * grad_z * (sq_z - quartic *...  2.47 us
    slice x2, local copies, waits for them, and re-layouts, packed_z_halo(): tails = jnp.concatenate([f[size - w:] for f, w in zip(fields, widths)], 0)  2.01 us
  transfers between devices with their start and end apart: 8, of which 8 were waited for; matrix products, arithmetic and copies ran while one was open for 1% of the time, Pallas kernels for 0%

profile of v15, /device:TPU:14, one launch (start us, length us, event | category | flops | bytes accessed | tf_op | source)
XLA Modules:
  0.0 96.2 jit_solution(10732527585670622658)
XLA Ops:
  0.7 1.1 %fusion.121 = (f32[4,16,512]{2,1,0:T(8,128)S(1)}, f32[4,16,512]{2,1,0:T(8,128)S(1)}) fusion(f32[8,16,512]{2,1,0:T(8,128)} %param.5), kind=kLoop, calls=%fused_computation.300 | loop fusion | bytes 524288 | tf_op jit(solution)/shard_map/slice | solution.py:41
  1.7 1.0 fusion.122
  2.7 1.9 %collective-permute-start = (f32[8,16,512]{2,1,0:T(8,128)S(1)}, f32[8,16,512]{2,1,0:T(8,128)S(1)}, u32[]{:S(2)}, u32[]{:S(2)}) collective-permute-start(f32[8,16,512]{2,1,0:T(8,128)S(1)} %pad_maximum_fusion.5), channel_id=1, source_target_pairs={{0,8},{8,16},{16,24},{24,32},{32,40},{40,48},{48,56},{56,64},{64,7... | collective-permute-start | bytes 786440 | tf_op jit(solution)/shard_map/ppermute | solution.py:19
  4.7 7.9 %collective-permute-start.1 = (f32[8,16,512]{2,1,0:T(8,128)S(1)}, f32[8,16,512]{2,1,0:T(8,128)S(1)}, u32[]{:S(2)}, u32[]{:S(2)}) collective-permute-start(f32[8,16,512]{2,1,0:T(8,128)S(1)} %pad_maximum_fusion.6), channel_id=1, source_target_pairs={{8,0},{16,8},{24,16},{32,24},{40,32},{48,40},{56,48},{64,56},{72,6... | collective-permute-start | bytes 786440 | tf_op jit(solution)/shard_map/ppermute | solution.py:19
  12.6 1.0 %broadcast_multiply_fusion.3 = f32[8,16,512]{2,1,0:T(8,128)S(1)} fusion(f32[8,16,512]{2,1,0:T(8,128)} %param.9), kind=kLoop, calls=%fused_computation.263 | loop fusion | flops 65536 | bytes 524288 | tf_op jit(solution)/shard_map/transpose(jvp())/mul | solution.py:217
  13.6 1.7 %collective-permute-done = f32[8,16,512]{2,1,0:T(8,128)S(1)} collective-permute-done((f32[8,16,512]{2,1,0:T(8,128)S(1)}, f32[8,16,512]{2,1,0:T(8,128)S(1)}, u32[]{:S(2)}, u32[]{:S(2)}) %collective-permute-start) | collective-permute-done | bytes 262176 | tf_op jit(solution)/shard_map/ppermute | solution.py:19
  15.3 4.0 %collective-permute-done.1 = f32[8,16,512]{2,1,0:T(8,128)S(1)} collective-permute-done((f32[8,16,512]{2,1,0:T(8,128)S(1)}, f32[8,16,512]{2,1,0:T(8,128)S(1)}, u32[]{:S(2)}, u32[]{:S(2)}) %collective-permute-start.1) | collective-permute-done | bytes 262176 | tf_op jit(solution)/shard_map/ppermute | solution.py:19
  19.5 0.1 maximum_maximum_fusion.1
  19.6 1.9 %collective-permute-start.2 = (f32[28,4,512]{2,1,0:T(4,128)S(1)}, f32[28,4,512]{2,1,0:T(4,128)S(1)}, u32[]{:S(2)}, u32[]{:S(2)}) collective-permute-start(f32[28,4,512]{2,1,0:T(4,128)S(1)} %maximum_maximum_fusion.1), channel_id=1, source_target_pairs={{0,1},{1,2},{2,3},{3,4},{4,5},{5,6},{6,7},{8,9},{9,10},{10,11},{11... | collective-permute-start | bytes 688136 | tf_op jit(solution)/shard_map/ppermute | solution.py:19
  21.6 0.1 maximum_maximum_fusion.2
  21.7 4.8 %collective-permute-start.3 = (f32[28,4,512]{2,1,0:T(4,128)S(1)}, f32[28,4,512]{2,1,0:T(4,128)S(1)}, u32[]{:S(2)}, u32[]{:S(2)}) collective-permute-start(f32[28,4,512]{2,1,0:T(4,128)S(1)} %maximum_maximum_fusion.2), channel_id=1, source_target_pairs={{1,0},{2,1},{3,2},{4,3},{5,4},{6,5},{7,6},{9,8},{10,9},{11,10},{12... | collective-permute-start | bytes 688136 | tf_op jit(solution)/shard_map/ppermute | solution.py:19
  26.5 4.4 %collective-permute-done.2 = f32[28,4,512]{2,1,0:T(4,128)S(1)} collective-permute-done((f32[28,4,512]{2,1,0:T(4,128)S(1)}, f32[28,4,512]{2,1,0:T(4,128)S(1)}, u32[]{:S(2)}, u32[]{:S(2)}) %collective-permute-start.2) | collective-permute-done | bytes 229408 | tf_op jit(solution)/shard_map/ppermute | solution.py:19
  31.0 4.2 %collective-permute-done.3 = f32[28,4,512]{2,1,0:T(4,128)S(1)} collective-permute-done((f32[28,4,512]{2,1,0:T(4,128)S(1)}, f32[28,4,512]{2,1,0:T(4,128)S(1)}, u32[]{:S(2)}, u32[]{:S(2)}) %collective-permute-start.3) | collective-permute-done | bytes 229408 | tf_op jit(solution)/shard_map/ppermute | solution.py:19
  35.3 0.7 maximum_maximum_fusion
  36.0 0.2 slice_bitcast_fusion
  36.2 1.4 %add_multiply_fusion.5 = (f32[14,22,514]{2,1,0:T(8,128)S(1)}, f32[14,22,514]{2,1,0:T(8,128)S(1)}, f32[14,22,514]{2,1,0:T(8,128)S(1)}, f32[14,22,514]{2,1,0:T(8,1...) fusion(f32[16,24,512]{2,1,0:T(8,128)S(1)} %get-tuple-element.61), kind=kLoop, calls=%fused_computation.67 | loop fusion | flops 5224296 | bytes 5219168 | tf_op jit(solution)/shard_map/mul | solution.py:196
  37.6 0.8 add_multiply_fusion.4
  38.4 1.8 %multiply_add_fusion.8 = (f32[12,20,512]{2,1,0:T(8,128)S(1)}, f32[12,20,512]{2,1,0:T(8,128)S(1)}, f32[12,20,512]{2,1,0:T(8,128)S(1)}, f32[12,20,512]{2,1,0:T(8,128)S(1)}, f32[12,20,512]{2,1,0:T(8,128)S(1)}) fusion(f32[16,24,512]{2,1,0:T(8,128)S(1)} %get-tuple-element.60, f32[16,24,512]{2,1,0:T(8,128)S(1)} %get-tuple-element.61, ...), kind=kLoop, calls=%fused_computation.148 | loop fusion | flops 2580480 | bytes 8847360 | tf_op jit(solution)/shard_map/add | solution.py:208
  40.2 0.4 pad_slice_fusion.17
  40.6 1.1 %add_multiply_fusion.8 = (f32[10,18,514]{2,1,0:T(8,128)S(1)}, f32[10,18,514]{2,1,0:T(8,128)S(1)}, f32[10,18,514]{2,1,0:T(8,128)S(1)}, f32[10,18,514]{2,1,0:T(8,128)S(1)}) fusion(f32[12,20,512]{2,1,0:T(8,128)S(1)} %get-tuple-element.38), kind=kLoop, calls=%fused_computation.114 | loop fusion | flops 3053160 | bytes 1971840 | tf_op jit(solution)/shard_map/jvp()/mul | solution.py:196
  41.7 0.6 fusion.82
  42.2 0.5 fusion.62
  42.7 2.7 %fusion.105 = (f32[10,18,514]{2,1,0:T(8,128)S(1)}, f32[10,18,514]{2,1,0:T(8,128)S(1)}, f32[10,18,514]{2,1,0:T(8,128)S(1)}, f32[10,18,514]{2,1,0:T(8,128)S(1)}, f32[10,18,514]{2,1,0:T(8,128)S(1)}) fusion(f32[10,18,514]{2,1,0:T(8,128)S(1)} %get-tuple-element.12, f32[8,16,512]{2,1,0:T(8,128)S(1)} %get-tuple-element.110, ...), kind=kLoop, calls=%fused_computation.292 | loop fusion | flops 8604360 | bytes 3484928 | tf_op jit(solution)/shard_map/transpose(jvp())/neg | solution.py:187
  45.5 1.5 %fusion.107 = (f32[10,18,514]{2,1,0:T(8,128)S(1)}, f32[10,18,514]{2,1,0:T(8,128)S(1)}, f32[10,18,514]{2,1,0:T(8,128)S(1)}, f32[10,18,514]{2,1,0:T(8,128)S(1)}, f32[10,18,514]{2,1,0:T(8,128)S(1)}) fusion(f32[10,18,514]{2,1,0:T(8,128)S(1)} %get-tuple-element.13, f32[10,18,514]{2,1,0:T(8,128)S(1)} %get-tuple-element.33, ...), kind=kLoop, calls=%fused_computation.293 | loop fusion | flops 5643720 | bytes 4225088 | tf_op jit(solution)/shard_map/transpose(jvp())/neg | solution.py:186
  47.0 0.2 broadcast_multiply_fusion
  47.3 2.1 %fusion.42 = (f32[12,20,512]{2,1,0:T(8,128)S(1)}, f32[12,20,512]{2,1,0:T(8,128)S(1)}) fusion(f32[16,24,512]{2,1,0:T(8,128)S(1)} %get-tuple-element.60, f32[16,24,512]{2,1,0:T(8,128)S(1)} %get-tuple-element.59, f32[16,24,512]{2,1,0:T(8,128)S(1)} %get-tuple-element.61, f32[8,16,512]{2,1,0:T(8,128)S(1)} %get-tuple-element.27, ...), kind=kLoop, calls=%fused_computation.125 | loop fusion | flops 4177920 | bytes 5464564 | tf_op jit(solution)/shard_map/transpose(jvp())/add_any | solution.py:206
  49.4 1.0 %fusion.103 = (f32[12,20,512]{2,1,0:T(8,128)S(1)}, f32[12,20,512]{2,1,0:T(8,128)S(1)}, f32[12,20,512]{2,1,0:T(8,128)S(1)}, f32[12,20,512]{2,1,0:T(8,128)S(1)}) fusion(f32[12,20,512]{2,1,0:T(8,128)S(1)} %get-tuple-element.16, f32[16,24,512]{2,1,0:T(8,128)S(1)} %get-tuple-element.60, f32[16,24,512]{2,1,0:T(8,128)S(1)} %get-tuple-element.59, ...), kind=kLoop, calls=%fused_computation.291 | loop fusion | flops 3563520 | bytes 5439540 | tf_op jit(solution)/shard_map/transpose(jvp())/neg | solution.py:201
  50.4 0.1 pad_bitcast_fusion
  50.6 3.5 %fusion.97 = (f32[14,22,514]{2,1,0:T(8,128)S(1)}, f32[14,22,514]{2,1,0:T(8,128)S(1)}, f32[14,22,514]{2,1,0:T(8,128)S(1)}, f32[14,22,514]{2,1,0:T(8,128)S(1)}) fusion(f32[14,22,514]{2,1,0:T(8,128)S(1)} %get-tuple-element.46, f32[14,22,514]{2,1,0:T(8,128)S(1)} %get-tuple-element.54, f32[14,22,514]{2,1,0:T(8,128)S(1)} %get-tuple-element.42, ...), kind=kLoop, calls=%fused_computation.288 | loop fusion | flops 13298208 | bytes 8582016 | tf_op jit(solution)/shard_map/transpose(jvp())/neg | solution.py:187
  54.1 1.9 %fusion.99 = (f32[14,22,514]{2,1,0:T(8,128)S(1)}, f32[14,22,514]{2,1,0:T(8,128)S(1)}, f32[14,22,514]{2,1,0:T(8,128)S(1)}, f32[14,22,514]{2,1,0:T(8,128)S(1)}) fusion(f32[14,22,514]{2,1,0:T(8,128)S(1)} %get-tuple-element.45, f32[14,22,514]{2,1,0:T(8,128)S(1)} %get-tuple-element.20, f32[14,22,514]{2,1,0:T(8,128)S(1)} %get-tuple-element.19, ...), kind=kLoop, calls=%fused_computation.289 | loop fusion | flops 7598976 | bytes 9215264 | tf_op jit(solution)/shard_map/transpose(jvp())/neg | solution.py:186
  56.0 1.2 %fusion.21 = f32[1,16,24,512]{3,2,1,0:T(8,128)S(1)} fusion(f32[14,22,514]{2,1,0:T(8,128)S(1)} %get-tuple-element.52, f32[14,22,514]{2,1,0:T(8,128)S(1)} %get-tuple-element.51, f32[14,22,514]{2,1,0:T(8,128)S(1)} %get-tuple-element.22, f32[14,22,514]{2,1,0:T(8,128)S(1)} %get-tuple-element.21, f32[14,22,514]{2,1,0:T(8,128)S(1)} %get-tuple-element.18, ...), kind=kLoop, calls=%fused_computation.76 | loop fusion | flops 1179648 | bytes 5077440 | tf_op jit(solution)/shard_map/stack | solution.py:285
  57.3 0.2 add_bitcast_fusion
  57.7 0.1 fusion.56
  57.8 0.1 fusion.58
  57.9 2.1 %collective-permute-start.5 = (f32[33,4,512]{2,1,0:T(4,128)S(1)}, f32[33,4,512]{2,1,0:T(4,128)S(1)}, u32[]{:S(2)}, u32[]{:S(2)}) collective-permute-start(f32[33,4,512]{2,1,0:T(4,128)S(1)} %fusion.58), channel_id=1, source_target_pairs={{1,0},{2,1},{3,2},{4,3},{5,4},{6,5},{7,6},{9,8},{10,9},{11,10},{12... | collective-permute-start | bytes 811016 | tf_op jit(solution)/shard_map/ppermute | solution.py:19
  60.0 4.0 %collective-permute-start.4 = (f32[33,4,512]{2,1,0:T(4,128)S(1)}, f32[33,4,512]{2,1,0:T(4,128)S(1)}, u32[]{:S(2)}, u32[]{:S(2)}) collective-permute-start(f32[33,4,512]{2,1,0:T(4,128)S(1)} %fusion.56), channel_id=1, source_target_pairs={{0,1},{1,2},{2,3},{3,4},{4,5},{5,6},{6,7},{8,9},{9,10},{10,11},{11... | collective-permute-start | bytes 811016 | tf_op jit(solution)/shard_map/ppermute | solution.py:19
  64.0 5.2 %collective-permute-done.5 = f32[33,4,512]{2,1,0:T(4,128)S(1)} collective-permute-done((f32[33,4,512]{2,1,0:T(4,128)S(1)}, f32[33,4,512]{2,1,0:T(4,128)S(1)}, u32[]{:S(2)}, u32[]{:S(2)}) %collective-permute-start.5) | collective-permute-done | bytes 270368 | tf_op jit(solution)/shard_map/ppermute | solution.py:19
  69.2 4.0 %collective-permute-done.4 = f32[33,4,512]{2,1,0:T(4,128)S(1)} collective-permute-done((f32[33,4,512]{2,1,0:T(4,128)S(1)}, f32[33,4,512]{2,1,0:T(4,128)S(1)}, u32[]{:S(2)}, u32[]{:S(2)}) %collective-permute-start.4) | collective-permute-done | bytes 270368 | tf_op jit(solution)/shard_map/ppermute | solution.py:19
  73.3 0.1 fusion.84
  73.6 0.3 maximum_add_fusion
  73.9 0.4 fusion.1
  74.4 5.9 %collective-permute-start.7 = (f32[9,16,512]{2,1,0:T(8,128)S(1)}, f32[9,16,512]{2,1,0:T(8,128)S(1)}, u32[]{:S(2)}, u32[]{:S(2)}) collective-permute-start(f32[9,16,512]{2,1,0:T(8,128)S(1)} %pad_maximum_fusion.2), channel_id=1, source_target_pairs={{8,0},{16,8},{24,16},{32,24},{40,32},{48,40},{56,48},{64,56},{72,6... | collective-permute-start | bytes 884744 | tf_op jit(solution)/shard_map/ppermute | solution.py:19
  80.3 1.9 %collective-permute-start.6 = (f32[9,16,512]{2,1,0:T(8,128)S(1)}, f32[9,16,512]{2,1,0:T(8,128)S(1)}, u32[]{:S(2)}, u32[]{:S(2)}) collective-permute-start(f32[9,16,512]{2,1,0:T(8,128)S(1)} %pad_maximum_fusion.3), channel_id=1, source_target_pairs={{0,8},{8,16},{16,24},{24,32},{32,40},{40,48},{48,56},{56,64},{64,7... | collective-permute-start | bytes 884744 | tf_op jit(solution)/shard_map/ppermute | solution.py:19
  82.2 5.1 %collective-permute-done.7 = f32[9,16,512]{2,1,0:T(8,128)S(1)} collective-permute-done((f32[9,16,512]{2,1,0:T(8,128)S(1)}, f32[9,16,512]{2,1,0:T(8,128)S(1)}, u32[]{:S(2)}, u32[]{:S(2)}) %collective-permute-start.7) | collective-permute-done | bytes 294944 | tf_op jit(solution)/shard_map/ppermute | solution.py:19
  87.4 6.3 %collective-permute-done.6 = f32[9,16,512]{2,1,0:T(8,128)S(1)} collective-permute-done((f32[9,16,512]{2,1,0:T(8,128)S(1)}, f32[9,16,512]{2,1,0:T(8,128)S(1)}, u32[]{:S(2)}, u32[]{:S(2)}) %collective-permute-start.6) | collective-permute-done | bytes 294944 | tf_op jit(solution)/shard_map/ppermute | solution.py:19
  93.8 0.2 slice_add_fusion.3
  94.0 0.8 fusion.64
  94.8 1.4 %fusion.68 = f32[8,16,512]{2,1,0:T(8,128)} fusion(f32[3,4,16,512]{3,2,1,0:T(8,128)S(1)} %get-tuple-element.64, f32[3,4,16,512]{3,2,1,0:T(8,128)S(1)} %get-tuple-element.65, f32[10,18,514]{2,1,0:T(8,128)S(1)} %get-tuple-element.63, f32[10,18,514]{2,1,0:T(8,128)S(1)} %get-tuple-element.62, f32[10,18,514]{2,1,0:T(8,128)S(1)} %get-tuple-element.11, ...), kind=kLoop, calls=%fused_computation.190 | loop fusion | flops 1245184 | bytes 3670016 | tf_op jit(solution)/shard_map/add | solution.py:288
  (64 shorter events, 1.2 us)
Async XLA Ops:
  0.6 18.7 %copy-start = (f32[8,16,512]{2,1,0:T(8,128)S(1)}, f32[8,16,512]{2,1,0:T(8,128)}, u32[]{:S(2)}) copy-start(f32[8,16,512]{2,1,0:T(8,128)} %param.5) | copy-start | bytes 786436
  0.6 18.7 %copy-start.1 = (f32[8,16,512]{2,1,0:T(8,128)S(1)}, f32[8,16,512]{2,1,0:T(8,128)}, u32[]{:S(2)}) copy-start(f32[8,16,512]{2,1,0:T(8,128)} %param.6) | copy-start | bytes 786436
  0.7 18.7 %copy-start.2 = (f32[8,16,512]{2,1,0:T(8,128)S(1)}, f32[8,16,512]{2,1,0:T(8,128)}, u32[]{:S(2)}) copy-start(f32[8,16,512]{2,1,0:T(8,128)} %param.7) | copy-start | bytes 786436
  2.7 12.6 %collective-permute-start = (f32[8,16,512]{2,1,0:T(8,128)S(1)}, f32[8,16,512]{2,1,0:T(8,128)S(1)}, u32[]{:S(2)}, u32[]{:S(2)}) collective-permute-start(f32[8,16,512]{2,1,0:T(8,128)S(1)} %pad_maximum_fusion.5), channel_id=1, source_target_pairs={{0,8},{8,16},{16,24},{24,32},{32,40},{40,48},{48,56},{56,64},{64,7... | collective-permute-start | bytes 786440 | tf_op jit(solution)/shard_map/ppermute | solution.py:19
  4.7 14.6 %collective-permute-start.1 = (f32[8,16,512]{2,1,0:T(8,128)S(1)}, f32[8,16,512]{2,1,0:T(8,128)S(1)}, u32[]{:S(2)}, u32[]{:S(2)}) collective-permute-start(f32[8,16,512]{2,1,0:T(8,128)S(1)} %pad_maximum_fusion.6), channel_id=1, source_target_pairs={{8,0},{16,8},{24,16},{32,24},{40,32},{48,40},{56,48},{64,56},{72,6... | collective-permute-start | bytes 786440 | tf_op jit(solution)/shard_map/ppermute | solution.py:19
  19.6 11.3 %collective-permute-start.2 = (f32[28,4,512]{2,1,0:T(4,128)S(1)}, f32[28,4,512]{2,1,0:T(4,128)S(1)}, u32[]{:S(2)}, u32[]{:S(2)}) collective-permute-start(f32[28,4,512]{2,1,0:T(4,128)S(1)} %maximum_maximum_fusion.1), channel_id=1, source_target_pairs={{0,1},{1,2},{2,3},{3,4},{4,5},{5,6},{6,7},{8,9},{9,10},{10,11},{11... | collective-permute-start | bytes 688136 | tf_op jit(solution)/shard_map/ppermute | solution.py:19
  21.7 13.5 %collective-permute-start.3 = (f32[28,4,512]{2,1,0:T(4,128)S(1)}, f32[28,4,512]{2,1,0:T(4,128)S(1)}, u32[]{:S(2)}, u32[]{:S(2)}) collective-permute-start(f32[28,4,512]{2,1,0:T(4,128)S(1)} %maximum_maximum_fusion.2), channel_id=1, source_target_pairs={{1,0},{2,1},{3,2},{4,3},{5,4},{6,5},{7,6},{9,8},{10,9},{11,10},{12... | collective-permute-start | bytes 688136 | tf_op jit(solution)/shard_map/ppermute | solution.py:19
  40.2 1.5 %copy-start.3 = (f32[8,16,512]{2,1,0:T(8,128)S(1)}, f32[8,16,512]{2,1,0:T(8,128)}, u32[]{:S(2)}) copy-start(f32[8,16,512]{2,1,0:T(8,128)} %param.9) | copy-start | bytes 786436
  40.2 1.4 %copy-start.4 = (f32[8,16,512]{2,1,0:T(8,128)S(1)}, f32[8,16,512]{2,1,0:T(8,128)}, u32[]{:S(2)}) copy-start(f32[8,16,512]{2,1,0:T(8,128)} %param.8) | copy-start | bytes 786436
  57.9 11.2 %collective-permute-start.5 = (f32[33,4,512]{2,1,0:T(4,128)S(1)}, f32[33,4,512]{2,1,0:T(4,128)S(1)}, u32[]{:S(2)}, u32[]{:S(2)}) collective-permute-start(f32[33,4,512]{2,1,0:T(4,128)S(1)} %fusion.58), channel_id=1, source_target_pairs={{1,0},{2,1},{3,2},{4,3},{5,4},{6,5},{7,6},{9,8},{10,9},{11,10},{12... | collective-permute-start | bytes 811016 | tf_op jit(solution)/shard_map/ppermute | solution.py:19
  60.0 13.2 %collective-permute-start.4 = (f32[33,4,512]{2,1,0:T(4,128)S(1)}, f32[33,4,512]{2,1,0:T(4,128)S(1)}, u32[]{:S(2)}, u32[]{:S(2)}) collective-permute-start(f32[33,4,512]{2,1,0:T(4,128)S(1)} %fusion.56), channel_id=1, source_target_pairs={{0,1},{1,2},{2,3},{3,4},{4,5},{5,6},{6,7},{8,9},{9,10},{10,11},{11... | collective-permute-start | bytes 811016 | tf_op jit(solution)/shard_map/ppermute | solution.py:19
  74.4 12.9 %collective-permute-start.7 = (f32[9,16,512]{2,1,0:T(8,128)S(1)}, f32[9,16,512]{2,1,0:T(8,128)S(1)}, u32[]{:S(2)}, u32[]{:S(2)}) collective-permute-start(f32[9,16,512]{2,1,0:T(8,128)S(1)} %pad_maximum_fusion.2), channel_id=1, source_target_pairs={{8,0},{16,8},{24,16},{32,24},{40,32},{48,40},{56,48},{64,56},{72,6... | collective-permute-start | bytes 884744 | tf_op jit(solution)/shard_map/ppermute | solution.py:19
  80.3 13.4 %collective-permute-start.6 = (f32[9,16,512]{2,1,0:T(8,128)S(1)}, f32[9,16,512]{2,1,0:T(8,128)S(1)}, u32[]{:S(2)}, u32[]{:S(2)}) collective-permute-start(f32[9,16,512]{2,1,0:T(8,128)S(1)} %pad_maximum_fusion.3), channel_id=1, source_target_pairs={{0,8},{8,16},{16,24},{24,32},{32,40},{40,48},{48,56},{56,64},{64,7... | collective-permute-start | bytes 884744 | tf_op jit(solution)/shard_map/ppermute | solution.py:19
